TPU v7x, 32 devices: a whole 2x2x4 slice. The times are simulated.
32 devices in a mesh: section: 4 (over z), dp: 8 (over y, x, core).
Axes of the slice: x: 2, y: 2, z: 4, core: 2. Of those that a mesh axis runs over, the one named last changes fastest.
Arguments:
- layer_inputs: bfloat16 [4, 8, 128, 2560], P('section', 'dp'), may hold values from -6 to 6
- w_bc: bfloat16 [4, 2560, 256], P('section'), may hold values from -0.125 to 0.125
- log_decay: float32 [4, 8, 128, 40], P('section', 'dp'), may hold values from -1.7 to 0, as said below
- top_grad: bfloat16 [8, 128, 2560], P('dp'), may hold values from -6 to 6
Outputs:
- grad_inputs: bfloat16 [4, 8, 128, 2560], P('section', 'dp')
- grad_w: float32 [4, 2560, 256], P('section', 'dp')
Inputs may be any that keep to these rules, and one draw needn't show every extreme that they name: `log_decay`: every entry is negative.
All inputs are finite; a program needn't handle non-finite values.
Results may differ from a plain program's by a relative error of at most 0.0085.
Values may be sent and summed in bfloat16 or wider, within the bound.
No kernel may reach another device: no remote copies, remote signals or barrier semaphores. Data moves between devices by JAX's collectives and lax.ppermute only.
A program may use at most 64 MiB of HBM per device.

v0:
```python
import jax
import jax.numpy as jnp
from jax import lax
from jax.sharding import PartitionSpec as P

MICRO = 4


def shortened(value):
    return jax.tree.map(lambda a: a.astype(jnp.bfloat16) if a.dtype == jnp.float32 else a, value)


def passed_along(block, axis, distance):
    devices = range(lax.axis_size(axis))
    route = [(i - distance, i) for i in devices if i - distance in devices]
    return lax.ppermute(block, axis, route)


def block_terms(inputs_b, in_b, out_b, rates, grads_b, carried, state_in, factor):
    length = inputs_b.shape[0]
    cumulative = jnp.cumsum(rates, axis=0)
    ending = cumulative[-1]
    locations = jnp.arange(length)
    lower_mask = (locations[:, None] >= locations[None, :])[:, :, None]
    spread = jnp.where(lower_mask, cumulative[:, None, :] - cumulative[None, :, :], 0.0)
    decays = jnp.where(lower_mask, jnp.exp(spread), 0.0)
    tail_decay = jnp.exp(ending[None, :] - cumulative)
    leading = jnp.exp(cumulative)
    scores = jnp.dot(out_b, in_b.T, preferred_element_type=jnp.float32)
    weighted = (factor * decays * scores[:, :, None]).astype(jnp.bfloat16)
    carried_b = carried.astype(jnp.bfloat16)
    state_b = state_in.astype(jnp.bfloat16)
    grad_feats = jnp.einsum("kjh,khp->jhp", weighted, grads_b, preferred_element_type=jnp.float32)
    grad_feats = grad_feats + tail_decay[:, :, None] * jnp.einsum(
        "hpn,jn->jhp", carried_b, in_b, preferred_element_type=jnp.float32
    )
    pair_dots = jnp.einsum("khp,jhp->kjh", grads_b, inputs_b, preferred_element_type=jnp.float32)
    mixing = jnp.sum(decays * pair_dots, axis=2).astype(jnp.bfloat16)
    tail_inputs = (tail_decay[:, :, None] * inputs_b.astype(jnp.float32)).astype(jnp.bfloat16)
    lead_grads = (leading[:, :, None] * grads_b.astype(jnp.float32)).astype(jnp.bfloat16)
    grad_inmap = factor * jnp.dot(mixing.T, out_b, preferred_element_type=jnp.float32)
    grad_inmap = grad_inmap + jnp.einsum(
        "jhp,hpn->jn", tail_inputs, carried_b, preferred_element_type=jnp.float32
    )
    grad_outmap = factor * (
        jnp.dot(mixing, in_b, preferred_element_type=jnp.float32)
        + jnp.einsum("ihp,hpn->in", lead_grads, state_b, preferred_element_type=jnp.float32)
    )
    carry_out = factor * jnp.einsum(
        "khp,kn->hpn", lead_grads, out_b, preferred_element_type=jnp.float32
    )
    carry_out = carry_out + jnp.exp(ending)[:, None, None] * carried
    return (grad_feats, grad_inmap, grad_outmap, carry_out)


def block_end(inputs_b, in_b, rates, state_in):
    cumulative = jnp.cumsum(rates, axis=0)
    ending = cumulative[-1]
    tail_decay = jnp.exp(ending[None, :] - cumulative)
    tail_inputs = (tail_decay[:, :, None] * inputs_b.astype(jnp.float32)).astype(jnp.bfloat16)
    fresh = jnp.einsum("jhp,jn->hpn", tail_inputs, in_b, preferred_element_type=jnp.float32)
    return jnp.exp(ending)[:, None, None] * state_in + fresh


def split_block(inputs_c, map_block, head_count):
    length, features = inputs_c.shape
    state_size = map_block.shape[1] // 2
    inputs_b = inputs_c.reshape(length, head_count, features // head_count)
    in_b = map_block[:, :state_size]
    out_b = map_block[:, state_size:]
    return (inputs_b, in_b, out_b)


def block_back(inputs_c, map_block, rates, grads_c, carried, state_in, weights):
    length, features = inputs_c.shape
    head_count = rates.shape[1]
    factor = 0.25 / (map_block.shape[1] // 2)
    inputs_b, in_b, out_b = split_block(inputs_c, map_block, head_count)
    grads_b = grads_c.reshape(length, head_count, features // head_count)
    grad_feats, grad_inmap, grad_outmap, carry_out = block_terms(
        inputs_b, in_b, out_b, rates, grads_b, carried, state_in, factor
    )
    grad_bc = jnp.concatenate([grad_inmap, grad_outmap], axis=1).astype(jnp.bfloat16)
    back_proj = lax.dot_general(
        grad_bc, weights, (((1,), (1,)), ((), ())), preferred_element_type=jnp.float32
    )
    summed = grads_c.astype(jnp.float32) + grad_feats.reshape(length, features) + back_proj
    return (summed.astype(jnp.bfloat16), carry_out, grad_bc)


def layer_starts(inputs_s, bc_s, rates_s):
    head_count = rates_s.shape[1]
    features = inputs_s.shape[1]
    state_size = bc_s.shape[1] // 2
    block_len = inputs_s.shape[0] // MICRO
    state_now = jnp.zeros((head_count, features // head_count, state_size), jnp.float32)
    saved = []
    for block_no in range(MICRO):
        lo_row = block_no * block_len
        inputs_b, in_b, out_b = split_block(
            inputs_s[lo_row : lo_row + block_len], bc_s[lo_row : lo_row + block_len], head_count
        )
        saved.append(state_now)
        state_now = block_end(inputs_b, in_b, rates_s[lo_row : lo_row + block_len], state_now)
    return jnp.stack(saved)


def shards(layer_inputs, w_bc, log_decay, top_grad):
    sections = lax.axis_size("section")
    section_id = lax.axis_index("section")
    lay_dev, seq_dev, tok_len, features = layer_inputs.shape
    block_len = tok_len // MICRO
    bc_all = jnp.einsum(
        "lstd,ldc->lstc", layer_inputs, w_bc, preferred_element_type=jnp.float32
    ).astype(jnp.bfloat16)
    starts = jax.vmap(jax.vmap(layer_starts))(layer_inputs, bc_all, log_decay)
    is_top = section_id == sections - 1
    back_all = jax.vmap(block_back, in_axes=(0, 0, 0, 0, 0, 0, None))

    def advance(counter, loop_state):
        incoming, carried, grad_store, map_store = loop_state
        offset = counter - (sections - 1 - section_id)
        is_valid = (offset >= 0) & (offset < MICRO)
        block_no = jnp.clip(MICRO - 1 - offset, 0, MICRO - 1)
        row_start = block_no * block_len
        from_top = lax.dynamic_slice_in_dim(top_grad, row_start, block_len, 1)
        grad_block = jnp.where(is_top, from_top, incoming)

        def compute(stores):
            carried_in, grads_in, maps_in = stores
            current = grad_block
            for level_no in reversed(range(lay_dev)):
                inputs_c = lax.dynamic_slice_in_dim(layer_inputs[level_no], row_start, block_len, 1)
                map_block = lax.dynamic_slice_in_dim(bc_all[level_no], row_start, block_len, 1)
                rates = lax.dynamic_slice_in_dim(log_decay[level_no], row_start, block_len, 1)
                state_in = lax.dynamic_index_in_dim(starts[level_no], block_no, 1, keepdims=False)
                level_grads, carry_out, grad_bc = back_all(
                    inputs_c,
                    map_block,
                    rates,
                    current,
                    carried_in[level_no],
                    state_in,
                    w_bc[level_no],
                )
                carried_in = carried_in.at[level_no].set(carry_out)
                grads_in = grads_in.at[level_no].set(
                    lax.dynamic_update_slice_in_dim(grads_in[level_no], level_grads, row_start, 1)
                )
                maps_in = maps_in.at[level_no].set(
                    lax.dynamic_update_slice_in_dim(maps_in[level_no], grad_bc, row_start, 1)
                )
                current = level_grads
            return (current, (carried_in, grads_in, maps_in))

        def passing(stores):
            return (jnp.zeros_like(grad_block), stores)

        outgoing, updated = lax.cond(is_valid, compute, passing, (carried, grad_store, map_store))
        received = jax.tree.map(
            lambda part, own: part.astype(own.dtype),
            passed_along(shortened(outgoing), "section", -1),
            outgoing,
        )
        return (received, updated[0], updated[1], updated[2])

    initial = (
        jnp.zeros((seq_dev, block_len, features), jnp.bfloat16),
        jnp.zeros((lay_dev,) + starts.shape[1:2] + starts.shape[3:], jnp.float32),
        jnp.zeros(layer_inputs.shape, jnp.bfloat16),
        jnp.zeros(bc_all.shape, jnp.bfloat16),
    )
    final_state = lax.fori_loop(0, MICRO + sections - 1, advance, initial)
    grad_inputs = final_state[2]
    map_store = final_state[3]
    divisor = lax.axis_size("dp") * seq_dev
    whole_terms = jnp.einsum(
        "lstd,lstc->ldc", layer_inputs, map_store, preferred_element_type=jnp.float32
    )
    grad_w = lax.psum_scatter(whole_terms, "dp", scatter_dimension=1, tiled=True) / divisor
    return (grad_inputs, grad_w)


def solution(mesh):
    in_specs = (
        P("section", "dp", None, None),
        P("section", None, None),
        P("section", "dp", None, None),
        P("dp", None, None),
    )
    out_specs = (P("section", "dp", None, None), P("section", "dp", None))
    return jax.shard_map(shards, mesh=mesh, in_specs=in_specs, out_specs=out_specs, check_vma=False)
```

profile of v0, /device:TPU:0, one launch (start us, length us, event | category | flops | bytes accessed | tf_op | source)
XLA Modules:
  0.0 236.4 jit_solution(6625981571378955069)
XLA Ops:
  8.6 1.4 copy.65
  12.9 1.4 fusion.60
  16.0 1.9 pad_maximum_fusion
  19.6 139.3 %while.24 = (s32[]{:T(128)}, bf16[1,32,2560]{2,1,0:T(8,128)(2,1)S(1)}, f32[1,1,40,64,128]{4,3,2,1,0:T(8,128)S(1)}, bf16[1,1,128,2560]{3,2,1,0:T(8,128)(2,1)}, bf...) while((s32[]{:T(128)}, ...), condition=%wide.region_8.9_spmd, body=%wide.region_3.8_spmd.sunk | while | flops 140346368 | bytes 17553168 | solution.py:173
  19.6 1.3 collective-permute-start
  20.9 7.8 %collective-permute-done = bf16[1,32,2560]{2,1,0:T(8,128)(2,1)S(1)} collective-permute-done((bf16[1,32,2560]{2,1,0:T(8,128)(2,1)S(1)}, bf16[1,32,2560]{2,1,0:T(8,128)(2,1)S(1)}, u32[]{:S(2)}, u32[]{:S(2)}) %collective-permute-start) | collective-permute-done | bytes 163872 | tf_op jit(solution)/shard_map/while/body/eval_jaxpr/ppermute | solution.py:16
  28.8 1.3 collective-permute-start
  30.1 6.0 %collective-permute-done = bf16[1,32,2560]{2,1,0:T(8,128)(2,1)S(1)} collective-permute-done((bf16[1,32,2560]{2,1,0:T(8,128)(2,1)S(1)}, bf16[1,32,2560]{2,1,0:T(8,128)(2,1)S(1)}, u32[]{:S(2)}, u32[]{:S(2)}) %collective-permute-start) | collective-permute-done | bytes 163872 | tf_op jit(solution)/shard_map/while/body/eval_jaxpr/ppermute | solution.py:16
  36.1 1.3 collective-permute-start
  37.4 42.3 %collective-permute-done = bf16[1,32,2560]{2,1,0:T(8,128)(2,1)S(1)} collective-permute-done((bf16[1,32,2560]{2,1,0:T(8,128)(2,1)S(1)}, bf16[1,32,2560]{2,1,0:T(8,128)(2,1)S(1)}, u32[]{:S(2)}, u32[]{:S(2)}) %collective-permute-start) | collective-permute-done | bytes 163872 | tf_op jit(solution)/shard_map/while/body/eval_jaxpr/ppermute | solution.py:16
  79.7 12.6 %conditional.2 = (bf16[1,32,2560]{2,1,0:T(8,128)(2,1)S(1)}, f32[1,1,40,64,128]{4,3,2,1,0:T(8,128)S(1)}, bf16[1,1,128,2560]{3,2,1,0:T(8,128)(2,1)}, bf16[1,1,128,256]{3,2,1,0:T(8,128)(2,1)}) conditional(s32[]{:T(128)} %convert_element_type.236, (f32[1,1,40,64,128]{4,3,2,1,0:T(8,128)S(1)}, bf16[1,1,128,2560]{3,2,1,0:T(8,128)(2,1)}, ...), branch_computations={%region_4.4_spmd, %region_5.7_spmd} | conditional | flops 140346368 | bytes 16897460 | solution.py:159
  85.1 1.4 fusion.13
  89.1 2.5 %bitcast_dynamic-update-slice_fusion = (bf16[1,1,128,2560]{3,2,1,0:T(8,128)(2,1)}, bf16[1,32,2560]{2,1,0:T(8,128)(2,1)S(1)}) fusion(bf16[1,1,128,2560]{3,2,1,0:T(8,128)(2,1)} %get-tuple-element.483, s32[]{:T(128)S(6)} %select_n.90, bf16[1,2560,256]{2,1,0:T(8,128)(2,1)} %get-tuple-element.482, bf16[32,128]{1,0:T(8,128)(2,1)S(1)} %fusion.13, ...), kind=kOutput, calls=%fused_computation.46 | convolution fusion | flops 42303488 | bytes 2146308 | tf_op jit(solution)/shard_map/while/body/eval_jaxpr/cond/branch_1_fun/vmap()/dot_general | solution.py:84
  92.3 1.3 collective-permute-start
  93.6 5.9 %collective-permute-done = bf16[1,32,2560]{2,1,0:T(8,128)(2,1)S(1)} collective-permute-done((bf16[1,32,2560]{2,1,0:T(8,128)(2,1)S(1)}, bf16[1,32,2560]{2,1,0:T(8,128)(2,1)S(1)}, u32[]{:S(2)}, u32[]{:S(2)}) %collective-permute-start) | collective-permute-done | bytes 163872 | tf_op jit(solution)/shard_map/while/body/eval_jaxpr/ppermute | solution.py:16
  99.5 12.6 %conditional.2 = (bf16[1,32,2560]{2,1,0:T(8,128)(2,1)S(1)}, f32[1,1,40,64,128]{4,3,2,1,0:T(8,128)S(1)}, bf16[1,1,128,2560]{3,2,1,0:T(8,128)(2,1)}, bf16[1,1,128,256]{3,2,1,0:T(8,128)(2,1)}) conditional(s32[]{:T(128)} %convert_element_type.236, (f32[1,1,40,64,128]{4,3,2,1,0:T(8,128)S(1)}, bf16[1,1,128,2560]{3,2,1,0:T(8,128)(2,1)}, ...), branch_computations={%region_4.4_spmd, %region_5.7_spmd} | conditional | flops 140346368 | bytes 16897460 | solution.py:159
  104.9 1.4 fusion.13
  108.9 2.5 %bitcast_dynamic-update-slice_fusion = (bf16[1,1,128,2560]{3,2,1,0:T(8,128)(2,1)}, bf16[1,32,2560]{2,1,0:T(8,128)(2,1)S(1)}) fusion(bf16[1,1,128,2560]{3,2,1,0:T(8,128)(2,1)} %get-tuple-element.483, s32[]{:T(128)S(6)} %select_n.90, bf16[1,2560,256]{2,1,0:T(8,128)(2,1)} %get-tuple-element.482, bf16[32,128]{1,0:T(8,128)(2,1)S(1)} %fusion.13, ...), kind=kOutput, calls=%fused_computation.46 | convolution fusion | flops 42303488 | bytes 2146308 | tf_op jit(solution)/shard_map/while/body/eval_jaxpr/cond/branch_1_fun/vmap()/dot_general | solution.py:84
  112.1 1.3 collective-permute-start
  113.4 5.9 %collective-permute-done = bf16[1,32,2560]{2,1,0:T(8,128)(2,1)S(1)} collective-permute-done((bf16[1,32,2560]{2,1,0:T(8,128)(2,1)S(1)}, bf16[1,32,2560]{2,1,0:T(8,128)(2,1)S(1)}, u32[]{:S(2)}, u32[]{:S(2)}) %collective-permute-start) | collective-permute-done | bytes 163872 | tf_op jit(solution)/shard_map/while/body/eval_jaxpr/ppermute | solution.py:16
  119.3 12.6 %conditional.2 = (bf16[1,32,2560]{2,1,0:T(8,128)(2,1)S(1)}, f32[1,1,40,64,128]{4,3,2,1,0:T(8,128)S(1)}, bf16[1,1,128,2560]{3,2,1,0:T(8,128)(2,1)}, bf16[1,1,128,256]{3,2,1,0:T(8,128)(2,1)}) conditional(s32[]{:T(128)} %convert_element_type.236, (f32[1,1,40,64,128]{4,3,2,1,0:T(8,128)S(1)}, bf16[1,1,128,2560]{3,2,1,0:T(8,128)(2,1)}, ...), branch_computations={%region_4.4_spmd, %region_5.7_spmd} | conditional | flops 140346368 | bytes 16897460 | solution.py:159
  124.7 1.4 fusion.13
  128.7 2.5 %bitcast_dynamic-update-slice_fusion = (bf16[1,1,128,2560]{3,2,1,0:T(8,128)(2,1)}, bf16[1,32,2560]{2,1,0:T(8,128)(2,1)S(1)}) fusion(bf16[1,1,128,2560]{3,2,1,0:T(8,128)(2,1)} %get-tuple-element.483, s32[]{:T(128)S(6)} %select_n.90, bf16[1,2560,256]{2,1,0:T(8,128)(2,1)} %get-tuple-element.482, bf16[32,128]{1,0:T(8,128)(2,1)S(1)} %fusion.13, ...), kind=kOutput, calls=%fused_computation.46 | convolution fusion | flops 42303488 | bytes 2146308 | tf_op jit(solution)/shard_map/while/body/eval_jaxpr/cond/branch_1_fun/vmap()/dot_general | solution.py:84
  131.9 1.3 collective-permute-start
  133.2 5.9 %collective-permute-done = bf16[1,32,2560]{2,1,0:T(8,128)(2,1)S(1)} collective-permute-done((bf16[1,32,2560]{2,1,0:T(8,128)(2,1)S(1)}, bf16[1,32,2560]{2,1,0:T(8,128)(2,1)S(1)}, u32[]{:S(2)}, u32[]{:S(2)}) %collective-permute-start) | collective-permute-done | bytes 163872 | tf_op jit(solution)/shard_map/while/body/eval_jaxpr/ppermute | solution.py:16
  139.1 12.6 %conditional.2 = (bf16[1,32,2560]{2,1,0:T(8,128)(2,1)S(1)}, f32[1,1,40,64,128]{4,3,2,1,0:T(8,128)S(1)}, bf16[1,1,128,2560]{3,2,1,0:T(8,128)(2,1)}, bf16[1,1,128,256]{3,2,1,0:T(8,128)(2,1)}) conditional(s32[]{:T(128)} %convert_element_type.236, (f32[1,1,40,64,128]{4,3,2,1,0:T(8,128)S(1)}, bf16[1,1,128,2560]{3,2,1,0:T(8,128)(2,1)}, ...), branch_computations={%region_4.4_spmd, %region_5.7_spmd} | conditional | flops 140346368 | bytes 16897460 | solution.py:159
  144.5 1.4 fusion.13
  148.5 2.5 %bitcast_dynamic-update-slice_fusion = (bf16[1,1,128,2560]{3,2,1,0:T(8,128)(2,1)}, bf16[1,32,2560]{2,1,0:T(8,128)(2,1)S(1)}) fusion(bf16[1,1,128,2560]{3,2,1,0:T(8,128)(2,1)} %get-tuple-element.483, s32[]{:T(128)S(6)} %select_n.90, bf16[1,2560,256]{2,1,0:T(8,128)(2,1)} %get-tuple-element.482, bf16[32,128]{1,0:T(8,128)(2,1)S(1)} %fusion.13, ...), kind=kOutput, calls=%fused_computation.46 | convolution fusion | flops 42303488 | bytes 2146308 | tf_op jit(solution)/shard_map/while/body/eval_jaxpr/cond/branch_1_fun/vmap()/dot_general | solution.py:84
  153.0 5.9 %collective-permute-done = bf16[1,32,2560]{2,1,0:T(8,128)(2,1)S(1)} collective-permute-done((bf16[1,32,2560]{2,1,0:T(8,128)(2,1)S(1)}, bf16[1,32,2560]{2,1,0:T(8,128)(2,1)S(1)}, u32[]{:S(2)}, u32[]{:S(2)}) %collective-permute-start) | collective-permute-done | bytes 163872 | tf_op jit(solution)/shard_map/while/body/eval_jaxpr/ppermute | solution.py:16
  158.9 1.6 convolution_bitcast_fusion.5
  160.5 4.0 %copy.66 = f32[1,2560,256]{2,0,1:T(1,128)} copy(f32[1,2560,256]{1,2,0:T(8,128)S(1)} %convolution_bitcast_fusion.5) | data formatting | bytes 5242880 | tf_op jit(solution)/shard_map/lstd,lstc->ldc/dot_general | solution.py:177
  166.4 61.1 %all-reduce.3.cloned.1.call-done = f32[1,2560,256]{2,0,1:T(1,128)} async-done(((f32[1,2560,256]{2,0,1:T(1,128)}), f32[1,2560,256]{2,0,1:T(1,128)}) %all-reduce.3.cloned.1.call-update) | async-done | bytes 2621456
  (174 shorter events, 46.4 us)
Async XLA Ops:
  7.2 220.4 %all-reduce.3.cloned.1.call-start = ((), (), s32[]{:S(2)}) async-start(), calls=%async_computation | async-start | bytes 5242880
  11.4 1.6 copy-start
  19.6 9.1 %collective-permute-start = (bf16[1,32,2560]{2,1,0:T(8,128)(2,1)S(1)}, bf16[1,32,2560]{2,1,0:T(8,128)(2,1)S(1)}, u32[]{:S(2)}, u32[]{:S(2)}) collective-permute-start(bf16[1,32,2560]{2,1,0:T(8,128)(2,1)S(1)} %get-tuple-element.677), channel_id=1, source_target_pairs={{8,0},{16,8},{24,16},{9,1},{17,9},{25,17},{10,2},{18,10},{26,18},{... | collective-permute-start | bytes 491528 | tf_op jit(solution)/shard_map/while/body/eval_jaxpr/ppermute | solution.py:16
  28.8 7.3 %collective-permute-start = (bf16[1,32,2560]{2,1,0:T(8,128)(2,1)S(1)}, bf16[1,32,2560]{2,1,0:T(8,128)(2,1)S(1)}, u32[]{:S(2)}, u32[]{:S(2)}) collective-permute-start(bf16[1,32,2560]{2,1,0:T(8,128)(2,1)S(1)} %get-tuple-element.677), channel_id=1, source_target_pairs={{8,0},{16,8},{24,16},{9,1},{17,9},{25,17},{10,2},{18,10},{26,18},{... | collective-permute-start | bytes 491528 | tf_op jit(solution)/shard_map/while/body/eval_jaxpr/ppermute | solution.py:16
  36.1 43.6 %collective-permute-start = (bf16[1,32,2560]{2,1,0:T(8,128)(2,1)S(1)}, bf16[1,32,2560]{2,1,0:T(8,128)(2,1)S(1)}, u32[]{:S(2)}, u32[]{:S(2)}) collective-permute-start(bf16[1,32,2560]{2,1,0:T(8,128)(2,1)S(1)} %get-tuple-element.677), channel_id=1, source_target_pairs={{8,0},{16,8},{24,16},{9,1},{17,9},{25,17},{10,2},{18,10},{26,18},{... | collective-permute-start | bytes 491528 | tf_op jit(solution)/shard_map/while/body/eval_jaxpr/ppermute | solution.py:16
  92.3 7.2 %collective-permute-start = (bf16[1,32,2560]{2,1,0:T(8,128)(2,1)S(1)}, bf16[1,32,2560]{2,1,0:T(8,128)(2,1)S(1)}, u32[]{:S(2)}, u32[]{:S(2)}) collective-permute-start(bf16[1,32,2560]{2,1,0:T(8,128)(2,1)S(1)} %get-tuple-element.677), channel_id=1, source_target_pairs={{8,0},{16,8},{24,16},{9,1},{17,9},{25,17},{10,2},{18,10},{26,18},{... | collective-permute-start | bytes 491528 | tf_op jit(solution)/shard_map/while/body/eval_jaxpr/ppermute | solution.py:16
  112.1 7.2 %collective-permute-start = (bf16[1,32,2560]{2,1,0:T(8,128)(2,1)S(1)}, bf16[1,32,2560]{2,1,0:T(8,128)(2,1)S(1)}, u32[]{:S(2)}, u32[]{:S(2)}) collective-permute-start(bf16[1,32,2560]{2,1,0:T(8,128)(2,1)S(1)} %get-tuple-element.677), channel_id=1, source_target_pairs={{8,0},{16,8},{24,16},{9,1},{17,9},{25,17},{10,2},{18,10},{26,18},{... | collective-permute-start | bytes 491528 | tf_op jit(solution)/shard_map/while/body/eval_jaxpr/ppermute | solution.py:16
  131.9 7.2 %collective-permute-start = (bf16[1,32,2560]{2,1,0:T(8,128)(2,1)S(1)}, bf16[1,32,2560]{2,1,0:T(8,128)(2,1)S(1)}, u32[]{:S(2)}, u32[]{:S(2)}) collective-permute-start(bf16[1,32,2560]{2,1,0:T(8,128)(2,1)S(1)} %get-tuple-element.677), channel_id=1, source_target_pairs={{8,0},{16,8},{24,16},{9,1},{17,9},{25,17},{10,2},{18,10},{26,18},{... | collective-permute-start | bytes 491528 | tf_op jit(solution)/shard_map/while/body/eval_jaxpr/ppermute | solution.py:16
  151.7 7.2 %collective-permute-start = (bf16[1,32,2560]{2,1,0:T(8,128)(2,1)S(1)}, bf16[1,32,2560]{2,1,0:T(8,128)(2,1)S(1)}, u32[]{:S(2)}, u32[]{:S(2)}) collective-permute-start(bf16[1,32,2560]{2,1,0:T(8,128)(2,1)S(1)} %get-tuple-element.677), channel_id=1, source_target_pairs={{8,0},{16,8},{24,16},{9,1},{17,9},{25,17},{10,2},{18,10},{26,18},{... | collective-permute-start | bytes 491528 | tf_op jit(solution)/shard_map/while/body/eval_jaxpr/ppermute | solution.py:16
  164.5 0.7 copy-start.1
Sparse Core Ops, SparseCore 0:
  164.7 62.8 all-reduce.2
where the time goes:
time: 238 us; the launch traced here: 236 us
  waiting for transfers between devices  141 us (59%)
  matrix products  30.8 us (13%)
  local copies, waits for them, and re-layouts  24.9 us (10%)
  other arithmetic  15.2 us (6%)
  between operations  14.9 us (6%)
  starting transfers between devices  9.08 us (4%)
    ppermute x7, waiting for transfers between devices, passed_along(): return lax.ppermute(block, axis, route)  79.8 us
    unnamed x2, waiting for transfers between devices  61.1 us
    dot_general x4, matrix products, block_back(): lax.dot_general(grad_bc, weights, (((1,), (1,)), ((), ())), preferred_ele...  9.93 us
    ppermute x7, starting transfers between devices, passed_along(): return lax.ppermute(block, axis, route)  9.04 us
    dot_general x4, matrix products, block_terms(): jnp.einsum('ihp,hpn->in', lead_grads, state_b, preferred_element_type=jnp...  5.47 us
  transfers between devices with their start and end apart: 8, of which 8 were waited for; matrix products, arithmetic and copies ran while one was open for 0% of the time, Pallas kernels for 0%

commit v1 on v0

--- a/solution.py
+++ b/solution.py
@@ -173,11 +173,15 @@
     final_state = lax.fori_loop(0, MICRO + sections - 1, advance, initial)
     grad_inputs = final_state[2]
     map_store = final_state[3]
-    divisor = lax.axis_size("dp") * seq_dev
-    whole_terms = jnp.einsum(
-        "lstd,lstc->ldc", layer_inputs, map_store, preferred_element_type=jnp.float32
-    )
-    grad_w = lax.psum_scatter(whole_terms, "dp", scatter_dimension=1, tiled=True) / divisor
+    ways = lax.axis_size("dp")
+    divisor = ways * seq_dev
+    rows_here = layer_inputs.reshape(lay_dev, seq_dev * tok_len, features)
+    rows_all = lax.all_to_all(rows_here, "dp", 2, 1, tiled=True)
+    maps_here = map_store.reshape(lay_dev, seq_dev * tok_len, map_store.shape[-1])
+    maps_all = lax.all_gather(maps_here, "dp", axis=1, tiled=True)
+    grad_w = jnp.einsum(
+        "lrd,lrc->ldc", rows_all, maps_all, preferred_element_type=jnp.float32
+    ) / divisor
     return (grad_inputs, grad_w)
 
 

time: 238 us -> 190 us (0.80)
  waiting for transfers between devices: 141 us -> 79.9 us
  between operations: 14.9 us -> 0.86 us
  other arithmetic: 15.2 us -> 28.2 us
  blocking collectives: 0 us -> 10.2 us
  starting transfers between devices: 9.08 us -> 14.2 us
    unnamed x2 -> x0, waiting for transfers between devices: 61.1 us -> none
    unnamed x0 -> x1, other arithmetic: none -> 14.3 us
    all_gather x0 -> x1, blocking collectives: none -> 10.2 us  [shards(): maps_all = lax.all_gather(maps_here, 'dp', axis=1, tiled=True)]
    all_to_all x0 -> x1, starting transfers between devices: none -> 5.17 us  [shards(): rows_all = lax.all_to_all(rows_here, 'dp', 2, 1, tiled=True)]
    dot_general x1 -> x0, local copies, waits for them, and re-layouts: 4.02 us -> none  [shards(): jnp.einsum('lstd,lstc->ldc', layer_inputs, map_store, preferred_element_t...]
    reshape x0 -> x1, local copies, waits for them, and re-layouts: none -> 2.51 us  [shards(): rows_here = layer_inputs.reshape(lay_dev, seq_dev * tok_len, features)]
  transfers between devices with their start and end apart: 8 -> 8, of which waited for: 8 -> 7; matrix products, arithmetic and copies ran while one was open for 0% -> 32% of each run, Pallas kernels for 0% -> 0%
where the time goes in v1:
time: 190 us; the launch traced here: 189 us
  waiting for transfers between devices  79.9 us (42%)
  matrix products  30.2 us (16%)
  other arithmetic  28.2 us (15%)
  local copies, waits for them, and re-layouts  24.2 us (13%)
  starting transfers between devices  14.2 us (7%)
  blocking collectives  10.2 us (5%)
    ppermute x7, waiting for transfers between devices, passed_along(): return lax.ppermute(block, axis, route)  79.9 us
    unnamed x1, other arithmetic  14.3 us
    all_gather x1, blocking collectives, shards(): maps_all = lax.all_gather(maps_here, 'dp', axis=1, tiled=True)  10.2 us
    dot_general x4, matrix products, block_back(): lax.dot_general(grad_bc, weights, (((1,), (1,)), ((), ())), preferred_ele...  9.94 us
    ppermute x7, starting transfers between devices, passed_along(): return lax.ppermute(block, axis, route)  9.04 us
    dot_general x4, matrix products, block_terms(): jnp.einsum('ihp,hpn->in', lead_grads, state_b, preferred_element_type=jnp...  5.47 us
    all_to_all x1, starting transfers between devices, shards(): rows_all = lax.all_to_all(rows_here, 'dp', 2, 1, tiled=True)  5.17 us
    unnamed x8, local copies, waits for them, and re-layouts  4 us
  transfers between devices with their start and end apart: 8, of which 7 were waited for; matrix products, arithmetic and copies ran while one was open for 32% of the time, Pallas kernels for 0%

profile of v1, /device:TPU:0, one launch (start us, length us, event | category | flops | bytes accessed | tf_op | source)
XLA Modules:
  0.0 188.5 jit_solution(8316372705247162726)
XLA Ops:
  0.6 2.5 %copy.89 = bf16[1,128,2560]{1,0,2:T(2,128)(2,1)S(1)} copy(bf16[1,128,2560]{2,1,0:T(8,128)(2,1)} %bitcast.43) | data formatting | bytes 1310720 | tf_op jit(solution)/shard_map/reshape | solution.py:178
  3.7 14.3 %reduce.10 = bf16[2560,128]{1,0:T(8,128)(2,1)S(1)} reduce(bf16[2560,1,128]{2,1,0:T(2,128)(2,1)S(1)} %bitcast.178, bf16[]{:T(256)} %broadcast.353), dimensions={1}, to_apply=%bitcast.170.reduce_sub_computation | reduce | bytes 1310722
  18.9 5.2 %all-to-all-start = ((bf16[8,2,20480]{2,1,0:T(2,128)(2,1)}), bf16[8,2,20480]{2,1,0:T(2,128)(2,1)}, u32[]{:S(2)}, u32[]{:S(2)}) async-start(bf16[8,2,20480]{2,1,0:T(2,128)(2,1)} %reshape.676), calls=%async_computation | async-start | bytes 1310720 | tf_op jit(solution)/shard_map/all_to_all | solution.py:179
  28.2 1.4 fusion.61
  31.3 1.9 %pad_maximum_fusion = bf16[1,1,4,40,64,128]{5,4,3,2,1,0:T(8,128)(2,1)} fusion(bf16[1,1,1,40,64,128]{5,4,3,2,1,0:T(8,128)(2,1)S(1)} %fusion.54, f32[1,1,1,40,64,128]{5,4,3,2,1,0:T(8,128)S(1)} %bitcast.177, f32[1,1,1,40,64,128]{5,4,3,2,1,0:T(8,128)S(1)} %bitcast.176, bf16[4]{0:T(256)(128)(2,1)S(1)} %pad.10.clone), kind=kLoop, calls=%fused_computation.78 | loop fusion | flops 3932160 | bytes 5898248 | tf_op jit(solution)/shard_map/vmap(vmap())/stack | solution.py:105
  34.9 139.4 %while.24 = (s32[]{:T(128)}, bf16[1,32,2560]{2,1,0:T(8,128)(2,1)S(1)}, f32[1,1,40,64,128]{4,3,2,1,0:T(8,128)S(1)}, bf16[1,1,128,2560]{3,2,1,0:T(8,128)(2,1)}, bf...) while((s32[]{:T(128)}, ...), condition=%wide.region_8.9_spmd, body=%wide.region_3.8_spmd.sunk | while | flops 140346368 | bytes 17553168 | solution.py:173
  35.0 1.3 collective-permute-start
  36.3 7.4 %collective-permute-done = bf16[1,32,2560]{2,1,0:T(8,128)(2,1)S(1)} collective-permute-done((bf16[1,32,2560]{2,1,0:T(8,128)(2,1)S(1)}, bf16[1,32,2560]{2,1,0:T(8,128)(2,1)S(1)}, u32[]{:S(2)}, u32[]{:S(2)}) %collective-permute-start) | collective-permute-done | bytes 163872 | tf_op jit(solution)/shard_map/while/body/eval_jaxpr/ppermute | solution.py:16
  43.7 1.3 collective-permute-start
  45.0 6.4 %collective-permute-done = bf16[1,32,2560]{2,1,0:T(8,128)(2,1)S(1)} collective-permute-done((bf16[1,32,2560]{2,1,0:T(8,128)(2,1)S(1)}, bf16[1,32,2560]{2,1,0:T(8,128)(2,1)S(1)}, u32[]{:S(2)}, u32[]{:S(2)}) %collective-permute-start) | collective-permute-done | bytes 163872 | tf_op jit(solution)/shard_map/while/body/eval_jaxpr/ppermute | solution.py:16
  51.4 1.3 collective-permute-start
  52.7 42.5 %collective-permute-done = bf16[1,32,2560]{2,1,0:T(8,128)(2,1)S(1)} collective-permute-done((bf16[1,32,2560]{2,1,0:T(8,128)(2,1)S(1)}, bf16[1,32,2560]{2,1,0:T(8,128)(2,1)S(1)}, u32[]{:S(2)}, u32[]{:S(2)}) %collective-permute-start) | collective-permute-done | bytes 163872 | tf_op jit(solution)/shard_map/while/body/eval_jaxpr/ppermute | solution.py:16
  95.2 12.6 %conditional.2 = (bf16[1,32,2560]{2,1,0:T(8,128)(2,1)S(1)}, f32[1,1,40,64,128]{4,3,2,1,0:T(8,128)S(1)}, bf16[1,1,128,2560]{3,2,1,0:T(8,128)(2,1)}, bf16[1,1,128,256]{3,2,1,0:T(8,128)(2,1)}) conditional(s32[]{:T(128)} %convert_element_type.236, (f32[1,1,40,64,128]{4,3,2,1,0:T(8,128)S(1)}, bf16[1,1,128,2560]{3,2,1,0:T(8,128)(2,1)}, ...), branch_computations={%region_4.4_spmd, %region_5.7_spmd} | conditional | flops 140346368 | bytes 16897460 | solution.py:159
  100.6 1.4 fusion.13
  104.6 2.5 %bitcast_dynamic-update-slice_fusion = (bf16[1,1,128,2560]{3,2,1,0:T(8,128)(2,1)}, bf16[1,32,2560]{2,1,0:T(8,128)(2,1)S(1)}) fusion(bf16[1,1,128,2560]{3,2,1,0:T(8,128)(2,1)} %get-tuple-element.483, s32[]{:T(128)S(6)} %select_n.90, bf16[1,2560,256]{2,1,0:T(8,128)(2,1)} %get-tuple-element.482, bf16[32,128]{1,0:T(8,128)(2,1)S(1)} %fusion.13, ...), kind=kOutput, calls=%fused_computation.46 | convolution fusion | flops 42303488 | bytes 2146308 | tf_op jit(solution)/shard_map/while/body/eval_jaxpr/cond/branch_1_fun/vmap()/dot_general | solution.py:84
  107.8 1.3 collective-permute-start
  109.1 5.9 %collective-permute-done = bf16[1,32,2560]{2,1,0:T(8,128)(2,1)S(1)} collective-permute-done((bf16[1,32,2560]{2,1,0:T(8,128)(2,1)S(1)}, bf16[1,32,2560]{2,1,0:T(8,128)(2,1)S(1)}, u32[]{:S(2)}, u32[]{:S(2)}) %collective-permute-start) | collective-permute-done | bytes 163872 | tf_op jit(solution)/shard_map/while/body/eval_jaxpr/ppermute | solution.py:16
  115.0 12.6 %conditional.2 = (bf16[1,32,2560]{2,1,0:T(8,128)(2,1)S(1)}, f32[1,1,40,64,128]{4,3,2,1,0:T(8,128)S(1)}, bf16[1,1,128,2560]{3,2,1,0:T(8,128)(2,1)}, bf16[1,1,128,256]{3,2,1,0:T(8,128)(2,1)}) conditional(s32[]{:T(128)} %convert_element_type.236, (f32[1,1,40,64,128]{4,3,2,1,0:T(8,128)S(1)}, bf16[1,1,128,2560]{3,2,1,0:T(8,128)(2,1)}, ...), branch_computations={%region_4.4_spmd, %region_5.7_spmd} | conditional | flops 140346368 | bytes 16897460 | solution.py:159
  120.4 1.4 fusion.13
  124.4 2.5 %bitcast_dynamic-update-slice_fusion = (bf16[1,1,128,2560]{3,2,1,0:T(8,128)(2,1)}, bf16[1,32,2560]{2,1,0:T(8,128)(2,1)S(1)}) fusion(bf16[1,1,128,2560]{3,2,1,0:T(8,128)(2,1)} %get-tuple-element.483, s32[]{:T(128)S(6)} %select_n.90, bf16[1,2560,256]{2,1,0:T(8,128)(2,1)} %get-tuple-element.482, bf16[32,128]{1,0:T(8,128)(2,1)S(1)} %fusion.13, ...), kind=kOutput, calls=%fused_computation.46 | convolution fusion | flops 42303488 | bytes 2146308 | tf_op jit(solution)/shard_map/while/body/eval_jaxpr/cond/branch_1_fun/vmap()/dot_general | solution.py:84
  127.6 1.3 collective-permute-start
  128.9 5.9 %collective-permute-done = bf16[1,32,2560]{2,1,0:T(8,128)(2,1)S(1)} collective-permute-done((bf16[1,32,2560]{2,1,0:T(8,128)(2,1)S(1)}, bf16[1,32,2560]{2,1,0:T(8,128)(2,1)S(1)}, u32[]{:S(2)}, u32[]{:S(2)}) %collective-permute-start) | collective-permute-done | bytes 163872 | tf_op jit(solution)/shard_map/while/body/eval_jaxpr/ppermute | solution.py:16
  134.8 12.6 %conditional.2 = (bf16[1,32,2560]{2,1,0:T(8,128)(2,1)S(1)}, f32[1,1,40,64,128]{4,3,2,1,0:T(8,128)S(1)}, bf16[1,1,128,2560]{3,2,1,0:T(8,128)(2,1)}, bf16[1,1,128,256]{3,2,1,0:T(8,128)(2,1)}) conditional(s32[]{:T(128)} %convert_element_type.236, (f32[1,1,40,64,128]{4,3,2,1,0:T(8,128)S(1)}, bf16[1,1,128,2560]{3,2,1,0:T(8,128)(2,1)}, ...), branch_computations={%region_4.4_spmd, %region_5.7_spmd} | conditional | flops 140346368 | bytes 16897460 | solution.py:159
  140.2 1.4 fusion.13
  144.2 2.5 %bitcast_dynamic-update-slice_fusion = (bf16[1,1,128,2560]{3,2,1,0:T(8,128)(2,1)}, bf16[1,32,2560]{2,1,0:T(8,128)(2,1)S(1)}) fusion(bf16[1,1,128,2560]{3,2,1,0:T(8,128)(2,1)} %get-tuple-element.483, s32[]{:T(128)S(6)} %select_n.90, bf16[1,2560,256]{2,1,0:T(8,128)(2,1)} %get-tuple-element.482, bf16[32,128]{1,0:T(8,128)(2,1)S(1)} %fusion.13, ...), kind=kOutput, calls=%fused_computation.46 | convolution fusion | flops 42303488 | bytes 2146308 | tf_op jit(solution)/shard_map/while/body/eval_jaxpr/cond/branch_1_fun/vmap()/dot_general | solution.py:84
  148.7 5.9 %collective-permute-done = bf16[1,32,2560]{2,1,0:T(8,128)(2,1)S(1)} collective-permute-done((bf16[1,32,2560]{2,1,0:T(8,128)(2,1)S(1)}, bf16[1,32,2560]{2,1,0:T(8,128)(2,1)S(1)}, u32[]{:S(2)}, u32[]{:S(2)}) %collective-permute-start) | collective-permute-done | bytes 163872 | tf_op jit(solution)/shard_map/while/body/eval_jaxpr/ppermute | solution.py:16
  154.6 12.6 %conditional.2 = (bf16[1,32,2560]{2,1,0:T(8,128)(2,1)S(1)}, f32[1,1,40,64,128]{4,3,2,1,0:T(8,128)S(1)}, bf16[1,1,128,2560]{3,2,1,0:T(8,128)(2,1)}, bf16[1,1,128,256]{3,2,1,0:T(8,128)(2,1)}) conditional(s32[]{:T(128)} %convert_element_type.236, (f32[1,1,40,64,128]{4,3,2,1,0:T(8,128)S(1)}, bf16[1,1,128,2560]{3,2,1,0:T(8,128)(2,1)}, ...), branch_computations={%region_4.4_spmd, %region_5.7_spmd} | conditional | flops 140346368 | bytes 16897460 | solution.py:159
  160.0 1.4 fusion.13
  164.0 2.5 %bitcast_dynamic-update-slice_fusion = (bf16[1,1,128,2560]{3,2,1,0:T(8,128)(2,1)}, bf16[1,32,2560]{2,1,0:T(8,128)(2,1)S(1)}) fusion(bf16[1,1,128,2560]{3,2,1,0:T(8,128)(2,1)} %get-tuple-element.483, s32[]{:T(128)S(6)} %select_n.90, bf16[1,2560,256]{2,1,0:T(8,128)(2,1)} %get-tuple-element.482, bf16[32,128]{1,0:T(8,128)(2,1)S(1)} %fusion.13, ...), kind=kOutput, calls=%fused_computation.46 | convolution fusion | flops 42303488 | bytes 2146308 | tf_op jit(solution)/shard_map/while/body/eval_jaxpr/cond/branch_1_fun/vmap()/dot_general | solution.py:84
  168.5 5.9 %collective-permute-done = bf16[1,32,2560]{2,1,0:T(8,128)(2,1)S(1)} collective-permute-done((bf16[1,32,2560]{2,1,0:T(8,128)(2,1)S(1)}, bf16[1,32,2560]{2,1,0:T(8,128)(2,1)S(1)}, u32[]{:S(2)}, u32[]{:S(2)}) %collective-permute-start) | collective-permute-done | bytes 163872 | tf_op jit(solution)/shard_map/while/body/eval_jaxpr/ppermute | solution.py:16
  174.4 10.2 %all-gather = bf16[1,1,1024,256]{3,2,1,0:T(8,128)(2,1)S(1)} all-gather(bf16[1,1,128,256]{3,2,1,0:T(8,128)(2,1)} %get-tuple-element.508), channel_id=2, replica_groups=mesh['section'=4,'dp'=8] {'dp'}, dimensions={2}, use_global_device_ids=true | all-gather | bytes 589824 | tf_op jit(solution)/shard_map/all_gather | solution.py:181
  184.6 2.3 %reshape.677 = bf16[2560,1,128]{2,1,0:T(2,128)(2,1)S(1)} reshape(bf16[8,2,20480]{2,1,0:T(2,128)(2,1)} %all-to-all-done) | data formatting | bytes 1310720
  (177 shorter events, 47.4 us)
Async XLA Ops:
  17.9 6.2 %copy-start.1 = (f32[1,1,128,40]{2,3,1,0:T(8,128)S(1)}, f32[1,1,128,40]{2,3,1,0:T(8,128)}, u32[]{:S(2)}) copy-start(f32[1,1,128,40]{2,3,1,0:T(8,128)} %param.16) | copy-start | bytes 61444
  18.9 165.6 %all-to-all-start = ((bf16[8,2,20480]{2,1,0:T(2,128)(2,1)}), bf16[8,2,20480]{2,1,0:T(2,128)(2,1)}, u32[]{:S(2)}, u32[]{:S(2)}) async-start(bf16[8,2,20480]{2,1,0:T(2,128)(2,1)} %reshape.676), calls=%async_computation | async-start | bytes 1310720 | tf_op jit(solution)/shard_map/all_to_all | solution.py:179
  26.7 1.6 copy-start
  35.0 8.7 %collective-permute-start = (bf16[1,32,2560]{2,1,0:T(8,128)(2,1)S(1)}, bf16[1,32,2560]{2,1,0:T(8,128)(2,1)S(1)}, u32[]{:S(2)}, u32[]{:S(2)}) collective-permute-start(bf16[1,32,2560]{2,1,0:T(8,128)(2,1)S(1)} %get-tuple-element.684), channel_id=1, source_target_pairs={{8,0},{16,8},{24,16},{9,1},{17,9},{25,17},{10,2},{18,10},{26,18},{... | collective-permute-start | bytes 491528 | tf_op jit(solution)/shard_map/while/body/eval_jaxpr/ppermute | solution.py:16
  43.7 7.7 %collective-permute-start = (bf16[1,32,2560]{2,1,0:T(8,128)(2,1)S(1)}, bf16[1,32,2560]{2,1,0:T(8,128)(2,1)S(1)}, u32[]{:S(2)}, u32[]{:S(2)}) collective-permute-start(bf16[1,32,2560]{2,1,0:T(8,128)(2,1)S(1)} %get-tuple-element.684), channel_id=1, source_target_pairs={{8,0},{16,8},{24,16},{9,1},{17,9},{25,17},{10,2},{18,10},{26,18},{... | collective-permute-start | bytes 491528 | tf_op jit(solution)/shard_map/while/body/eval_jaxpr/ppermute | solution.py:16
  51.4 43.8 %collective-permute-start = (bf16[1,32,2560]{2,1,0:T(8,128)(2,1)S(1)}, bf16[1,32,2560]{2,1,0:T(8,128)(2,1)S(1)}, u32[]{:S(2)}, u32[]{:S(2)}) collective-permute-start(bf16[1,32,2560]{2,1,0:T(8,128)(2,1)S(1)} %get-tuple-element.684), channel_id=1, source_target_pairs={{8,0},{16,8},{24,16},{9,1},{17,9},{25,17},{10,2},{18,10},{26,18},{... | collective-permute-start | bytes 491528 | tf_op jit(solution)/shard_map/while/body/eval_jaxpr/ppermute | solution.py:16
  107.8 7.2 %collective-permute-start = (bf16[1,32,2560]{2,1,0:T(8,128)(2,1)S(1)}, bf16[1,32,2560]{2,1,0:T(8,128)(2,1)S(1)}, u32[]{:S(2)}, u32[]{:S(2)}) collective-permute-start(bf16[1,32,2560]{2,1,0:T(8,128)(2,1)S(1)} %get-tuple-element.684), channel_id=1, source_target_pairs={{8,0},{16,8},{24,16},{9,1},{17,9},{25,17},{10,2},{18,10},{26,18},{... | collective-permute-start | bytes 491528 | tf_op jit(solution)/shard_map/while/body/eval_jaxpr/ppermute | solution.py:16
  127.6 7.2 %collective-permute-start = (bf16[1,32,2560]{2,1,0:T(8,128)(2,1)S(1)}, bf16[1,32,2560]{2,1,0:T(8,128)(2,1)S(1)}, u32[]{:S(2)}, u32[]{:S(2)}) collective-permute-start(bf16[1,32,2560]{2,1,0:T(8,128)(2,1)S(1)} %get-tuple-element.684), channel_id=1, source_target_pairs={{8,0},{16,8},{24,16},{9,1},{17,9},{25,17},{10,2},{18,10},{26,18},{... | collective-permute-start | bytes 491528 | tf_op jit(solution)/shard_map/while/body/eval_jaxpr/ppermute | solution.py:16
  147.4 7.2 %collective-permute-start = (bf16[1,32,2560]{2,1,0:T(8,128)(2,1)S(1)}, bf16[1,32,2560]{2,1,0:T(8,128)(2,1)S(1)}, u32[]{:S(2)}, u32[]{:S(2)}) collective-permute-start(bf16[1,32,2560]{2,1,0:T(8,128)(2,1)S(1)} %get-tuple-element.684), channel_id=1, source_target_pairs={{8,0},{16,8},{24,16},{9,1},{17,9},{25,17},{10,2},{18,10},{26,18},{... | collective-permute-start | bytes 491528 | tf_op jit(solution)/shard_map/while/body/eval_jaxpr/ppermute | solution.py:16
  167.2 7.2 %collective-permute-start = (bf16[1,32,2560]{2,1,0:T(8,128)(2,1)S(1)}, bf16[1,32,2560]{2,1,0:T(8,128)(2,1)S(1)}, u32[]{:S(2)}, u32[]{:S(2)}) collective-permute-start(bf16[1,32,2560]{2,1,0:T(8,128)(2,1)S(1)} %get-tuple-element.684), channel_id=1, source_target_pairs={{8,0},{16,8},{24,16},{9,1},{17,9},{25,17},{10,2},{18,10},{26,18},{... | collective-permute-start | bytes 491528 | tf_op jit(solution)/shard_map/while/body/eval_jaxpr/ppermute | solution.py:16

commit v2 on v1

--- a/solution.py
+++ b/solution.py
@@ -105,74 +105,159 @@
     return jnp.stack(saved)
 
 
+def block_consts(inputs_b, in_b, out_b, rates, factor):
+    length = inputs_b.shape[0]
+    cumulative = jnp.cumsum(rates, axis=0)
+    ending = cumulative[-1]
+    locations = jnp.arange(length)
+    lower_mask = (locations[:, None] >= locations[None, :])[:, :, None]
+    spread = jnp.where(lower_mask, cumulative[:, None, :] - cumulative[None, :, :], 0.0)
+    decays = jnp.where(lower_mask, jnp.exp(spread), 0.0)
+    tail_decay = jnp.exp(ending[None, :] - cumulative)
+    leading = jnp.exp(cumulative)
+    scores = jnp.dot(out_b, in_b.T, preferred_element_type=jnp.float32)
+    weighted = (factor * decays * scores[:, :, None]).astype(jnp.bfloat16)
+    tail_inputs = (tail_decay[:, :, None] * inputs_b.astype(jnp.float32)).astype(jnp.bfloat16)
+    fresh = jnp.einsum("jhp,jn->hpn", tail_inputs, in_b, preferred_element_type=jnp.float32)
+    return dict(
+        decays=decays,
+        tail=tail_decay,
+        lead=leading,
+        weighted=weighted,
+        tail_inputs=tail_inputs,
+        fresh=fresh,
+        ending=jnp.exp(ending),
+    )
+
+
+def block_step(consts, inputs_b, in_b, out_b, state_b, grads_c, carried, weights, factor):
+    length, features = grads_c.shape
+    head_count = consts["tail"].shape[1]
+    grads_b = grads_c.reshape(length, head_count, features // head_count)
+    carried_b = carried.astype(jnp.bfloat16)
+    grad_feats = jnp.einsum(
+        "kjh,khp->jhp", consts["weighted"], grads_b, preferred_element_type=jnp.float32
+    )
+    grad_feats = grad_feats + consts["tail"][:, :, None] * jnp.einsum(
+        "hpn,jn->jhp", carried_b, in_b, preferred_element_type=jnp.float32
+    )
+    pair_dots = jnp.einsum("khp,jhp->kjh", grads_b, inputs_b, preferred_element_type=jnp.float32)
+    mixing = jnp.sum(consts["decays"] * pair_dots, axis=2).astype(jnp.bfloat16)
+    lead_grads = (consts["lead"][:, :, None] * grads_b.astype(jnp.float32)).astype(jnp.bfloat16)
+    grad_inmap = factor * jnp.dot(mixing.T, out_b, preferred_element_type=jnp.float32)
+    grad_inmap = grad_inmap + jnp.einsum(
+        "jhp,hpn->jn", consts["tail_inputs"], carried_b, preferred_element_type=jnp.float32
+    )
+    grad_outmap = factor * (
+        jnp.dot(mixing, in_b, preferred_element_type=jnp.float32)
+        + jnp.einsum("ihp,hpn->in", lead_grads, state_b, preferred_element_type=jnp.float32)
+    )
+    carry_out = factor * jnp.einsum(
+        "khp,kn->hpn", lead_grads, out_b, preferred_element_type=jnp.float32
+    )
+    carry_out = carry_out + consts["ending"][:, None, None] * carried
+    grad_bc = jnp.concatenate([grad_inmap, grad_outmap], axis=1).astype(jnp.bfloat16)
+    back_proj = lax.dot_general(
+        grad_bc, weights, (((1,), (1,)), ((), ())), preferred_element_type=jnp.float32
+    )
+    summed = grads_c.astype(jnp.float32) + grad_feats.reshape(length, features) + back_proj
+    return (summed.astype(jnp.bfloat16), carry_out, grad_bc)
+
+
 def shards(layer_inputs, w_bc, log_decay, top_grad):
     sections = lax.axis_size("section")
     section_id = lax.axis_index("section")
     lay_dev, seq_dev, tok_len, features = layer_inputs.shape
+    head_count = log_decay.shape[-1]
     block_len = tok_len // MICRO
+    state_size = w_bc.shape[-1] // 2
+    factor = 0.25 / state_size
     bc_all = jnp.einsum(
         "lstd,ldc->lstc", layer_inputs, w_bc, preferred_element_type=jnp.float32
     ).astype(jnp.bfloat16)
-    starts = jax.vmap(jax.vmap(layer_starts))(layer_inputs, bc_all, log_decay)
+
+    def blocked(a):
+        split = a.reshape(a.shape[:2] + (MICRO, block_len) + a.shape[3:])
+        return jnp.moveaxis(split, 2, 0)
+
+    x_blk = blocked(layer_inputs).reshape(
+        (MICRO, lay_dev, seq_dev, block_len, head_count, features // head_count)
+    )
+    bc_blk = blocked(bc_all)
+    in_blk = bc_blk[..., :state_size]
+    out_blk = bc_blk[..., state_size:]
+    rates_blk = blocked(log_decay)
+    consts_fn = jax.vmap(jax.vmap(jax.vmap(lambda x, b, c, r: block_consts(x, b, c, r, factor))))
+    consts = consts_fn(x_blk, in_blk, out_blk, rates_blk)
+
+    state_now = jnp.zeros(consts["fresh"].shape[1:], jnp.float32)
+    saved = []
+    for block_no in range(MICRO):
+        saved.append(state_now.astype(jnp.bfloat16))
+        state_now = consts["ending"][block_no][..., None, None] * state_now + consts["fresh"][block_no]
+    states_b = jnp.stack(saved)
+    del consts["fresh"]
+
+    top_blk = jnp.moveaxis(
+        top_grad.reshape((seq_dev, MICRO, block_len, features)), 1, 0
+    )
     is_top = section_id == sections - 1
-    back_all = jax.vmap(block_back, in_axes=(0, 0, 0, 0, 0, 0, None))
+    step_fn = jax.vmap(
+        lambda k, x, b, c, sb, g, r, w: block_step(k, x, b, c, sb, g, r, w, factor),
+        in_axes=(0, 0, 0, 0, 0, 0, 0, None),
+    )
 
     def advance(counter, loop_state):
         incoming, carried, grad_store, map_store = loop_state
         offset = counter - (sections - 1 - section_id)
         is_valid = (offset >= 0) & (offset < MICRO)
         block_no = jnp.clip(MICRO - 1 - offset, 0, MICRO - 1)
-        row_start = block_no * block_len
-        from_top = lax.dynamic_slice_in_dim(top_grad, row_start, block_len, 1)
-        grad_block = jnp.where(is_top, from_top, incoming)
-
-        def compute(stores):
-            carried_in, grads_in, maps_in = stores
-            current = grad_block
-            for level_no in reversed(range(lay_dev)):
-                inputs_c = lax.dynamic_slice_in_dim(layer_inputs[level_no], row_start, block_len, 1)
-                map_block = lax.dynamic_slice_in_dim(bc_all[level_no], row_start, block_len, 1)
-                rates = lax.dynamic_slice_in_dim(log_decay[level_no], row_start, block_len, 1)
-                state_in = lax.dynamic_index_in_dim(starts[level_no], block_no, 1, keepdims=False)
-                level_grads, carry_out, grad_bc = back_all(
-                    inputs_c,
-                    map_block,
-                    rates,
-                    current,
-                    carried_in[level_no],
-                    state_in,
-                    w_bc[level_no],
-                )
-                carried_in = carried_in.at[level_no].set(carry_out)
-                grads_in = grads_in.at[level_no].set(
-                    lax.dynamic_update_slice_in_dim(grads_in[level_no], level_grads, row_start, 1)
-                )
-                maps_in = maps_in.at[level_no].set(
-                    lax.dynamic_update_slice_in_dim(maps_in[level_no], grad_bc, row_start, 1)
-                )
-                current = level_grads
-            return (current, (carried_in, grads_in, maps_in))
-
-        def passing(stores):
-            return (jnp.zeros_like(grad_block), stores)
-
-        outgoing, updated = lax.cond(is_valid, compute, passing, (carried, grad_store, map_store))
-        received = jax.tree.map(
-            lambda part, own: part.astype(own.dtype),
-            passed_along(shortened(outgoing), "section", -1),
-            outgoing,
+        slot = jnp.where(is_valid, block_no, MICRO)
+        from_top = lax.dynamic_index_in_dim(top_blk, block_no, 0, keepdims=False)
+        current = jnp.where(is_top, from_top, incoming)
+        picked = jax.tree.map(
+            lambda a: lax.dynamic_index_in_dim(a, block_no, 0, keepdims=False), consts
         )
-        return (received, updated[0], updated[1], updated[2])
+        x_now = lax.dynamic_index_in_dim(x_blk, block_no, 0, keepdims=False)
+        in_now = lax.dynamic_index_in_dim(in_blk, block_no, 0, keepdims=False)
+        out_now = lax.dynamic_index_in_dim(out_blk, block_no, 0, keepdims=False)
+        st_now = lax.dynamic_index_in_dim(states_b, block_no, 0, keepdims=False)
+        new_carried = []
+        for level_no in reversed(range(lay_dev)):
+            level_grads, carry_out, grad_bc = step_fn(
+                jax.tree.map(lambda a: a[level_no], picked),
+                x_now[level_no],
+                in_now[level_no],
+                out_now[level_no],
+                st_now[level_no],
+                current,
+                carried[level_no],
+                w_bc[level_no],
+            )
+            new_carried.append(carry_out)
+            grad_store = lax.dynamic_update_slice(
+                grad_store, level_grads[None, None], (slot, level_no, 0, 0, 0)
+            )
+            map_store = lax.dynamic_update_slice(
+                map_store, grad_bc[None, None], (slot, level_no, 0, 0, 0)
+            )
+            current = level_grads
+        carried = jnp.stack(new_carried[::-1])
+        received = passed_along(current, "section", -1)
+        return (received, carried, grad_store, map_store)
 
     initial = (
         jnp.zeros((seq_dev, block_len, features), jnp.bfloat16),
-        jnp.zeros((lay_dev,) + starts.shape[1:2] + starts.shape[3:], jnp.float32),
-        jnp.zeros(layer_inputs.shape, jnp.bfloat16),
-        jnp.zeros(bc_all.shape, jnp.bfloat16),
+        jnp.zeros((lay_dev,) + states_b.shape[2:], jnp.float32),
+        jnp.zeros((MICRO + 1, lay_dev, seq_dev, block_len, features), jnp.bfloat16),
+        jnp.zeros((MICRO + 1, lay_dev, seq_dev, block_len, 2 * state_size), jnp.bfloat16),
     )
     final_state = lax.fori_loop(0, MICRO + sections - 1, advance, initial)
-    grad_inputs = final_state[2]
+    grad_store = final_state[2]
     map_store = final_state[3]
+
+    grad_inputs = jnp.moveaxis(grad_store[:MICRO], 0, 2).reshape(layer_inputs.shape)
+    map_store = jnp.moveaxis(map_store[:MICRO], 0, 2).reshape(bc_all.shape)
     ways = lax.axis_size("dp")
     divisor = ways * seq_dev
     rows_here = layer_inputs.reshape(lay_dev, seq_dev * tok_len, features)

time: 190 us -> 182 us (0.958)
  waiting for transfers between devices: 79.9 us -> 38 us
  matrix products: 30.2 us -> 55 us
  local copies, waits for them, and re-layouts: 24.2 us -> 32.7 us
    ppermute x7, waiting for transfers between devices: 79.9 us -> 38 us  [passed_along(): return lax.ppermute(block, axis, route)]
    dot_general x43 -> x65, matrix products: 27.8 us -> 53.6 us  [the longest x7 10.3 us: block_step(): jnp.einsum('ihp,hpn->in', lead_grads, state_b, preferred_element_type=jnp...]
    dynamic_slice x8 -> x21, local copies, waits for them, and re-layouts: 2.92 us -> 8.54 us  [advance(): lax.dynamic_index_in_dim(a, block_no, 0, keepdims=False)]
    scatter x4 -> x0, other arithmetic: 2.46 us -> none  [compute(): maps_in.at[level_no]]
    select_n x0 -> x1, other arithmetic: none -> 2.42 us  [block_consts(): decays = jnp.where(lower_mask, jnp.exp(spread), 0.0)]
    mul x26 -> x29, local copies, waits for them, and re-layouts: 4.83 us -> 3.06 us  [the longest x21 2.92 us: block_step(): consts['lead'][:, :, None] * grads_b.astype(jnp.float32)]
    unnamed x8 -> x12, local copies, waits for them, and re-layouts: 4 us -> 3.95 us
  transfers between devices with their start and end apart: 8 -> 8, of which waited for: 7 -> 7; matrix products, arithmetic and copies ran while one was open for 32% -> 52% of each run, Pallas kernels for 0% -> 0%
where the time goes in v2:
time: 182 us; the launch traced here: 180 us
  matrix products  55 us (30%)
  waiting for transfers between devices  38 us (21%)
  local copies, waits for them, and re-layouts  32.7 us (18%)
  other arithmetic  28.9 us (16%)
  starting transfers between devices  14.1 us (8%)
  blocking collectives  9.76 us (5%)
    ppermute x7, waiting for transfers between devices, passed_along(): return lax.ppermute(block, axis, route)  38 us
    unnamed x1, other arithmetic  14.3 us
    dot_general x7, matrix products, block_step(): jnp.einsum('ihp,hpn->in', lead_grads, state_b, preferred_element_type=jnp...  10.3 us
    all_gather x1, blocking collectives, shards(): maps_all = lax.all_gather(maps_here, 'dp', axis=1, tiled=True)  9.76 us
    dot_general x7, matrix products, block_step(): jnp.einsum('khp,jhp->kjh', grads_b, inputs_b, preferred_element_type=jnp....  9.71 us
    ppermute x7, starting transfers between devices, passed_along(): return lax.ppermute(block, axis, route)  8.96 us
    dynamic_slice x21, local copies, waits for them, and re-layouts, advance(): lax.dynamic_index_in_dim(a, block_no, 0, keepdims=False)  8.54 us
    dot_general x7, matrix products, block_step(): jnp.einsum('kjh,khp->jhp', consts['weighted'], grads_b, preferred_element...  8.52 us
  transfers between devices with their start and end apart: 8, of which 7 were waited for; matrix products, arithmetic and copies ran while one was open for 52% of the time, Pallas kernels for 0%

profile of v2, /device:TPU:0, one launch (start us, length us, event | category | flops | bytes accessed | tf_op | source)
XLA Modules:
  0.0 180.4 jit_solution(18196928765464437511)
XLA Ops:
  0.6 2.5 %copy.76 = bf16[1,128,2560]{1,0,2:T(2,128)(2,1)S(1)} copy(bf16[1,128,2560]{2,1,0:T(8,128)(2,1)} %bitcast.243) | data formatting | bytes 1310720 | tf_op jit(solution)/shard_map/reshape | solution.py:263
  3.7 14.3 %reduce.5 = bf16[2560,128]{1,0:T(8,128)(2,1)S(1)} reduce(bf16[2560,1,128]{2,1,0:T(2,128)(2,1)S(1)} %bitcast.244, bf16[]{:T(256)} %broadcast.242), dimensions={1}, to_apply=%bitcast.182.reduce_sub_computation | reduce | bytes 1310722
  18.9 5.2 %all-to-all-start = ((bf16[8,2,20480]{2,1,0:T(2,128)(2,1)}), bf16[8,2,20480]{2,1,0:T(2,128)(2,1)}, u32[]{:S(2)}, u32[]{:S(2)}) async-start(bf16[8,2,20480]{2,1,0:T(2,128)(2,1)} %reshape.526), calls=%async_computation | async-start | bytes 1310720 | tf_op jit(solution)/shard_map/all_to_all | solution.py:264
  24.1 2.1 %reshape.519 = f32[4,32,40,64]{3,2,1,0:T(8,128)} reshape(bf16[1,1,128,2560]{3,2,1,0:T(8,128)(2,1)S(1)} %copy-done.3) | data formatting | bytes 1966080 | tf_op jit(solution)/shard_map/vmap(vmap(vmap()))/convert_element_type | solution.py:120
  26.2 1.9 %reshape_transpose_reshape.3 = bf16[4,1,1,32,40,64]{5,4,3,0,2,1:T(8,128)(2,1)} reshape(bf16[1,1,128,2560]{3,2,1,0:T(8,128)(2,1)S(1)} %copy-done.3) | data formatting | bytes 1310720 | tf_op jit(solution)/shard_map/reshape;transpose;reshape | solution.py:183
  29.0 2.9 %multiply_convert_fusion = bf16[4,1,1,32,40,64]{5,4,3,0,2,1:T(8,128)(2,1)} fusion(bf16[4,1,1,32,40,64]{5,4,3,0,2,1:T(8,128)(2,1)} %reshape_transpose_reshape.3, f32[4,32,40]{2,1,0:T(8,128)S(1)} %subtract_exponential_fusion), kind=kLoop, calls=%fused_computation.73 | loop fusion | flops 983040 | bytes 1331200 | tf_op jit(solution)/shard_map/vmap(vmap(vmap()))/convert_element_type | solution.py:120
  32.1 2.7 %fusion.50 = f32[4,40,64,128]{3,2,1,0:T(8,128)S(1)} fusion(f32[4,32,40,64]{3,2,1,0:T(8,128)S(1)} %copy-done.2, f32[4,32,40]{1,2,0:T(8,128)S(1)} %copy.68, bf16[4,1,1,32,256]{4,3,0,2,1:T(8,128)(2,1)S(1)} %bitcast.254), kind=kOutput, calls=%fused_computation.76 | convolution fusion | flops 84541440 | bytes 7979008 | tf_op jit(solution)/shard_map/vmap(vmap(vmap(jhp,jn->hpn)))/dot_general | solution.py:121
  34.8 2.4 %exponential_select_fusion = (f32[4,1,1,32,32,40]{3,4,5,2,1,0:T(8,128)}, bf16[4,1,1,32,32,40]{3,4,5,2,1,0:T(8,128)(2,1)}) fusion(f32[4,32,40]{1,2,0:T(8,128)S(1)} %copy.65, pred[32,32]{0,1:T(8,128)(4,1)S(1)} %iota_compare_fusion, f32[4,32,32]{1,2,0:T(8,128)S(1)} %copy.67), kind=kLoop, calls=%fused_computation.75 | loop fusion | flops 819200 | bytes 1020928 | tf_op jit(solution)/shard_map/vmap(vmap(vmap(jit(_where))))/select_n | solution.py:115
  37.7 1.8 pad_maximum_fusion
  40.7 124.0 %while.21 = (s32[]{:T(128)}, bf16[1,32,2560]{2,1,0:T(8,128)(2,1)S(1)}, f32[1,1,40,64,128]{4,3,2,1,0:T(8,128)S(1)}, bf16[5,1,1,32,2560]{4,3,2,1,0:T(8,128)(2,1)},...) while((s32[]{:T(128)}, ...), condition=%wide.region_3.4_spmd, body=%wide.region_1.3_spmd.sunk | while | flops 139467776 | bytes 21375196 | solution.py:255
  46.1 1.4 fusion.118
  48.3 1.5 fusion.120
  53.0 6.6 %collective-permute-done = bf16[1,32,2560]{2,1,0:T(8,128)(2,1)S(1)} collective-permute-done((bf16[1,32,2560]{2,1,0:T(8,128)(2,1)S(1)}, bf16[1,32,2560]{2,1,0:T(8,128)(2,1)S(1)}, u32[]{:S(2)}, u32[]{:S(2)}) %collective-permute-start) | collective-permute-done | bytes 163872 | tf_op jit(solution)/shard_map/while/body/eval_jaxpr/ppermute | solution.py:16
  65.0 1.4 fusion.118
  67.2 1.5 fusion.120
  71.9 5.6 %collective-permute-done = bf16[1,32,2560]{2,1,0:T(8,128)(2,1)S(1)} collective-permute-done((bf16[1,32,2560]{2,1,0:T(8,128)(2,1)S(1)}, bf16[1,32,2560]{2,1,0:T(8,128)(2,1)S(1)}, u32[]{:S(2)}, u32[]{:S(2)}) %collective-permute-start) | collective-permute-done | bytes 163872 | tf_op jit(solution)/shard_map/while/body/eval_jaxpr/ppermute | solution.py:16
  82.9 1.4 fusion.118
  85.1 1.5 fusion.120
  89.8 5.1 %collective-permute-done = bf16[1,32,2560]{2,1,0:T(8,128)(2,1)S(1)} collective-permute-done((bf16[1,32,2560]{2,1,0:T(8,128)(2,1)S(1)}, bf16[1,32,2560]{2,1,0:T(8,128)(2,1)S(1)}, u32[]{:S(2)}, u32[]{:S(2)}) %collective-permute-start) | collective-permute-done | bytes 163872 | tf_op jit(solution)/shard_map/while/body/eval_jaxpr/ppermute | solution.py:16
  100.4 1.4 fusion.118
  102.6 1.5 fusion.120
  107.3 5.1 %collective-permute-done = bf16[1,32,2560]{2,1,0:T(8,128)(2,1)S(1)} collective-permute-done((bf16[1,32,2560]{2,1,0:T(8,128)(2,1)S(1)}, bf16[1,32,2560]{2,1,0:T(8,128)(2,1)S(1)}, u32[]{:S(2)}, u32[]{:S(2)}) %collective-permute-start) | collective-permute-done | bytes 163872 | tf_op jit(solution)/shard_map/while/body/eval_jaxpr/ppermute | solution.py:16
  117.8 1.4 fusion.118
  120.0 1.5 fusion.120
  124.7 5.1 %collective-permute-done = bf16[1,32,2560]{2,1,0:T(8,128)(2,1)S(1)} collective-permute-done((bf16[1,32,2560]{2,1,0:T(8,128)(2,1)S(1)}, bf16[1,32,2560]{2,1,0:T(8,128)(2,1)S(1)}, u32[]{:S(2)}, u32[]{:S(2)}) %collective-permute-start) | collective-permute-done | bytes 163872 | tf_op jit(solution)/shard_map/while/body/eval_jaxpr/ppermute | solution.py:16
  137.4 1.5 fusion.120
  142.2 5.1 %collective-permute-done = bf16[1,32,2560]{2,1,0:T(8,128)(2,1)S(1)} collective-permute-done((bf16[1,32,2560]{2,1,0:T(8,128)(2,1)S(1)}, bf16[1,32,2560]{2,1,0:T(8,128)(2,1)S(1)}, u32[]{:S(2)}, u32[]{:S(2)}) %collective-permute-start) | collective-permute-done | bytes 163872 | tf_op jit(solution)/shard_map/while/body/eval_jaxpr/ppermute | solution.py:16
  154.9 1.5 fusion.120
  159.6 5.1 %collective-permute-done = bf16[1,32,2560]{2,1,0:T(8,128)(2,1)S(1)} collective-permute-done((bf16[1,32,2560]{2,1,0:T(8,128)(2,1)S(1)}, bf16[1,32,2560]{2,1,0:T(8,128)(2,1)S(1)}, u32[]{:S(2)}, u32[]{:S(2)}) %collective-permute-start) | collective-permute-done | bytes 163872 | tf_op jit(solution)/shard_map/while/body/eval_jaxpr/ppermute | solution.py:16
  164.7 2.0 %slice.48 = bf16[4,1,1,32,2560]{4,3,2,1,0:T(8,128)(2,1)} slice(bf16[5,1,1,32,2560]{4,3,2,1,0:T(8,128)(2,1)} %get-tuple-element.425), slice={[0:4], [0:1], [0:1], [0:32], [0:2560]} | slice | bytes 1310720 | tf_op jit(solution)/shard_map/slice | solution.py:259
  166.7 9.8 %all_gather.3 = bf16[1,1024,256]{2,1,0:T(8,128)(2,1)S(1)} all-gather(bf16[1,128,256]{2,1,0:T(8,128)(2,1)S(1)} %bitcast.257), channel_id=1, replica_groups=mesh['section'=4,'dp'=8] {'dp'}, dimensions={1}, use_global_device_ids=true | all-gather | bytes 589824 | tf_op jit(solution)/shard_map/all_gather | solution.py:266
  176.5 2.3 %reshape.527 = bf16[2560,1,128]{2,1,0:T(2,128)(2,1)S(1)} reshape(bf16[8,2,20480]{2,1,0:T(2,128)(2,1)} %all-to-all-done) | data formatting | bytes 1310720
  (197 shorter events, 73.5 us)
Async XLA Ops:
  17.9 6.2 %copy-start.3 = (bf16[1,1,128,2560]{3,2,1,0:T(8,128)(2,1)S(1)}, bf16[1,1,128,2560]{3,2,1,0:T(8,128)(2,1)}, u32[]{:S(2)}) copy-start(bf16[1,1,128,2560]{3,2,1,0:T(8,128)(2,1)} %param.6) | copy-start | bytes 1966084
  18.9 157.5 %all-to-all-start = ((bf16[8,2,20480]{2,1,0:T(2,128)(2,1)}), bf16[8,2,20480]{2,1,0:T(2,128)(2,1)}, u32[]{:S(2)}, u32[]{:S(2)}) async-start(bf16[8,2,20480]{2,1,0:T(2,128)(2,1)} %reshape.526), calls=%async_computation | async-start | bytes 1310720 | tf_op jit(solution)/shard_map/all_to_all | solution.py:264
  26.2 1.9 %copy-start.4 = (f32[1,1,128,40]{2,3,1,0:T(8,128)S(1)}, f32[1,1,128,40]{2,3,1,0:T(8,128)}, u32[]{:S(2)}) copy-start(f32[1,1,128,40]{2,3,1,0:T(8,128)} %param.8) | copy-start | bytes 61444
  26.2 2.1 %copy-start = (bf16[1,2560,256]{2,1,0:T(8,128)(2,1)S(1)}, bf16[1,2560,256]{2,1,0:T(8,128)(2,1)}, u32[]{:S(2)}) copy-start(bf16[1,2560,256]{2,1,0:T(8,128)(2,1)} %param.7) | copy-start | bytes 3932164
  29.0 3.1 %copy-start.2 = (f32[4,32,40,64]{3,2,1,0:T(8,128)S(1)}, f32[4,32,40,64]{3,2,1,0:T(8,128)}, u32[]{:S(2)}) copy-start(f32[4,32,40,64]{3,2,1,0:T(8,128)} %reshape.519) | copy-start | bytes 3932164
  48.0 1.8 copy-start.1
  51.0 8.7 %collective-permute-start = (bf16[1,32,2560]{2,1,0:T(8,128)(2,1)S(1)}, bf16[1,32,2560]{2,1,0:T(8,128)(2,1)S(1)}, u32[]{:S(2)}, u32[]{:S(2)}) collective-permute-start(bf16[1,32,2560]{2,1,0:T(8,128)(2,1)S(1)} %get-tuple-element.687), channel_id=1, source_target_pairs={{8,0},{16,8},{24,16},{9,1},{17,9},{25,17},{10,2},{18,10},{26,18},{... | collective-permute-start | bytes 491528 | tf_op jit(solution)/shard_map/while/body/eval_jaxpr/ppermute | solution.py:16
  66.9 1.8 copy-start.1
  69.9 7.7 %collective-permute-start = (bf16[1,32,2560]{2,1,0:T(8,128)(2,1)S(1)}, bf16[1,32,2560]{2,1,0:T(8,128)(2,1)S(1)}, u32[]{:S(2)}, u32[]{:S(2)}) collective-permute-start(bf16[1,32,2560]{2,1,0:T(8,128)(2,1)S(1)} %get-tuple-element.687), channel_id=1, source_target_pairs={{8,0},{16,8},{24,16},{9,1},{17,9},{25,17},{10,2},{18,10},{26,18},{... | collective-permute-start | bytes 491528 | tf_op jit(solution)/shard_map/while/body/eval_jaxpr/ppermute | solution.py:16
  84.8 1.8 copy-start.1
  87.8 7.2 %collective-permute-start = (bf16[1,32,2560]{2,1,0:T(8,128)(2,1)S(1)}, bf16[1,32,2560]{2,1,0:T(8,128)(2,1)S(1)}, u32[]{:S(2)}, u32[]{:S(2)}) collective-permute-start(bf16[1,32,2560]{2,1,0:T(8,128)(2,1)S(1)} %get-tuple-element.687), channel_id=1, source_target_pairs={{8,0},{16,8},{24,16},{9,1},{17,9},{25,17},{10,2},{18,10},{26,18},{... | collective-permute-start | bytes 491528 | tf_op jit(solution)/shard_map/while/body/eval_jaxpr/ppermute | solution.py:16
  102.3 1.8 copy-start.1
  105.2 7.2 %collective-permute-start = (bf16[1,32,2560]{2,1,0:T(8,128)(2,1)S(1)}, bf16[1,32,2560]{2,1,0:T(8,128)(2,1)S(1)}, u32[]{:S(2)}, u32[]{:S(2)}) collective-permute-start(bf16[1,32,2560]{2,1,0:T(8,128)(2,1)S(1)} %get-tuple-element.687), channel_id=1, source_target_pairs={{8,0},{16,8},{24,16},{9,1},{17,9},{25,17},{10,2},{18,10},{26,18},{... | collective-permute-start | bytes 491528 | tf_op jit(solution)/shard_map/while/body/eval_jaxpr/ppermute | solution.py:16
  119.7 1.8 copy-start.1
  122.7 7.2 %collective-permute-start = (bf16[1,32,2560]{2,1,0:T(8,128)(2,1)S(1)}, bf16[1,32,2560]{2,1,0:T(8,128)(2,1)S(1)}, u32[]{:S(2)}, u32[]{:S(2)}) collective-permute-start(bf16[1,32,2560]{2,1,0:T(8,128)(2,1)S(1)} %get-tuple-element.687), channel_id=1, source_target_pairs={{8,0},{16,8},{24,16},{9,1},{17,9},{25,17},{10,2},{18,10},{26,18},{... | collective-permute-start | bytes 491528 | tf_op jit(solution)/shard_map/while/body/eval_jaxpr/ppermute | solution.py:16
  137.2 1.8 copy-start.1
  140.1 7.2 %collective-permute-start = (bf16[1,32,2560]{2,1,0:T(8,128)(2,1)S(1)}, bf16[1,32,2560]{2,1,0:T(8,128)(2,1)S(1)}, u32[]{:S(2)}, u32[]{:S(2)}) collective-permute-start(bf16[1,32,2560]{2,1,0:T(8,128)(2,1)S(1)} %get-tuple-element.687), channel_id=1, source_target_pairs={{8,0},{16,8},{24,16},{9,1},{17,9},{25,17},{10,2},{18,10},{26,18},{... | collective-permute-start | bytes 491528 | tf_op jit(solution)/shard_map/while/body/eval_jaxpr/ppermute | solution.py:16
  154.6 1.8 copy-start.1
  157.5 7.2 %collective-permute-start = (bf16[1,32,2560]{2,1,0:T(8,128)(2,1)S(1)}, bf16[1,32,2560]{2,1,0:T(8,128)(2,1)S(1)}, u32[]{:S(2)}, u32[]{:S(2)}) collective-permute-start(bf16[1,32,2560]{2,1,0:T(8,128)(2,1)S(1)} %get-tuple-element.687), channel_id=1, source_target_pairs={{8,0},{16,8},{24,16},{9,1},{17,9},{25,17},{10,2},{18,10},{26,18},{... | collective-permute-start | bytes 491528 | tf_op jit(solution)/shard_map/while/body/eval_jaxpr/ppermute | solution.py:16

commit v3 on v2

--- a/solution.py
+++ b/solution.py
@@ -1,6 +1,10 @@
+import functools
+
 import jax
 import jax.numpy as jnp
 from jax import lax
+from jax.experimental import pallas as pl
+from jax.experimental.pallas import tpu as pltpu
 from jax.sharding import PartitionSpec as P
 
 MICRO = 4
@@ -130,38 +134,71 @@
     )
 
 
-def block_step(consts, inputs_b, in_b, out_b, state_b, grads_c, carried, weights, factor):
-    length, features = grads_c.shape
-    head_count = consts["tail"].shape[1]
-    grads_b = grads_c.reshape(length, head_count, features // head_count)
-    carried_b = carried.astype(jnp.bfloat16)
-    grad_feats = jnp.einsum(
-        "kjh,khp->jhp", consts["weighted"], grads_b, preferred_element_type=jnp.float32
-    )
-    grad_feats = grad_feats + consts["tail"][:, :, None] * jnp.einsum(
-        "hpn,jn->jhp", carried_b, in_b, preferred_element_type=jnp.float32
-    )
-    pair_dots = jnp.einsum("khp,jhp->kjh", grads_b, inputs_b, preferred_element_type=jnp.float32)
-    mixing = jnp.sum(consts["decays"] * pair_dots, axis=2).astype(jnp.bfloat16)
-    lead_grads = (consts["lead"][:, :, None] * grads_b.astype(jnp.float32)).astype(jnp.bfloat16)
-    grad_inmap = factor * jnp.dot(mixing.T, out_b, preferred_element_type=jnp.float32)
-    grad_inmap = grad_inmap + jnp.einsum(
-        "jhp,hpn->jn", consts["tail_inputs"], carried_b, preferred_element_type=jnp.float32
-    )
+def step_kernel(
+    wt_ref, dec_ref, v_ref, x_ref, b_ref, c_ref, tail_ref, lead_ref, xt_ref, sb_ref, r_ref, end_ref,
+    w_ref, out_ref, rnew_ref, dbc_ref, gx_ref, *, factor, width
+):
+    f32 = jnp.float32
+    bf16 = jnp.bfloat16
+    length, features = v_ref.shape
+    lanes = 128
+    per_pair = lanes // width
+    nt = (((1,), (1,)), ((), ()))
+    tn = (((0,), (0,)), ((), ()))
+    rb_t = r_ref[...].astype(bf16)
+    in_map = b_ref[...]
+    out_map = c_ref[...]
+    lane_id = lax.broadcasted_iota(jnp.int32, (length, lanes), 1)
+    masks = [(lane_id >= e * width) & (lane_id < (e + 1) * width) for e in range(per_pair)]
+    mix_acc = jnp.zeros((per_pair * length, length), f32)
+    for q in range(features // lanes):
+        cols = slice(q * lanes, (q + 1) * lanes)
+        v_q = v_ref[:, cols]
+        x_q = x_ref[:, cols]
+        stacked = jnp.concatenate([jnp.where(m, v_q, jnp.zeros_like(v_q)) for m in masks], axis=0)
+        gx_q = jnp.dot(wt_ref[q], stacked, preferred_element_type=f32)
+        rbb_q = jnp.dot(in_map, rb_t[:, cols], preferred_element_type=f32)
+        gx_ref[:, cols] = gx_q + tail_ref[:, cols] * rbb_q
+        pair_dots = lax.dot_general(stacked, x_q, nt, preferred_element_type=f32)
+        mix_acc = mix_acc + dec_ref[q] * pair_dots
+    mixing = mix_acc[0:length]
+    for e in range(1, per_pair):
+        mixing = mixing + mix_acc[e * length:(e + 1) * length]
+    mixing = mixing.astype(bf16)
+    v = v_ref[...]
+    lead_grads = (lead_ref[...] * v.astype(f32)).astype(bf16)
+    grad_inmap = factor * lax.dot_general(mixing, out_map, tn, preferred_element_type=f32)
+    grad_inmap = grad_inmap + lax.dot_general(xt_ref[...], rb_t, nt, preferred_element_type=f32)
     grad_outmap = factor * (
-        jnp.dot(mixing, in_b, preferred_element_type=jnp.float32)
-        + jnp.einsum("ihp,hpn->in", lead_grads, state_b, preferred_element_type=jnp.float32)
-    )
-    carry_out = factor * jnp.einsum(
-        "khp,kn->hpn", lead_grads, out_b, preferred_element_type=jnp.float32
-    )
-    carry_out = carry_out + consts["ending"][:, None, None] * carried
-    grad_bc = jnp.concatenate([grad_inmap, grad_outmap], axis=1).astype(jnp.bfloat16)
-    back_proj = lax.dot_general(
-        grad_bc, weights, (((1,), (1,)), ((), ())), preferred_element_type=jnp.float32
-    )
-    summed = grads_c.astype(jnp.float32) + grad_feats.reshape(length, features) + back_proj
-    return (summed.astype(jnp.bfloat16), carry_out, grad_bc)
+        jnp.dot(mixing, in_map, preferred_element_type=f32)
+        + lax.dot_general(lead_grads, sb_ref[...], nt, preferred_element_type=f32)
+    )
+    carry = factor * lax.dot_general(out_map, lead_grads, tn, preferred_element_type=f32)
+    rnew_ref[...] = carry + end_ref[...] * r_ref[...]
+    grad_bc = jnp.concatenate([grad_inmap, grad_outmap], axis=1).astype(bf16)
+    dbc_ref[...] = grad_bc
+    back = lax.dot_general(grad_bc, w_ref[...], nt, preferred_element_type=f32)
+    out_ref[...] = (v.astype(f32) + gx_ref[...] + back).astype(out_ref.dtype)
+
+
+def fused_step(wt, dec, v, x, in_map, out_map, tail, lead, xt, sb_t, r_t, end_col, w, factor, width):
+    length, features = v.shape
+    state_size = in_map.shape[1]
+    vmem = pl.BlockSpec(memory_space=pltpu.VMEM)
+    flops = 2 * length * features * (6 * state_size + 4 * length)
+    moved = 2 * (4 * features * state_size * 2 + 6 * length * features) + 4 * 4 * length * features
+    return pl.pallas_call(
+        functools.partial(step_kernel, factor=factor, width=width),
+        out_shape=(
+            jax.ShapeDtypeStruct((length, features), jnp.bfloat16),
+            jax.ShapeDtypeStruct(r_t.shape, jnp.float32),
+            jax.ShapeDtypeStruct((length, 2 * state_size), jnp.bfloat16),
+        ),
+        in_specs=[vmem] * 13,
+        out_specs=(vmem, vmem, vmem),
+        scratch_shapes=[pltpu.VMEM((length, features), jnp.float32)],
+        cost_estimate=pl.CostEstimate(flops=flops, bytes_accessed=moved, transcendentals=0),
+    )(wt, dec, v, x, in_map, out_map, tail, lead, xt, sb_t, r_t, end_col, w)
 
 
 def shards(layer_inputs, w_bc, log_decay, top_grad):
@@ -189,23 +226,36 @@
     rates_blk = blocked(log_decay)
     consts_fn = jax.vmap(jax.vmap(jax.vmap(lambda x, b, c, r: block_consts(x, b, c, r, factor))))
     consts = consts_fn(x_blk, in_blk, out_blk, rates_blk)
-
-    state_now = jnp.zeros(consts["fresh"].shape[1:], jnp.float32)
+    width = features // head_count
+    lead_dims = consts["tail"].shape[:3]
+    pairs = head_count * width // 128
+    per_pair = 128 // width
+    weighted = jnp.swapaxes(consts["weighted"], -1, -3)
+    weighted = weighted.reshape(lead_dims + (pairs, per_pair, block_len, block_len))
+    wt2 = jnp.swapaxes(weighted, -3, -2).reshape(lead_dims + (pairs, block_len, per_pair * block_len))
+    dec2 = jnp.moveaxis(consts["decays"], -1, -3).reshape(
+        lead_dims + (pairs, per_pair * block_len, block_len)
+    )
+    tail_full = jnp.repeat(consts["tail"], width, axis=-1)
+    lead_full = jnp.repeat(consts["lead"], width, axis=-1)
+    xt_full = consts["tail_inputs"].reshape(lead_dims + (block_len, features))
+    end_row = jnp.repeat(consts["ending"], width, axis=-1)[..., None, :]
+    fresh_t = jnp.einsum(
+        "mlsjn,mlsjd->mlsnd", in_blk, xt_full, preferred_element_type=jnp.float32
+    )
+    state_now = jnp.zeros(fresh_t.shape[1:], jnp.float32)
     saved = []
     for block_no in range(MICRO):
         saved.append(state_now.astype(jnp.bfloat16))
-        state_now = consts["ending"][block_no][..., None, None] * state_now + consts["fresh"][block_no]
-    states_b = jnp.stack(saved)
-    del consts["fresh"]
+        state_now = end_row[block_no] * state_now + fresh_t[block_no]
+    states_t = jnp.stack(saved)
+    x_flat = x_blk.reshape(lead_dims + (block_len, features))
+    per_block = (wt2, dec2, x_flat, in_blk, out_blk, tail_full, lead_full, xt_full, states_t, end_row)
 
     top_blk = jnp.moveaxis(
         top_grad.reshape((seq_dev, MICRO, block_len, features)), 1, 0
     )
     is_top = section_id == sections - 1
-    step_fn = jax.vmap(
-        lambda k, x, b, c, sb, g, r, w: block_step(k, x, b, c, sb, g, r, w, factor),
-        in_axes=(0, 0, 0, 0, 0, 0, 0, None),
-    )
 
     def advance(counter, loop_state):
         incoming, carried, grad_store, map_store = loop_state
@@ -215,40 +265,34 @@
         slot = jnp.where(is_valid, block_no, MICRO)
         from_top = lax.dynamic_index_in_dim(top_blk, block_no, 0, keepdims=False)
         current = jnp.where(is_top, from_top, incoming)
-        picked = jax.tree.map(
-            lambda a: lax.dynamic_index_in_dim(a, block_no, 0, keepdims=False), consts
-        )
-        x_now = lax.dynamic_index_in_dim(x_blk, block_no, 0, keepdims=False)
-        in_now = lax.dynamic_index_in_dim(in_blk, block_no, 0, keepdims=False)
-        out_now = lax.dynamic_index_in_dim(out_blk, block_no, 0, keepdims=False)
-        st_now = lax.dynamic_index_in_dim(states_b, block_no, 0, keepdims=False)
-        new_carried = []
+        picked = [lax.dynamic_index_in_dim(a, block_no, 0, keepdims=False) for a in per_block]
+        new_carried = [[None] * seq_dev for _ in range(lay_dev)]
         for level_no in reversed(range(lay_dev)):
-            level_grads, carry_out, grad_bc = step_fn(
-                jax.tree.map(lambda a: a[level_no], picked),
-                x_now[level_no],
-                in_now[level_no],
-                out_now[level_no],
-                st_now[level_no],
-                current,
-                carried[level_no],
-                w_bc[level_no],
-            )
-            new_carried.append(carry_out)
-            grad_store = lax.dynamic_update_slice(
-                grad_store, level_grads[None, None], (slot, level_no, 0, 0, 0)
-            )
-            map_store = lax.dynamic_update_slice(
-                map_store, grad_bc[None, None], (slot, level_no, 0, 0, 0)
-            )
-            current = level_grads
-        carried = jnp.stack(new_carried[::-1])
+            level_out = []
+            for seq_no in range(seq_dev):
+                wt_b, dec_b, x_b, in_b, out_b, tail_b, lead_b, xt_b, st_b, end_b = [
+                    a[level_no, seq_no] for a in picked
+                ]
+                level_grads, carry_out, grad_bc = fused_step(
+                    wt_b, dec_b, current[seq_no], x_b, in_b, out_b, tail_b, lead_b, xt_b, st_b,
+                    carried[level_no, seq_no], end_b, w_bc[level_no], factor, width,
+                )
+                new_carried[level_no][seq_no] = carry_out
+                grad_store = lax.dynamic_update_slice(
+                    grad_store, level_grads[None, None, None], (slot, level_no, seq_no, 0, 0)
+                )
+                map_store = lax.dynamic_update_slice(
+                    map_store, grad_bc[None, None, None], (slot, level_no, seq_no, 0, 0)
+                )
+                level_out.append(level_grads)
+            current = jnp.stack(level_out)
+        carried = jnp.stack([jnp.stack(row) for row in new_carried])
         received = passed_along(current, "section", -1)
         return (received, carried, grad_store, map_store)
 
     initial = (
         jnp.zeros((seq_dev, block_len, features), jnp.bfloat16),
-        jnp.zeros((lay_dev,) + states_b.shape[2:], jnp.float32),
+        jnp.zeros(states_t.shape[1:], jnp.float32),
         jnp.zeros((MICRO + 1, lay_dev, seq_dev, block_len, features), jnp.bfloat16),
         jnp.zeros((MICRO + 1, lay_dev, seq_dev, block_len, 2 * state_size), jnp.bfloat16),
     )

time: 182 us -> 268 us (1.47)
  local copies, waits for them, and re-layouts: 32.7 us -> 145 us
  matrix products: 55 us -> 3.73 us
  Pallas kernels: 0 us -> 30.4 us
  waiting for transfers between devices: 38 us -> 28.5 us
  other arithmetic: 28.9 us -> 32.4 us
    squeeze x0 -> x49, local copies, waits for them, and re-layouts: none -> 82.9 us  [advance(): a[level_no, seq_no]]
    dot_general x64 -> x1, matrix products: 53.5 us -> 2.2 us  [shards(): jnp.einsum('mlsjn,mlsjd->mlsnd', in_blk, xt_full, preferred_element_type=...]
    pallas_call x0 -> x7, Pallas kernels: none -> 30.4 us  [fused_step(): pl.pallas_call(functools.partial(step_kernel, factor=factor, width=width)...]
    dynamic_update_slice x0 -> x14, local copies, waits for them, and re-layouts: none -> 16.2 us  [the longest x7 11.2 us: advance(): lax.dynamic_update_slice(grad_store, level_grads[None, None, None], (slot...]
    broadcast_in_dim x0 -> x9, local copies, waits for them, and re-layouts: none -> 11.7 us  [the longest x2 4.78 us: shards(): lead_full = jnp.repeat(consts['lead'], width, axis=-1)]
    squeeze x0 -> x7, other arithmetic: none -> 11.2 us  [advance(): current[seq_no]]
    ppermute x7, waiting for transfers between devices: 38 us -> 28.5 us  [passed_along(): return lax.ppermute(block, axis, route)]
    dynamic_slice x21 -> x0, local copies, waits for them, and re-layouts: 8.54 us -> none  [advance(): lax.dynamic_index_in_dim(a, block_no, 0, keepdims=False)]
  transfers between devices with their start and end apart: 8 -> 8, of which waited for: 7 -> 7; matrix products, arithmetic and copies ran while one was open for 52% -> 60% of each run, Pallas kernels for 0% -> 11%
where the time goes in v3:
time: 268 us; the launch traced here: 265 us
  local copies, waits for them, and re-layouts  145 us (54%)
  other arithmetic  32.4 us (12%)
  Pallas kernels  30.4 us (11%)
  waiting for transfers between devices  28.5 us (11%)
  starting transfers between devices  14.1 us (5%)
  blocking collectives  9.77 us (4%)
  matrix products  3.73 us (1%)
    squeeze x49, local copies, waits for them, and re-layouts, advance(): a[level_no, seq_no]  82.9 us
    pallas_call x7, Pallas kernels, fused_step(): pl.pallas_call(functools.partial(step_kernel, factor=factor, width=width)...  30.4 us
    ppermute x7, waiting for transfers between devices, passed_along(): return lax.ppermute(block, axis, route)  28.5 us
    unnamed x1, other arithmetic  14.3 us
    squeeze x7, other arithmetic, advance(): current[seq_no]  11.2 us
    dynamic_update_slice x7, local copies, waits for them, and re-layouts, advance(): lax.dynamic_update_slice(grad_store, level_grads[None, None, None], (slot...  11.2 us
    all_gather x1, blocking collectives, shards(): maps_all = lax.all_gather(maps_here, 'dp', axis=1, tiled=True)  9.77 us
    ppermute x7, starting transfers between devices, passed_along(): return lax.ppermute(block, axis, route)  8.96 us
  transfers between devices with their start and end apart: 8, of which 7 were waited for; matrix products, arithmetic and copies ran while one was open for 60% of the time, Pallas kernels for 11%

profile of v3, /device:TPU:0, one launch (start us, length us, event | category | flops | bytes accessed | tf_op | source)
XLA Modules:
  0.0 264.5 jit_solution(7239862257025690065)
XLA Ops:
  0.6 2.5 copy.34
  3.7 14.3 %reduce = bf16[2560,128]{1,0:T(8,128)(2,1)S(1)} reduce(bf16[2560,1,128]{2,1,0:T(2,128)(2,1)S(1)} %bitcast.173, bf16[]{:T(256)} %broadcast.297), dimensions={1}, to_apply=%bitcast.132.reduce_sub_computation | reduce | bytes 1310722
  19.0 5.2 %all-to-all-start = ((bf16[8,2,20480]{2,1,0:T(2,128)(2,1)}), bf16[8,2,20480]{2,1,0:T(2,128)(2,1)}, u32[]{:S(2)}, u32[]{:S(2)}) async-start(bf16[8,2,20480]{2,1,0:T(2,128)(2,1)} %reshape.441), calls=%async_computation | async-start | bytes 1310720 | tf_op jit(solution)/shard_map/all_to_all | solution.py:308
  26.3 2.9 %mul.113 = f32[4,32,2560]{2,1,0:T(8,128)} reshape(f32[4,32,40,64]{3,2,1,0:T(8,128)} %broadcast_in_dim.90) | data formatting | bytes 2621440 | tf_op jit(solution)/shard_map/vmap(vmap(vmap()))/mul | solution.py:124
  29.2 2.2 broadcast_in_dim.91
  41.3 2.9 %broadcast_in_dim.93 = f32[4,1,1,32,2560]{4,3,2,1,0:T(8,128)} reshape(f32[4,32,40,64]{3,2,1,0:T(8,128)} %broadcast_in_dim.92) | data formatting | bytes 2621440 | tf_op jit(solution)/shard_map/broadcast_in_dim | solution.py:240
  44.3 3.0 %exponential_select_fusion = (f32[4,1,1,32,32,40]{4,3,5,0,2,1:T(8,128)}, bf16[4,1,1,32,32,40]{4,3,5,0,2,1:T(8,128)(2,1)}) fusion(f32[4,32,40]{1,2,0:T(8,128)S(1)} %copy.29, pred[32,32]{1,0:T(8,128)(4,1)} %iota_compare_fusion, f32[4,32,32]{2,1,0:T(8,128)S(1)} %convolution_multiply_fusion.1), kind=kLoop, calls=%fused_computation.16 | loop fusion | flops 819200 | bytes 1020928 | tf_op jit(solution)/shard_map/vmap(vmap(vmap(jit(_where))))/select_n | solution.py:119
  47.3 4.3 %copy.31 = bf16[4,1,1,20,2,32,32]{6,4,5,3,0,2,1:T(2,128)(2,1)} copy(bf16[4,1,1,20,2,32,32]{5,6,4,3,0,2,1:T(8,128)(2,1)} %bitcast.172) | data formatting | bytes 655360 | tf_op jit(solution)/shard_map/reshape | solution.py:234
  51.7 3.4 %reshape.434 = bf16[4,1,1,20,32,64]{5,4,3,2,1,0:T(8,128)(2,1)} reshape(bf16[4,1,1,20,32,2,32]{6,5,4,3,0,2,1:T(2,128)(2,1)} %bitcast.174) | data formatting | bytes 655360 | tf_op jit(solution)/shard_map/reshape | solution.py:235
  55.9 2.2 fusion.13
  62.4 186.4 %while.21 = (s32[]{:T(128)}, bf16[1,32,2560]{2,1,0:T(8,128)(2,1)S(1)}, f32[1,1,128,2560]{3,2,1,0:T(8,128)S(1)}, bf16[5,1,1,32,2560]{4,3,2,1,0:T(8,128)(2,1)}, bf...) while((s32[]{:T(128)}, ...), condition=%wide.region_2.3_spmd, body=%wide.region_1.2_spmd.sunk | while | flops 146882560 | bytes 15487344 | solution.py:299
  64.4 2.0 dynamic-slice_bitcast_fusion.22.sb_ref
  77.0 4.3 %eval_jaxpr.7 = (bf16[32,2560]{1,0:T(8,128)(2,1)}, f32[128,2560]{1,0:T(8,128)S(1)}, bf16[32,256]{1,0:T(8,128)(2,1)}) custom-call(bf16[20,32,64]{2,1,0:T(8,128)(2,1)} %dynamic-slice_bitcast_fusion.17.wt_ref, f32[20,64,32]{2,1,0:T(8,128)} %dynamic-slice_bitcast_fusion.18.dec_ref, bf16[32,2560]{1,0:T(8,128)(2,1)} %fusion.27.v_ref, ...), custom_call_target="tpu_custom_call" | custom-call | flops 146800640 | bytes 7536640 | tf_op jit(solution)/shard_map/while/body/eval_jaxpr/pallas_call | solution.py:190
  85.0 5.3 %collective-permute-done = bf16[1,32,2560]{2,1,0:T(8,128)(2,1)S(1)} collective-permute-done((bf16[1,32,2560]{2,1,0:T(8,128)(2,1)}, bf16[1,32,2560]{2,1,0:T(8,128)(2,1)S(1)}, u32[]{:S(2)}, u32[]{:S(2)}) %collective-permute-start) | collective-permute-done | bytes 163872 | tf_op jit(solution)/shard_map/while/body/eval_jaxpr/ppermute | solution.py:20
  92.3 2.0 dynamic-slice_bitcast_fusion.22.sb_ref
  104.9 4.3 %eval_jaxpr.7 = (bf16[32,2560]{1,0:T(8,128)(2,1)}, f32[128,2560]{1,0:T(8,128)S(1)}, bf16[32,256]{1,0:T(8,128)(2,1)}) custom-call(bf16[20,32,64]{2,1,0:T(8,128)(2,1)} %dynamic-slice_bitcast_fusion.17.wt_ref, f32[20,64,32]{2,1,0:T(8,128)} %dynamic-slice_bitcast_fusion.18.dec_ref, bf16[32,2560]{1,0:T(8,128)(2,1)} %fusion.27.v_ref, ...), custom_call_target="tpu_custom_call" | custom-call | flops 146800640 | bytes 7536640 | tf_op jit(solution)/shard_map/while/body/eval_jaxpr/pallas_call | solution.py:190
  112.8 4.3 %collective-permute-done = bf16[1,32,2560]{2,1,0:T(8,128)(2,1)S(1)} collective-permute-done((bf16[1,32,2560]{2,1,0:T(8,128)(2,1)}, bf16[1,32,2560]{2,1,0:T(8,128)(2,1)S(1)}, u32[]{:S(2)}, u32[]{:S(2)}) %collective-permute-start) | collective-permute-done | bytes 163872 | tf_op jit(solution)/shard_map/while/body/eval_jaxpr/ppermute | solution.py:20
  119.1 2.0 dynamic-slice_bitcast_fusion.22.sb_ref
  131.7 4.3 %eval_jaxpr.7 = (bf16[32,2560]{1,0:T(8,128)(2,1)}, f32[128,2560]{1,0:T(8,128)S(1)}, bf16[32,256]{1,0:T(8,128)(2,1)}) custom-call(bf16[20,32,64]{2,1,0:T(8,128)(2,1)} %dynamic-slice_bitcast_fusion.17.wt_ref, f32[20,64,32]{2,1,0:T(8,128)} %dynamic-slice_bitcast_fusion.18.dec_ref, bf16[32,2560]{1,0:T(8,128)(2,1)} %fusion.27.v_ref, ...), custom_call_target="tpu_custom_call" | custom-call | flops 146800640 | bytes 7536640 | tf_op jit(solution)/shard_map/while/body/eval_jaxpr/pallas_call | solution.py:190
  139.6 3.8 %collective-permute-done = bf16[1,32,2560]{2,1,0:T(8,128)(2,1)S(1)} collective-permute-done((bf16[1,32,2560]{2,1,0:T(8,128)(2,1)}, bf16[1,32,2560]{2,1,0:T(8,128)(2,1)S(1)}, u32[]{:S(2)}, u32[]{:S(2)}) %collective-permute-start) | collective-permute-done | bytes 163872 | tf_op jit(solution)/shard_map/while/body/eval_jaxpr/ppermute | solution.py:20
  145.4 2.0 dynamic-slice_bitcast_fusion.22.sb_ref
  158.0 4.3 %eval_jaxpr.7 = (bf16[32,2560]{1,0:T(8,128)(2,1)}, f32[128,2560]{1,0:T(8,128)S(1)}, bf16[32,256]{1,0:T(8,128)(2,1)}) custom-call(bf16[20,32,64]{2,1,0:T(8,128)(2,1)} %dynamic-slice_bitcast_fusion.17.wt_ref, f32[20,64,32]{2,1,0:T(8,128)} %dynamic-slice_bitcast_fusion.18.dec_ref, bf16[32,2560]{1,0:T(8,128)(2,1)} %fusion.27.v_ref, ...), custom_call_target="tpu_custom_call" | custom-call | flops 146800640 | bytes 7536640 | tf_op jit(solution)/shard_map/while/body/eval_jaxpr/pallas_call | solution.py:190
  166.0 3.8 %collective-permute-done = bf16[1,32,2560]{2,1,0:T(8,128)(2,1)S(1)} collective-permute-done((bf16[1,32,2560]{2,1,0:T(8,128)(2,1)}, bf16[1,32,2560]{2,1,0:T(8,128)(2,1)S(1)}, u32[]{:S(2)}, u32[]{:S(2)}) %collective-permute-start) | collective-permute-done | bytes 163872 | tf_op jit(solution)/shard_map/while/body/eval_jaxpr/ppermute | solution.py:20
  171.8 2.0 dynamic-slice_bitcast_fusion.22.sb_ref
  184.4 4.3 %eval_jaxpr.7 = (bf16[32,2560]{1,0:T(8,128)(2,1)}, f32[128,2560]{1,0:T(8,128)S(1)}, bf16[32,256]{1,0:T(8,128)(2,1)}) custom-call(bf16[20,32,64]{2,1,0:T(8,128)(2,1)} %dynamic-slice_bitcast_fusion.17.wt_ref, f32[20,64,32]{2,1,0:T(8,128)} %dynamic-slice_bitcast_fusion.18.dec_ref, bf16[32,2560]{1,0:T(8,128)(2,1)} %fusion.27.v_ref, ...), custom_call_target="tpu_custom_call" | custom-call | flops 146800640 | bytes 7536640 | tf_op jit(solution)/shard_map/while/body/eval_jaxpr/pallas_call | solution.py:190
  192.4 3.8 %collective-permute-done = bf16[1,32,2560]{2,1,0:T(8,128)(2,1)S(1)} collective-permute-done((bf16[1,32,2560]{2,1,0:T(8,128)(2,1)}, bf16[1,32,2560]{2,1,0:T(8,128)(2,1)S(1)}, u32[]{:S(2)}, u32[]{:S(2)}) %collective-permute-start) | collective-permute-done | bytes 163872 | tf_op jit(solution)/shard_map/while/body/eval_jaxpr/ppermute | solution.py:20
  210.7 4.3 %eval_jaxpr.7 = (bf16[32,2560]{1,0:T(8,128)(2,1)}, f32[128,2560]{1,0:T(8,128)S(1)}, bf16[32,256]{1,0:T(8,128)(2,1)}) custom-call(bf16[20,32,64]{2,1,0:T(8,128)(2,1)} %dynamic-slice_bitcast_fusion.17.wt_ref, f32[20,64,32]{2,1,0:T(8,128)} %dynamic-slice_bitcast_fusion.18.dec_ref, bf16[32,2560]{1,0:T(8,128)(2,1)} %fusion.27.v_ref, ...), custom_call_target="tpu_custom_call" | custom-call | flops 146800640 | bytes 7536640 | tf_op jit(solution)/shard_map/while/body/eval_jaxpr/pallas_call | solution.py:190
  218.7 3.8 %collective-permute-done = bf16[1,32,2560]{2,1,0:T(8,128)(2,1)S(1)} collective-permute-done((bf16[1,32,2560]{2,1,0:T(8,128)(2,1)}, bf16[1,32,2560]{2,1,0:T(8,128)(2,1)S(1)}, u32[]{:S(2)}, u32[]{:S(2)}) %collective-permute-start) | collective-permute-done | bytes 163872 | tf_op jit(solution)/shard_map/while/body/eval_jaxpr/ppermute | solution.py:20
  237.1 4.3 %eval_jaxpr.7 = (bf16[32,2560]{1,0:T(8,128)(2,1)}, f32[128,2560]{1,0:T(8,128)S(1)}, bf16[32,256]{1,0:T(8,128)(2,1)}) custom-call(bf16[20,32,64]{2,1,0:T(8,128)(2,1)} %dynamic-slice_bitcast_fusion.17.wt_ref, f32[20,64,32]{2,1,0:T(8,128)} %dynamic-slice_bitcast_fusion.18.dec_ref, bf16[32,2560]{1,0:T(8,128)(2,1)} %fusion.27.v_ref, ...), custom_call_target="tpu_custom_call" | custom-call | flops 146800640 | bytes 7536640 | tf_op jit(solution)/shard_map/while/body/eval_jaxpr/pallas_call | solution.py:190
  245.1 3.8 %collective-permute-done = bf16[1,32,2560]{2,1,0:T(8,128)(2,1)S(1)} collective-permute-done((bf16[1,32,2560]{2,1,0:T(8,128)(2,1)}, bf16[1,32,2560]{2,1,0:T(8,128)(2,1)S(1)}, u32[]{:S(2)}, u32[]{:S(2)}) %collective-permute-start) | collective-permute-done | bytes 163872 | tf_op jit(solution)/shard_map/while/body/eval_jaxpr/ppermute | solution.py:20
  250.8 9.8 %all_gather.3 = bf16[1,1024,256]{2,1,0:T(8,128)(2,1)S(1)} all-gather(bf16[1,128,256]{2,1,0:T(8,128)(2,1)S(1)} %bitcast.185), channel_id=1, replica_groups=mesh['section'=4,'dp'=8] {'dp'}, dimensions={1}, use_global_device_ids=true | all-gather | bytes 589824 | tf_op jit(solution)/shard_map/all_gather | solution.py:310
  260.6 2.3 reshape.442
  (134 shorter events, 139.4 us)
Async XLA Ops:
  17.9 6.2 %copy-start.6 = (f32[1,1,128,40]{2,3,1,0:T(8,128)S(1)}, f32[1,1,128,40]{2,3,1,0:T(8,128)}, u32[]{:S(2)}) copy-start(f32[1,1,128,40]{2,3,1,0:T(8,128)} %param.8) | copy-start | bytes 61444
  19.0 241.6 %all-to-all-start = ((bf16[8,2,20480]{2,1,0:T(2,128)(2,1)}), bf16[8,2,20480]{2,1,0:T(2,128)(2,1)}, u32[]{:S(2)}, u32[]{:S(2)}) async-start(bf16[8,2,20480]{2,1,0:T(2,128)(2,1)} %reshape.441), calls=%async_computation | async-start | bytes 1310720 | tf_op jit(solution)/shard_map/all_to_all | solution.py:308
  24.4 8.8 %copy-start.7 = (f32[4,40]{1,0:T(4,128)}, f32[4,40]{1,0:T(4,128)S(1)}, u32[]{:S(2)}) copy-start(f32[4,40]{1,0:T(4,128)S(1)} %exp.40) | copy-start | bytes 1924
  29.2 2.9 %copy-start = (bf16[1,2560,256]{2,1,0:T(8,128)(2,1)S(1)}, bf16[1,2560,256]{2,1,0:T(8,128)(2,1)}, u32[]{:S(2)}) copy-start(bf16[1,2560,256]{2,1,0:T(8,128)(2,1)} %param.7) | copy-start | bytes 3932164
  29.2 2.9 %copy-start.1 = (bf16[1,1,128,2560]{3,2,1,0:T(8,128)(2,1)S(1)}, bf16[1,1,128,2560]{3,2,1,0:T(8,128)(2,1)}, u32[]{:S(2)}) copy-start(bf16[1,1,128,2560]{3,2,1,0:T(8,128)(2,1)} %param.6) | copy-start | bytes 1966084
  31.4 26.7 %copy-start.2 = (f32[4,1,1,32,2560]{4,3,2,1,0:T(8,128)}, f32[4,1,1,32,2560]{4,3,2,1,0:T(8,128)S(1)}, u32[]{:S(2)}) copy-start(f32[4,1,1,32,2560]{4,3,2,1,0:T(8,128)S(1)} %broadcast_in_dim.91) | copy-start | bytes 3932164
  51.7 3.4 %copy-start.8 = (f32[4,40]{1,0:T(4,128)S(1)}, f32[4,40]{1,0:T(4,128)}, u32[]{:S(2)}) copy-start(f32[4,40]{1,0:T(4,128)} %copy-done.7) | copy-start | bytes 1924
  58.1 1.0 copy-start.3
  58.1 1.0 copy-start.4
  58.1 1.0 copy-start.5
  81.4 8.9 %collective-permute-start = (bf16[1,32,2560]{2,1,0:T(8,128)(2,1)}, bf16[1,32,2560]{2,1,0:T(8,128)(2,1)S(1)}, u32[]{:S(2)}, u32[]{:S(2)}) collective-permute-start(bf16[1,32,2560]{2,1,0:T(8,128)(2,1)} %bitcast.176), channel_id=1, source_target_pairs={{8,0},{16,8},{24,16},{9,1},{17,9},{25,17},{10,2},{18,10},{26,18},{... | collective-permute-start | bytes 491528 | tf_op jit(solution)/shard_map/while/body/eval_jaxpr/ppermute | solution.py:20
  109.2 7.9 %collective-permute-start = (bf16[1,32,2560]{2,1,0:T(8,128)(2,1)}, bf16[1,32,2560]{2,1,0:T(8,128)(2,1)S(1)}, u32[]{:S(2)}, u32[]{:S(2)}) collective-permute-start(bf16[1,32,2560]{2,1,0:T(8,128)(2,1)} %bitcast.176), channel_id=1, source_target_pairs={{8,0},{16,8},{24,16},{9,1},{17,9},{25,17},{10,2},{18,10},{26,18},{... | collective-permute-start | bytes 491528 | tf_op jit(solution)/shard_map/while/body/eval_jaxpr/ppermute | solution.py:20
  136.0 7.4 %collective-permute-start = (bf16[1,32,2560]{2,1,0:T(8,128)(2,1)}, bf16[1,32,2560]{2,1,0:T(8,128)(2,1)S(1)}, u32[]{:S(2)}, u32[]{:S(2)}) collective-permute-start(bf16[1,32,2560]{2,1,0:T(8,128)(2,1)} %bitcast.176), channel_id=1, source_target_pairs={{8,0},{16,8},{24,16},{9,1},{17,9},{25,17},{10,2},{18,10},{26,18},{... | collective-permute-start | bytes 491528 | tf_op jit(solution)/shard_map/while/body/eval_jaxpr/ppermute | solution.py:20
  162.4 7.4 %collective-permute-start = (bf16[1,32,2560]{2,1,0:T(8,128)(2,1)}, bf16[1,32,2560]{2,1,0:T(8,128)(2,1)S(1)}, u32[]{:S(2)}, u32[]{:S(2)}) collective-permute-start(bf16[1,32,2560]{2,1,0:T(8,128)(2,1)} %bitcast.176), channel_id=1, source_target_pairs={{8,0},{16,8},{24,16},{9,1},{17,9},{25,17},{10,2},{18,10},{26,18},{... | collective-permute-start | bytes 491528 | tf_op jit(solution)/shard_map/while/body/eval_jaxpr/ppermute | solution.py:20
  188.7 7.4 %collective-permute-start = (bf16[1,32,2560]{2,1,0:T(8,128)(2,1)}, bf16[1,32,2560]{2,1,0:T(8,128)(2,1)S(1)}, u32[]{:S(2)}, u32[]{:S(2)}) collective-permute-start(bf16[1,32,2560]{2,1,0:T(8,128)(2,1)} %bitcast.176), channel_id=1, source_target_pairs={{8,0},{16,8},{24,16},{9,1},{17,9},{25,17},{10,2},{18,10},{26,18},{... | collective-permute-start | bytes 491528 | tf_op jit(solution)/shard_map/while/body/eval_jaxpr/ppermute | solution.py:20
  215.1 7.4 %collective-permute-start = (bf16[1,32,2560]{2,1,0:T(8,128)(2,1)}, bf16[1,32,2560]{2,1,0:T(8,128)(2,1)S(1)}, u32[]{:S(2)}, u32[]{:S(2)}) collective-permute-start(bf16[1,32,2560]{2,1,0:T(8,128)(2,1)} %bitcast.176), channel_id=1, source_target_pairs={{8,0},{16,8},{24,16},{9,1},{17,9},{25,17},{10,2},{18,10},{26,18},{... | collective-permute-start | bytes 491528 | tf_op jit(solution)/shard_map/while/body/eval_jaxpr/ppermute | solution.py:20
  241.4 7.4 %collective-permute-start = (bf16[1,32,2560]{2,1,0:T(8,128)(2,1)}, bf16[1,32,2560]{2,1,0:T(8,128)(2,1)S(1)}, u32[]{:S(2)}, u32[]{:S(2)}) collective-permute-start(bf16[1,32,2560]{2,1,0:T(8,128)(2,1)} %bitcast.176), channel_id=1, source_target_pairs={{8,0},{16,8},{24,16},{9,1},{17,9},{25,17},{10,2},{18,10},{26,18},{... | collective-permute-start | bytes 491528 | tf_op jit(solution)/shard_map/while/body/eval_jaxpr/ppermute | solution.py:20

commit v4 on v3

--- a/solution.py
+++ b/solution.py
@@ -135,8 +135,9 @@
 
 
 def step_kernel(
-    wt_ref, dec_ref, v_ref, x_ref, b_ref, c_ref, tail_ref, lead_ref, xt_ref, sb_ref, r_ref, end_ref,
-    w_ref, out_ref, rnew_ref, dbc_ref, gx_ref, *, factor, width
+    picks_ref, wt_ref, dec_ref, inc_ref, top_ref, x_ref, b_ref, c_ref, tail_ref, lead_ref, xt_ref,
+    sb_ref, r_ref, end_ref, w_ref, gs_ref, ms_ref, out_ref, rnew_ref, dbc_ref, gstore_ref, mstore_ref,
+    v_ref, gx_ref, *, factor, width
 ):
     f32 = jnp.float32
     bf16 = jnp.bfloat16
@@ -145,6 +146,7 @@
     per_pair = lanes // width
     nt = (((1,), (1,)), ((), ()))
     tn = (((0,), (0,)), ((), ()))
+    v_ref[...] = jnp.where(picks_ref[1] > 0, top_ref[...], inc_ref[...])
     rb_t = r_ref[...].astype(bf16)
     in_map = b_ref[...]
     out_map = c_ref[...]
@@ -177,28 +179,64 @@
     rnew_ref[...] = carry + end_ref[...] * r_ref[...]
     grad_bc = jnp.concatenate([grad_inmap, grad_outmap], axis=1).astype(bf16)
     dbc_ref[...] = grad_bc
+    mstore_ref[...] = grad_bc
     back = lax.dot_general(grad_bc, w_ref[...], nt, preferred_element_type=f32)
-    out_ref[...] = (v.astype(f32) + gx_ref[...] + back).astype(out_ref.dtype)
-
-
-def fused_step(wt, dec, v, x, in_map, out_map, tail, lead, xt, sb_t, r_t, end_col, w, factor, width):
-    length, features = v.shape
-    state_size = in_map.shape[1]
-    vmem = pl.BlockSpec(memory_space=pltpu.VMEM)
+    summed = (v.astype(f32) + gx_ref[...] + back).astype(out_ref.dtype)
+    out_ref[...] = summed
+    gstore_ref[...] = summed
+
+
+def fused_step(picks, per_block, incoming, top_blk, carried, w_bc, grad_store, map_store, level_no, seq_no, factor, width):
+    wt2, dec2, x_flat, in_blk, out_blk, tail_full, lead_full, xt_full, states_t, end_row = per_block
+    length, features = incoming.shape[1:]
+    state_size = in_blk.shape[-1]
+
+    def lead_block(a):
+        shape = (None, None, None) + a.shape[3:]
+        tail = (0,) * (a.ndim - 3)
+        return pl.BlockSpec(shape, lambda i, p: (p[0], level_no, seq_no) + tail)
+
+    in_specs = [lead_block(a) for a in (wt2, dec2)]
+    in_specs.append(pl.BlockSpec((None, length, features), lambda i, p: (seq_no, 0, 0)))
+    in_specs.append(pl.BlockSpec((None, None, length, features), lambda i, p: (p[0], seq_no, 0, 0)))
+    in_specs += [lead_block(a) for a in (x_flat, in_blk, out_blk, tail_full, lead_full, xt_full, states_t)]
+    in_specs.append(pl.BlockSpec((None, None) + carried.shape[2:], lambda i, p: (level_no, seq_no, 0, 0)))
+    in_specs.append(lead_block(end_row))
+    in_specs.append(pl.BlockSpec((None,) + w_bc.shape[1:], lambda i, p: (level_no, 0, 0)))
+    store_g = pl.BlockSpec((None, None, None, length, features), lambda i, p: (p[2], level_no, seq_no, 0, 0))
+    store_m = pl.BlockSpec((None, None, None, length, 2 * state_size), lambda i, p: (p[2], level_no, seq_no, 0, 0))
+    in_specs += [store_g, store_m]
+    out_specs = (
+        pl.BlockSpec((length, features), lambda i, p: (0, 0)),
+        pl.BlockSpec((None, None) + carried.shape[2:], lambda i, p: (level_no, seq_no, 0, 0)),
+        pl.BlockSpec((length, 2 * state_size), lambda i, p: (0, 0)),
+        store_g,
+        store_m,
+    )
     flops = 2 * length * features * (6 * state_size + 4 * length)
     moved = 2 * (4 * features * state_size * 2 + 6 * length * features) + 4 * 4 * length * features
     return pl.pallas_call(
         functools.partial(step_kernel, factor=factor, width=width),
         out_shape=(
             jax.ShapeDtypeStruct((length, features), jnp.bfloat16),
-            jax.ShapeDtypeStruct(r_t.shape, jnp.float32),
+            jax.ShapeDtypeStruct(carried.shape, jnp.float32),
             jax.ShapeDtypeStruct((length, 2 * state_size), jnp.bfloat16),
+            jax.ShapeDtypeStruct(grad_store.shape, grad_store.dtype),
+            jax.ShapeDtypeStruct(map_store.shape, map_store.dtype),
         ),
-        in_specs=[vmem] * 13,
-        out_specs=(vmem, vmem, vmem),
-        scratch_shapes=[pltpu.VMEM((length, features), jnp.float32)],
+        grid_spec=pltpu.PrefetchScalarGridSpec(
+            num_scalar_prefetch=1,
+            grid=(1,),
+            in_specs=in_specs,
+            out_specs=out_specs,
+            scratch_shapes=[
+                pltpu.VMEM((length, features), jnp.bfloat16),
+                pltpu.VMEM((length, features), jnp.float32),
+            ],
+        ),
+        input_output_aliases={12: 1, 15: 3, 16: 4},
         cost_estimate=pl.CostEstimate(flops=flops, bytes_accessed=moved, transcendentals=0),
-    )(wt, dec, v, x, in_map, out_map, tail, lead, xt, sb_t, r_t, end_col, w)
+    )(picks, wt2, dec2, incoming, top_blk, x_flat, in_blk, out_blk, tail_full, lead_full, xt_full, states_t, carried, end_row, w_bc, grad_store, map_store)
 
 
 def shards(layer_inputs, w_bc, log_decay, top_grad):
@@ -263,31 +301,18 @@
         is_valid = (offset >= 0) & (offset < MICRO)
         block_no = jnp.clip(MICRO - 1 - offset, 0, MICRO - 1)
         slot = jnp.where(is_valid, block_no, MICRO)
-        from_top = lax.dynamic_index_in_dim(top_blk, block_no, 0, keepdims=False)
-        current = jnp.where(is_top, from_top, incoming)
-        picked = [lax.dynamic_index_in_dim(a, block_no, 0, keepdims=False) for a in per_block]
-        new_carried = [[None] * seq_dev for _ in range(lay_dev)]
+        picks = jnp.stack([block_no, is_top.astype(jnp.int32), slot]).astype(jnp.int32)
         for level_no in reversed(range(lay_dev)):
             level_out = []
             for seq_no in range(seq_dev):
-                wt_b, dec_b, x_b, in_b, out_b, tail_b, lead_b, xt_b, st_b, end_b = [
-                    a[level_no, seq_no] for a in picked
-                ]
-                level_grads, carry_out, grad_bc = fused_step(
-                    wt_b, dec_b, current[seq_no], x_b, in_b, out_b, tail_b, lead_b, xt_b, st_b,
-                    carried[level_no, seq_no], end_b, w_bc[level_no], factor, width,
-                )
-                new_carried[level_no][seq_no] = carry_out
-                grad_store = lax.dynamic_update_slice(
-                    grad_store, level_grads[None, None, None], (slot, level_no, seq_no, 0, 0)
-                )
-                map_store = lax.dynamic_update_slice(
-                    map_store, grad_bc[None, None, None], (slot, level_no, seq_no, 0, 0)
+                level_grads, carried, grad_bc, grad_store, map_store = fused_step(
+                    picks, per_block, incoming, top_blk, carried, w_bc, grad_store, map_store,
+                    level_no, seq_no, factor, width,
                 )
                 level_out.append(level_grads)
-            current = jnp.stack(level_out)
-        carried = jnp.stack([jnp.stack(row) for row in new_carried])
-        received = passed_along(current, "section", -1)
+            incoming = jnp.stack(level_out)
+            picks = picks.at[1].set(0)
+        received = passed_along(incoming, "section", -1)
         return (received, carried, grad_store, map_store)
 
     initial = (

time: 268 us -> 253 us (0.944)
  local copies, waits for them, and re-layouts: 145 us -> 95.8 us
  waiting for transfers between devices: 28.5 us -> 44.8 us
  Pallas kernels: 30.4 us -> 40.4 us
  other arithmetic: 32.4 us -> 42.2 us
    squeeze x49 -> x0, local copies, waits for them, and re-layouts: 82.9 us -> none  [advance(): a[level_no, seq_no]]
    broadcast_in_dim x2 -> x14, local copies, waits for them, and re-layouts: 4.78 us -> 22.7 us  [shards(): lead_full = jnp.repeat(consts['lead'], width, axis=-1)]
    broadcast_in_dim x2 -> x16, local copies, waits for them, and re-layouts: 4.13 us -> 20.8 us  [shards(): tail_full = jnp.repeat(consts['tail'], width, axis=-1)]
    ppermute x7, waiting for transfers between devices: 28.5 us -> 44.8 us  [passed_along(): return lax.ppermute(block, axis, route)]
    dynamic_update_slice x14 -> x0, local copies, waits for them, and re-layouts: 16.2 us -> none  [the longest x7 11.2 us: advance(): lax.dynamic_update_slice(grad_store, level_grads[None, None, None], (slot...]
    squeeze x7 -> x0, other arithmetic: 11.2 us -> none  [advance(): current[seq_no]]
    select_n x1 -> x7, other arithmetic: 3.05 us -> 13.5 us  [block_consts(): decays = jnp.where(lower_mask, jnp.exp(spread), 0.0)]
    pallas_call x7, Pallas kernels: 30.4 us -> 40.4 us  [fused_step(): pl.pallas_call(functools.partial(step_kernel, factor=factor, width=width)...]
  transfers between devices with their start and end apart: 8 -> 8, of which waited for: 7 -> 7; matrix products, arithmetic and copies ran while one was open for 60% -> 46% of each run, Pallas kernels for 11% -> 16%
where the time goes in v4:
time: 253 us; the launch traced here: 252 us
  local copies, waits for them, and re-layouts  95.8 us (38%)
  waiting for transfers between devices  44.8 us (18%)
  other arithmetic  42.2 us (17%)
  Pallas kernels  40.4 us (16%)
  starting transfers between devices  14.1 us (6%)
  blocking collectives  9.77 us (4%)
  matrix products  3.05 us (1%)
    ppermute x7, waiting for transfers between devices, passed_along(): return lax.ppermute(block, axis, route)  44.8 us
    pallas_call x7, Pallas kernels, fused_step(): pl.pallas_call(functools.partial(step_kernel, factor=factor, width=width)...  40.4 us
    broadcast_in_dim x14, local copies, waits for them, and re-layouts, shards(): lead_full = jnp.repeat(consts['lead'], width, axis=-1)  22.7 us
    broadcast_in_dim x16, local copies, waits for them, and re-layouts, shards(): tail_full = jnp.repeat(consts['tail'], width, axis=-1)  20.8 us
    unnamed x1, other arithmetic  14.3 us
    select_n x7, other arithmetic, block_consts(): decays = jnp.where(lower_mask, jnp.exp(spread), 0.0)  13.5 us
    reshape x7, local copies, waits for them, and re-layouts, shards(): jnp.swapaxes(weighted, -3, -2)  10.6 us
    broadcast_in_dim x17, local copies, waits for them, and re-layouts, shards(): end_row = jnp.repeat(consts['ending'], width, axis=-1)[..., None, :]  10.5 us
  transfers between devices with their start and end apart: 8, of which 7 were waited for; matrix products, arithmetic and copies ran while one was open for 46% of the time, Pallas kernels for 16%

profile of v4, /device:TPU:0, one launch (start us, length us, event | category | flops | bytes accessed | tf_op | source)
XLA Modules:
  0.0 251.5 jit_solution(7917165624958050773)
XLA Ops:
  0.6 2.5 copy.40
  3.7 14.3 %reduce = bf16[2560,128]{1,0:T(8,128)(2,1)S(1)} reduce(bf16[2560,1,128]{2,1,0:T(2,128)(2,1)S(1)} %bitcast.126, bf16[]{:T(256)} %broadcast.297), dimensions={1}, to_apply=%bitcast.105.reduce_sub_computation | reduce | bytes 1310722
  18.9 5.2 %all-to-all-start = ((bf16[8,2,20480]{2,1,0:T(2,128)(2,1)}), bf16[8,2,20480]{2,1,0:T(2,128)(2,1)}, u32[]{:S(2)}, u32[]{:S(2)}) async-start(bf16[8,2,20480]{2,1,0:T(2,128)(2,1)} %reshape.449), calls=%async_computation | async-start | bytes 1310720 | tf_op jit(solution)/shard_map/all_to_all | solution.py:333
  29.5 3.0 %broadcast_in_dim.73 = f32[4,1,1,32,2560]{4,3,2,1,0:T(8,128)} reshape(f32[4,32,40,64]{3,2,1,0:T(8,128)} %copy-done.3) | data formatting | bytes 2621440 | tf_op jit(solution)/shard_map/broadcast_in_dim | solution.py:277
  40.9 1.8 pad_maximum_fusion
  45.5 189.5 %while.23 = (s32[]{:T(128)}, bf16[1,32,2560]{2,1,0:T(8,128)(2,1)S(1)}, f32[1,1,128,2560]{3,2,1,0:T(8,128)}, bf16[5,1,1,32,2560]{4,3,2,1,0:T(8,128)(2,1)}, bf16[5...) while((s32[]{:T(128)}, ...), condition=%wide.region_2.3_spmd.clone.clone, body=%wide.region_1.2_spmd.clone.clone.sunk | while | flops 148111376 | bytes 23970932 | solution.py:324
  49.4 1.9 exponential_select_fusion.2
  52.1 1.7 broadcast_in_dim.150.tail_ref
  59.1 5.8 %eval_jaxpr.7 = (bf16[32,2560]{1,0:T(8,128)(2,1)}, f32[1,1,128,2560]{3,2,1,0:T(8,128)}, bf16[32,256]{1,0:T(8,128)(2,1)}, bf16[5,1,1,32,2560]{4,3,2,1,0:T(8,128)(2,1)}, bf16[5,1,1,32,256]{4,3,2,1,0:T(8,128)(2,1)}) custom-call(s32[3]{0:T(128)} %pad_add_fusion.2.picks_ref, ...), custom_call_target="tpu_custom_call", output_to_operand_aliasing={{1}: (12, {}), {3}: (15, {}), {4}: (16, {})} | custom-call | flops 146800640 | bytes 7536640 | tf_op jit(solution)/shard_map/while/body/eval_jaxpr/pallas_call | solution.py:218
  66.2 7.6 %collective-permute-done = bf16[1,32,2560]{2,1,0:T(8,128)(2,1)S(1)} collective-permute-done((bf16[1,32,2560]{2,1,0:T(8,128)(2,1)}, bf16[1,32,2560]{2,1,0:T(8,128)(2,1)S(1)}, u32[]{:S(2)}, u32[]{:S(2)}) %collective-permute-start) | collective-permute-done | bytes 163872 | tf_op jit(solution)/shard_map/while/body/eval_jaxpr/ppermute | solution.py:20
  77.7 1.9 exponential_select_fusion.2
  80.4 1.7 broadcast_in_dim.150.tail_ref
  87.4 5.8 %eval_jaxpr.7 = (bf16[32,2560]{1,0:T(8,128)(2,1)}, f32[1,1,128,2560]{3,2,1,0:T(8,128)}, bf16[32,256]{1,0:T(8,128)(2,1)}, bf16[5,1,1,32,2560]{4,3,2,1,0:T(8,128)(2,1)}, bf16[5,1,1,32,256]{4,3,2,1,0:T(8,128)(2,1)}) custom-call(s32[3]{0:T(128)} %pad_add_fusion.2.picks_ref, ...), custom_call_target="tpu_custom_call", output_to_operand_aliasing={{1}: (12, {}), {3}: (15, {}), {4}: (16, {})} | custom-call | flops 146800640 | bytes 7536640 | tf_op jit(solution)/shard_map/while/body/eval_jaxpr/pallas_call | solution.py:218
  94.5 6.6 %collective-permute-done = bf16[1,32,2560]{2,1,0:T(8,128)(2,1)S(1)} collective-permute-done((bf16[1,32,2560]{2,1,0:T(8,128)(2,1)}, bf16[1,32,2560]{2,1,0:T(8,128)(2,1)S(1)}, u32[]{:S(2)}, u32[]{:S(2)}) %collective-permute-start) | collective-permute-done | bytes 163872 | tf_op jit(solution)/shard_map/while/body/eval_jaxpr/ppermute | solution.py:20
  105.0 1.9 exponential_select_fusion.2
  114.7 5.8 %eval_jaxpr.7 = (bf16[32,2560]{1,0:T(8,128)(2,1)}, f32[1,1,128,2560]{3,2,1,0:T(8,128)}, bf16[32,256]{1,0:T(8,128)(2,1)}, bf16[5,1,1,32,2560]{4,3,2,1,0:T(8,128)(2,1)}, bf16[5,1,1,32,256]{4,3,2,1,0:T(8,128)(2,1)}) custom-call(s32[3]{0:T(128)} %pad_add_fusion.2.picks_ref, ...), custom_call_target="tpu_custom_call", output_to_operand_aliasing={{1}: (12, {}), {3}: (15, {}), {4}: (16, {})} | custom-call | flops 146800640 | bytes 7536640 | tf_op jit(solution)/shard_map/while/body/eval_jaxpr/pallas_call | solution.py:218
  121.8 6.1 %collective-permute-done = bf16[1,32,2560]{2,1,0:T(8,128)(2,1)S(1)} collective-permute-done((bf16[1,32,2560]{2,1,0:T(8,128)(2,1)}, bf16[1,32,2560]{2,1,0:T(8,128)(2,1)S(1)}, u32[]{:S(2)}, u32[]{:S(2)}) %collective-permute-start) | collective-permute-done | bytes 163872 | tf_op jit(solution)/shard_map/while/body/eval_jaxpr/ppermute | solution.py:20
  131.8 1.9 exponential_select_fusion.2
  141.5 5.7 %eval_jaxpr.7 = (bf16[32,2560]{1,0:T(8,128)(2,1)}, f32[1,1,128,2560]{3,2,1,0:T(8,128)}, bf16[32,256]{1,0:T(8,128)(2,1)}, bf16[5,1,1,32,2560]{4,3,2,1,0:T(8,128)(2,1)}, bf16[5,1,1,32,256]{4,3,2,1,0:T(8,128)(2,1)}) custom-call(s32[3]{0:T(128)} %pad_add_fusion.2.picks_ref, ...), custom_call_target="tpu_custom_call", output_to_operand_aliasing={{1}: (12, {}), {3}: (15, {}), {4}: (16, {})} | custom-call | flops 146800640 | bytes 7536640 | tf_op jit(solution)/shard_map/while/body/eval_jaxpr/pallas_call | solution.py:218
  148.5 6.1 %collective-permute-done = bf16[1,32,2560]{2,1,0:T(8,128)(2,1)S(1)} collective-permute-done((bf16[1,32,2560]{2,1,0:T(8,128)(2,1)}, bf16[1,32,2560]{2,1,0:T(8,128)(2,1)S(1)}, u32[]{:S(2)}, u32[]{:S(2)}) %collective-permute-start) | collective-permute-done | bytes 163872 | tf_op jit(solution)/shard_map/while/body/eval_jaxpr/ppermute | solution.py:20
  158.6 1.9 exponential_select_fusion.2
  168.2 5.8 %eval_jaxpr.7 = (bf16[32,2560]{1,0:T(8,128)(2,1)}, f32[1,1,128,2560]{3,2,1,0:T(8,128)}, bf16[32,256]{1,0:T(8,128)(2,1)}, bf16[5,1,1,32,2560]{4,3,2,1,0:T(8,128)(2,1)}, bf16[5,1,1,32,256]{4,3,2,1,0:T(8,128)(2,1)}) custom-call(s32[3]{0:T(128)} %pad_add_fusion.2.picks_ref, ...), custom_call_target="tpu_custom_call", output_to_operand_aliasing={{1}: (12, {}), {3}: (15, {}), {4}: (16, {})} | custom-call | flops 146800640 | bytes 7536640 | tf_op jit(solution)/shard_map/while/body/eval_jaxpr/pallas_call | solution.py:218
  175.3 6.1 %collective-permute-done = bf16[1,32,2560]{2,1,0:T(8,128)(2,1)S(1)} collective-permute-done((bf16[1,32,2560]{2,1,0:T(8,128)(2,1)}, bf16[1,32,2560]{2,1,0:T(8,128)(2,1)S(1)}, u32[]{:S(2)}, u32[]{:S(2)}) %collective-permute-start) | collective-permute-done | bytes 163872 | tf_op jit(solution)/shard_map/while/body/eval_jaxpr/ppermute | solution.py:20
  185.4 1.9 exponential_select_fusion.2
  195.0 5.8 %eval_jaxpr.7 = (bf16[32,2560]{1,0:T(8,128)(2,1)}, f32[1,1,128,2560]{3,2,1,0:T(8,128)}, bf16[32,256]{1,0:T(8,128)(2,1)}, bf16[5,1,1,32,2560]{4,3,2,1,0:T(8,128)(2,1)}, bf16[5,1,1,32,256]{4,3,2,1,0:T(8,128)(2,1)}) custom-call(s32[3]{0:T(128)} %pad_add_fusion.2.picks_ref, ...), custom_call_target="tpu_custom_call", output_to_operand_aliasing={{1}: (12, {}), {3}: (15, {}), {4}: (16, {})} | custom-call | flops 146800640 | bytes 7536640 | tf_op jit(solution)/shard_map/while/body/eval_jaxpr/pallas_call | solution.py:218
  202.1 6.1 %collective-permute-done = bf16[1,32,2560]{2,1,0:T(8,128)(2,1)S(1)} collective-permute-done((bf16[1,32,2560]{2,1,0:T(8,128)(2,1)}, bf16[1,32,2560]{2,1,0:T(8,128)(2,1)S(1)}, u32[]{:S(2)}, u32[]{:S(2)}) %collective-permute-start) | collective-permute-done | bytes 163872 | tf_op jit(solution)/shard_map/while/body/eval_jaxpr/ppermute | solution.py:20
  212.1 1.9 exponential_select_fusion.2
  221.8 5.8 %eval_jaxpr.7 = (bf16[32,2560]{1,0:T(8,128)(2,1)}, f32[1,1,128,2560]{3,2,1,0:T(8,128)}, bf16[32,256]{1,0:T(8,128)(2,1)}, bf16[5,1,1,32,2560]{4,3,2,1,0:T(8,128)(2,1)}, bf16[5,1,1,32,256]{4,3,2,1,0:T(8,128)(2,1)}) custom-call(s32[3]{0:T(128)} %pad_add_fusion.2.picks_ref, ...), custom_call_target="tpu_custom_call", output_to_operand_aliasing={{1}: (12, {}), {3}: (15, {}), {4}: (16, {})} | custom-call | flops 146800640 | bytes 7536640 | tf_op jit(solution)/shard_map/while/body/eval_jaxpr/pallas_call | solution.py:218
  228.9 6.1 %collective-permute-done = bf16[1,32,2560]{2,1,0:T(8,128)(2,1)S(1)} collective-permute-done((bf16[1,32,2560]{2,1,0:T(8,128)(2,1)}, bf16[1,32,2560]{2,1,0:T(8,128)(2,1)S(1)}, u32[]{:S(2)}, u32[]{:S(2)}) %collective-permute-start) | collective-permute-done | bytes 163872 | tf_op jit(solution)/shard_map/while/body/eval_jaxpr/ppermute | solution.py:20
  235.9 2.0 slice.57
  237.8 9.8 %all_gather.3 = bf16[1,1024,256]{2,1,0:T(8,128)(2,1)S(1)} all-gather(bf16[1,128,256]{2,1,0:T(8,128)(2,1)S(1)} %bitcast.135), channel_id=1, replica_groups=mesh['section'=4,'dp'=8] {'dp'}, dimensions={1}, use_global_device_ids=true | all-gather | bytes 589824 | tf_op jit(solution)/shard_map/all_gather | solution.py:335
  247.6 2.3 reshape.450
  (197 shorter events, 107.2 us)
Async XLA Ops:
  17.9 6.2 %copy-start.15 = (f32[1,1,128,40]{2,3,1,0:T(8,128)S(1)}, f32[1,1,128,40]{2,3,1,0:T(8,128)}, u32[]{:S(2)}) copy-start(f32[1,1,128,40]{2,3,1,0:T(8,128)} %param.8) | copy-start | bytes 61444
  18.9 228.7 %all-to-all-start = ((bf16[8,2,20480]{2,1,0:T(2,128)(2,1)}), bf16[8,2,20480]{2,1,0:T(2,128)(2,1)}, u32[]{:S(2)}, u32[]{:S(2)}) async-start(bf16[8,2,20480]{2,1,0:T(2,128)(2,1)} %reshape.449), calls=%async_computation | async-start | bytes 1310720 | tf_op jit(solution)/shard_map/all_to_all | solution.py:333
  25.0 9.9 %copy-start.12 = (f32[4,40]{1,0:T(4,128)}, f32[4,40]{1,0:T(4,128)S(1)}, u32[]{:S(2)}) copy-start(f32[4,40]{1,0:T(4,128)S(1)} %exp.40) | copy-start | bytes 1924
  32.5 5.7 %copy-start.4 = (f32[4,32,2560]{2,1,0:T(8,128)S(1)}, f32[4,32,2560]{2,1,0:T(8,128)}, u32[]{:S(2)}) copy-start(f32[4,32,2560]{2,1,0:T(8,128)} %mul.113) | copy-start | bytes 3932164
  59.1 14.7 %copy-start.2 = (bf16[1,2560,256]{2,1,0:T(8,128)(2,1)S(1)}, bf16[1,2560,256]{2,1,0:T(8,128)(2,1)}, u32[]{:S(2)}) copy-start(bf16[1,2560,256]{2,1,0:T(8,128)(2,1)} %get-tuple-element.878) | copy-start | bytes 3932164 | tf_op jit(solution)/shard_map/while
  59.1 14.7 %copy-start.9 = (f32[4,32,32]{1,2,0:T(8,128)S(1)}, f32[4,32,32]{1,2,0:T(8,128)}, u32[]{:S(2)}) copy-start(f32[4,32,32]{1,2,0:T(8,128)} %get-tuple-element.905) | copy-start | bytes 49156 | tf_op jit(solution)/shard_map/while
  59.1 14.7 %copy-start.11 = (pred[32,32]{0,1:T(8,128)(4,1)S(1)}, pred[32,32]{0,1:T(8,128)(4,1)}, u32[]{:S(2)}) copy-start(pred[32,32]{0,1:T(8,128)(4,1)} %get-tuple-element.932) | copy-start | bytes 3076 | tf_op jit(solution)/shard_map/while
  64.9 8.9 %collective-permute-start = (bf16[1,32,2560]{2,1,0:T(8,128)(2,1)}, bf16[1,32,2560]{2,1,0:T(8,128)(2,1)S(1)}, u32[]{:S(2)}, u32[]{:S(2)}) collective-permute-start(bf16[1,32,2560]{2,1,0:T(8,128)(2,1)} %bitcast.139), channel_id=1, source_target_pairs={{8,0},{16,8},{24,16},{9,1},{17,9},{25,17},{10,2},{18,10},{26,18},{... | collective-permute-start | bytes 491528 | tf_op jit(solution)/shard_map/while/body/eval_jaxpr/ppermute | solution.py:20
  87.4 13.7 %copy-start.2 = (bf16[1,2560,256]{2,1,0:T(8,128)(2,1)S(1)}, bf16[1,2560,256]{2,1,0:T(8,128)(2,1)}, u32[]{:S(2)}) copy-start(bf16[1,2560,256]{2,1,0:T(8,128)(2,1)} %get-tuple-element.878) | copy-start | bytes 3932164 | tf_op jit(solution)/shard_map/while
  87.4 13.7 %copy-start.9 = (f32[4,32,32]{1,2,0:T(8,128)S(1)}, f32[4,32,32]{1,2,0:T(8,128)}, u32[]{:S(2)}) copy-start(f32[4,32,32]{1,2,0:T(8,128)} %get-tuple-element.905) | copy-start | bytes 49156 | tf_op jit(solution)/shard_map/while
  87.4 13.7 %copy-start.11 = (pred[32,32]{0,1:T(8,128)(4,1)S(1)}, pred[32,32]{0,1:T(8,128)(4,1)}, u32[]{:S(2)}) copy-start(pred[32,32]{0,1:T(8,128)(4,1)} %get-tuple-element.932) | copy-start | bytes 3076 | tf_op jit(solution)/shard_map/while
  93.2 7.9 %collective-permute-start = (bf16[1,32,2560]{2,1,0:T(8,128)(2,1)}, bf16[1,32,2560]{2,1,0:T(8,128)(2,1)S(1)}, u32[]{:S(2)}, u32[]{:S(2)}) collective-permute-start(bf16[1,32,2560]{2,1,0:T(8,128)(2,1)} %bitcast.139), channel_id=1, source_target_pairs={{8,0},{16,8},{24,16},{9,1},{17,9},{25,17},{10,2},{18,10},{26,18},{... | collective-permute-start | bytes 491528 | tf_op jit(solution)/shard_map/while/body/eval_jaxpr/ppermute | solution.py:20
  114.7 13.2 %copy-start.2 = (bf16[1,2560,256]{2,1,0:T(8,128)(2,1)S(1)}, bf16[1,2560,256]{2,1,0:T(8,128)(2,1)}, u32[]{:S(2)}) copy-start(bf16[1,2560,256]{2,1,0:T(8,128)(2,1)} %get-tuple-element.878) | copy-start | bytes 3932164 | tf_op jit(solution)/shard_map/while
  114.7 13.2 %copy-start.9 = (f32[4,32,32]{1,2,0:T(8,128)S(1)}, f32[4,32,32]{1,2,0:T(8,128)}, u32[]{:S(2)}) copy-start(f32[4,32,32]{1,2,0:T(8,128)} %get-tuple-element.905) | copy-start | bytes 49156 | tf_op jit(solution)/shard_map/while
  114.7 13.2 %copy-start.11 = (pred[32,32]{0,1:T(8,128)(4,1)S(1)}, pred[32,32]{0,1:T(8,128)(4,1)}, u32[]{:S(2)}) copy-start(pred[32,32]{0,1:T(8,128)(4,1)} %get-tuple-element.932) | copy-start | bytes 3076 | tf_op jit(solution)/shard_map/while
  120.5 7.4 %collective-permute-start = (bf16[1,32,2560]{2,1,0:T(8,128)(2,1)}, bf16[1,32,2560]{2,1,0:T(8,128)(2,1)S(1)}, u32[]{:S(2)}, u32[]{:S(2)}) collective-permute-start(bf16[1,32,2560]{2,1,0:T(8,128)(2,1)} %bitcast.139), channel_id=1, source_target_pairs={{8,0},{16,8},{24,16},{9,1},{17,9},{25,17},{10,2},{18,10},{26,18},{... | collective-permute-start | bytes 491528 | tf_op jit(solution)/shard_map/while/body/eval_jaxpr/ppermute | solution.py:20
  141.5 13.2 %copy-start.2 = (bf16[1,2560,256]{2,1,0:T(8,128)(2,1)S(1)}, bf16[1,2560,256]{2,1,0:T(8,128)(2,1)}, u32[]{:S(2)}) copy-start(bf16[1,2560,256]{2,1,0:T(8,128)(2,1)} %get-tuple-element.878) | copy-start | bytes 3932164 | tf_op jit(solution)/shard_map/while
  141.5 13.2 %copy-start.9 = (f32[4,32,32]{1,2,0:T(8,128)S(1)}, f32[4,32,32]{1,2,0:T(8,128)}, u32[]{:S(2)}) copy-start(f32[4,32,32]{1,2,0:T(8,128)} %get-tuple-element.905) | copy-start | bytes 49156 | tf_op jit(solution)/shard_map/while
  141.5 13.2 %copy-start.11 = (pred[32,32]{0,1:T(8,128)(4,1)S(1)}, pred[32,32]{0,1:T(8,128)(4,1)}, u32[]{:S(2)}) copy-start(pred[32,32]{0,1:T(8,128)(4,1)} %get-tuple-element.932) | copy-start | bytes 3076 | tf_op jit(solution)/shard_map/while
  147.2 7.4 %collective-permute-start = (bf16[1,32,2560]{2,1,0:T(8,128)(2,1)}, bf16[1,32,2560]{2,1,0:T(8,128)(2,1)S(1)}, u32[]{:S(2)}, u32[]{:S(2)}) collective-permute-start(bf16[1,32,2560]{2,1,0:T(8,128)(2,1)} %bitcast.139), channel_id=1, source_target_pairs={{8,0},{16,8},{24,16},{9,1},{17,9},{25,17},{10,2},{18,10},{26,18},{... | collective-permute-start | bytes 491528 | tf_op jit(solution)/shard_map/while/body/eval_jaxpr/ppermute | solution.py:20
  168.2 13.2 %copy-start.2 = (bf16[1,2560,256]{2,1,0:T(8,128)(2,1)S(1)}, bf16[1,2560,256]{2,1,0:T(8,128)(2,1)}, u32[]{:S(2)}) copy-start(bf16[1,2560,256]{2,1,0:T(8,128)(2,1)} %get-tuple-element.878) | copy-start | bytes 3932164 | tf_op jit(solution)/shard_map/while
  168.2 13.2 %copy-start.9 = (f32[4,32,32]{1,2,0:T(8,128)S(1)}, f32[4,32,32]{1,2,0:T(8,128)}, u32[]{:S(2)}) copy-start(f32[4,32,32]{1,2,0:T(8,128)} %get-tuple-element.905) | copy-start | bytes 49156 | tf_op jit(solution)/shard_map/while
  168.2 13.2 %copy-start.11 = (pred[32,32]{0,1:T(8,128)(4,1)S(1)}, pred[32,32]{0,1:T(8,128)(4,1)}, u32[]{:S(2)}) copy-start(pred[32,32]{0,1:T(8,128)(4,1)} %get-tuple-element.932) | copy-start | bytes 3076 | tf_op jit(solution)/shard_map/while
  174.0 7.4 %collective-permute-start = (bf16[1,32,2560]{2,1,0:T(8,128)(2,1)}, bf16[1,32,2560]{2,1,0:T(8,128)(2,1)S(1)}, u32[]{:S(2)}, u32[]{:S(2)}) collective-permute-start(bf16[1,32,2560]{2,1,0:T(8,128)(2,1)} %bitcast.139), channel_id=1, source_target_pairs={{8,0},{16,8},{24,16},{9,1},{17,9},{25,17},{10,2},{18,10},{26,18},{... | collective-permute-start | bytes 491528 | tf_op jit(solution)/shard_map/while/body/eval_jaxpr/ppermute | solution.py:20
  195.0 13.2 %copy-start.2 = (bf16[1,2560,256]{2,1,0:T(8,128)(2,1)S(1)}, bf16[1,2560,256]{2,1,0:T(8,128)(2,1)}, u32[]{:S(2)}) copy-start(bf16[1,2560,256]{2,1,0:T(8,128)(2,1)} %get-tuple-element.878) | copy-start | bytes 3932164 | tf_op jit(solution)/shard_map/while
  195.0 13.2 %copy-start.9 = (f32[4,32,32]{1,2,0:T(8,128)S(1)}, f32[4,32,32]{1,2,0:T(8,128)}, u32[]{:S(2)}) copy-start(f32[4,32,32]{1,2,0:T(8,128)} %get-tuple-element.905) | copy-start | bytes 49156 | tf_op jit(solution)/shard_map/while
  195.0 13.2 %copy-start.11 = (pred[32,32]{0,1:T(8,128)(4,1)S(1)}, pred[32,32]{0,1:T(8,128)(4,1)}, u32[]{:S(2)}) copy-start(pred[32,32]{0,1:T(8,128)(4,1)} %get-tuple-element.932) | copy-start | bytes 3076 | tf_op jit(solution)/shard_map/while
  200.8 7.4 %collective-permute-start = (bf16[1,32,2560]{2,1,0:T(8,128)(2,1)}, bf16[1,32,2560]{2,1,0:T(8,128)(2,1)S(1)}, u32[]{:S(2)}, u32[]{:S(2)}) collective-permute-start(bf16[1,32,2560]{2,1,0:T(8,128)(2,1)} %bitcast.139), channel_id=1, source_target_pairs={{8,0},{16,8},{24,16},{9,1},{17,9},{25,17},{10,2},{18,10},{26,18},{... | collective-permute-start | bytes 491528 | tf_op jit(solution)/shard_map/while/body/eval_jaxpr/ppermute | solution.py:20
  221.8 13.2 %copy-start.2 = (bf16[1,2560,256]{2,1,0:T(8,128)(2,1)S(1)}, bf16[1,2560,256]{2,1,0:T(8,128)(2,1)}, u32[]{:S(2)}) copy-start(bf16[1,2560,256]{2,1,0:T(8,128)(2,1)} %get-tuple-element.878) | copy-start | bytes 3932164 | tf_op jit(solution)/shard_map/while
  221.8 13.2 %copy-start.9 = (f32[4,32,32]{1,2,0:T(8,128)S(1)}, f32[4,32,32]{1,2,0:T(8,128)}, u32[]{:S(2)}) copy-start(f32[4,32,32]{1,2,0:T(8,128)} %get-tuple-element.905) | copy-start | bytes 49156 | tf_op jit(solution)/shard_map/while
  221.8 13.2 %copy-start.11 = (pred[32,32]{0,1:T(8,128)(4,1)S(1)}, pred[32,32]{0,1:T(8,128)(4,1)}, u32[]{:S(2)}) copy-start(pred[32,32]{0,1:T(8,128)(4,1)} %get-tuple-element.932) | copy-start | bytes 3076 | tf_op jit(solution)/shard_map/while
  227.6 7.4 %collective-permute-start = (bf16[1,32,2560]{2,1,0:T(8,128)(2,1)}, bf16[1,32,2560]{2,1,0:T(8,128)(2,1)S(1)}, u32[]{:S(2)}, u32[]{:S(2)}) collective-permute-start(bf16[1,32,2560]{2,1,0:T(8,128)(2,1)} %bitcast.139), channel_id=1, source_target_pairs={{8,0},{16,8},{24,16},{9,1},{17,9},{25,17},{10,2},{18,10},{26,18},{... | collective-permute-start | bytes 491528 | tf_op jit(solution)/shard_map/while/body/eval_jaxpr/ppermute | solution.py:20
  (16 other events, 30.9 us)

commit v5 on v4

--- a/solution.py
+++ b/solution.py
@@ -289,6 +289,7 @@
     states_t = jnp.stack(saved)
     x_flat = x_blk.reshape(lead_dims + (block_len, features))
     per_block = (wt2, dec2, x_flat, in_blk, out_blk, tail_full, lead_full, xt_full, states_t, end_row)
+    per_block = lax.optimization_barrier(per_block)
 
     top_blk = jnp.moveaxis(
         top_grad.reshape((seq_dev, MICRO, block_len, features)), 1, 0

time: 253 us -> 169 us (0.67)
  local copies, waits for them, and re-layouts: 95.8 us -> 31.4 us
  other arithmetic: 42.2 us -> 25.2 us
  Pallas kernels: 40.4 us -> 37.7 us
    broadcast_in_dim x14 -> x2, local copies, waits for them, and re-layouts: 22.7 us -> 2.39 us  [shards(): lead_full = jnp.repeat(consts['lead'], width, axis=-1)]
    broadcast_in_dim x16 -> x2, local copies, waits for them, and re-layouts: 20.8 us -> 3.77 us  [shards(): tail_full = jnp.repeat(consts['tail'], width, axis=-1)]
    select_n x7 -> x1, other arithmetic: 13.5 us -> 2.48 us  [block_consts(): decays = jnp.where(lower_mask, jnp.exp(spread), 0.0)]
    transpose x7 -> x0, local copies, waits for them, and re-layouts: 9.86 us -> none  [shards(): jnp.swapaxes(weighted, -3, -2)]
    broadcast_in_dim x17 -> x5, local copies, waits for them, and re-layouts: 10.5 us -> 1 us  [shards(): end_row = jnp.repeat(consts['ending'], width, axis=-1)[..., None, :]]
    reshape x7 -> x1, local copies, waits for them, and re-layouts: 10.6 us -> 3.41 us  [shards(): jnp.swapaxes(weighted, -3, -2)]
    convert_element_type x7 -> x0, other arithmetic: 6.05 us -> none  [block_consts(): weighted = (factor * decays * scores[:, :, None]).astype(jnp.bfloat16)]
    reshape x0 -> x1, local copies, waits for them, and re-layouts: none -> 4.29 us  [shards(): weighted.reshape(lead_dims + (pairs, per_pair, block_len, block_len))]
  transfers between devices with their start and end apart: 8 -> 8, of which waited for: 7 -> 7; matrix products, arithmetic and copies ran while one was open for 46% -> 22% of each run, Pallas kernels for 16% -> 22%
where the time goes in v5:
time: 169 us; the launch traced here: 168 us
  waiting for transfers between devices  44.8 us (27%)
  Pallas kernels  37.7 us (22%)
  local copies, waits for them, and re-layouts  31.4 us (19%)
  other arithmetic  25.2 us (15%)
  starting transfers between devices  14.1 us (8%)
  blocking collectives  9.77 us (6%)
  matrix products  4.47 us (3%)
    ppermute x7, waiting for transfers between devices, passed_along(): return lax.ppermute(block, axis, route)  44.8 us
    pallas_call x7, Pallas kernels, fused_step(): pl.pallas_call(functools.partial(step_kernel, factor=factor, width=width)...  37.7 us
    unnamed x1, other arithmetic  14.3 us
    all_gather x1, blocking collectives, shards(): maps_all = lax.all_gather(maps_here, 'dp', axis=1, tiled=True)  9.77 us
    ppermute x7, starting transfers between devices, passed_along(): return lax.ppermute(block, axis, route)  8.96 us
    unnamed x24, local copies, waits for them, and re-layouts  5.51 us
    all_to_all x1, starting transfers between devices, shards(): rows_all = lax.all_to_all(rows_here, 'dp', 2, 1, tiled=True)  5.17 us
    another operation x7, other arithmetic, advance(): jnp.stack([block_no, is_top.astype(jnp.int32), slot]).astype(jnp.int32)  4.49 us
  transfers between devices with their start and end apart: 8, of which 7 were waited for; matrix products, arithmetic and copies ran while one was open for 22% of the time, Pallas kernels for 22%

profile of v5, /device:TPU:0, one launch (start us, length us, event | category | flops | bytes accessed | tf_op | source)
XLA Modules:
  0.0 168.5 jit_solution(6562946653581781060)
XLA Ops:
  0.6 2.5 %copy.37 = bf16[1,128,2560]{1,0,2:T(2,128)(2,1)S(1)} copy(bf16[1,128,2560]{2,1,0:T(8,128)(2,1)} %bitcast.111) | data formatting | bytes 1310720 | tf_op jit(solution)/shard_map/reshape | solution.py:333
  3.7 14.3 %reduce = bf16[2560,128]{1,0:T(8,128)(2,1)S(1)} reduce(bf16[2560,1,128]{2,1,0:T(2,128)(2,1)S(1)} %bitcast.117, bf16[]{:T(256)} %broadcast.297), dimensions={1}, to_apply=%bitcast.100.reduce_sub_computation | reduce | bytes 1310722
  19.0 5.2 %all-to-all-start = ((bf16[8,2,20480]{2,1,0:T(2,128)(2,1)}), bf16[8,2,20480]{2,1,0:T(2,128)(2,1)}, u32[]{:S(2)}, u32[]{:S(2)}) async-start(bf16[8,2,20480]{2,1,0:T(2,128)(2,1)} %reshape.432), calls=%async_computation | async-start | bytes 1310720 | tf_op jit(solution)/shard_map/all_to_all | solution.py:334
  25.2 1.5 copy-done.3
  26.7 1.7 %mul.113 = f32[4,32,2560]{2,1,0:T(8,128)} reshape(f32[4,32,40,64]{3,2,1,0:T(8,128)S(1)} %broadcast_in_dim.72) | data formatting | bytes 2621440 | tf_op jit(solution)/shard_map/vmap(vmap(vmap()))/mul | solution.py:124
  28.4 3.0 %broadcast_in_dim.73 = f32[4,1,1,32,2560]{4,3,2,1,0:T(8,128)} reshape(f32[4,32,40,64]{3,2,1,0:T(8,128)} %copy-done.3) | data formatting | bytes 2621440 | tf_op jit(solution)/shard_map/broadcast_in_dim | solution.py:277
  36.1 1.6 broadcast_in_dim.75
  37.9 2.5 %exponential_select_fusion = (f32[4,1,1,32,32,40]{4,3,5,0,2,1:T(8,128)S(1)}, bf16[4,1,1,32,32,40]{4,3,5,0,2,1:T(8,128)(2,1)}) fusion(f32[4,32,40]{1,2,0:T(8,128)S(1)} %copy.32, pred[32,32]{1,0:T(8,128)(4,1)S(1)} %copy-done.7, f32[4,32,32]{2,1,0:T(8,128)} %convolution_multiply_fusion.1), kind=kLoop, calls=%fused_computation.3 | loop fusion | flops 819200 | bytes 1020928 | tf_op jit(solution)/shard_map/vmap(vmap(vmap(jit(_where))))/select_n | solution.py:119
  40.4 4.3 %copy.34 = bf16[4,1,1,20,2,32,32]{6,4,5,3,0,2,1:T(2,128)(2,1)} copy(bf16[4,1,1,20,2,32,32]{5,6,4,3,0,2,1:T(8,128)(2,1)} %bitcast.116) | data formatting | bytes 655360 | tf_op jit(solution)/shard_map/reshape | solution.py:272
  44.6 3.4 %reshape.424 = bf16[4,1,1,20,32,64]{5,4,3,2,1,0:T(8,128)(2,1)} reshape(bf16[4,1,1,20,32,2,32]{6,5,4,3,0,2,1:T(2,128)(2,1)} %bitcast.118) | data formatting | bytes 655360 | tf_op jit(solution)/shard_map/reshape | solution.py:273
  48.9 2.3 %fusion.12 = f32[4,128,2560]{2,1,0:T(8,128)S(1)} fusion(f32[4,32,2560]{2,1,0:T(8,128)} %mul.113, bf16[4,32,2560]{2,1,0:T(8,128)(2,1)S(1)} %bitcast.112, bf16[4,1,1,32,256]{4,3,0,2,1:T(8,128)(2,1)S(1)} %bitcast.125), kind=kOutput, calls=%fused_computation.21 | convolution fusion | flops 84869120 | bytes 7241728 | tf_op jit(solution)/shard_map/mlsjn,mlsjd->mlsnd/dot_general | solution.py:281
  52.7 1.8 %pad_maximum_fusion = bf16[4,1,1,128,2560]{4,3,2,1,0:T(8,128)(2,1)} fusion(bf16[1,1,1,128,2560]{4,3,2,1,0:T(8,128)(2,1)S(1)} %get-tuple-element.542, bf16[1,1,1,128,2560]{4,3,2,1,0:T(8,128)(2,1)S(1)} %get-tuple-element.541, bf16[1,1,1,128,2560]{4,3,2,1,0:T(8,128)(2,1)S(1)} %get-tuple-element.543, bf16[4]{0:T(256)(128)(2,1)S(1)} %pad.3.clone), kind=kLoop, calls=%fused_computation.1 | loop fusion | flops 3932160 | bytes 4587528 | tf_op jit(solution)/shard_map/stack | solution.py:289
  56.7 96.1 %while.21 = (s32[]{:T(128)}, bf16[1,32,2560]{2,1,0:T(8,128)(2,1)S(1)}, f32[1,1,128,2560]{3,2,1,0:T(8,128)}, bf16[5,1,1,32,2560]{4,3,2,1,0:T(8,128)(2,1)}, bf16[5...) while((s32[]{:T(128)}, ...), condition=%wide.region_2.3_spmd, body=%wide.region_1.2_spmd.sunk | while | flops 146800656 | bytes 8192356 | solution.py:325
  57.4 5.4 %eval_jaxpr.7 = (bf16[32,2560]{1,0:T(8,128)(2,1)}, f32[1,1,128,2560]{3,2,1,0:T(8,128)}, bf16[32,256]{1,0:T(8,128)(2,1)}, bf16[5,1,1,32,2560]{4,3,2,1,0:T(8,128)(2,1)}, bf16[5,1,1,32,256]{4,3,2,1,0:T(8,128)(2,1)S(1)}) custom-call(s32[3]{0:T(128)} %pad_add_fusion.2.picks_ref, ...), custom_call_target="tpu_custom_call", output_to_operand_aliasing={{1}: (12, {}), {3}: (15, {}), {4}: (16, {})} | custom-call | flops 146800640 | bytes 7536640 | tf_op jit(solution)/shard_map/while/body/eval_jaxpr/pallas_call | solution.py:218
  62.8 1.3 collective-permute-start
  64.1 7.6 %collective-permute-done = bf16[1,32,2560]{2,1,0:T(8,128)(2,1)S(1)} collective-permute-done((bf16[1,32,2560]{2,1,0:T(8,128)(2,1)}, bf16[1,32,2560]{2,1,0:T(8,128)(2,1)S(1)}, u32[]{:S(2)}, u32[]{:S(2)}) %collective-permute-start) | collective-permute-done | bytes 163872 | tf_op jit(solution)/shard_map/while/body/eval_jaxpr/ppermute | solution.py:20
  72.3 5.4 %eval_jaxpr.7 = (bf16[32,2560]{1,0:T(8,128)(2,1)}, f32[1,1,128,2560]{3,2,1,0:T(8,128)}, bf16[32,256]{1,0:T(8,128)(2,1)}, bf16[5,1,1,32,2560]{4,3,2,1,0:T(8,128)(2,1)}, bf16[5,1,1,32,256]{4,3,2,1,0:T(8,128)(2,1)S(1)}) custom-call(s32[3]{0:T(128)} %pad_add_fusion.2.picks_ref, ...), custom_call_target="tpu_custom_call", output_to_operand_aliasing={{1}: (12, {}), {3}: (15, {}), {4}: (16, {})} | custom-call | flops 146800640 | bytes 7536640 | tf_op jit(solution)/shard_map/while/body/eval_jaxpr/pallas_call | solution.py:218
  77.7 1.3 collective-permute-start
  79.0 6.6 %collective-permute-done = bf16[1,32,2560]{2,1,0:T(8,128)(2,1)S(1)} collective-permute-done((bf16[1,32,2560]{2,1,0:T(8,128)(2,1)}, bf16[1,32,2560]{2,1,0:T(8,128)(2,1)S(1)}, u32[]{:S(2)}, u32[]{:S(2)}) %collective-permute-start) | collective-permute-done | bytes 163872 | tf_op jit(solution)/shard_map/while/body/eval_jaxpr/ppermute | solution.py:20
  86.2 5.4 %eval_jaxpr.7 = (bf16[32,2560]{1,0:T(8,128)(2,1)}, f32[1,1,128,2560]{3,2,1,0:T(8,128)}, bf16[32,256]{1,0:T(8,128)(2,1)}, bf16[5,1,1,32,2560]{4,3,2,1,0:T(8,128)(2,1)}, bf16[5,1,1,32,256]{4,3,2,1,0:T(8,128)(2,1)S(1)}) custom-call(s32[3]{0:T(128)} %pad_add_fusion.2.picks_ref, ...), custom_call_target="tpu_custom_call", output_to_operand_aliasing={{1}: (12, {}), {3}: (15, {}), {4}: (16, {})} | custom-call | flops 146800640 | bytes 7536640 | tf_op jit(solution)/shard_map/while/body/eval_jaxpr/pallas_call | solution.py:218
  92.9 6.1 %collective-permute-done = bf16[1,32,2560]{2,1,0:T(8,128)(2,1)S(1)} collective-permute-done((bf16[1,32,2560]{2,1,0:T(8,128)(2,1)}, bf16[1,32,2560]{2,1,0:T(8,128)(2,1)S(1)}, u32[]{:S(2)}, u32[]{:S(2)}) %collective-permute-start) | collective-permute-done | bytes 163872 | tf_op jit(solution)/shard_map/while/body/eval_jaxpr/ppermute | solution.py:20
  99.7 5.4 %eval_jaxpr.7 = (bf16[32,2560]{1,0:T(8,128)(2,1)}, f32[1,1,128,2560]{3,2,1,0:T(8,128)}, bf16[32,256]{1,0:T(8,128)(2,1)}, bf16[5,1,1,32,2560]{4,3,2,1,0:T(8,128)(2,1)}, bf16[5,1,1,32,256]{4,3,2,1,0:T(8,128)(2,1)S(1)}) custom-call(s32[3]{0:T(128)} %pad_add_fusion.2.picks_ref, ...), custom_call_target="tpu_custom_call", output_to_operand_aliasing={{1}: (12, {}), {3}: (15, {}), {4}: (16, {})} | custom-call | flops 146800640 | bytes 7536640 | tf_op jit(solution)/shard_map/while/body/eval_jaxpr/pallas_call | solution.py:218
  106.3 6.1 %collective-permute-done = bf16[1,32,2560]{2,1,0:T(8,128)(2,1)S(1)} collective-permute-done((bf16[1,32,2560]{2,1,0:T(8,128)(2,1)}, bf16[1,32,2560]{2,1,0:T(8,128)(2,1)S(1)}, u32[]{:S(2)}, u32[]{:S(2)}) %collective-permute-start) | collective-permute-done | bytes 163872 | tf_op jit(solution)/shard_map/while/body/eval_jaxpr/ppermute | solution.py:20
  113.1 5.4 %eval_jaxpr.7 = (bf16[32,2560]{1,0:T(8,128)(2,1)}, f32[1,1,128,2560]{3,2,1,0:T(8,128)}, bf16[32,256]{1,0:T(8,128)(2,1)}, bf16[5,1,1,32,2560]{4,3,2,1,0:T(8,128)(2,1)}, bf16[5,1,1,32,256]{4,3,2,1,0:T(8,128)(2,1)S(1)}) custom-call(s32[3]{0:T(128)} %pad_add_fusion.2.picks_ref, ...), custom_call_target="tpu_custom_call", output_to_operand_aliasing={{1}: (12, {}), {3}: (15, {}), {4}: (16, {})} | custom-call | flops 146800640 | bytes 7536640 | tf_op jit(solution)/shard_map/while/body/eval_jaxpr/pallas_call | solution.py:218
  119.8 6.1 %collective-permute-done = bf16[1,32,2560]{2,1,0:T(8,128)(2,1)S(1)} collective-permute-done((bf16[1,32,2560]{2,1,0:T(8,128)(2,1)}, bf16[1,32,2560]{2,1,0:T(8,128)(2,1)S(1)}, u32[]{:S(2)}, u32[]{:S(2)}) %collective-permute-start) | collective-permute-done | bytes 163872 | tf_op jit(solution)/shard_map/while/body/eval_jaxpr/ppermute | solution.py:20
  126.6 5.4 %eval_jaxpr.7 = (bf16[32,2560]{1,0:T(8,128)(2,1)}, f32[1,1,128,2560]{3,2,1,0:T(8,128)}, bf16[32,256]{1,0:T(8,128)(2,1)}, bf16[5,1,1,32,2560]{4,3,2,1,0:T(8,128)(2,1)}, bf16[5,1,1,32,256]{4,3,2,1,0:T(8,128)(2,1)S(1)}) custom-call(s32[3]{0:T(128)} %pad_add_fusion.2.picks_ref, ...), custom_call_target="tpu_custom_call", output_to_operand_aliasing={{1}: (12, {}), {3}: (15, {}), {4}: (16, {})} | custom-call | flops 146800640 | bytes 7536640 | tf_op jit(solution)/shard_map/while/body/eval_jaxpr/pallas_call | solution.py:218
  133.2 6.1 %collective-permute-done = bf16[1,32,2560]{2,1,0:T(8,128)(2,1)S(1)} collective-permute-done((bf16[1,32,2560]{2,1,0:T(8,128)(2,1)}, bf16[1,32,2560]{2,1,0:T(8,128)(2,1)S(1)}, u32[]{:S(2)}, u32[]{:S(2)}) %collective-permute-start) | collective-permute-done | bytes 163872 | tf_op jit(solution)/shard_map/while/body/eval_jaxpr/ppermute | solution.py:20
  140.0 5.4 %eval_jaxpr.7 = (bf16[32,2560]{1,0:T(8,128)(2,1)}, f32[1,1,128,2560]{3,2,1,0:T(8,128)}, bf16[32,256]{1,0:T(8,128)(2,1)}, bf16[5,1,1,32,2560]{4,3,2,1,0:T(8,128)(2,1)}, bf16[5,1,1,32,256]{4,3,2,1,0:T(8,128)(2,1)S(1)}) custom-call(s32[3]{0:T(128)} %pad_add_fusion.2.picks_ref, ...), custom_call_target="tpu_custom_call", output_to_operand_aliasing={{1}: (12, {}), {3}: (15, {}), {4}: (16, {})} | custom-call | flops 146800640 | bytes 7536640 | tf_op jit(solution)/shard_map/while/body/eval_jaxpr/pallas_call | solution.py:218
  146.7 6.1 %collective-permute-done = bf16[1,32,2560]{2,1,0:T(8,128)(2,1)S(1)} collective-permute-done((bf16[1,32,2560]{2,1,0:T(8,128)(2,1)}, bf16[1,32,2560]{2,1,0:T(8,128)(2,1)S(1)}, u32[]{:S(2)}, u32[]{:S(2)}) %collective-permute-start) | collective-permute-done | bytes 163872 | tf_op jit(solution)/shard_map/while/body/eval_jaxpr/ppermute | solution.py:20
  152.8 2.0 %slice.57 = bf16[4,1,1,32,2560]{4,3,2,1,0:T(8,128)(2,1)} slice(bf16[5,1,1,32,2560]{4,3,2,1,0:T(8,128)(2,1)} %get-tuple-element.425), slice={[0:4], [0:1], [0:1], [0:32], [0:2560]} | slice | bytes 1310720 | tf_op jit(solution)/shard_map/slice | solution.py:329
  154.8 9.8 %all_gather.3 = bf16[1,1024,256]{2,1,0:T(8,128)(2,1)S(1)} all-gather(bf16[1,128,256]{2,1,0:T(8,128)(2,1)S(1)} %bitcast.129), channel_id=1, replica_groups=mesh['section'=4,'dp'=8] {'dp'}, dimensions={1}, use_global_device_ids=true | all-gather | bytes 589824 | tf_op jit(solution)/shard_map/all_gather | solution.py:336
  164.5 2.3 %reshape.433 = bf16[2560,1,128]{2,1,0:T(2,128)(2,1)S(1)} reshape(bf16[8,2,20480]{2,1,0:T(2,128)(2,1)} %all-to-all-done) | data formatting | bytes 1310720
  (66 shorter events, 24.3 us)
Async XLA Ops:
  17.9 6.2 %copy-start.6 = (f32[1,1,128,40]{2,3,1,0:T(8,128)S(1)}, f32[1,1,128,40]{2,3,1,0:T(8,128)}, u32[]{:S(2)}) copy-start(f32[1,1,128,40]{2,3,1,0:T(8,128)} %param.8) | copy-start | bytes 61444
  19.0 145.6 %all-to-all-start = ((bf16[8,2,20480]{2,1,0:T(2,128)(2,1)}), bf16[8,2,20480]{2,1,0:T(2,128)(2,1)}, u32[]{:S(2)}, u32[]{:S(2)}) async-start(bf16[8,2,20480]{2,1,0:T(2,128)(2,1)} %reshape.432), calls=%async_computation | async-start | bytes 1310720 | tf_op jit(solution)/shard_map/all_to_all | solution.py:334
  24.4 9.3 %copy-start.8 = (f32[4,40]{1,0:T(4,128)}, f32[4,40]{1,0:T(4,128)S(1)}, u32[]{:S(2)}) copy-start(f32[4,40]{1,0:T(4,128)S(1)} %exp.40) | copy-start | bytes 1924
  25.1 1.5 copy-start.3
  28.4 3.6 %copy-start.1 = (bf16[1,1,128,2560]{3,2,1,0:T(8,128)(2,1)S(1)}, bf16[1,1,128,2560]{3,2,1,0:T(8,128)(2,1)}, u32[]{:S(2)}) copy-start(bf16[1,1,128,2560]{3,2,1,0:T(8,128)(2,1)} %param.6) | copy-start | bytes 1966084
  28.4 3.6 %copy-start.2 = (bf16[1,2560,256]{2,1,0:T(8,128)(2,1)S(1)}, bf16[1,2560,256]{2,1,0:T(8,128)(2,1)}, u32[]{:S(2)}) copy-start(bf16[1,2560,256]{2,1,0:T(8,128)(2,1)} %param.7) | copy-start | bytes 3932164
  36.1 1.8 %copy-start.7 = (pred[32,32]{1,0:T(8,128)(4,1)S(1)}, pred[32,32]{1,0:T(8,128)(4,1)}, u32[]{:S(2)}) copy-start(pred[32,32]{1,0:T(8,128)(4,1)} %iota_compare_fusion) | copy-start | bytes 3076
  44.6 3.4 %copy-start.9 = (f32[4,40]{1,0:T(4,128)S(1)}, f32[4,40]{1,0:T(4,128)}, u32[]{:S(2)}) copy-start(f32[4,40]{1,0:T(4,128)} %copy-done.8) | copy-start | bytes 1924
  48.9 2.3 %copy-start = (f32[4,1,1,32,2560]{4,3,2,1,0:T(8,128)S(1)}, f32[4,1,1,32,2560]{4,3,2,1,0:T(8,128)}, u32[]{:S(2)}) copy-start(f32[4,1,1,32,2560]{4,3,2,1,0:T(8,128)} %broadcast_in_dim.73) | copy-start | bytes 3932164
  51.2 1.1 copy-start.4
  51.2 1.1 copy-start.5
  62.8 8.9 %collective-permute-start = (bf16[1,32,2560]{2,1,0:T(8,128)(2,1)}, bf16[1,32,2560]{2,1,0:T(8,128)(2,1)S(1)}, u32[]{:S(2)}, u32[]{:S(2)}) collective-permute-start(bf16[1,32,2560]{2,1,0:T(8,128)(2,1)} %bitcast.133), channel_id=1, source_target_pairs={{8,0},{16,8},{24,16},{9,1},{17,9},{25,17},{10,2},{18,10},{26,18},{... | collective-permute-start | bytes 491528 | tf_op jit(solution)/shard_map/while/body/eval_jaxpr/ppermute | solution.py:20
  77.7 7.9 %collective-permute-start = (bf16[1,32,2560]{2,1,0:T(8,128)(2,1)}, bf16[1,32,2560]{2,1,0:T(8,128)(2,1)S(1)}, u32[]{:S(2)}, u32[]{:S(2)}) collective-permute-start(bf16[1,32,2560]{2,1,0:T(8,128)(2,1)} %bitcast.133), channel_id=1, source_target_pairs={{8,0},{16,8},{24,16},{9,1},{17,9},{25,17},{10,2},{18,10},{26,18},{... | collective-permute-start | bytes 491528 | tf_op jit(solution)/shard_map/while/body/eval_jaxpr/ppermute | solution.py:20
  91.6 7.4 %collective-permute-start = (bf16[1,32,2560]{2,1,0:T(8,128)(2,1)}, bf16[1,32,2560]{2,1,0:T(8,128)(2,1)S(1)}, u32[]{:S(2)}, u32[]{:S(2)}) collective-permute-start(bf16[1,32,2560]{2,1,0:T(8,128)(2,1)} %bitcast.133), channel_id=1, source_target_pairs={{8,0},{16,8},{24,16},{9,1},{17,9},{25,17},{10,2},{18,10},{26,18},{... | collective-permute-start | bytes 491528 | tf_op jit(solution)/shard_map/while/body/eval_jaxpr/ppermute | solution.py:20
  105.1 7.4 %collective-permute-start = (bf16[1,32,2560]{2,1,0:T(8,128)(2,1)}, bf16[1,32,2560]{2,1,0:T(8,128)(2,1)S(1)}, u32[]{:S(2)}, u32[]{:S(2)}) collective-permute-start(bf16[1,32,2560]{2,1,0:T(8,128)(2,1)} %bitcast.133), channel_id=1, source_target_pairs={{8,0},{16,8},{24,16},{9,1},{17,9},{25,17},{10,2},{18,10},{26,18},{... | collective-permute-start | bytes 491528 | tf_op jit(solution)/shard_map/while/body/eval_jaxpr/ppermute | solution.py:20
  118.5 7.4 %collective-permute-start = (bf16[1,32,2560]{2,1,0:T(8,128)(2,1)}, bf16[1,32,2560]{2,1,0:T(8,128)(2,1)S(1)}, u32[]{:S(2)}, u32[]{:S(2)}) collective-permute-start(bf16[1,32,2560]{2,1,0:T(8,128)(2,1)} %bitcast.133), channel_id=1, source_target_pairs={{8,0},{16,8},{24,16},{9,1},{17,9},{25,17},{10,2},{18,10},{26,18},{... | collective-permute-start | bytes 491528 | tf_op jit(solution)/shard_map/while/body/eval_jaxpr/ppermute | solution.py:20
  131.9 7.4 %collective-permute-start = (bf16[1,32,2560]{2,1,0:T(8,128)(2,1)}, bf16[1,32,2560]{2,1,0:T(8,128)(2,1)S(1)}, u32[]{:S(2)}, u32[]{:S(2)}) collective-permute-start(bf16[1,32,2560]{2,1,0:T(8,128)(2,1)} %bitcast.133), channel_id=1, source_target_pairs={{8,0},{16,8},{24,16},{9,1},{17,9},{25,17},{10,2},{18,10},{26,18},{... | collective-permute-start | bytes 491528 | tf_op jit(solution)/shard_map/while/body/eval_jaxpr/ppermute | solution.py:20
  145.4 7.4 %collective-permute-start = (bf16[1,32,2560]{2,1,0:T(8,128)(2,1)}, bf16[1,32,2560]{2,1,0:T(8,128)(2,1)S(1)}, u32[]{:S(2)}, u32[]{:S(2)}) collective-permute-start(bf16[1,32,2560]{2,1,0:T(8,128)(2,1)} %bitcast.133), channel_id=1, source_target_pairs={{8,0},{16,8},{24,16},{9,1},{17,9},{25,17},{10,2},{18,10},{26,18},{... | collective-permute-start | bytes 491528 | tf_op jit(solution)/shard_map/while/body/eval_jaxpr/ppermute | solution.py:20

commit v6 on v5

--- a/solution.py
+++ b/solution.py
@@ -330,12 +330,13 @@
     map_store = jnp.moveaxis(map_store[:MICRO], 0, 2).reshape(bc_all.shape)
     ways = lax.axis_size("dp")
     divisor = ways * seq_dev
-    rows_here = layer_inputs.reshape(lay_dev, seq_dev * tok_len, features)
-    rows_all = lax.all_to_all(rows_here, "dp", 2, 1, tiled=True)
-    maps_here = map_store.reshape(lay_dev, seq_dev * tok_len, map_store.shape[-1])
-    maps_all = lax.all_gather(maps_here, "dp", axis=1, tiled=True)
+    rows_here = layer_inputs.reshape(lay_dev, seq_dev * tok_len, ways, features // ways)
+    rows_here = jnp.transpose(rows_here, (2, 0, 1, 3))
+    rows_all = lax.all_to_all(rows_here, "dp", 0, 0, tiled=True)
+    maps_here = map_store.reshape(1, lay_dev, seq_dev * tok_len, map_store.shape[-1])
+    maps_all = lax.all_gather(maps_here, "dp", axis=0, tiled=True)
     grad_w = jnp.einsum(
-        "lrd,lrc->ldc", rows_all, maps_all, preferred_element_type=jnp.float32
+        "glrd,glrc->ldc", rows_all, maps_all, preferred_element_type=jnp.float32
     ) / divisor
     return (grad_inputs, grad_w)
 

time: 169 us -> 152 us (0.90)
  other arithmetic: 25.2 us -> 11.1 us
  local copies, waits for them, and re-layouts: 31.4 us -> 26.8 us
    unnamed x1 -> x0, other arithmetic: 14.3 us -> none
    reshape x1 -> x0, local copies, waits for them, and re-layouts: 2.51 us -> none  [shards(): rows_here = layer_inputs.reshape(lay_dev, seq_dev * tok_len, features)]
    unnamed x24 -> x21, local copies, waits for them, and re-layouts: 5.51 us -> 3.75 us
  transfers between devices with their start and end apart: 8 -> 8, of which waited for: 7 -> 7; matrix products, arithmetic and copies ran while one was open for 22% -> 25% of each run, Pallas kernels for 22% -> 25%
where the time goes in v6:
time: 152 us; the launch traced here: 151 us
  waiting for transfers between devices  44.9 us (30%)
  Pallas kernels  37.7 us (25%)
  local copies, waits for them, and re-layouts  26.8 us (18%)
  starting transfers between devices  14.1 us (9%)
  other arithmetic  11.1 us (7%)
  blocking collectives  9.8 us (6%)
  matrix products  5.55 us (4%)
    ppermute x7, waiting for transfers between devices, passed_along(): return lax.ppermute(block, axis, route)  44.9 us
    pallas_call x7, Pallas kernels, fused_step(): pl.pallas_call(functools.partial(step_kernel, factor=factor, width=width)...  37.7 us
    all_gather x1, blocking collectives, shards(): maps_all = lax.all_gather(maps_here, 'dp', axis=0, tiled=True)  9.8 us
    ppermute x7, starting transfers between devices, passed_along(): return lax.ppermute(block, axis, route)  8.96 us
    all_to_all x1, starting transfers between devices, shards(): rows_all = lax.all_to_all(rows_here, 'dp', 0, 0, tiled=True)  5.17 us
    another operation x7, other arithmetic, advance(): jnp.stack([block_no, is_top.astype(jnp.int32), slot]).astype(jnp.int32)  4.67 us
    reshape x1, local copies, waits for them, and re-layouts, shards(): weighted.reshape(lead_dims + (pairs, per_pair, block_len, block_len))  4.27 us
    broadcast_in_dim x2, local copies, waits for them, and re-layouts, shards(): tail_full = jnp.repeat(consts['tail'], width, axis=-1)  3.76 us
  transfers between devices with their start and end apart: 8, of which 7 were waited for; matrix products, arithmetic and copies ran while one was open for 25% of the time, Pallas kernels for 25%

profile of v6, /device:TPU:0, one launch (start us, length us, event | category | flops | bytes accessed | tf_op | source)
XLA Modules:
  0.0 150.8 jit_solution(10455215856726920109)
XLA Ops:
  0.6 2.2 %copy.29 = bf16[1,1,128,2560]{2,3,1,0:T(8,128)(2,1)} copy(bf16[1,1,128,2560]{3,2,1,0:T(8,128)(2,1)} %param.6) | data formatting | bytes 1310720 | tf_op args[0]
  2.9 5.2 %all-to-all-start = ((bf16[8,1,128,320]{2,3,1,0:T(8,128)(2,1)}), bf16[8,1,128,320]{2,3,1,0:T(8,128)(2,1)}, u32[]{:S(2)}, u32[]{:S(2)}) async-start(bf16[8,1,128,320]{2,3,1,0:T(8,128)(2,1)} %bitcast.32), calls=%async_computation | async-start | bytes 1310720 | tf_op jit(solution)/shard_map/all_to_all | solution.py:335
  9.0 1.5 copy-done.3
  10.5 1.7 %mul.113 = f32[4,32,2560]{2,1,0:T(8,128)} reshape(f32[4,32,40,64]{3,2,1,0:T(8,128)S(1)} %broadcast_in_dim.72) | data formatting | bytes 2621440 | tf_op jit(solution)/shard_map/vmap(vmap(vmap()))/mul | solution.py:124
  12.2 3.0 %broadcast_in_dim.73 = f32[4,1,1,32,2560]{4,3,2,1,0:T(8,128)} reshape(f32[4,32,40,64]{3,2,1,0:T(8,128)} %copy-done.3) | data formatting | bytes 2621440 | tf_op jit(solution)/shard_map/broadcast_in_dim | solution.py:277
  20.0 1.7 %broadcast_in_dim.75 = f32[4,1,1,32,2560]{4,3,2,1,0:T(8,128)} reshape(f32[4,32,40,64]{3,2,1,0:T(8,128)S(1)} %broadcast_in_dim.74) | data formatting | bytes 2621440 | tf_op jit(solution)/shard_map/broadcast_in_dim | solution.py:278
  21.8 2.5 %exponential_select_fusion = (f32[4,1,1,32,32,40]{4,3,5,0,2,1:T(8,128)S(1)}, bf16[4,1,1,32,32,40]{4,3,5,0,2,1:T(8,128)(2,1)}) fusion(f32[4,32,40]{1,2,0:T(8,128)S(1)} %copy.24, pred[32,32]{1,0:T(8,128)(4,1)S(1)} %copy-done.7, f32[4,32,32]{2,1,0:T(8,128)} %convolution_multiply_fusion), kind=kLoop, calls=%fused_computation.3 | loop fusion | flops 819200 | bytes 1020928 | tf_op jit(solution)/shard_map/vmap(vmap(vmap(jit(_where))))/select_n | solution.py:119
  24.2 4.3 %copy.26 = bf16[4,1,1,20,2,32,32]{6,4,5,3,0,2,1:T(2,128)(2,1)} copy(bf16[4,1,1,20,2,32,32]{5,6,4,3,0,2,1:T(8,128)(2,1)} %bitcast.114) | data formatting | bytes 655360 | tf_op jit(solution)/shard_map/reshape | solution.py:272
  28.5 3.4 %reshape.423 = bf16[4,1,1,20,32,64]{5,4,3,2,1,0:T(8,128)(2,1)} reshape(bf16[4,1,1,20,32,2,32]{6,5,4,3,0,2,1:T(2,128)(2,1)} %bitcast.115) | data formatting | bytes 655360 | tf_op jit(solution)/shard_map/reshape | solution.py:273
  32.7 2.3 %fusion.13 = f32[4,128,2560]{2,1,0:T(8,128)S(1)} fusion(f32[4,32,2560]{2,1,0:T(8,128)} %mul.113, bf16[4,32,2560]{2,1,0:T(8,128)(2,1)S(1)} %bitcast.110, bf16[4,1,1,32,256]{4,3,0,2,1:T(8,128)(2,1)S(1)} %bitcast.120), kind=kOutput, calls=%fused_computation.22 | convolution fusion | flops 84869120 | bytes 7241728 | tf_op jit(solution)/shard_map/mlsjn,mlsjd->mlsnd/dot_general | solution.py:281
  36.5 1.8 %pad_maximum_fusion = bf16[4,1,1,128,2560]{4,3,2,1,0:T(8,128)(2,1)} fusion(bf16[1,1,1,128,2560]{4,3,2,1,0:T(8,128)(2,1)S(1)} %get-tuple-element.523, bf16[1,1,1,128,2560]{4,3,2,1,0:T(8,128)(2,1)S(1)} %get-tuple-element.522, bf16[1,1,1,128,2560]{4,3,2,1,0:T(8,128)(2,1)S(1)} %get-tuple-element.524, bf16[4]{0:T(256)(128)(2,1)S(1)} %pad.3.clone), kind=kLoop, calls=%fused_computation.1 | loop fusion | flops 3932160 | bytes 4587528 | tf_op jit(solution)/shard_map/stack | solution.py:289
  40.6 96.3 %while.21 = (s32[]{:T(128)}, bf16[1,32,2560]{2,1,0:T(8,128)(2,1)S(1)}, f32[1,1,128,2560]{3,2,1,0:T(8,128)}, bf16[5,1,1,32,2560]{4,3,2,1,0:T(8,128)(2,1)}, bf16[5...) while((s32[]{:T(128)}, ...), condition=%wide.region_2.3_spmd, body=%wide.region_1.2_spmd.sunk | while | flops 146800656 | bytes 8192356 | solution.py:325
  41.3 5.4 %eval_jaxpr.7 = (bf16[32,2560]{1,0:T(8,128)(2,1)}, f32[1,1,128,2560]{3,2,1,0:T(8,128)}, bf16[32,256]{1,0:T(8,128)(2,1)}, bf16[5,1,1,32,2560]{4,3,2,1,0:T(8,128)(2,1)}, bf16[5,1,1,32,256]{4,3,2,1,0:T(8,128)(2,1)S(1)}) custom-call(s32[3]{0:T(128)} %pad_add_fusion.2.picks_ref, ...), custom_call_target="tpu_custom_call", output_to_operand_aliasing={{1}: (12, {}), {3}: (15, {}), {4}: (16, {})} | custom-call | flops 146800640 | bytes 7536640 | tf_op jit(solution)/shard_map/while/body/eval_jaxpr/pallas_call | solution.py:218
  46.7 1.3 collective-permute-start
  47.9 7.6 %collective-permute-done = bf16[1,32,2560]{2,1,0:T(8,128)(2,1)S(1)} collective-permute-done((bf16[1,32,2560]{2,1,0:T(8,128)(2,1)}, bf16[1,32,2560]{2,1,0:T(8,128)(2,1)S(1)}, u32[]{:S(2)}, u32[]{:S(2)}) %collective-permute-start) | collective-permute-done | bytes 163872 | tf_op jit(solution)/shard_map/while/body/eval_jaxpr/ppermute | solution.py:20
  56.2 5.4 %eval_jaxpr.7 = (bf16[32,2560]{1,0:T(8,128)(2,1)}, f32[1,1,128,2560]{3,2,1,0:T(8,128)}, bf16[32,256]{1,0:T(8,128)(2,1)}, bf16[5,1,1,32,2560]{4,3,2,1,0:T(8,128)(2,1)}, bf16[5,1,1,32,256]{4,3,2,1,0:T(8,128)(2,1)S(1)}) custom-call(s32[3]{0:T(128)} %pad_add_fusion.2.picks_ref, ...), custom_call_target="tpu_custom_call", output_to_operand_aliasing={{1}: (12, {}), {3}: (15, {}), {4}: (16, {})} | custom-call | flops 146800640 | bytes 7536640 | tf_op jit(solution)/shard_map/while/body/eval_jaxpr/pallas_call | solution.py:218
  61.6 1.3 collective-permute-start
  62.9 6.7 %collective-permute-done = bf16[1,32,2560]{2,1,0:T(8,128)(2,1)S(1)} collective-permute-done((bf16[1,32,2560]{2,1,0:T(8,128)(2,1)}, bf16[1,32,2560]{2,1,0:T(8,128)(2,1)S(1)}, u32[]{:S(2)}, u32[]{:S(2)}) %collective-permute-start) | collective-permute-done | bytes 163872 | tf_op jit(solution)/shard_map/while/body/eval_jaxpr/ppermute | solution.py:20
  70.3 5.4 %eval_jaxpr.7 = (bf16[32,2560]{1,0:T(8,128)(2,1)}, f32[1,1,128,2560]{3,2,1,0:T(8,128)}, bf16[32,256]{1,0:T(8,128)(2,1)}, bf16[5,1,1,32,2560]{4,3,2,1,0:T(8,128)(2,1)}, bf16[5,1,1,32,256]{4,3,2,1,0:T(8,128)(2,1)S(1)}) custom-call(s32[3]{0:T(128)} %pad_add_fusion.2.picks_ref, ...), custom_call_target="tpu_custom_call", output_to_operand_aliasing={{1}: (12, {}), {3}: (15, {}), {4}: (16, {})} | custom-call | flops 146800640 | bytes 7536640 | tf_op jit(solution)/shard_map/while/body/eval_jaxpr/pallas_call | solution.py:218
  75.6 1.3 collective-permute-start
  76.9 6.1 %collective-permute-done = bf16[1,32,2560]{2,1,0:T(8,128)(2,1)S(1)} collective-permute-done((bf16[1,32,2560]{2,1,0:T(8,128)(2,1)}, bf16[1,32,2560]{2,1,0:T(8,128)(2,1)S(1)}, u32[]{:S(2)}, u32[]{:S(2)}) %collective-permute-start) | collective-permute-done | bytes 163872 | tf_op jit(solution)/shard_map/while/body/eval_jaxpr/ppermute | solution.py:20
  83.7 5.4 %eval_jaxpr.7 = (bf16[32,2560]{1,0:T(8,128)(2,1)}, f32[1,1,128,2560]{3,2,1,0:T(8,128)}, bf16[32,256]{1,0:T(8,128)(2,1)}, bf16[5,1,1,32,2560]{4,3,2,1,0:T(8,128)(2,1)}, bf16[5,1,1,32,256]{4,3,2,1,0:T(8,128)(2,1)S(1)}) custom-call(s32[3]{0:T(128)} %pad_add_fusion.2.picks_ref, ...), custom_call_target="tpu_custom_call", output_to_operand_aliasing={{1}: (12, {}), {3}: (15, {}), {4}: (16, {})} | custom-call | flops 146800640 | bytes 7536640 | tf_op jit(solution)/shard_map/while/body/eval_jaxpr/pallas_call | solution.py:218
  90.4 6.1 %collective-permute-done = bf16[1,32,2560]{2,1,0:T(8,128)(2,1)S(1)} collective-permute-done((bf16[1,32,2560]{2,1,0:T(8,128)(2,1)}, bf16[1,32,2560]{2,1,0:T(8,128)(2,1)S(1)}, u32[]{:S(2)}, u32[]{:S(2)}) %collective-permute-start) | collective-permute-done | bytes 163872 | tf_op jit(solution)/shard_map/while/body/eval_jaxpr/ppermute | solution.py:20
  97.2 5.4 %eval_jaxpr.7 = (bf16[32,2560]{1,0:T(8,128)(2,1)}, f32[1,1,128,2560]{3,2,1,0:T(8,128)}, bf16[32,256]{1,0:T(8,128)(2,1)}, bf16[5,1,1,32,2560]{4,3,2,1,0:T(8,128)(2,1)}, bf16[5,1,1,32,256]{4,3,2,1,0:T(8,128)(2,1)S(1)}) custom-call(s32[3]{0:T(128)} %pad_add_fusion.2.picks_ref, ...), custom_call_target="tpu_custom_call", output_to_operand_aliasing={{1}: (12, {}), {3}: (15, {}), {4}: (16, {})} | custom-call | flops 146800640 | bytes 7536640 | tf_op jit(solution)/shard_map/while/body/eval_jaxpr/pallas_call | solution.py:218
  103.9 6.1 %collective-permute-done = bf16[1,32,2560]{2,1,0:T(8,128)(2,1)S(1)} collective-permute-done((bf16[1,32,2560]{2,1,0:T(8,128)(2,1)}, bf16[1,32,2560]{2,1,0:T(8,128)(2,1)S(1)}, u32[]{:S(2)}, u32[]{:S(2)}) %collective-permute-start) | collective-permute-done | bytes 163872 | tf_op jit(solution)/shard_map/while/body/eval_jaxpr/ppermute | solution.py:20
  110.6 5.4 %eval_jaxpr.7 = (bf16[32,2560]{1,0:T(8,128)(2,1)}, f32[1,1,128,2560]{3,2,1,0:T(8,128)}, bf16[32,256]{1,0:T(8,128)(2,1)}, bf16[5,1,1,32,2560]{4,3,2,1,0:T(8,128)(2,1)}, bf16[5,1,1,32,256]{4,3,2,1,0:T(8,128)(2,1)S(1)}) custom-call(s32[3]{0:T(128)} %pad_add_fusion.2.picks_ref, ...), custom_call_target="tpu_custom_call", output_to_operand_aliasing={{1}: (12, {}), {3}: (15, {}), {4}: (16, {})} | custom-call | flops 146800640 | bytes 7536640 | tf_op jit(solution)/shard_map/while/body/eval_jaxpr/pallas_call | solution.py:218
  117.3 6.1 %collective-permute-done = bf16[1,32,2560]{2,1,0:T(8,128)(2,1)S(1)} collective-permute-done((bf16[1,32,2560]{2,1,0:T(8,128)(2,1)}, bf16[1,32,2560]{2,1,0:T(8,128)(2,1)S(1)}, u32[]{:S(2)}, u32[]{:S(2)}) %collective-permute-start) | collective-permute-done | bytes 163872 | tf_op jit(solution)/shard_map/while/body/eval_jaxpr/ppermute | solution.py:20
  124.1 5.4 %eval_jaxpr.7 = (bf16[32,2560]{1,0:T(8,128)(2,1)}, f32[1,1,128,2560]{3,2,1,0:T(8,128)}, bf16[32,256]{1,0:T(8,128)(2,1)}, bf16[5,1,1,32,2560]{4,3,2,1,0:T(8,128)(2,1)}, bf16[5,1,1,32,256]{4,3,2,1,0:T(8,128)(2,1)S(1)}) custom-call(s32[3]{0:T(128)} %pad_add_fusion.2.picks_ref, ...), custom_call_target="tpu_custom_call", output_to_operand_aliasing={{1}: (12, {}), {3}: (15, {}), {4}: (16, {})} | custom-call | flops 146800640 | bytes 7536640 | tf_op jit(solution)/shard_map/while/body/eval_jaxpr/pallas_call | solution.py:218
  130.8 6.1 %collective-permute-done = bf16[1,32,2560]{2,1,0:T(8,128)(2,1)S(1)} collective-permute-done((bf16[1,32,2560]{2,1,0:T(8,128)(2,1)}, bf16[1,32,2560]{2,1,0:T(8,128)(2,1)S(1)}, u32[]{:S(2)}, u32[]{:S(2)}) %collective-permute-start) | collective-permute-done | bytes 163872 | tf_op jit(solution)/shard_map/while/body/eval_jaxpr/ppermute | solution.py:20
  136.9 2.0 %slice.57 = bf16[4,1,1,32,2560]{4,3,2,1,0:T(8,128)(2,1)} slice(bf16[5,1,1,32,2560]{4,3,2,1,0:T(8,128)(2,1)} %get-tuple-element.425), slice={[0:4], [0:1], [0:1], [0:32], [0:2560]} | slice | bytes 1310720 | tf_op jit(solution)/shard_map/slice | solution.py:329
  138.9 9.8 %all_gather.3 = bf16[8,1,128,256]{3,2,1,0:T(8,128)(2,1)S(1)} all-gather(bf16[1,1,128,256]{3,2,1,0:T(8,128)(2,1)S(1)} %bitcast.123), channel_id=1, replica_groups=mesh['section'=4,'dp'=8] {'dp'}, dimensions={0}, use_global_device_ids=true | all-gather | bytes 589824 | tf_op jit(solution)/shard_map/all_gather | solution.py:337
  148.7 2.1 %fusion.8 = f32[1,320,256]{2,1,0:T(8,128)} fusion(bf16[8,1,128,320]{2,3,1,0:T(8,128)(2,1)} %all-to-all-done, bf16[8,1,128,256]{3,2,1,0:T(8,128)(2,1)S(1)} %all_gather.3), kind=kOutput, calls=%fused_computation.18 | convolution fusion | flops 167854080 | bytes 1507328 | tf_op jit(solution)/shard_map/glrd,glrc->ldc/dot_general | solution.py:338
  (60 shorter events, 20.0 us)
Async XLA Ops:
  0.6 7.4 %copy-start.6 = (f32[1,1,128,40]{2,3,1,0:T(8,128)S(1)}, f32[1,1,128,40]{2,3,1,0:T(8,128)}, u32[]{:S(2)}) copy-start(f32[1,1,128,40]{2,3,1,0:T(8,128)} %param.8) | copy-start | bytes 61444
  2.9 145.8 %all-to-all-start = ((bf16[8,1,128,320]{2,3,1,0:T(8,128)(2,1)}), bf16[8,1,128,320]{2,3,1,0:T(8,128)(2,1)}, u32[]{:S(2)}, u32[]{:S(2)}) async-start(bf16[8,1,128,320]{2,3,1,0:T(8,128)(2,1)} %bitcast.32), calls=%async_computation | async-start | bytes 1310720 | tf_op jit(solution)/shard_map/all_to_all | solution.py:335
  8.3 9.3 %copy-start.8 = (f32[4,40]{1,0:T(4,128)}, f32[4,40]{1,0:T(4,128)S(1)}, u32[]{:S(2)}) copy-start(f32[4,40]{1,0:T(4,128)S(1)} %exp.40) | copy-start | bytes 1924
  9.0 1.5 copy-start.3
  12.2 3.6 %copy-start.1 = (bf16[1,1,128,2560]{3,2,1,0:T(8,128)(2,1)S(1)}, bf16[1,1,128,2560]{3,2,1,0:T(8,128)(2,1)}, u32[]{:S(2)}) copy-start(bf16[1,1,128,2560]{3,2,1,0:T(8,128)(2,1)} %param.6) | copy-start | bytes 1966084
  12.2 3.6 %copy-start.2 = (bf16[1,2560,256]{2,1,0:T(8,128)(2,1)S(1)}, bf16[1,2560,256]{2,1,0:T(8,128)(2,1)}, u32[]{:S(2)}) copy-start(bf16[1,2560,256]{2,1,0:T(8,128)(2,1)} %param.7) | copy-start | bytes 3932164
  20.0 1.8 %copy-start.7 = (pred[32,32]{1,0:T(8,128)(4,1)S(1)}, pred[32,32]{1,0:T(8,128)(4,1)}, u32[]{:S(2)}) copy-start(pred[32,32]{1,0:T(8,128)(4,1)} %iota_compare_fusion) | copy-start | bytes 3076
  28.5 3.4 %copy-start.9 = (f32[4,40]{1,0:T(4,128)S(1)}, f32[4,40]{1,0:T(4,128)}, u32[]{:S(2)}) copy-start(f32[4,40]{1,0:T(4,128)} %copy-done.8) | copy-start | bytes 1924
  32.7 2.3 %copy-start = (f32[4,1,1,32,2560]{4,3,2,1,0:T(8,128)S(1)}, f32[4,1,1,32,2560]{4,3,2,1,0:T(8,128)}, u32[]{:S(2)}) copy-start(f32[4,1,1,32,2560]{4,3,2,1,0:T(8,128)} %broadcast_in_dim.73) | copy-start | bytes 3932164
  35.1 1.1 copy-start.4
  35.1 1.1 copy-start.5
  46.7 8.9 %collective-permute-start = (bf16[1,32,2560]{2,1,0:T(8,128)(2,1)}, bf16[1,32,2560]{2,1,0:T(8,128)(2,1)S(1)}, u32[]{:S(2)}, u32[]{:S(2)}) collective-permute-start(bf16[1,32,2560]{2,1,0:T(8,128)(2,1)} %bitcast.127), channel_id=1, source_target_pairs={{8,0},{16,8},{24,16},{9,1},{17,9},{25,17},{10,2},{18,10},{26,18},{... | collective-permute-start | bytes 491528 | tf_op jit(solution)/shard_map/while/body/eval_jaxpr/ppermute | solution.py:20
  61.6 8.0 %collective-permute-start = (bf16[1,32,2560]{2,1,0:T(8,128)(2,1)}, bf16[1,32,2560]{2,1,0:T(8,128)(2,1)S(1)}, u32[]{:S(2)}, u32[]{:S(2)}) collective-permute-start(bf16[1,32,2560]{2,1,0:T(8,128)(2,1)} %bitcast.127), channel_id=1, source_target_pairs={{8,0},{16,8},{24,16},{9,1},{17,9},{25,17},{10,2},{18,10},{26,18},{... | collective-permute-start | bytes 491528 | tf_op jit(solution)/shard_map/while/body/eval_jaxpr/ppermute | solution.py:20
  75.6 7.4 %collective-permute-start = (bf16[1,32,2560]{2,1,0:T(8,128)(2,1)}, bf16[1,32,2560]{2,1,0:T(8,128)(2,1)S(1)}, u32[]{:S(2)}, u32[]{:S(2)}) collective-permute-start(bf16[1,32,2560]{2,1,0:T(8,128)(2,1)} %bitcast.127), channel_id=1, source_target_pairs={{8,0},{16,8},{24,16},{9,1},{17,9},{25,17},{10,2},{18,10},{26,18},{... | collective-permute-start | bytes 491528 | tf_op jit(solution)/shard_map/while/body/eval_jaxpr/ppermute | solution.py:20
  89.1 7.4 %collective-permute-start = (bf16[1,32,2560]{2,1,0:T(8,128)(2,1)}, bf16[1,32,2560]{2,1,0:T(8,128)(2,1)S(1)}, u32[]{:S(2)}, u32[]{:S(2)}) collective-permute-start(bf16[1,32,2560]{2,1,0:T(8,128)(2,1)} %bitcast.127), channel_id=1, source_target_pairs={{8,0},{16,8},{24,16},{9,1},{17,9},{25,17},{10,2},{18,10},{26,18},{... | collective-permute-start | bytes 491528 | tf_op jit(solution)/shard_map/while/body/eval_jaxpr/ppermute | solution.py:20
  102.6 7.4 %collective-permute-start = (bf16[1,32,2560]{2,1,0:T(8,128)(2,1)}, bf16[1,32,2560]{2,1,0:T(8,128)(2,1)S(1)}, u32[]{:S(2)}, u32[]{:S(2)}) collective-permute-start(bf16[1,32,2560]{2,1,0:T(8,128)(2,1)} %bitcast.127), channel_id=1, source_target_pairs={{8,0},{16,8},{24,16},{9,1},{17,9},{25,17},{10,2},{18,10},{26,18},{... | collective-permute-start | bytes 491528 | tf_op jit(solution)/shard_map/while/body/eval_jaxpr/ppermute | solution.py:20
  116.0 7.4 %collective-permute-start = (bf16[1,32,2560]{2,1,0:T(8,128)(2,1)}, bf16[1,32,2560]{2,1,0:T(8,128)(2,1)S(1)}, u32[]{:S(2)}, u32[]{:S(2)}) collective-permute-start(bf16[1,32,2560]{2,1,0:T(8,128)(2,1)} %bitcast.127), channel_id=1, source_target_pairs={{8,0},{16,8},{24,16},{9,1},{17,9},{25,17},{10,2},{18,10},{26,18},{... | collective-permute-start | bytes 491528 | tf_op jit(solution)/shard_map/while/body/eval_jaxpr/ppermute | solution.py:20
  129.5 7.4 %collective-permute-start = (bf16[1,32,2560]{2,1,0:T(8,128)(2,1)}, bf16[1,32,2560]{2,1,0:T(8,128)(2,1)S(1)}, u32[]{:S(2)}, u32[]{:S(2)}) collective-permute-start(bf16[1,32,2560]{2,1,0:T(8,128)(2,1)} %bitcast.127), channel_id=1, source_target_pairs={{8,0},{16,8},{24,16},{9,1},{17,9},{25,17},{10,2},{18,10},{26,18},{... | collective-permute-start | bytes 491528 | tf_op jit(solution)/shard_map/while/body/eval_jaxpr/ppermute | solution.py:20

commit v7 on v6

--- a/solution.py
+++ b/solution.py
@@ -120,16 +120,19 @@
     tail_decay = jnp.exp(ending[None, :] - cumulative)
     leading = jnp.exp(cumulative)
     scores = jnp.dot(out_b, in_b.T, preferred_element_type=jnp.float32)
-    weighted = (factor * decays * scores[:, :, None]).astype(jnp.bfloat16)
+    cum_t = cumulative.T
+    upper = (locations[:, None] <= locations[None, :])[None]
+    spread_t = jnp.where(upper, cum_t[:, None, :] - cum_t[:, :, None], 0.0)
+    decays_t = jnp.where(upper, jnp.exp(spread_t), 0.0)
+    scores_t = jnp.dot(in_b, out_b.T, preferred_element_type=jnp.float32)
+    weighted = (factor * decays_t * scores_t[None]).astype(jnp.bfloat16)
     tail_inputs = (tail_decay[:, :, None] * inputs_b.astype(jnp.float32)).astype(jnp.bfloat16)
-    fresh = jnp.einsum("jhp,jn->hpn", tail_inputs, in_b, preferred_element_type=jnp.float32)
     return dict(
         decays=decays,
         tail=tail_decay,
         lead=leading,
         weighted=weighted,
         tail_inputs=tail_inputs,
-        fresh=fresh,
         ending=jnp.exp(ending),
     )
 
@@ -158,7 +161,15 @@
         v_q = v_ref[:, cols]
         x_q = x_ref[:, cols]
         stacked = jnp.concatenate([jnp.where(m, v_q, jnp.zeros_like(v_q)) for m in masks], axis=0)
-        gx_q = jnp.dot(wt_ref[q], stacked, preferred_element_type=f32)
+        gx_q = jnp.dot(
+            wt_ref[per_pair * q], stacked[0:length], preferred_element_type=f32
+        )
+        for e in range(1, per_pair):
+            gx_q = gx_q + jnp.dot(
+                wt_ref[per_pair * q + e],
+                stacked[e * length:(e + 1) * length],
+                preferred_element_type=f32,
+            )
         rbb_q = jnp.dot(in_map, rb_t[:, cols], preferred_element_type=f32)
         gx_ref[:, cols] = gx_q + tail_ref[:, cols] * rbb_q
         pair_dots = lax.dot_general(stacked, x_q, nt, preferred_element_type=f32)
@@ -179,11 +190,11 @@
     rnew_ref[...] = carry + end_ref[...] * r_ref[...]
     grad_bc = jnp.concatenate([grad_inmap, grad_outmap], axis=1).astype(bf16)
     dbc_ref[...] = grad_bc
-    mstore_ref[...] = grad_bc
+    mstore_ref[...] = jnp.where(picks_ref[2] > 0, grad_bc, ms_ref[...])
     back = lax.dot_general(grad_bc, w_ref[...], nt, preferred_element_type=f32)
     summed = (v.astype(f32) + gx_ref[...] + back).astype(out_ref.dtype)
     out_ref[...] = summed
-    gstore_ref[...] = summed
+    gstore_ref[...] = jnp.where(picks_ref[2] > 0, summed, gs_ref[...])
 
 
 def fused_step(picks, per_block, incoming, top_blk, carried, w_bc, grad_store, map_store, level_no, seq_no, factor, width):
@@ -203,8 +214,8 @@
     in_specs.append(pl.BlockSpec((None, None) + carried.shape[2:], lambda i, p: (level_no, seq_no, 0, 0)))
     in_specs.append(lead_block(end_row))
     in_specs.append(pl.BlockSpec((None,) + w_bc.shape[1:], lambda i, p: (level_no, 0, 0)))
-    store_g = pl.BlockSpec((None, None, None, length, features), lambda i, p: (p[2], level_no, seq_no, 0, 0))
-    store_m = pl.BlockSpec((None, None, None, length, 2 * state_size), lambda i, p: (p[2], level_no, seq_no, 0, 0))
+    store_g = pl.BlockSpec((None, None, None, length, features), lambda i, p: (p[0], level_no, seq_no, 0, 0))
+    store_m = pl.BlockSpec((None, None, None, length, 2 * state_size), lambda i, p: (p[0], level_no, seq_no, 0, 0))
     in_specs += [store_g, store_m]
     out_specs = (
         pl.BlockSpec((length, features), lambda i, p: (0, 0)),
@@ -268,9 +279,7 @@
     lead_dims = consts["tail"].shape[:3]
     pairs = head_count * width // 128
     per_pair = 128 // width
-    weighted = jnp.swapaxes(consts["weighted"], -1, -3)
-    weighted = weighted.reshape(lead_dims + (pairs, per_pair, block_len, block_len))
-    wt2 = jnp.swapaxes(weighted, -3, -2).reshape(lead_dims + (pairs, block_len, per_pair * block_len))
+    wt2 = consts["weighted"]
     dec2 = jnp.moveaxis(consts["decays"], -1, -3).reshape(
         lead_dims + (pairs, per_pair * block_len, block_len)
     )
@@ -296,13 +305,13 @@
     )
     is_top = section_id == sections - 1
 
-    def advance(counter, loop_state):
+    def advance(counter, loop_state, send=True):
         incoming, carried, grad_store, map_store = loop_state
         offset = counter - (sections - 1 - section_id)
         is_valid = (offset >= 0) & (offset < MICRO)
         block_no = jnp.clip(MICRO - 1 - offset, 0, MICRO - 1)
-        slot = jnp.where(is_valid, block_no, MICRO)
-        picks = jnp.stack([block_no, is_top.astype(jnp.int32), slot]).astype(jnp.int32)
+        picks = jnp.stack([block_no, is_top.astype(jnp.int32), is_valid.astype(jnp.int32)])
+        picks = picks.astype(jnp.int32)
         for level_no in reversed(range(lay_dev)):
             level_out = []
             for seq_no in range(seq_dev):
@@ -313,21 +322,24 @@
                 level_out.append(level_grads)
             incoming = jnp.stack(level_out)
             picks = picks.at[1].set(0)
-        received = passed_along(incoming, "section", -1)
-        return (received, carried, grad_store, map_store)
+        if send:
+            incoming = passed_along(incoming, "section", -1)
+        return (incoming, carried, grad_store, map_store)
 
     initial = (
         jnp.zeros((seq_dev, block_len, features), jnp.bfloat16),
         jnp.zeros(states_t.shape[1:], jnp.float32),
-        jnp.zeros((MICRO + 1, lay_dev, seq_dev, block_len, features), jnp.bfloat16),
-        jnp.zeros((MICRO + 1, lay_dev, seq_dev, block_len, 2 * state_size), jnp.bfloat16),
-    )
-    final_state = lax.fori_loop(0, MICRO + sections - 1, advance, initial)
+        jnp.zeros((MICRO, lay_dev, seq_dev, block_len, features), jnp.bfloat16),
+        jnp.zeros((MICRO, lay_dev, seq_dev, block_len, 2 * state_size), jnp.bfloat16),
+    )
+    steps = MICRO + sections - 1
+    final_state = lax.fori_loop(0, steps - 1, advance, initial)
+    final_state = advance(steps - 1, final_state, send=False)
     grad_store = final_state[2]
     map_store = final_state[3]
 
-    grad_inputs = jnp.moveaxis(grad_store[:MICRO], 0, 2).reshape(layer_inputs.shape)
-    map_store = jnp.moveaxis(map_store[:MICRO], 0, 2).reshape(bc_all.shape)
+    grad_inputs = jnp.moveaxis(grad_store, 0, 2).reshape(layer_inputs.shape)
+    map_store = jnp.moveaxis(map_store, 0, 2).reshape(bc_all.shape)
     ways = lax.axis_size("dp")
     divisor = ways * seq_dev
     rows_here = layer_inputs.reshape(lay_dev, seq_dev * tok_len, ways, features // ways)

time: 152 us -> 135 us (0.89)
  local copies, waits for them, and re-layouts: 26.8 us -> 20.4 us
  waiting for transfers between devices: 44.9 us -> 38.8 us
    reshape x2 -> x0, local copies, waits for them, and re-layouts: 7.68 us -> none  [the longest x1 4.27 us: shards(): weighted.reshape(lead_dims + (pairs, per_pair, block_len, block_len))]
    ppermute x7 -> x6, waiting for transfers between devices: 44.9 us -> 38.8 us  [passed_along(): return lax.ppermute(block, axis, route)]
    broadcast_in_dim x2, local copies, waits for them, and re-layouts: 2.4 us -> 4.9 us  [shards(): lead_full = jnp.repeat(consts['lead'], width, axis=-1)]
    slice x2 -> x0, local copies, waits for them, and re-layouts: 1.97 us -> none  [the longest x1 1.97 us: shards(): grad_store[:MICRO]]
    convert_element_type x0 -> x1, other arithmetic: none -> 1.7 us  [block_consts(): weighted = (factor * decays_t * scores_t[None]).astype(jnp.bfloat16)]
    ppermute x7 -> x6, starting transfers between devices: 8.96 us -> 7.68 us  [passed_along(): return lax.ppermute(block, axis, route)]
  transfers between devices with their start and end apart: 8 -> 7, of which waited for: 7 -> 6; matrix products, arithmetic and copies ran while one was open for 25% -> 21% of each run, Pallas kernels for 25% -> 28%
where the time goes in v7:
time: 135 us; the launch traced here: 134 us
  waiting for transfers between devices  38.8 us (29%)
  Pallas kernels  37.6 us (28%)
  local copies, waits for them, and re-layouts  20.4 us (15%)
  starting transfers between devices  12.9 us (10%)
  other arithmetic  9.97 us (7%)
  blocking collectives  9.79 us (7%)
  matrix products  4.13 us (3%)
    ppermute x6, waiting for transfers between devices, passed_along(): return lax.ppermute(block, axis, route)  38.8 us
    pallas_call x7, Pallas kernels, fused_step(): pl.pallas_call(functools.partial(step_kernel, factor=factor, width=width)...  37.6 us
    all_gather x1, blocking collectives, shards(): maps_all = lax.all_gather(maps_here, 'dp', axis=0, tiled=True)  9.79 us
    ppermute x6, starting transfers between devices, passed_along(): return lax.ppermute(block, axis, route)  7.68 us
    all_to_all x1, starting transfers between devices, shards(): rows_all = lax.all_to_all(rows_here, 'dp', 0, 0, tiled=True)  5.17 us
    broadcast_in_dim x2, local copies, waits for them, and re-layouts, shards(): lead_full = jnp.repeat(consts['lead'], width, axis=-1)  4.9 us
    another operation x7, other arithmetic, advance(): jnp.stack([block_no, is_top.astype(jnp.int32), is_valid.astype(jnp.int32)])  4.6 us
    unnamed x21, local copies, waits for them, and re-layouts  3.81 us
  transfers between devices with their start and end apart: 7, of which 6 were waited for; matrix products, arithmetic and copies ran while one was open for 21% of the time, Pallas kernels for 28%

profile of v7, /device:TPU:0, one launch (start us, length us, event | category | flops | bytes accessed | tf_op | source)
XLA Modules:
  0.0 134.4 jit_solution(17611734884899602403)
XLA Ops:
  0.6 2.2 %copy.31 = bf16[1,1,128,2560]{2,3,1,0:T(8,128)(2,1)} copy(bf16[1,1,128,2560]{3,2,1,0:T(8,128)(2,1)} %param.6) | data formatting | bytes 1310720 | tf_op args[0]
  2.9 5.2 %all-to-all-start = ((bf16[8,1,128,320]{2,3,1,0:T(8,128)(2,1)}), bf16[8,1,128,320]{2,3,1,0:T(8,128)(2,1)}, u32[]{:S(2)}, u32[]{:S(2)}) async-start(bf16[8,1,128,320]{2,3,1,0:T(8,128)(2,1)} %bitcast.33), calls=%async_computation | async-start | bytes 1310720 | tf_op jit(solution)/shard_map/all_to_all | solution.py:347
  9.1 1.5 %copy-done.3 = f32[4,32,40,64]{3,2,1,0:T(8,128)} copy-done((f32[4,32,40,64]{3,2,1,0:T(8,128)}, f32[4,32,40,64]{3,2,1,0:T(8,128)S(1)}, u32[]{:S(2)}) %copy-start.3) | copy-done | bytes 1310744
  10.5 1.7 %mul.113 = f32[4,32,2560]{2,1,0:T(8,128)} reshape(f32[4,32,40,64]{3,2,1,0:T(8,128)S(1)} %broadcast_in_dim.106) | data formatting | bytes 2621440 | tf_op jit(solution)/shard_map/vmap(vmap(vmap()))/mul | solution.py:129
  12.3 2.2 %broadcast_in_dim.107.tail_ref = f32[4,1,1,32,2560]{4,3,2,1,0:T(8,128)S(1)} reshape(f32[4,32,40,64]{3,2,1,0:T(8,128)} %copy-done.3) | data formatting | bytes 2621440 | tf_op jit(solution)/shard_map/broadcast_in_dim | solution.py:286
  17.9 1.9 %broadcast_in_dim.108 = f32[4,32,40,64]{3,2,1,0:T(8,128)} broadcast(f32[4,32,40]{2,1,0:T(8,128)S(1)} %get-tuple-element.476), dimensions={0,1,2} | broadcast | bytes 1331200 | tf_op jit(solution)/shard_map/broadcast_in_dim | solution.py:287
  19.8 3.0 %broadcast_in_dim.109.lead_ref = f32[4,1,1,32,2560]{4,3,2,1,0:T(8,128)} reshape(f32[4,32,40,64]{3,2,1,0:T(8,128)} %broadcast_in_dim.108) | data formatting | bytes 2621440 | tf_op jit(solution)/shard_map/broadcast_in_dim | solution.py:287
  27.2 1.9 %exponential_select_fusion = f32[4,1,1,32,32,40]{4,3,5,0,2,1:T(8,128)} fusion(f32[4,32,40]{1,2,0:T(8,128)S(1)} %copy-done.5, pred[32,32]{1,0:T(8,128)(4,1)S(1)} %iota_compare_fusion), kind=kLoop, calls=%fused_computation.2 | loop fusion | flops 491520 | bytes 676864 | tf_op jit(solution)/shard_map/vmap(vmap(vmap(jit(_where))))/select_n | solution.py:119
  29.2 1.7 %multiply_convert_fusion.wt_ref = bf16[4,1,1,40,32,32]{5,4,3,2,1,0:T(8,128)(2,1)} fusion(f32[4,32,32]{2,1,0:T(8,128)S(1)} %copy-done.6, f32[4,40,32]{2,1,0:T(8,128)S(1)} %copy.27, pred[32,32]{1,0:T(8,128)(4,1)S(1)} %iota_compare_fusion.1), kind=kLoop, calls=%fused_computation.3 | loop fusion | flops 819200 | bytes 365568 | tf_op jit(solution)/shard_map/vmap(vmap(vmap()))/convert_element_type | solution.py:128
  32.2 1.2 broadcast.326
  34.3 82.8 %while.21 = (s32[]{:T(128)}, bf16[1,32,2560]{2,1,0:T(8,128)(2,1)S(1)}, f32[1,1,128,2560]{3,2,1,0:T(8,128)}, bf16[4,1,1,32,2560]{4,3,2,1,0:T(8,128)(2,1)}, bf16[4...) while((s32[]{:T(128)}, ...), condition=%wide.region_2.3_spmd, body=%wide.region_1.2_spmd.sunk | while | flops 146800656 | bytes 8192348 | solution.py:336
  35.0 5.4 %eval_jaxpr.7 = (bf16[32,2560]{1,0:T(8,128)(2,1)}, f32[1,1,128,2560]{3,2,1,0:T(8,128)}, bf16[32,256]{1,0:T(8,128)(2,1)}, bf16[4,1,1,32,2560]{4,3,2,1,0:T(8,128)(2,1)}, bf16[4,1,1,32,256]{4,3,2,1,0:T(8,128)(2,1)S(1)}) custom-call(s32[3]{0:T(128)} %pad_add_fusion.3.picks_ref, ...), custom_call_target="tpu_custom_call", output_to_operand_aliasing={{1}: (12, {}), {3}: (15, {}), {4}: (16, {})} | custom-call | flops 146800640 | bytes 7536640 | tf_op jit(solution)/shard_map/while/body/eval_jaxpr/pallas_call | solution.py:229
  40.4 1.3 collective-permute-start
  41.7 7.6 %collective-permute-done = bf16[1,32,2560]{2,1,0:T(8,128)(2,1)S(1)} collective-permute-done((bf16[1,32,2560]{2,1,0:T(8,128)(2,1)}, bf16[1,32,2560]{2,1,0:T(8,128)(2,1)S(1)}, u32[]{:S(2)}, u32[]{:S(2)}) %collective-permute-start) | collective-permute-done | bytes 163872 | tf_op jit(solution)/shard_map/while/body/eval_jaxpr/ppermute | solution.py:20
  49.9 5.4 %eval_jaxpr.7 = (bf16[32,2560]{1,0:T(8,128)(2,1)}, f32[1,1,128,2560]{3,2,1,0:T(8,128)}, bf16[32,256]{1,0:T(8,128)(2,1)}, bf16[4,1,1,32,2560]{4,3,2,1,0:T(8,128)(2,1)}, bf16[4,1,1,32,256]{4,3,2,1,0:T(8,128)(2,1)S(1)}) custom-call(s32[3]{0:T(128)} %pad_add_fusion.3.picks_ref, ...), custom_call_target="tpu_custom_call", output_to_operand_aliasing={{1}: (12, {}), {3}: (15, {}), {4}: (16, {})} | custom-call | flops 146800640 | bytes 7536640 | tf_op jit(solution)/shard_map/while/body/eval_jaxpr/pallas_call | solution.py:229
  55.3 1.3 collective-permute-start
  56.6 6.7 %collective-permute-done = bf16[1,32,2560]{2,1,0:T(8,128)(2,1)S(1)} collective-permute-done((bf16[1,32,2560]{2,1,0:T(8,128)(2,1)}, bf16[1,32,2560]{2,1,0:T(8,128)(2,1)S(1)}, u32[]{:S(2)}, u32[]{:S(2)}) %collective-permute-start) | collective-permute-done | bytes 163872 | tf_op jit(solution)/shard_map/while/body/eval_jaxpr/ppermute | solution.py:20
  64.0 5.4 %eval_jaxpr.7 = (bf16[32,2560]{1,0:T(8,128)(2,1)}, f32[1,1,128,2560]{3,2,1,0:T(8,128)}, bf16[32,256]{1,0:T(8,128)(2,1)}, bf16[4,1,1,32,2560]{4,3,2,1,0:T(8,128)(2,1)}, bf16[4,1,1,32,256]{4,3,2,1,0:T(8,128)(2,1)S(1)}) custom-call(s32[3]{0:T(128)} %pad_add_fusion.3.picks_ref, ...), custom_call_target="tpu_custom_call", output_to_operand_aliasing={{1}: (12, {}), {3}: (15, {}), {4}: (16, {})} | custom-call | flops 146800640 | bytes 7536640 | tf_op jit(solution)/shard_map/while/body/eval_jaxpr/pallas_call | solution.py:229
  69.3 1.3 collective-permute-start
  70.6 6.1 %collective-permute-done = bf16[1,32,2560]{2,1,0:T(8,128)(2,1)S(1)} collective-permute-done((bf16[1,32,2560]{2,1,0:T(8,128)(2,1)}, bf16[1,32,2560]{2,1,0:T(8,128)(2,1)S(1)}, u32[]{:S(2)}, u32[]{:S(2)}) %collective-permute-start) | collective-permute-done | bytes 163872 | tf_op jit(solution)/shard_map/while/body/eval_jaxpr/ppermute | solution.py:20
  77.4 5.4 %eval_jaxpr.7 = (bf16[32,2560]{1,0:T(8,128)(2,1)}, f32[1,1,128,2560]{3,2,1,0:T(8,128)}, bf16[32,256]{1,0:T(8,128)(2,1)}, bf16[4,1,1,32,2560]{4,3,2,1,0:T(8,128)(2,1)}, bf16[4,1,1,32,256]{4,3,2,1,0:T(8,128)(2,1)S(1)}) custom-call(s32[3]{0:T(128)} %pad_add_fusion.3.picks_ref, ...), custom_call_target="tpu_custom_call", output_to_operand_aliasing={{1}: (12, {}), {3}: (15, {}), {4}: (16, {})} | custom-call | flops 146800640 | bytes 7536640 | tf_op jit(solution)/shard_map/while/body/eval_jaxpr/pallas_call | solution.py:229
  82.8 1.3 collective-permute-start
  84.1 6.1 %collective-permute-done = bf16[1,32,2560]{2,1,0:T(8,128)(2,1)S(1)} collective-permute-done((bf16[1,32,2560]{2,1,0:T(8,128)(2,1)}, bf16[1,32,2560]{2,1,0:T(8,128)(2,1)S(1)}, u32[]{:S(2)}, u32[]{:S(2)}) %collective-permute-start) | collective-permute-done | bytes 163872 | tf_op jit(solution)/shard_map/while/body/eval_jaxpr/ppermute | solution.py:20
  90.9 5.4 %eval_jaxpr.7 = (bf16[32,2560]{1,0:T(8,128)(2,1)}, f32[1,1,128,2560]{3,2,1,0:T(8,128)}, bf16[32,256]{1,0:T(8,128)(2,1)}, bf16[4,1,1,32,2560]{4,3,2,1,0:T(8,128)(2,1)}, bf16[4,1,1,32,256]{4,3,2,1,0:T(8,128)(2,1)S(1)}) custom-call(s32[3]{0:T(128)} %pad_add_fusion.3.picks_ref, ...), custom_call_target="tpu_custom_call", output_to_operand_aliasing={{1}: (12, {}), {3}: (15, {}), {4}: (16, {})} | custom-call | flops 146800640 | bytes 7536640 | tf_op jit(solution)/shard_map/while/body/eval_jaxpr/pallas_call | solution.py:229
  96.2 1.3 collective-permute-start
  97.5 6.1 %collective-permute-done = bf16[1,32,2560]{2,1,0:T(8,128)(2,1)S(1)} collective-permute-done((bf16[1,32,2560]{2,1,0:T(8,128)(2,1)}, bf16[1,32,2560]{2,1,0:T(8,128)(2,1)S(1)}, u32[]{:S(2)}, u32[]{:S(2)}) %collective-permute-start) | collective-permute-done | bytes 163872 | tf_op jit(solution)/shard_map/while/body/eval_jaxpr/ppermute | solution.py:20
  104.3 5.4 %eval_jaxpr.7 = (bf16[32,2560]{1,0:T(8,128)(2,1)}, f32[1,1,128,2560]{3,2,1,0:T(8,128)}, bf16[32,256]{1,0:T(8,128)(2,1)}, bf16[4,1,1,32,2560]{4,3,2,1,0:T(8,128)(2,1)}, bf16[4,1,1,32,256]{4,3,2,1,0:T(8,128)(2,1)S(1)}) custom-call(s32[3]{0:T(128)} %pad_add_fusion.3.picks_ref, ...), custom_call_target="tpu_custom_call", output_to_operand_aliasing={{1}: (12, {}), {3}: (15, {}), {4}: (16, {})} | custom-call | flops 146800640 | bytes 7536640 | tf_op jit(solution)/shard_map/while/body/eval_jaxpr/pallas_call | solution.py:229
  109.7 1.3 collective-permute-start
  111.0 6.1 %collective-permute-done = bf16[1,32,2560]{2,1,0:T(8,128)(2,1)S(1)} collective-permute-done((bf16[1,32,2560]{2,1,0:T(8,128)(2,1)}, bf16[1,32,2560]{2,1,0:T(8,128)(2,1)S(1)}, u32[]{:S(2)}, u32[]{:S(2)}) %collective-permute-start) | collective-permute-done | bytes 163872 | tf_op jit(solution)/shard_map/while/body/eval_jaxpr/ppermute | solution.py:20
  117.1 5.4 %shard_map.59 = (bf16[32,2560]{1,0:T(8,128)(2,1)}, f32[1,1,128,2560]{3,2,1,0:T(8,128)}, bf16[32,256]{1,0:T(8,128)(2,1)}, bf16[4,1,1,32,2560]{4,3,2,1,0:T(8,128)(2,1)}, bf16[4,1,1,32,256]{4,3,2,1,0:T(8,128)(2,1)S(1)}) custom-call(s32[3]{0:T(128)} %pad_add_fusion.1.picks_ref, ...), custom_call_target="tpu_custom_call", output_to_operand_aliasing={{1}: (12, {}), {3}: (15, {}), {4}: (16, {})} | custom-call | flops 146800640 | bytes 7536640 | tf_op jit(solution)/shard_map/pallas_call | solution.py:229
  122.5 9.8 %all_gather.3 = bf16[8,1,128,256]{3,2,1,0:T(8,128)(2,1)S(1)} all-gather(bf16[1,1,128,256]{3,2,1,0:T(8,128)(2,1)S(1)} %bitcast.113), channel_id=1, replica_groups=mesh['section'=4,'dp'=8] {'dp'}, dimensions={0}, use_global_device_ids=true | all-gather | bytes 589824 | tf_op jit(solution)/shard_map/all_gather | solution.py:349
  132.3 2.1 %fusion.8 = f32[1,320,256]{2,1,0:T(8,128)} fusion(bf16[8,1,128,320]{2,3,1,0:T(8,128)(2,1)} %all-to-all-done, bf16[8,1,128,256]{3,2,1,0:T(8,128)(2,1)S(1)} %all_gather.3), kind=kOutput, calls=%fused_computation.18 | convolution fusion | flops 167854080 | bytes 1507328 | tf_op jit(solution)/shard_map/glrd,glrc->ldc/dot_general | solution.py:350
  (57 shorter events, 14.9 us)
Async XLA Ops:
  0.6 7.4 %copy-start.9 = (f32[1,1,128,40]{2,3,1,0:T(8,128)S(1)}, f32[1,1,128,40]{2,3,1,0:T(8,128)}, u32[]{:S(2)}) copy-start(f32[1,1,128,40]{2,3,1,0:T(8,128)} %param.8) | copy-start | bytes 61444
  2.9 129.4 %all-to-all-start = ((bf16[8,1,128,320]{2,3,1,0:T(8,128)(2,1)}), bf16[8,1,128,320]{2,3,1,0:T(8,128)(2,1)}, u32[]{:S(2)}, u32[]{:S(2)}) async-start(bf16[8,1,128,320]{2,3,1,0:T(8,128)(2,1)} %bitcast.33), calls=%async_computation | async-start | bytes 1310720 | tf_op jit(solution)/shard_map/all_to_all | solution.py:347
  9.0 1.5 %copy-start.3 = (f32[4,32,40,64]{3,2,1,0:T(8,128)}, f32[4,32,40,64]{3,2,1,0:T(8,128)S(1)}, u32[]{:S(2)}) copy-start(f32[4,32,40,64]{3,2,1,0:T(8,128)S(1)} %broadcast_in_dim.106) | copy-start | bytes 3932164
  12.3 2.3 %copy-start.1 = (bf16[1,1,128,2560]{3,2,1,0:T(8,128)(2,1)S(1)}, bf16[1,1,128,2560]{3,2,1,0:T(8,128)(2,1)}, u32[]{:S(2)}) copy-start(bf16[1,1,128,2560]{3,2,1,0:T(8,128)(2,1)} %param.6) | copy-start | bytes 1966084
  12.3 2.3 %copy-start.2 = (bf16[1,2560,256]{2,1,0:T(8,128)(2,1)S(1)}, bf16[1,2560,256]{2,1,0:T(8,128)(2,1)}, u32[]{:S(2)}) copy-start(bf16[1,2560,256]{2,1,0:T(8,128)(2,1)} %w_ref.1) | copy-start | bytes 3932164
  14.5 11.8 %copy-start = (f32[4,1,1,32,2560]{4,3,2,1,0:T(8,128)}, f32[4,1,1,32,2560]{4,3,2,1,0:T(8,128)S(1)}, u32[]{:S(2)}) copy-start(f32[4,1,1,32,2560]{4,3,2,1,0:T(8,128)S(1)} %broadcast_in_dim.107.tail_ref) | copy-start | bytes 3932164
  19.8 5.5 %copy-start.4 = (f32[4,32,2560]{2,1,0:T(8,128)S(1)}, f32[4,32,2560]{2,1,0:T(8,128)}, u32[]{:S(2)}) copy-start(f32[4,32,2560]{2,1,0:T(8,128)} %mul.113) | copy-start | bytes 3932164
  26.3 1.0 copy-start.5
  27.2 1.9 %copy-start.6 = (f32[4,32,32]{2,1,0:T(8,128)S(1)}, f32[4,32,32]{2,1,0:T(8,128)}, u32[]{:S(2)}) copy-start(f32[4,32,32]{2,1,0:T(8,128)} %convolution_multiply_fusion) | copy-start | bytes 49156
  29.2 1.7 %copy-start.7 = (f32[2560]{0:T(1024)S(1)}, f32[2560]{0:T(1024)}, u32[]{:S(2)}) copy-start(f32[2560]{0:T(1024)} %mul.115) | copy-start | bytes 30724
  29.2 1.7 %copy-start.8 = (f32[2560]{0:T(1024)S(1)}, f32[2560]{0:T(1024)}, u32[]{:S(2)}) copy-start(f32[2560]{0:T(1024)} %mul.118) | copy-start | bytes 30724
  40.4 8.9 %collective-permute-start = (bf16[1,32,2560]{2,1,0:T(8,128)(2,1)}, bf16[1,32,2560]{2,1,0:T(8,128)(2,1)S(1)}, u32[]{:S(2)}, u32[]{:S(2)}) collective-permute-start(bf16[1,32,2560]{2,1,0:T(8,128)(2,1)} %bitcast.122), channel_id=1, source_target_pairs={{8,0},{16,8},{24,16},{9,1},{17,9},{25,17},{10,2},{18,10},{26,18},{... | collective-permute-start | bytes 491528 | tf_op jit(solution)/shard_map/while/body/eval_jaxpr/ppermute | solution.py:20
  55.3 8.0 %collective-permute-start = (bf16[1,32,2560]{2,1,0:T(8,128)(2,1)}, bf16[1,32,2560]{2,1,0:T(8,128)(2,1)S(1)}, u32[]{:S(2)}, u32[]{:S(2)}) collective-permute-start(bf16[1,32,2560]{2,1,0:T(8,128)(2,1)} %bitcast.122), channel_id=1, source_target_pairs={{8,0},{16,8},{24,16},{9,1},{17,9},{25,17},{10,2},{18,10},{26,18},{... | collective-permute-start | bytes 491528 | tf_op jit(solution)/shard_map/while/body/eval_jaxpr/ppermute | solution.py:20
  69.3 7.4 %collective-permute-start = (bf16[1,32,2560]{2,1,0:T(8,128)(2,1)}, bf16[1,32,2560]{2,1,0:T(8,128)(2,1)S(1)}, u32[]{:S(2)}, u32[]{:S(2)}) collective-permute-start(bf16[1,32,2560]{2,1,0:T(8,128)(2,1)} %bitcast.122), channel_id=1, source_target_pairs={{8,0},{16,8},{24,16},{9,1},{17,9},{25,17},{10,2},{18,10},{26,18},{... | collective-permute-start | bytes 491528 | tf_op jit(solution)/shard_map/while/body/eval_jaxpr/ppermute | solution.py:20
  82.8 7.4 %collective-permute-start = (bf16[1,32,2560]{2,1,0:T(8,128)(2,1)}, bf16[1,32,2560]{2,1,0:T(8,128)(2,1)S(1)}, u32[]{:S(2)}, u32[]{:S(2)}) collective-permute-start(bf16[1,32,2560]{2,1,0:T(8,128)(2,1)} %bitcast.122), channel_id=1, source_target_pairs={{8,0},{16,8},{24,16},{9,1},{17,9},{25,17},{10,2},{18,10},{26,18},{... | collective-permute-start | bytes 491528 | tf_op jit(solution)/shard_map/while/body/eval_jaxpr/ppermute | solution.py:20
  96.2 7.4 %collective-permute-start = (bf16[1,32,2560]{2,1,0:T(8,128)(2,1)}, bf16[1,32,2560]{2,1,0:T(8,128)(2,1)S(1)}, u32[]{:S(2)}, u32[]{:S(2)}) collective-permute-start(bf16[1,32,2560]{2,1,0:T(8,128)(2,1)} %bitcast.122), channel_id=1, source_target_pairs={{8,0},{16,8},{24,16},{9,1},{17,9},{25,17},{10,2},{18,10},{26,18},{... | collective-permute-start | bytes 491528 | tf_op jit(solution)/shard_map/while/body/eval_jaxpr/ppermute | solution.py:20
  109.7 7.4 %collective-permute-start = (bf16[1,32,2560]{2,1,0:T(8,128)(2,1)}, bf16[1,32,2560]{2,1,0:T(8,128)(2,1)S(1)}, u32[]{:S(2)}, u32[]{:S(2)}) collective-permute-start(bf16[1,32,2560]{2,1,0:T(8,128)(2,1)} %bitcast.122), channel_id=1, source_target_pairs={{8,0},{16,8},{24,16},{9,1},{17,9},{25,17},{10,2},{18,10},{26,18},{... | collective-permute-start | bytes 491528 | tf_op jit(solution)/shard_map/while/body/eval_jaxpr/ppermute | solution.py:20

commit v8 on v7

--- a/solution.py
+++ b/solution.py
@@ -283,10 +283,20 @@
     dec2 = jnp.moveaxis(consts["decays"], -1, -3).reshape(
         lead_dims + (pairs, per_pair * block_len, block_len)
     )
-    tail_full = jnp.repeat(consts["tail"], width, axis=-1)
-    lead_full = jnp.repeat(consts["lead"], width, axis=-1)
+    spread_heads = (
+        jnp.arange(features)[None, :] // width == jnp.arange(head_count)[:, None]
+    ).astype(jnp.float32)
+
+    def per_lane(a):
+        return jnp.einsum(
+            "...h,hd->...d", a, spread_heads, precision=lax.Precision.HIGHEST,
+            preferred_element_type=jnp.float32,
+        )
+
+    tail_full = per_lane(consts["tail"])
+    lead_full = per_lane(consts["lead"])
     xt_full = consts["tail_inputs"].reshape(lead_dims + (block_len, features))
-    end_row = jnp.repeat(consts["ending"], width, axis=-1)[..., None, :]
+    end_row = per_lane(consts["ending"])[..., None, :]
     fresh_t = jnp.einsum(
         "mlsjn,mlsjd->mlsnd", in_blk, xt_full, preferred_element_type=jnp.float32
     )

time: 135 us -> 127 us (0.941)
  local copies, waits for them, and re-layouts: 20.4 us -> 9.78 us
  matrix products: 4.13 us -> 7.22 us
    broadcast_in_dim x9 -> x1, local copies, waits for them, and re-layouts: 9.77 us -> 0.03 us  [shards(): end_row = per_lane(consts['ending'])[..., None, :]]
    dot_general x0 -> x3, matrix products: none -> 3.72 us  [per_lane(): jnp.einsum('...h,hd->...d', a, spread_heads, precision=lax.Precision.HIGH...]
    mul x1 -> x3, local copies, waits for them, and re-layouts: 1.71 us -> 4.08 us  [block_consts(): tail_decay[:, :, None] * inputs_b.astype(jnp.float32)]
    mul x3 -> x0, local copies, waits for them, and re-layouts: 1.42 us -> none  [shards(): state_now = end_row[block_no] * state_now + fresh_t[block_no]]
    unnamed x21 -> x11, local copies, waits for them, and re-layouts: 3.81 us -> 2.65 us
  transfers between devices with their start and end apart: 7 -> 7, of which waited for: 6 -> 6; matrix products, arithmetic and copies ran while one was open for 21% -> 17% of each run, Pallas kernels for 28% -> 30%
where the time goes in v8:
time: 127 us
  waiting for transfers between devices  38.8 us (31%)
  Pallas kernels  37.6 us (30%)
  starting transfers between devices  12.9 us (10%)
  other arithmetic  9.98 us (8%)
  blocking collectives  9.79 us (8%)
  local copies, waits for them, and re-layouts  9.78 us (8%)
  matrix products  7.22 us (6%)
    ppermute x6, waiting for transfers between devices, passed_along(): return lax.ppermute(block, axis, route)  38.8 us
    pallas_call x7, Pallas kernels, fused_step(): pl.pallas_call(functools.partial(step_kernel, factor=factor, width=width)...  37.6 us
    all_gather x1, blocking collectives, shards(): maps_all = lax.all_gather(maps_here, 'dp', axis=0, tiled=True)  9.79 us
    ppermute x6, starting transfers between devices, passed_along(): return lax.ppermute(block, axis, route)  7.68 us
    all_to_all x1, starting transfers between devices, shards(): rows_all = lax.all_to_all(rows_here, 'dp', 0, 0, tiled=True)  5.17 us
    another operation x7, other arithmetic, advance(): jnp.stack([block_no, is_top.astype(jnp.int32), is_valid.astype(jnp.int32)])  4.45 us
    mul x3, local copies, waits for them, and re-layouts, block_consts(): tail_decay[:, :, None] * inputs_b.astype(jnp.float32)  4.08 us
    dot_general x3, matrix products, per_lane(): jnp.einsum('...h,hd->...d', a, spread_heads, precision=lax.Precision.HIGH...  3.72 us
  transfers between devices with their start and end apart: 7, of which 6 were waited for; matrix products, arithmetic and copies ran while one was open for 17% of the time, Pallas kernels for 30%

profile of v8, /device:TPU:0, one launch (start us, length us, event | category | flops | bytes accessed | tf_op | source)
XLA Modules:
  0.0 127.0 jit_solution(635162003591354820)
XLA Ops:
  0.6 2.2 %copy.31 = bf16[1,1,128,2560]{2,3,1,0:T(8,128)(2,1)} copy(bf16[1,1,128,2560]{3,2,1,0:T(8,128)(2,1)} %param.6) | data formatting | bytes 1310720 | tf_op args[0]
  2.9 5.2 %all-to-all-start = ((bf16[8,1,128,320]{2,3,1,0:T(8,128)(2,1)}), bf16[8,1,128,320]{2,3,1,0:T(8,128)(2,1)}, u32[]{:S(2)}, u32[]{:S(2)}) async-start(bf16[8,1,128,320]{2,3,1,0:T(8,128)(2,1)} %bitcast.33), calls=%async_computation | async-start | bytes 1310720 | tf_op jit(solution)/shard_map/all_to_all | solution.py:357
  9.0 1.7 %mul.114 = f32[4,32,2560]{2,1,0:T(8,128)} reshape(f32[4,32,40,64]{3,2,1,0:T(8,128)S(1)} %mul.108) | data formatting | bytes 2621440 | tf_op jit(solution)/shard_map/vmap(vmap(vmap()))/mul | solution.py:129
  10.7 1.7 %mul.109 = f32[4,1,1,32,2560]{4,3,2,1,0:T(8,128)} reshape(f32[4,32,40,64]{3,2,1,0:T(8,128)S(1)} %mul.108) | data formatting | bytes 2621440 | tf_op jit(solution)/shard_map/vmap(vmap(vmap()))/mul | solution.py:129
  12.6 1.7 %convolution_bitcast_fusion.1.tail_ref = f32[4,1,1,32,2560]{4,3,2,1,0:T(8,128)} fusion(f32[4,32,40]{2,1,0:T(8,128)S(1)} %subtract_exponential_fusion, s32[2560]{0:T(1024)S(1)} %add_select_fusion), kind=kOutput, calls=%fused_computation.2 | convolution fusion | flops 157388800 | bytes 1341440 | tf_op jit(solution)/shard_map/...h,hd->...d/dot_general | solution.py:291
  14.5 1.7 %convolution_bitcast_fusion.lead_ref = f32[4,1,1,32,2560]{4,3,2,1,0:T(8,128)} fusion(s32[2560]{0:T(1024)S(1)} %add_select_fusion, f32[4,1,1,32,40]{4,3,2,1,0:T(8,128)S(1)} %reduce_window_sum.11), kind=kOutput, calls=%fused_computation.1 | convolution fusion | flops 157388800 | bytes 1341440 | tf_op jit(solution)/shard_map/...h,hd->...d/dot_general | solution.py:291
  18.9 1.0 multiply_convert_fusion.1.xt_ref
  19.9 1.9 %exponential_select_fusion = f32[4,1,1,32,32,40]{4,3,5,0,2,1:T(8,128)} fusion(f32[4,32,40]{1,2,0:T(8,128)S(1)} %copy.29, pred[32,32]{1,0:T(8,128)(4,1)S(1)} %iota_compare_fusion.2), kind=kLoop, calls=%fused_computation.4 | loop fusion | flops 491520 | bytes 676864 | tf_op jit(solution)/shard_map/vmap(vmap(vmap(jit(_where))))/select_n | solution.py:119
  21.8 1.7 %multiply_convert_fusion.wt_ref = bf16[4,1,1,40,32,32]{5,4,3,2,1,0:T(8,128)(2,1)} fusion(f32[4,32,32]{2,1,0:T(8,128)S(1)} %convolution_multiply_fusion, f32[4,40,32]{2,1,0:T(8,128)S(1)} %copy.27, pred[32,32]{1,0:T(8,128)(4,1)S(1)} %iota_compare_fusion.3), kind=kLoop, calls=%fused_computation.5 | loop fusion | flops 819200 | bytes 365568 | tf_op jit(solution)/shard_map/vmap(vmap(vmap()))/convert_element_type | solution.py:128
  24.8 1.2 broadcast.343
  26.9 82.7 %while.21 = (s32[]{:T(128)}, bf16[1,32,2560]{2,1,0:T(8,128)(2,1)S(1)}, f32[1,1,128,2560]{3,2,1,0:T(8,128)}, bf16[4,1,1,32,2560]{4,3,2,1,0:T(8,128)(2,1)}, bf16[4...) while((s32[]{:T(128)}, ...), condition=%wide.region_2.3_spmd, body=%wide.region_1.2_spmd.sunk | while | flops 146800656 | bytes 8192348 | solution.py:346
  27.6 5.4 %eval_jaxpr.7 = (bf16[32,2560]{1,0:T(8,128)(2,1)}, f32[1,1,128,2560]{3,2,1,0:T(8,128)}, bf16[32,256]{1,0:T(8,128)(2,1)}, bf16[4,1,1,32,2560]{4,3,2,1,0:T(8,128)(2,1)}, bf16[4,1,1,32,256]{4,3,2,1,0:T(8,128)(2,1)S(1)}) custom-call(s32[3]{0:T(128)} %pad_add_fusion.3.picks_ref, ...), custom_call_target="tpu_custom_call", output_to_operand_aliasing={{1}: (12, {}), {3}: (15, {}), {4}: (16, {})} | custom-call | flops 146800640 | bytes 7536640 | tf_op jit(solution)/shard_map/while/body/eval_jaxpr/pallas_call | solution.py:229
  33.0 1.3 %collective-permute-start = (bf16[1,32,2560]{2,1,0:T(8,128)(2,1)}, bf16[1,32,2560]{2,1,0:T(8,128)(2,1)S(1)}, u32[]{:S(2)}, u32[]{:S(2)}) collective-permute-start(bf16[1,32,2560]{2,1,0:T(8,128)(2,1)} %bitcast.126), channel_id=1, source_target_pairs={{8,0},{16,8},{24,16},{9,1},{17,9},{25,17},{10,2},{18,10},{26,18},{... | collective-permute-start | bytes 491528 | tf_op jit(solution)/shard_map/while/body/eval_jaxpr/ppermute | solution.py:20
  34.3 7.6 %collective-permute-done = bf16[1,32,2560]{2,1,0:T(8,128)(2,1)S(1)} collective-permute-done((bf16[1,32,2560]{2,1,0:T(8,128)(2,1)}, bf16[1,32,2560]{2,1,0:T(8,128)(2,1)S(1)}, u32[]{:S(2)}, u32[]{:S(2)}) %collective-permute-start) | collective-permute-done | bytes 163872 | tf_op jit(solution)/shard_map/while/body/eval_jaxpr/ppermute | solution.py:20
  42.5 5.4 %eval_jaxpr.7 = (bf16[32,2560]{1,0:T(8,128)(2,1)}, f32[1,1,128,2560]{3,2,1,0:T(8,128)}, bf16[32,256]{1,0:T(8,128)(2,1)}, bf16[4,1,1,32,2560]{4,3,2,1,0:T(8,128)(2,1)}, bf16[4,1,1,32,256]{4,3,2,1,0:T(8,128)(2,1)S(1)}) custom-call(s32[3]{0:T(128)} %pad_add_fusion.3.picks_ref, ...), custom_call_target="tpu_custom_call", output_to_operand_aliasing={{1}: (12, {}), {3}: (15, {}), {4}: (16, {})} | custom-call | flops 146800640 | bytes 7536640 | tf_op jit(solution)/shard_map/while/body/eval_jaxpr/pallas_call | solution.py:229
  47.9 1.3 %collective-permute-start = (bf16[1,32,2560]{2,1,0:T(8,128)(2,1)}, bf16[1,32,2560]{2,1,0:T(8,128)(2,1)S(1)}, u32[]{:S(2)}, u32[]{:S(2)}) collective-permute-start(bf16[1,32,2560]{2,1,0:T(8,128)(2,1)} %bitcast.126), channel_id=1, source_target_pairs={{8,0},{16,8},{24,16},{9,1},{17,9},{25,17},{10,2},{18,10},{26,18},{... | collective-permute-start | bytes 491528 | tf_op jit(solution)/shard_map/while/body/eval_jaxpr/ppermute | solution.py:20
  49.2 6.7 %collective-permute-done = bf16[1,32,2560]{2,1,0:T(8,128)(2,1)S(1)} collective-permute-done((bf16[1,32,2560]{2,1,0:T(8,128)(2,1)}, bf16[1,32,2560]{2,1,0:T(8,128)(2,1)S(1)}, u32[]{:S(2)}, u32[]{:S(2)}) %collective-permute-start) | collective-permute-done | bytes 163872 | tf_op jit(solution)/shard_map/while/body/eval_jaxpr/ppermute | solution.py:20
  56.5 5.4 %eval_jaxpr.7 = (bf16[32,2560]{1,0:T(8,128)(2,1)}, f32[1,1,128,2560]{3,2,1,0:T(8,128)}, bf16[32,256]{1,0:T(8,128)(2,1)}, bf16[4,1,1,32,2560]{4,3,2,1,0:T(8,128)(2,1)}, bf16[4,1,1,32,256]{4,3,2,1,0:T(8,128)(2,1)S(1)}) custom-call(s32[3]{0:T(128)} %pad_add_fusion.3.picks_ref, ...), custom_call_target="tpu_custom_call", output_to_operand_aliasing={{1}: (12, {}), {3}: (15, {}), {4}: (16, {})} | custom-call | flops 146800640 | bytes 7536640 | tf_op jit(solution)/shard_map/while/body/eval_jaxpr/pallas_call | solution.py:229
  61.9 1.3 %collective-permute-start = (bf16[1,32,2560]{2,1,0:T(8,128)(2,1)}, bf16[1,32,2560]{2,1,0:T(8,128)(2,1)S(1)}, u32[]{:S(2)}, u32[]{:S(2)}) collective-permute-start(bf16[1,32,2560]{2,1,0:T(8,128)(2,1)} %bitcast.126), channel_id=1, source_target_pairs={{8,0},{16,8},{24,16},{9,1},{17,9},{25,17},{10,2},{18,10},{26,18},{... | collective-permute-start | bytes 491528 | tf_op jit(solution)/shard_map/while/body/eval_jaxpr/ppermute | solution.py:20
  63.2 6.1 %collective-permute-done = bf16[1,32,2560]{2,1,0:T(8,128)(2,1)S(1)} collective-permute-done((bf16[1,32,2560]{2,1,0:T(8,128)(2,1)}, bf16[1,32,2560]{2,1,0:T(8,128)(2,1)S(1)}, u32[]{:S(2)}, u32[]{:S(2)}) %collective-permute-start) | collective-permute-done | bytes 163872 | tf_op jit(solution)/shard_map/while/body/eval_jaxpr/ppermute | solution.py:20
  70.0 5.4 %eval_jaxpr.7 = (bf16[32,2560]{1,0:T(8,128)(2,1)}, f32[1,1,128,2560]{3,2,1,0:T(8,128)}, bf16[32,256]{1,0:T(8,128)(2,1)}, bf16[4,1,1,32,2560]{4,3,2,1,0:T(8,128)(2,1)}, bf16[4,1,1,32,256]{4,3,2,1,0:T(8,128)(2,1)S(1)}) custom-call(s32[3]{0:T(128)} %pad_add_fusion.3.picks_ref, ...), custom_call_target="tpu_custom_call", output_to_operand_aliasing={{1}: (12, {}), {3}: (15, {}), {4}: (16, {})} | custom-call | flops 146800640 | bytes 7536640 | tf_op jit(solution)/shard_map/while/body/eval_jaxpr/pallas_call | solution.py:229
  75.3 1.3 %collective-permute-start = (bf16[1,32,2560]{2,1,0:T(8,128)(2,1)}, bf16[1,32,2560]{2,1,0:T(8,128)(2,1)S(1)}, u32[]{:S(2)}, u32[]{:S(2)}) collective-permute-start(bf16[1,32,2560]{2,1,0:T(8,128)(2,1)} %bitcast.126), channel_id=1, source_target_pairs={{8,0},{16,8},{24,16},{9,1},{17,9},{25,17},{10,2},{18,10},{26,18},{... | collective-permute-start | bytes 491528 | tf_op jit(solution)/shard_map/while/body/eval_jaxpr/ppermute | solution.py:20
  76.6 6.1 %collective-permute-done = bf16[1,32,2560]{2,1,0:T(8,128)(2,1)S(1)} collective-permute-done((bf16[1,32,2560]{2,1,0:T(8,128)(2,1)}, bf16[1,32,2560]{2,1,0:T(8,128)(2,1)S(1)}, u32[]{:S(2)}, u32[]{:S(2)}) %collective-permute-start) | collective-permute-done | bytes 163872 | tf_op jit(solution)/shard_map/while/body/eval_jaxpr/ppermute | solution.py:20
  83.4 5.4 %eval_jaxpr.7 = (bf16[32,2560]{1,0:T(8,128)(2,1)}, f32[1,1,128,2560]{3,2,1,0:T(8,128)}, bf16[32,256]{1,0:T(8,128)(2,1)}, bf16[4,1,1,32,2560]{4,3,2,1,0:T(8,128)(2,1)}, bf16[4,1,1,32,256]{4,3,2,1,0:T(8,128)(2,1)S(1)}) custom-call(s32[3]{0:T(128)} %pad_add_fusion.3.picks_ref, ...), custom_call_target="tpu_custom_call", output_to_operand_aliasing={{1}: (12, {}), {3}: (15, {}), {4}: (16, {})} | custom-call | flops 146800640 | bytes 7536640 | tf_op jit(solution)/shard_map/while/body/eval_jaxpr/pallas_call | solution.py:229
  88.8 1.3 %collective-permute-start = (bf16[1,32,2560]{2,1,0:T(8,128)(2,1)}, bf16[1,32,2560]{2,1,0:T(8,128)(2,1)S(1)}, u32[]{:S(2)}, u32[]{:S(2)}) collective-permute-start(bf16[1,32,2560]{2,1,0:T(8,128)(2,1)} %bitcast.126), channel_id=1, source_target_pairs={{8,0},{16,8},{24,16},{9,1},{17,9},{25,17},{10,2},{18,10},{26,18},{... | collective-permute-start | bytes 491528 | tf_op jit(solution)/shard_map/while/body/eval_jaxpr/ppermute | solution.py:20
  90.1 6.1 %collective-permute-done = bf16[1,32,2560]{2,1,0:T(8,128)(2,1)S(1)} collective-permute-done((bf16[1,32,2560]{2,1,0:T(8,128)(2,1)}, bf16[1,32,2560]{2,1,0:T(8,128)(2,1)S(1)}, u32[]{:S(2)}, u32[]{:S(2)}) %collective-permute-start) | collective-permute-done | bytes 163872 | tf_op jit(solution)/shard_map/while/body/eval_jaxpr/ppermute | solution.py:20
  96.8 5.4 %eval_jaxpr.7 = (bf16[32,2560]{1,0:T(8,128)(2,1)}, f32[1,1,128,2560]{3,2,1,0:T(8,128)}, bf16[32,256]{1,0:T(8,128)(2,1)}, bf16[4,1,1,32,2560]{4,3,2,1,0:T(8,128)(2,1)}, bf16[4,1,1,32,256]{4,3,2,1,0:T(8,128)(2,1)S(1)}) custom-call(s32[3]{0:T(128)} %pad_add_fusion.3.picks_ref, ...), custom_call_target="tpu_custom_call", output_to_operand_aliasing={{1}: (12, {}), {3}: (15, {}), {4}: (16, {})} | custom-call | flops 146800640 | bytes 7536640 | tf_op jit(solution)/shard_map/while/body/eval_jaxpr/pallas_call | solution.py:229
  102.2 1.3 %collective-permute-start = (bf16[1,32,2560]{2,1,0:T(8,128)(2,1)}, bf16[1,32,2560]{2,1,0:T(8,128)(2,1)S(1)}, u32[]{:S(2)}, u32[]{:S(2)}) collective-permute-start(bf16[1,32,2560]{2,1,0:T(8,128)(2,1)} %bitcast.126), channel_id=1, source_target_pairs={{8,0},{16,8},{24,16},{9,1},{17,9},{25,17},{10,2},{18,10},{26,18},{... | collective-permute-start | bytes 491528 | tf_op jit(solution)/shard_map/while/body/eval_jaxpr/ppermute | solution.py:20
  103.5 6.1 %collective-permute-done = bf16[1,32,2560]{2,1,0:T(8,128)(2,1)S(1)} collective-permute-done((bf16[1,32,2560]{2,1,0:T(8,128)(2,1)}, bf16[1,32,2560]{2,1,0:T(8,128)(2,1)S(1)}, u32[]{:S(2)}, u32[]{:S(2)}) %collective-permute-start) | collective-permute-done | bytes 163872 | tf_op jit(solution)/shard_map/while/body/eval_jaxpr/ppermute | solution.py:20
  109.6 5.4 %shard_map.59 = (bf16[32,2560]{1,0:T(8,128)(2,1)}, f32[1,1,128,2560]{3,2,1,0:T(8,128)}, bf16[32,256]{1,0:T(8,128)(2,1)}, bf16[4,1,1,32,2560]{4,3,2,1,0:T(8,128)(2,1)}, bf16[4,1,1,32,256]{4,3,2,1,0:T(8,128)(2,1)S(1)}) custom-call(s32[3]{0:T(128)} %pad_add_fusion.1.picks_ref, ...), custom_call_target="tpu_custom_call", output_to_operand_aliasing={{1}: (12, {}), {3}: (15, {}), {4}: (16, {})} | custom-call | flops 146800640 | bytes 7536640 | tf_op jit(solution)/shard_map/pallas_call | solution.py:229
  115.0 9.8 %all_gather.3 = bf16[8,1,128,256]{3,2,1,0:T(8,128)(2,1)S(1)} all-gather(bf16[1,1,128,256]{3,2,1,0:T(8,128)(2,1)S(1)} %bitcast.117), channel_id=1, replica_groups=mesh['section'=4,'dp'=8] {'dp'}, dimensions={0}, use_global_device_ids=true | all-gather | bytes 589824 | tf_op jit(solution)/shard_map/all_gather | solution.py:359
  124.8 2.1 %fusion.8 = f32[1,320,256]{2,1,0:T(8,128)} fusion(bf16[8,1,128,320]{2,3,1,0:T(8,128)(2,1)} %all-to-all-done, bf16[8,1,128,256]{3,2,1,0:T(8,128)(2,1)S(1)} %all_gather.3), kind=kOutput, calls=%fused_computation.20 | convolution fusion | flops 167854080 | bytes 1507328 | tf_op jit(solution)/shard_map/glrd,glrc->ldc/dot_general | solution.py:360
  (41 shorter events, 9.9 us)
Async XLA Ops:
  0.6 7.4 %copy-start.4 = (f32[1,1,128,40]{2,3,1,0:T(8,128)S(1)}, f32[1,1,128,40]{2,3,1,0:T(8,128)}, u32[]{:S(2)}) copy-start(f32[1,1,128,40]{2,3,1,0:T(8,128)} %param.8) | copy-start | bytes 61444
  2.9 121.9 %all-to-all-start = ((bf16[8,1,128,320]{2,3,1,0:T(8,128)(2,1)}), bf16[8,1,128,320]{2,3,1,0:T(8,128)(2,1)}, u32[]{:S(2)}, u32[]{:S(2)}) async-start(bf16[8,1,128,320]{2,3,1,0:T(8,128)(2,1)} %bitcast.33), calls=%async_computation | async-start | bytes 1310720 | tf_op jit(solution)/shard_map/all_to_all | solution.py:357
  12.6 3.7 %copy-start = (bf16[1,1,128,2560]{3,2,1,0:T(8,128)(2,1)S(1)}, bf16[1,1,128,2560]{3,2,1,0:T(8,128)(2,1)}, u32[]{:S(2)}) copy-start(bf16[1,1,128,2560]{3,2,1,0:T(8,128)(2,1)} %param.6) | copy-start | bytes 1966084
  12.6 3.7 %copy-start.1 = (bf16[1,2560,256]{2,1,0:T(8,128)(2,1)S(1)}, bf16[1,2560,256]{2,1,0:T(8,128)(2,1)}, u32[]{:S(2)}) copy-start(bf16[1,2560,256]{2,1,0:T(8,128)(2,1)} %w_ref.1) | copy-start | bytes 3932164
  16.2 1.3 %copy-start.2 = (f32[4,32,2560]{2,1,0:T(8,128)S(1)}, f32[4,32,2560]{2,1,0:T(8,128)}, u32[]{:S(2)}) copy-start(f32[4,32,2560]{2,1,0:T(8,128)} %mul.114) | copy-start | bytes 3932164
  17.6 1.3 %copy-start.3 = (f32[4,1,1,32,2560]{4,3,2,1,0:T(8,128)S(1)}, f32[4,1,1,32,2560]{4,3,2,1,0:T(8,128)}, u32[]{:S(2)}) copy-start(f32[4,1,1,32,2560]{4,3,2,1,0:T(8,128)} %mul.109) | copy-start | bytes 3932164
  33.0 8.9 %collective-permute-start = (bf16[1,32,2560]{2,1,0:T(8,128)(2,1)}, bf16[1,32,2560]{2,1,0:T(8,128)(2,1)S(1)}, u32[]{:S(2)}, u32[]{:S(2)}) collective-permute-start(bf16[1,32,2560]{2,1,0:T(8,128)(2,1)} %bitcast.126), channel_id=1, source_target_pairs={{8,0},{16,8},{24,16},{9,1},{17,9},{25,17},{10,2},{18,10},{26,18},{... | collective-permute-start | bytes 491528 | tf_op jit(solution)/shard_map/while/body/eval_jaxpr/ppermute | solution.py:20
  47.9 8.0 %collective-permute-start = (bf16[1,32,2560]{2,1,0:T(8,128)(2,1)}, bf16[1,32,2560]{2,1,0:T(8,128)(2,1)S(1)}, u32[]{:S(2)}, u32[]{:S(2)}) collective-permute-start(bf16[1,32,2560]{2,1,0:T(8,128)(2,1)} %bitcast.126), channel_id=1, source_target_pairs={{8,0},{16,8},{24,16},{9,1},{17,9},{25,17},{10,2},{18,10},{26,18},{... | collective-permute-start | bytes 491528 | tf_op jit(solution)/shard_map/while/body/eval_jaxpr/ppermute | solution.py:20
  61.9 7.4 %collective-permute-start = (bf16[1,32,2560]{2,1,0:T(8,128)(2,1)}, bf16[1,32,2560]{2,1,0:T(8,128)(2,1)S(1)}, u32[]{:S(2)}, u32[]{:S(2)}) collective-permute-start(bf16[1,32,2560]{2,1,0:T(8,128)(2,1)} %bitcast.126), channel_id=1, source_target_pairs={{8,0},{16,8},{24,16},{9,1},{17,9},{25,17},{10,2},{18,10},{26,18},{... | collective-permute-start | bytes 491528 | tf_op jit(solution)/shard_map/while/body/eval_jaxpr/ppermute | solution.py:20
  75.3 7.4 %collective-permute-start = (bf16[1,32,2560]{2,1,0:T(8,128)(2,1)}, bf16[1,32,2560]{2,1,0:T(8,128)(2,1)S(1)}, u32[]{:S(2)}, u32[]{:S(2)}) collective-permute-start(bf16[1,32,2560]{2,1,0:T(8,128)(2,1)} %bitcast.126), channel_id=1, source_target_pairs={{8,0},{16,8},{24,16},{9,1},{17,9},{25,17},{10,2},{18,10},{26,18},{... | collective-permute-start | bytes 491528 | tf_op jit(solution)/shard_map/while/body/eval_jaxpr/ppermute | solution.py:20
  88.8 7.4 %collective-permute-start = (bf16[1,32,2560]{2,1,0:T(8,128)(2,1)}, bf16[1,32,2560]{2,1,0:T(8,128)(2,1)S(1)}, u32[]{:S(2)}, u32[]{:S(2)}) collective-permute-start(bf16[1,32,2560]{2,1,0:T(8,128)(2,1)} %bitcast.126), channel_id=1, source_target_pairs={{8,0},{16,8},{24,16},{9,1},{17,9},{25,17},{10,2},{18,10},{26,18},{... | collective-permute-start | bytes 491528 | tf_op jit(solution)/shard_map/while/body/eval_jaxpr/ppermute | solution.py:20
  102.2 7.4 %collective-permute-start = (bf16[1,32,2560]{2,1,0:T(8,128)(2,1)}, bf16[1,32,2560]{2,1,0:T(8,128)(2,1)S(1)}, u32[]{:S(2)}, u32[]{:S(2)}) collective-permute-start(bf16[1,32,2560]{2,1,0:T(8,128)(2,1)} %bitcast.126), channel_id=1, source_target_pairs={{8,0},{16,8},{24,16},{9,1},{17,9},{25,17},{10,2},{18,10},{26,18},{... | collective-permute-start | bytes 491528 | tf_op jit(solution)/shard_map/while/body/eval_jaxpr/ppermute | solution.py:20

commit v9 on v8

--- a/solution.py
+++ b/solution.py
@@ -138,10 +138,11 @@
 
 
 def step_kernel(
-    picks_ref, wt_ref, dec_ref, inc_ref, top_ref, x_ref, b_ref, c_ref, tail_ref, lead_ref, xt_ref,
+    step_ref, tab_ref, wt_ref, dec_ref, inc_ref, top_ref, x_ref, b_ref, c_ref, tail_ref, lead_ref, xt_ref,
     sb_ref, r_ref, end_ref, w_ref, gs_ref, ms_ref, out_ref, rnew_ref, dbc_ref, gstore_ref, mstore_ref,
-    v_ref, gx_ref, *, factor, width
+    v_ref, gx_ref, *, factor, width, level_pos, levels
 ):
+    base = (step_ref[0] * levels + level_pos) * 3
     f32 = jnp.float32
     bf16 = jnp.bfloat16
     length, features = v_ref.shape
@@ -149,7 +150,7 @@
     per_pair = lanes // width
     nt = (((1,), (1,)), ((), ()))
     tn = (((0,), (0,)), ((), ()))
-    v_ref[...] = jnp.where(picks_ref[1] > 0, top_ref[...], inc_ref[...])
+    v_ref[...] = jnp.where(tab_ref[base + 1] > 0, top_ref[...], inc_ref[...])
     rb_t = r_ref[...].astype(bf16)
     in_map = b_ref[...]
     out_map = c_ref[...]
@@ -190,14 +191,14 @@
     rnew_ref[...] = carry + end_ref[...] * r_ref[...]
     grad_bc = jnp.concatenate([grad_inmap, grad_outmap], axis=1).astype(bf16)
     dbc_ref[...] = grad_bc
-    mstore_ref[...] = jnp.where(picks_ref[2] > 0, grad_bc, ms_ref[...])
+    mstore_ref[...] = jnp.where(tab_ref[base + 2] > 0, grad_bc, ms_ref[...])
     back = lax.dot_general(grad_bc, w_ref[...], nt, preferred_element_type=f32)
     summed = (v.astype(f32) + gx_ref[...] + back).astype(out_ref.dtype)
     out_ref[...] = summed
-    gstore_ref[...] = jnp.where(picks_ref[2] > 0, summed, gs_ref[...])
-
-
-def fused_step(picks, per_block, incoming, top_blk, carried, w_bc, grad_store, map_store, level_no, seq_no, factor, width):
+    gstore_ref[...] = jnp.where(tab_ref[base + 2] > 0, summed, gs_ref[...])
+
+
+def fused_step(step_arr, table, level_pos, levels, per_block, incoming, top_blk, carried, w_bc, grad_store, map_store, level_no, seq_no, factor, width):
     wt2, dec2, x_flat, in_blk, out_blk, tail_full, lead_full, xt_full, states_t, end_row = per_block
     length, features = incoming.shape[1:]
     state_size = in_blk.shape[-1]
@@ -205,29 +206,31 @@
     def lead_block(a):
         shape = (None, None, None) + a.shape[3:]
         tail = (0,) * (a.ndim - 3)
-        return pl.BlockSpec(shape, lambda i, p: (p[0], level_no, seq_no) + tail)
+        return pl.BlockSpec(shape, lambda i, c, t: (t[(c[0] * levels + level_pos) * 3], level_no, seq_no) + tail)
 
     in_specs = [lead_block(a) for a in (wt2, dec2)]
-    in_specs.append(pl.BlockSpec((None, length, features), lambda i, p: (seq_no, 0, 0)))
-    in_specs.append(pl.BlockSpec((None, None, length, features), lambda i, p: (p[0], seq_no, 0, 0)))
+    in_specs.append(pl.BlockSpec((None, length, features), lambda i, c, t: (seq_no, 0, 0)))
+    in_specs.append(pl.BlockSpec((None, None, length, features), lambda i, c, t: (t[(c[0] * levels + level_pos) * 3], seq_no, 0, 0)))
     in_specs += [lead_block(a) for a in (x_flat, in_blk, out_blk, tail_full, lead_full, xt_full, states_t)]
-    in_specs.append(pl.BlockSpec((None, None) + carried.shape[2:], lambda i, p: (level_no, seq_no, 0, 0)))
+    in_specs.append(pl.BlockSpec((None, None) + carried.shape[2:], lambda i, c, t: (level_no, seq_no, 0, 0)))
     in_specs.append(lead_block(end_row))
-    in_specs.append(pl.BlockSpec((None,) + w_bc.shape[1:], lambda i, p: (level_no, 0, 0)))
-    store_g = pl.BlockSpec((None, None, None, length, features), lambda i, p: (p[0], level_no, seq_no, 0, 0))
-    store_m = pl.BlockSpec((None, None, None, length, 2 * state_size), lambda i, p: (p[0], level_no, seq_no, 0, 0))
+    in_specs.append(pl.BlockSpec((None,) + w_bc.shape[1:], lambda i, c, t: (level_no, 0, 0)))
+    store_g = pl.BlockSpec((None, None, None, length, features), lambda i, c, t: (t[(c[0] * levels + level_pos) * 3], level_no, seq_no, 0, 0))
+    store_m = pl.BlockSpec((None, None, None, length, 2 * state_size), lambda i, c, t: (t[(c[0] * levels + level_pos) * 3], level_no, seq_no, 0, 0))
     in_specs += [store_g, store_m]
     out_specs = (
-        pl.BlockSpec((length, features), lambda i, p: (0, 0)),
-        pl.BlockSpec((None, None) + carried.shape[2:], lambda i, p: (level_no, seq_no, 0, 0)),
-        pl.BlockSpec((length, 2 * state_size), lambda i, p: (0, 0)),
+        pl.BlockSpec((length, features), lambda i, c, t: (0, 0)),
+        pl.BlockSpec((None, None) + carried.shape[2:], lambda i, c, t: (level_no, seq_no, 0, 0)),
+        pl.BlockSpec((length, 2 * state_size), lambda i, c, t: (0, 0)),
         store_g,
         store_m,
     )
     flops = 2 * length * features * (6 * state_size + 4 * length)
     moved = 2 * (4 * features * state_size * 2 + 6 * length * features) + 4 * 4 * length * features
     return pl.pallas_call(
-        functools.partial(step_kernel, factor=factor, width=width),
+        functools.partial(
+            step_kernel, factor=factor, width=width, level_pos=level_pos, levels=levels
+        ),
         out_shape=(
             jax.ShapeDtypeStruct((length, features), jnp.bfloat16),
             jax.ShapeDtypeStruct(carried.shape, jnp.float32),
@@ -236,7 +239,7 @@
             jax.ShapeDtypeStruct(map_store.shape, map_store.dtype),
         ),
         grid_spec=pltpu.PrefetchScalarGridSpec(
-            num_scalar_prefetch=1,
+            num_scalar_prefetch=2,
             grid=(1,),
             in_specs=in_specs,
             out_specs=out_specs,
@@ -245,9 +248,9 @@
                 pltpu.VMEM((length, features), jnp.float32),
             ],
         ),
-        input_output_aliases={12: 1, 15: 3, 16: 4},
+        input_output_aliases={13: 1, 16: 3, 17: 4},
         cost_estimate=pl.CostEstimate(flops=flops, bytes_accessed=moved, transcendentals=0),
-    )(picks, wt2, dec2, incoming, top_blk, x_flat, in_blk, out_blk, tail_full, lead_full, xt_full, states_t, carried, end_row, w_bc, grad_store, map_store)
+    )(step_arr, table, wt2, dec2, incoming, top_blk, x_flat, in_blk, out_blk, tail_full, lead_full, xt_full, states_t, carried, end_row, w_bc, grad_store, map_store)
 
 
 def shards(layer_inputs, w_bc, log_decay, top_grad):
@@ -315,23 +318,28 @@
     )
     is_top = section_id == sections - 1
 
+    steps = MICRO + sections - 1
+    counters = jnp.arange(steps, dtype=jnp.int32)[:, None]
+    offsets = counters - (sections - 1 - section_id)
+    valid_tab = ((offsets >= 0) & (offsets < MICRO)).astype(jnp.int32)
+    block_tab = jnp.clip(MICRO - 1 - offsets, 0, MICRO - 1).astype(jnp.int32)
+    top_tab = (jnp.arange(lay_dev)[None, ::-1] == lay_dev - 1) & is_top
+    table = jnp.stack(
+        jnp.broadcast_arrays(block_tab, top_tab.astype(jnp.int32), valid_tab), axis=-1
+    ).reshape(-1).astype(jnp.int32)
+
     def advance(counter, loop_state, send=True):
         incoming, carried, grad_store, map_store = loop_state
-        offset = counter - (sections - 1 - section_id)
-        is_valid = (offset >= 0) & (offset < MICRO)
-        block_no = jnp.clip(MICRO - 1 - offset, 0, MICRO - 1)
-        picks = jnp.stack([block_no, is_top.astype(jnp.int32), is_valid.astype(jnp.int32)])
-        picks = picks.astype(jnp.int32)
-        for level_no in reversed(range(lay_dev)):
+        step_arr = jnp.reshape(counter, (1,)).astype(jnp.int32)
+        for level_pos, level_no in enumerate(reversed(range(lay_dev))):
             level_out = []
             for seq_no in range(seq_dev):
                 level_grads, carried, grad_bc, grad_store, map_store = fused_step(
-                    picks, per_block, incoming, top_blk, carried, w_bc, grad_store, map_store,
-                    level_no, seq_no, factor, width,
+                    step_arr, table, level_pos, lay_dev, per_block, incoming, top_blk, carried,
+                    w_bc, grad_store, map_store, level_no, seq_no, factor, width,
                 )
                 level_out.append(level_grads)
             incoming = jnp.stack(level_out)
-            picks = picks.at[1].set(0)
         if send:
             incoming = passed_along(incoming, "section", -1)
         return (incoming, carried, grad_store, map_store)
@@ -342,7 +350,6 @@
         jnp.zeros((MICRO, lay_dev, seq_dev, block_len, features), jnp.bfloat16),
         jnp.zeros((MICRO, lay_dev, seq_dev, block_len, 2 * state_size), jnp.bfloat16),
     )
-    steps = MICRO + sections - 1
     final_state = lax.fori_loop(0, steps - 1, advance, initial)
     final_state = advance(steps - 1, final_state, send=False)
     grad_store = final_state[2]

time: 127 us -> 127 us (level)
  matrix products: 7.22 us -> 9.53 us
  other arithmetic: 9.98 us -> 8.08 us
    another operation x7 -> x1, other arithmetic: 4.45 us -> 0.08 us  [shards(): jnp.stack(jnp.broadcast_arrays(block_tab, top_tab.astype(jnp.int32), vali...]
    dot_general x1, matrix products: 0.88 us -> 3.18 us  [shards(): jnp.einsum('mlsjn,mlsjd->mlsnd', in_blk, xt_full, preferred_element_type=...]
    convert_element_type x1, other arithmetic: 0.39 us -> 2.49 us  [shards(): saved.append(state_now.astype(jnp.bfloat16))]
    another operation x1, other arithmetic: 0.29 us -> 1.79 us  [shards(): states_t = jnp.stack(saved)]
    unnamed x11 -> x15, local copies, waits for them, and re-layouts: 2.65 us -> 2.19 us
  transfers between devices with their start and end apart: 7 -> 7, of which waited for: 6 -> 6; matrix products, arithmetic and copies ran while one was open for 17% -> 18% of each run, Pallas kernels for 30% -> 29%
where the time goes in v9:
time: 127 us
  waiting for transfers between devices  38.8 us (31%)
  Pallas kernels  37.1 us (29%)
  starting transfers between devices  12.9 us (10%)
  blocking collectives  9.81 us (8%)
  local copies, waits for them, and re-layouts  9.65 us (8%)
  matrix products  9.53 us (8%)
  other arithmetic  8.08 us (6%)
    ppermute x6, waiting for transfers between devices, passed_along(): return lax.ppermute(block, axis, route)  38.8 us
    pallas_call x7, Pallas kernels, fused_step(): pl.pallas_call(functools.partial(step_kernel, factor=factor, width=width,...  37.1 us
    all_gather x1, blocking collectives, shards(): maps_all = lax.all_gather(maps_here, 'dp', axis=0, tiled=True)  9.81 us
    ppermute x6, starting transfers between devices, passed_along(): return lax.ppermute(block, axis, route)  7.68 us
    all_to_all x1, starting transfers between devices, shards(): rows_all = lax.all_to_all(rows_here, 'dp', 0, 0, tiled=True)  5.17 us
    mul x3, local copies, waits for them, and re-layouts, block_consts(): tail_decay[:, :, None] * inputs_b.astype(jnp.float32)  4.17 us
    dot_general x3, matrix products, per_lane(): jnp.einsum('...h,hd->...d', a, spread_heads, precision=lax.Precision.HIGH...  3.73 us
    dot_general x1, matrix products, shards(): jnp.einsum('mlsjn,mlsjd->mlsnd', in_blk, xt_full, preferred_element_type=...  3.18 us
  transfers between devices with their start and end apart: 7, of which 6 were waited for; matrix products, arithmetic and copies ran while one was open for 18% of the time, Pallas kernels for 29%

profile of v9, /device:TPU:0, one launch (start us, length us, event | category | flops | bytes accessed | tf_op | source)
XLA Modules:
  0.0 126.7 jit_solution(15457711825706030531)
XLA Ops:
  0.6 2.2 %copy.32 = bf16[1,1,128,2560]{2,3,1,0:T(8,128)(2,1)} copy(bf16[1,1,128,2560]{3,2,1,0:T(8,128)(2,1)} %param.6) | data formatting | bytes 1310720 | tf_op args[0]
  2.8 5.2 %all-to-all-start = ((bf16[8,1,128,320]{2,3,1,0:T(8,128)(2,1)}), bf16[8,1,128,320]{2,3,1,0:T(8,128)(2,1)}, u32[]{:S(2)}, u32[]{:S(2)}) async-start(bf16[8,1,128,320]{2,3,1,0:T(8,128)(2,1)} %bitcast.28), calls=%async_computation | async-start | bytes 1310720 | tf_op jit(solution)/shard_map/all_to_all | solution.py:364
  8.9 1.7 %mul.114 = f32[4,32,2560]{2,1,0:T(8,128)} reshape(f32[4,32,40,64]{3,2,1,0:T(8,128)S(1)} %mul.108) | data formatting | bytes 2621440 | tf_op jit(solution)/shard_map/vmap(vmap(vmap()))/mul | solution.py:129
  10.6 1.8 %mul.109 = f32[4,1,1,32,2560]{4,3,2,1,0:T(8,128)} reshape(f32[4,32,40,64]{3,2,1,0:T(8,128)S(1)} %mul.108) | data formatting | bytes 2621440 | tf_op jit(solution)/shard_map/vmap(vmap(vmap()))/mul | solution.py:129
  12.6 1.8 %convolution_bitcast_fusion.1.tail_ref = f32[4,1,1,32,2560]{4,3,2,1,0:T(8,128)} fusion(f32[4,32,40]{2,1,0:T(8,128)S(1)} %subtract_exponential_fusion, s32[2560]{0:T(1024)S(1)} %add_select_fusion), kind=kOutput, calls=%fused_computation.1 | convolution fusion | flops 157388800 | bytes 1341440 | tf_op jit(solution)/shard_map/...h,hd->...d/dot_general | solution.py:294
  14.4 1.7 %convolution_bitcast_fusion.lead_ref = f32[4,1,1,32,2560]{4,3,2,1,0:T(8,128)} fusion(s32[2560]{0:T(1024)S(1)} %add_select_fusion, f32[4,1,1,32,40]{4,3,2,1,0:T(8,128)S(1)} %reduce_window_sum.11), kind=kOutput, calls=%fused_computation | convolution fusion | flops 157388800 | bytes 1341440 | tf_op jit(solution)/shard_map/...h,hd->...d/dot_general | solution.py:294
  17.6 3.2 %fusion.13 = f32[4,128,2560]{2,1,0:T(8,128)} fusion(f32[4,32,2560]{2,1,0:T(8,128)S(1)} %copy-done.2, bf16[4,32,2560]{2,1,0:T(8,128)(2,1)S(1)} %bitcast.106, bf16[4,1,1,32,256]{4,3,2,1,0:T(8,128)(2,1)S(1)} %bitcast.116), kind=kOutput, calls=%fused_computation.23 | convolution fusion | flops 84869120 | bytes 7241728 | tf_op jit(solution)/shard_map/mlsjn,mlsjd->mlsnd/dot_general | solution.py:303
  22.5 1.8 %multiply_convert_fusion.wt_ref = bf16[4,1,1,40,32,32]{5,4,3,2,1,0:T(8,128)(2,1)} fusion(f32[4,32,32]{2,1,0:T(8,128)S(1)} %convolution_multiply_fusion, f32[4,40,32]{2,1,0:T(8,128)S(1)} %copy.28, pred[32,32]{1,0:T(8,128)(4,1)S(1)} %iota_compare_fusion.3), kind=kLoop, calls=%fused_computation.4 | loop fusion | flops 819200 | bytes 365568 | tf_op jit(solution)/shard_map/vmap(vmap(vmap()))/convert_element_type | solution.py:128
  24.3 2.5 %fusion.22 = (bf16[1,1,1,128,2560]{4,3,2,1,0:T(8,128)(2,1)S(1)}, bf16[1,1,1,128,2560]{4,3,2,1,0:T(8,128)(2,1)S(1)}, bf16[1,1,1,128,2560]{4,3,2,1,0:T(8,128)(2,1)S(1)}) fusion(f32[4,128,2560]{2,1,0:T(8,128)} %fusion.13, f32[2560]{0:T(1024)S(1)} %get-tuple-element.296, f32[2560]{0:T(1024)S(1)} %get-tuple-element.294, f32[2560]{0:T(1024)S(1)} %get-tuple-element.295), kind=kLoop, calls=%fused_computation.30 | loop fusion | flops 2621440 | bytes 5928960 | tf_op jit(solution)/shard_map/convert_element_type | solution.py:309
  26.8 1.8 %pad_maximum_fusion.sb_ref = bf16[4,1,1,128,2560]{4,3,2,1,0:T(8,128)(2,1)} fusion(bf16[1,1,1,128,2560]{4,3,2,1,0:T(8,128)(2,1)S(1)} %get-tuple-element.334, bf16[1,1,1,128,2560]{4,3,2,1,0:T(8,128)(2,1)S(1)} %get-tuple-element.333, bf16[1,1,1,128,2560]{4,3,2,1,0:T(8,128)(2,1)S(1)} %get-tuple-element.335, bf16[4]{0:T(256)(128)(2,1)S(1)} %pad.clone), kind=kLoop, calls=%fused_computation.2 | loop fusion | flops 3932160 | bytes 4587528 | tf_op jit(solution)/shard_map/stack | solution.py:311
  31.1 78.3 %while.19 = (s32[]{:T(128)}, bf16[1,32,2560]{2,1,0:T(8,128)(2,1)S(1)}, f32[1,1,128,2560]{3,2,1,0:T(8,128)}, bf16[4,1,1,32,2560]{4,3,2,1,0:T(8,128)(2,1)}, bf16[4...) while((s32[]{:T(128)}, ...), condition=%wide.region_2.3_spmd, body=%wide.region_1.2_spmd.sunk | while | flops 146800640 | bytes 8192213 | solution.py:353
  31.1 5.3 %eval_jaxpr.5 = (bf16[32,2560]{1,0:T(8,128)(2,1)}, f32[1,1,128,2560]{3,2,1,0:T(8,128)}, bf16[32,256]{1,0:T(8,128)(2,1)}, bf16[4,1,1,32,2560]{4,3,2,1,0:T(8,128)(2,1)}, bf16[4,1,1,32,256]{4,3,2,1,0:T(8,128)(2,1)S(1)}) custom-call(s32[1]{0:T(128)} %bitcast.103.step_ref, ...), custom_call_target="tpu_custom_call", output_to_operand_aliasing={{1}: (13, {}), {3}: (16, {}), {4}: (17, {})} | custom-call | flops 146800640 | bytes 7536640 | tf_op jit(solution)/shard_map/while/body/eval_jaxpr/pallas_call | solution.py:230
  36.4 1.3 %collective-permute-start = (bf16[1,32,2560]{2,1,0:T(8,128)(2,1)}, bf16[1,32,2560]{2,1,0:T(8,128)(2,1)S(1)}, u32[]{:S(2)}, u32[]{:S(2)}) collective-permute-start(bf16[1,32,2560]{2,1,0:T(8,128)(2,1)} %bitcast.120), channel_id=1, source_target_pairs={{8,0},{16,8},{24,16},{9,1},{17,9},{25,17},{10,2},{18,10},{26,18},{... | collective-permute-start | bytes 491528 | tf_op jit(solution)/shard_map/while/body/eval_jaxpr/ppermute | solution.py:20
  37.7 7.6 %collective-permute-done = bf16[1,32,2560]{2,1,0:T(8,128)(2,1)S(1)} collective-permute-done((bf16[1,32,2560]{2,1,0:T(8,128)(2,1)}, bf16[1,32,2560]{2,1,0:T(8,128)(2,1)S(1)}, u32[]{:S(2)}, u32[]{:S(2)}) %collective-permute-start) | collective-permute-done | bytes 163872 | tf_op jit(solution)/shard_map/while/body/eval_jaxpr/ppermute | solution.py:20
  45.3 5.3 %eval_jaxpr.5 = (bf16[32,2560]{1,0:T(8,128)(2,1)}, f32[1,1,128,2560]{3,2,1,0:T(8,128)}, bf16[32,256]{1,0:T(8,128)(2,1)}, bf16[4,1,1,32,2560]{4,3,2,1,0:T(8,128)(2,1)}, bf16[4,1,1,32,256]{4,3,2,1,0:T(8,128)(2,1)S(1)}) custom-call(s32[1]{0:T(128)} %bitcast.103.step_ref, ...), custom_call_target="tpu_custom_call", output_to_operand_aliasing={{1}: (13, {}), {3}: (16, {}), {4}: (17, {})} | custom-call | flops 146800640 | bytes 7536640 | tf_op jit(solution)/shard_map/while/body/eval_jaxpr/pallas_call | solution.py:230
  50.6 1.3 %collective-permute-start = (bf16[1,32,2560]{2,1,0:T(8,128)(2,1)}, bf16[1,32,2560]{2,1,0:T(8,128)(2,1)S(1)}, u32[]{:S(2)}, u32[]{:S(2)}) collective-permute-start(bf16[1,32,2560]{2,1,0:T(8,128)(2,1)} %bitcast.120), channel_id=1, source_target_pairs={{8,0},{16,8},{24,16},{9,1},{17,9},{25,17},{10,2},{18,10},{26,18},{... | collective-permute-start | bytes 491528 | tf_op jit(solution)/shard_map/while/body/eval_jaxpr/ppermute | solution.py:20
  51.9 6.7 %collective-permute-done = bf16[1,32,2560]{2,1,0:T(8,128)(2,1)S(1)} collective-permute-done((bf16[1,32,2560]{2,1,0:T(8,128)(2,1)}, bf16[1,32,2560]{2,1,0:T(8,128)(2,1)S(1)}, u32[]{:S(2)}, u32[]{:S(2)}) %collective-permute-start) | collective-permute-done | bytes 163872 | tf_op jit(solution)/shard_map/while/body/eval_jaxpr/ppermute | solution.py:20
  58.6 5.3 %eval_jaxpr.5 = (bf16[32,2560]{1,0:T(8,128)(2,1)}, f32[1,1,128,2560]{3,2,1,0:T(8,128)}, bf16[32,256]{1,0:T(8,128)(2,1)}, bf16[4,1,1,32,2560]{4,3,2,1,0:T(8,128)(2,1)}, bf16[4,1,1,32,256]{4,3,2,1,0:T(8,128)(2,1)S(1)}) custom-call(s32[1]{0:T(128)} %bitcast.103.step_ref, ...), custom_call_target="tpu_custom_call", output_to_operand_aliasing={{1}: (13, {}), {3}: (16, {}), {4}: (17, {})} | custom-call | flops 146800640 | bytes 7536640 | tf_op jit(solution)/shard_map/while/body/eval_jaxpr/pallas_call | solution.py:230
  63.9 1.3 %collective-permute-start = (bf16[1,32,2560]{2,1,0:T(8,128)(2,1)}, bf16[1,32,2560]{2,1,0:T(8,128)(2,1)S(1)}, u32[]{:S(2)}, u32[]{:S(2)}) collective-permute-start(bf16[1,32,2560]{2,1,0:T(8,128)(2,1)} %bitcast.120), channel_id=1, source_target_pairs={{8,0},{16,8},{24,16},{9,1},{17,9},{25,17},{10,2},{18,10},{26,18},{... | collective-permute-start | bytes 491528 | tf_op jit(solution)/shard_map/while/body/eval_jaxpr/ppermute | solution.py:20
  65.2 6.1 %collective-permute-done = bf16[1,32,2560]{2,1,0:T(8,128)(2,1)S(1)} collective-permute-done((bf16[1,32,2560]{2,1,0:T(8,128)(2,1)}, bf16[1,32,2560]{2,1,0:T(8,128)(2,1)S(1)}, u32[]{:S(2)}, u32[]{:S(2)}) %collective-permute-start) | collective-permute-done | bytes 163872 | tf_op jit(solution)/shard_map/while/body/eval_jaxpr/ppermute | solution.py:20
  71.3 5.3 %eval_jaxpr.5 = (bf16[32,2560]{1,0:T(8,128)(2,1)}, f32[1,1,128,2560]{3,2,1,0:T(8,128)}, bf16[32,256]{1,0:T(8,128)(2,1)}, bf16[4,1,1,32,2560]{4,3,2,1,0:T(8,128)(2,1)}, bf16[4,1,1,32,256]{4,3,2,1,0:T(8,128)(2,1)S(1)}) custom-call(s32[1]{0:T(128)} %bitcast.103.step_ref, ...), custom_call_target="tpu_custom_call", output_to_operand_aliasing={{1}: (13, {}), {3}: (16, {}), {4}: (17, {})} | custom-call | flops 146800640 | bytes 7536640 | tf_op jit(solution)/shard_map/while/body/eval_jaxpr/pallas_call | solution.py:230
  76.6 1.3 %collective-permute-start = (bf16[1,32,2560]{2,1,0:T(8,128)(2,1)}, bf16[1,32,2560]{2,1,0:T(8,128)(2,1)S(1)}, u32[]{:S(2)}, u32[]{:S(2)}) collective-permute-start(bf16[1,32,2560]{2,1,0:T(8,128)(2,1)} %bitcast.120), channel_id=1, source_target_pairs={{8,0},{16,8},{24,16},{9,1},{17,9},{25,17},{10,2},{18,10},{26,18},{... | collective-permute-start | bytes 491528 | tf_op jit(solution)/shard_map/while/body/eval_jaxpr/ppermute | solution.py:20
  77.9 6.1 %collective-permute-done = bf16[1,32,2560]{2,1,0:T(8,128)(2,1)S(1)} collective-permute-done((bf16[1,32,2560]{2,1,0:T(8,128)(2,1)}, bf16[1,32,2560]{2,1,0:T(8,128)(2,1)S(1)}, u32[]{:S(2)}, u32[]{:S(2)}) %collective-permute-start) | collective-permute-done | bytes 163872 | tf_op jit(solution)/shard_map/while/body/eval_jaxpr/ppermute | solution.py:20
  84.0 5.3 %eval_jaxpr.5 = (bf16[32,2560]{1,0:T(8,128)(2,1)}, f32[1,1,128,2560]{3,2,1,0:T(8,128)}, bf16[32,256]{1,0:T(8,128)(2,1)}, bf16[4,1,1,32,2560]{4,3,2,1,0:T(8,128)(2,1)}, bf16[4,1,1,32,256]{4,3,2,1,0:T(8,128)(2,1)S(1)}) custom-call(s32[1]{0:T(128)} %bitcast.103.step_ref, ...), custom_call_target="tpu_custom_call", output_to_operand_aliasing={{1}: (13, {}), {3}: (16, {}), {4}: (17, {})} | custom-call | flops 146800640 | bytes 7536640 | tf_op jit(solution)/shard_map/while/body/eval_jaxpr/pallas_call | solution.py:230
  89.3 1.3 %collective-permute-start = (bf16[1,32,2560]{2,1,0:T(8,128)(2,1)}, bf16[1,32,2560]{2,1,0:T(8,128)(2,1)S(1)}, u32[]{:S(2)}, u32[]{:S(2)}) collective-permute-start(bf16[1,32,2560]{2,1,0:T(8,128)(2,1)} %bitcast.120), channel_id=1, source_target_pairs={{8,0},{16,8},{24,16},{9,1},{17,9},{25,17},{10,2},{18,10},{26,18},{... | collective-permute-start | bytes 491528 | tf_op jit(solution)/shard_map/while/body/eval_jaxpr/ppermute | solution.py:20
  90.6 6.1 %collective-permute-done = bf16[1,32,2560]{2,1,0:T(8,128)(2,1)S(1)} collective-permute-done((bf16[1,32,2560]{2,1,0:T(8,128)(2,1)}, bf16[1,32,2560]{2,1,0:T(8,128)(2,1)S(1)}, u32[]{:S(2)}, u32[]{:S(2)}) %collective-permute-start) | collective-permute-done | bytes 163872 | tf_op jit(solution)/shard_map/while/body/eval_jaxpr/ppermute | solution.py:20
  96.7 5.3 %eval_jaxpr.5 = (bf16[32,2560]{1,0:T(8,128)(2,1)}, f32[1,1,128,2560]{3,2,1,0:T(8,128)}, bf16[32,256]{1,0:T(8,128)(2,1)}, bf16[4,1,1,32,2560]{4,3,2,1,0:T(8,128)(2,1)}, bf16[4,1,1,32,256]{4,3,2,1,0:T(8,128)(2,1)S(1)}) custom-call(s32[1]{0:T(128)} %bitcast.103.step_ref, ...), custom_call_target="tpu_custom_call", output_to_operand_aliasing={{1}: (13, {}), {3}: (16, {}), {4}: (17, {})} | custom-call | flops 146800640 | bytes 7536640 | tf_op jit(solution)/shard_map/while/body/eval_jaxpr/pallas_call | solution.py:230
  102.0 1.3 %collective-permute-start = (bf16[1,32,2560]{2,1,0:T(8,128)(2,1)}, bf16[1,32,2560]{2,1,0:T(8,128)(2,1)S(1)}, u32[]{:S(2)}, u32[]{:S(2)}) collective-permute-start(bf16[1,32,2560]{2,1,0:T(8,128)(2,1)} %bitcast.120), channel_id=1, source_target_pairs={{8,0},{16,8},{24,16},{9,1},{17,9},{25,17},{10,2},{18,10},{26,18},{... | collective-permute-start | bytes 491528 | tf_op jit(solution)/shard_map/while/body/eval_jaxpr/ppermute | solution.py:20
  103.3 6.1 %collective-permute-done = bf16[1,32,2560]{2,1,0:T(8,128)(2,1)S(1)} collective-permute-done((bf16[1,32,2560]{2,1,0:T(8,128)(2,1)}, bf16[1,32,2560]{2,1,0:T(8,128)(2,1)S(1)}, u32[]{:S(2)}, u32[]{:S(2)}) %collective-permute-start) | collective-permute-done | bytes 163872 | tf_op jit(solution)/shard_map/while/body/eval_jaxpr/ppermute | solution.py:20
  109.4 5.3 %shard_map.59 = (bf16[32,2560]{1,0:T(8,128)(2,1)}, f32[1,1,128,2560]{3,2,1,0:T(8,128)}, bf16[32,256]{1,0:T(8,128)(2,1)}, bf16[4,1,1,32,2560]{4,3,2,1,0:T(8,128)(2,1)}, bf16[4,1,1,32,256]{4,3,2,1,0:T(8,128)(2,1)S(1)}) custom-call(s32[1]{0:T(128)} %constant.45.clone.1.step_ref, ...), custom_call_target="tpu_custom_call", output_to_operand_aliasing={{1}: (13, {}), {3}: (16, {}), {4}: (17, {})} | custom-call | flops 146800640 | bytes 7536640 | tf_op jit(solution)/shard_map/pallas_call | solution.py:230
  114.7 9.8 %all_gather.3 = bf16[8,1,128,256]{3,2,1,0:T(8,128)(2,1)S(1)} all-gather(bf16[1,1,128,256]{3,2,1,0:T(8,128)(2,1)S(1)} %bitcast.111), channel_id=1, replica_groups=mesh['section'=4,'dp'=8] {'dp'}, dimensions={0}, use_global_device_ids=true | all-gather | bytes 589824 | tf_op jit(solution)/shard_map/all_gather | solution.py:366
  124.5 2.1 %fusion.8 = f32[1,320,256]{2,1,0:T(8,128)} fusion(bf16[8,1,128,320]{2,3,1,0:T(8,128)(2,1)} %all-to-all-done, bf16[8,1,128,256]{3,2,1,0:T(8,128)(2,1)S(1)} %all_gather.3), kind=kOutput, calls=%fused_computation.19 | convolution fusion | flops 167854080 | bytes 1507328 | tf_op jit(solution)/shard_map/glrd,glrc->ldc/dot_general | solution.py:367
  (44 shorter events, 6.8 us)
Async XLA Ops:
  0.6 7.3 %copy-start.6 = (f32[1,1,128,40]{2,3,1,0:T(8,128)S(1)}, f32[1,1,128,40]{2,3,1,0:T(8,128)}, u32[]{:S(2)}) copy-start(f32[1,1,128,40]{2,3,1,0:T(8,128)} %param.8) | copy-start | bytes 61444
  2.8 121.7 %all-to-all-start = ((bf16[8,1,128,320]{2,3,1,0:T(8,128)(2,1)}), bf16[8,1,128,320]{2,3,1,0:T(8,128)(2,1)}, u32[]{:S(2)}, u32[]{:S(2)}) async-start(bf16[8,1,128,320]{2,3,1,0:T(8,128)(2,1)} %bitcast.28), calls=%async_computation | async-start | bytes 1310720 | tf_op jit(solution)/shard_map/all_to_all | solution.py:364
  12.6 4.7 %copy-start.4 = (f32[4,2560]{1,0:T(4,128)}, f32[4,2560]{1,0:T(4,128)S(1)}, u32[]{:S(2)}) copy-start(f32[4,2560]{1,0:T(4,128)S(1)} %fusion.18) | copy-start | bytes 122884
  12.6 3.5 %copy-start = (bf16[1,1,128,2560]{3,2,1,0:T(8,128)(2,1)S(1)}, bf16[1,1,128,2560]{3,2,1,0:T(8,128)(2,1)}, u32[]{:S(2)}) copy-start(bf16[1,1,128,2560]{3,2,1,0:T(8,128)(2,1)} %param.6) | copy-start | bytes 1966084
  12.6 3.5 %copy-start.1 = (bf16[1,2560,256]{2,1,0:T(8,128)(2,1)S(1)}, bf16[1,2560,256]{2,1,0:T(8,128)(2,1)}, u32[]{:S(2)}) copy-start(bf16[1,2560,256]{2,1,0:T(8,128)(2,1)} %w_ref.1) | copy-start | bytes 3932164
  16.2 1.4 %copy-start.2 = (f32[4,32,2560]{2,1,0:T(8,128)S(1)}, f32[4,32,2560]{2,1,0:T(8,128)}, u32[]{:S(2)}) copy-start(f32[4,32,2560]{2,1,0:T(8,128)} %mul.114) | copy-start | bytes 3932164
  17.6 3.2 %copy-start.3 = (f32[4,1,1,32,2560]{4,3,2,1,0:T(8,128)S(1)}, f32[4,1,1,32,2560]{4,3,2,1,0:T(8,128)}, u32[]{:S(2)}) copy-start(f32[4,1,1,32,2560]{4,3,2,1,0:T(8,128)} %mul.109) | copy-start | bytes 3932164
  26.8 1.8 %copy-start.5 = (f32[4,2560]{1,0:T(4,128)S(1)}, f32[4,2560]{1,0:T(4,128)}, u32[]{:S(2)}) copy-start(f32[4,2560]{1,0:T(4,128)} %copy-done.4) | copy-start | bytes 122884
  36.4 8.9 %collective-permute-start = (bf16[1,32,2560]{2,1,0:T(8,128)(2,1)}, bf16[1,32,2560]{2,1,0:T(8,128)(2,1)S(1)}, u32[]{:S(2)}, u32[]{:S(2)}) collective-permute-start(bf16[1,32,2560]{2,1,0:T(8,128)(2,1)} %bitcast.120), channel_id=1, source_target_pairs={{8,0},{16,8},{24,16},{9,1},{17,9},{25,17},{10,2},{18,10},{26,18},{... | collective-permute-start | bytes 491528 | tf_op jit(solution)/shard_map/while/body/eval_jaxpr/ppermute | solution.py:20
  50.6 8.0 %collective-permute-start = (bf16[1,32,2560]{2,1,0:T(8,128)(2,1)}, bf16[1,32,2560]{2,1,0:T(8,128)(2,1)S(1)}, u32[]{:S(2)}, u32[]{:S(2)}) collective-permute-start(bf16[1,32,2560]{2,1,0:T(8,128)(2,1)} %bitcast.120), channel_id=1, source_target_pairs={{8,0},{16,8},{24,16},{9,1},{17,9},{25,17},{10,2},{18,10},{26,18},{... | collective-permute-start | bytes 491528 | tf_op jit(solution)/shard_map/while/body/eval_jaxpr/ppermute | solution.py:20
  63.9 7.4 %collective-permute-start = (bf16[1,32,2560]{2,1,0:T(8,128)(2,1)}, bf16[1,32,2560]{2,1,0:T(8,128)(2,1)S(1)}, u32[]{:S(2)}, u32[]{:S(2)}) collective-permute-start(bf16[1,32,2560]{2,1,0:T(8,128)(2,1)} %bitcast.120), channel_id=1, source_target_pairs={{8,0},{16,8},{24,16},{9,1},{17,9},{25,17},{10,2},{18,10},{26,18},{... | collective-permute-start | bytes 491528 | tf_op jit(solution)/shard_map/while/body/eval_jaxpr/ppermute | solution.py:20
  76.6 7.4 %collective-permute-start = (bf16[1,32,2560]{2,1,0:T(8,128)(2,1)}, bf16[1,32,2560]{2,1,0:T(8,128)(2,1)S(1)}, u32[]{:S(2)}, u32[]{:S(2)}) collective-permute-start(bf16[1,32,2560]{2,1,0:T(8,128)(2,1)} %bitcast.120), channel_id=1, source_target_pairs={{8,0},{16,8},{24,16},{9,1},{17,9},{25,17},{10,2},{18,10},{26,18},{... | collective-permute-start | bytes 491528 | tf_op jit(solution)/shard_map/while/body/eval_jaxpr/ppermute | solution.py:20
  89.3 7.4 %collective-permute-start = (bf16[1,32,2560]{2,1,0:T(8,128)(2,1)}, bf16[1,32,2560]{2,1,0:T(8,128)(2,1)S(1)}, u32[]{:S(2)}, u32[]{:S(2)}) collective-permute-start(bf16[1,32,2560]{2,1,0:T(8,128)(2,1)} %bitcast.120), channel_id=1, source_target_pairs={{8,0},{16,8},{24,16},{9,1},{17,9},{25,17},{10,2},{18,10},{26,18},{... | collective-permute-start | bytes 491528 | tf_op jit(solution)/shard_map/while/body/eval_jaxpr/ppermute | solution.py:20
  102.0 7.4 %collective-permute-start = (bf16[1,32,2560]{2,1,0:T(8,128)(2,1)}, bf16[1,32,2560]{2,1,0:T(8,128)(2,1)S(1)}, u32[]{:S(2)}, u32[]{:S(2)}) collective-permute-start(bf16[1,32,2560]{2,1,0:T(8,128)(2,1)} %bitcast.120), channel_id=1, source_target_pairs={{8,0},{16,8},{24,16},{9,1},{17,9},{25,17},{10,2},{18,10},{26,18},{... | collective-permute-start | bytes 491528 | tf_op jit(solution)/shard_map/while/body/eval_jaxpr/ppermute | solution.py:20

commit v10 on v9

--- a/solution.py
+++ b/solution.py
@@ -140,9 +140,21 @@
 def step_kernel(
     step_ref, tab_ref, wt_ref, dec_ref, inc_ref, top_ref, x_ref, b_ref, c_ref, tail_ref, lead_ref, xt_ref,
     sb_ref, r_ref, end_ref, w_ref, gs_ref, ms_ref, out_ref, rnew_ref, dbc_ref, gstore_ref, mstore_ref,
-    v_ref, gx_ref, *, factor, width, level_pos, levels
+    v_ref, gx_ref, tail_buf, lead_buf, xt_buf, sb_buf, r_buf, w_buf, sems, *, factor, width,
+    level_pos, levels, level_no, seq_no
 ):
     base = (step_ref[0] * levels + level_pos) * 3
+    blk = tab_ref[base]
+    fetches = [
+        pltpu.make_async_copy(r_ref.at[level_no, seq_no], r_buf, sems.at[0]),
+        pltpu.make_async_copy(tail_ref.at[blk, level_no, seq_no], tail_buf, sems.at[1]),
+        pltpu.make_async_copy(xt_ref.at[blk, level_no, seq_no], xt_buf, sems.at[2]),
+        pltpu.make_async_copy(lead_ref.at[blk, level_no, seq_no], lead_buf, sems.at[3]),
+        pltpu.make_async_copy(sb_ref.at[blk, level_no, seq_no], sb_buf, sems.at[4]),
+        pltpu.make_async_copy(w_ref.at[level_no], w_buf, sems.at[5]),
+    ]
+    for fetch in fetches:
+        fetch.start()
     f32 = jnp.float32
     bf16 = jnp.bfloat16
     length, features = v_ref.shape
@@ -151,7 +163,6 @@
     nt = (((1,), (1,)), ((), ()))
     tn = (((0,), (0,)), ((), ()))
     v_ref[...] = jnp.where(tab_ref[base + 1] > 0, top_ref[...], inc_ref[...])
-    rb_t = r_ref[...].astype(bf16)
     in_map = b_ref[...]
     out_map = c_ref[...]
     lane_id = lax.broadcasted_iota(jnp.int32, (length, lanes), 1)
@@ -171,28 +182,36 @@
                 stacked[e * length:(e + 1) * length],
                 preferred_element_type=f32,
             )
-        rbb_q = jnp.dot(in_map, rb_t[:, cols], preferred_element_type=f32)
-        gx_ref[:, cols] = gx_q + tail_ref[:, cols] * rbb_q
+        gx_ref[:, cols] = gx_q
         pair_dots = lax.dot_general(stacked, x_q, nt, preferred_element_type=f32)
         mix_acc = mix_acc + dec_ref[q] * pair_dots
     mixing = mix_acc[0:length]
     for e in range(1, per_pair):
         mixing = mixing + mix_acc[e * length:(e + 1) * length]
     mixing = mixing.astype(bf16)
+    fetches[0].wait()
+    fetches[1].wait()
+    rb_t = r_buf[...].astype(bf16)
+    rbb = jnp.dot(in_map, rb_t, preferred_element_type=f32)
+    gx_ref[...] = gx_ref[...] + tail_buf[...] * rbb
     v = v_ref[...]
-    lead_grads = (lead_ref[...] * v.astype(f32)).astype(bf16)
+    fetches[2].wait()
     grad_inmap = factor * lax.dot_general(mixing, out_map, tn, preferred_element_type=f32)
-    grad_inmap = grad_inmap + lax.dot_general(xt_ref[...], rb_t, nt, preferred_element_type=f32)
+    grad_inmap = grad_inmap + lax.dot_general(xt_buf[...], rb_t, nt, preferred_element_type=f32)
+    fetches[3].wait()
+    fetches[4].wait()
+    lead_grads = (lead_buf[...] * v.astype(f32)).astype(bf16)
     grad_outmap = factor * (
         jnp.dot(mixing, in_map, preferred_element_type=f32)
-        + lax.dot_general(lead_grads, sb_ref[...], nt, preferred_element_type=f32)
+        + lax.dot_general(lead_grads, sb_buf[...], nt, preferred_element_type=f32)
     )
     carry = factor * lax.dot_general(out_map, lead_grads, tn, preferred_element_type=f32)
-    rnew_ref[...] = carry + end_ref[...] * r_ref[...]
+    rnew_ref[...] = carry + end_ref[...] * r_buf[...]
     grad_bc = jnp.concatenate([grad_inmap, grad_outmap], axis=1).astype(bf16)
     dbc_ref[...] = grad_bc
     mstore_ref[...] = jnp.where(tab_ref[base + 2] > 0, grad_bc, ms_ref[...])
-    back = lax.dot_general(grad_bc, w_ref[...], nt, preferred_element_type=f32)
+    fetches[5].wait()
+    back = lax.dot_general(grad_bc, w_buf[...], nt, preferred_element_type=f32)
     summed = (v.astype(f32) + gx_ref[...] + back).astype(out_ref.dtype)
     out_ref[...] = summed
     gstore_ref[...] = jnp.where(tab_ref[base + 2] > 0, summed, gs_ref[...])
@@ -211,10 +230,11 @@
     in_specs = [lead_block(a) for a in (wt2, dec2)]
     in_specs.append(pl.BlockSpec((None, length, features), lambda i, c, t: (seq_no, 0, 0)))
     in_specs.append(pl.BlockSpec((None, None, length, features), lambda i, c, t: (t[(c[0] * levels + level_pos) * 3], seq_no, 0, 0)))
-    in_specs += [lead_block(a) for a in (x_flat, in_blk, out_blk, tail_full, lead_full, xt_full, states_t)]
-    in_specs.append(pl.BlockSpec((None, None) + carried.shape[2:], lambda i, c, t: (level_no, seq_no, 0, 0)))
+    in_hbm = pl.BlockSpec(memory_space=pl.ANY)
+    in_specs += [lead_block(a) for a in (x_flat, in_blk, out_blk)]
+    in_specs += [in_hbm] * 5
     in_specs.append(lead_block(end_row))
-    in_specs.append(pl.BlockSpec((None,) + w_bc.shape[1:], lambda i, c, t: (level_no, 0, 0)))
+    in_specs.append(in_hbm)
     store_g = pl.BlockSpec((None, None, None, length, features), lambda i, c, t: (t[(c[0] * levels + level_pos) * 3], level_no, seq_no, 0, 0))
     store_m = pl.BlockSpec((None, None, None, length, 2 * state_size), lambda i, c, t: (t[(c[0] * levels + level_pos) * 3], level_no, seq_no, 0, 0))
     in_specs += [store_g, store_m]
@@ -229,7 +249,8 @@
     moved = 2 * (4 * features * state_size * 2 + 6 * length * features) + 4 * 4 * length * features
     return pl.pallas_call(
         functools.partial(
-            step_kernel, factor=factor, width=width, level_pos=level_pos, levels=levels
+            step_kernel, factor=factor, width=width, level_pos=level_pos, levels=levels,
+            level_no=level_no, seq_no=seq_no,
         ),
         out_shape=(
             jax.ShapeDtypeStruct((length, features), jnp.bfloat16),
@@ -246,6 +267,13 @@
             scratch_shapes=[
                 pltpu.VMEM((length, features), jnp.bfloat16),
                 pltpu.VMEM((length, features), jnp.float32),
+                pltpu.VMEM((length, features), jnp.float32),
+                pltpu.VMEM((length, features), jnp.float32),
+                pltpu.VMEM((length, features), jnp.bfloat16),
+                pltpu.VMEM(states_t.shape[3:], states_t.dtype),
+                pltpu.VMEM(carried.shape[2:], jnp.float32),
+                pltpu.VMEM(w_bc.shape[1:], w_bc.dtype),
+                pltpu.SemaphoreType.DMA((6,)),
             ],
         ),
         input_output_aliases={13: 1, 16: 3, 17: 4},

time: 127 us -> 129 us (1.016)
  transfers between devices with their start and end apart: 7 -> 7, of which waited for: 6 -> 6; matrix products, arithmetic and copies ran while one was open for 18% -> 18% of each run, Pallas kernels for 29% -> 30%
where the time goes in v10:
time: 129 us; the launch traced here: 128 us
  waiting for transfers between devices  38.8 us (30%)
  Pallas kernels  38.3 us (30%)
  starting transfers between devices  12.9 us (10%)
  blocking collectives  9.83 us (8%)
  local copies, waits for them, and re-layouts  9.65 us (7%)
  matrix products  9.53 us (7%)
  other arithmetic  8.08 us (6%)
    ppermute x6, waiting for transfers between devices, passed_along(): return lax.ppermute(block, axis, route)  38.8 us
    pallas_call x7, Pallas kernels, fused_step(): pl.pallas_call(functools.partial(step_kernel, factor=factor, width=width,...  38.3 us
    all_gather x1, blocking collectives, shards(): maps_all = lax.all_gather(maps_here, 'dp', axis=0, tiled=True)  9.83 us
    ppermute x6, starting transfers between devices, passed_along(): return lax.ppermute(block, axis, route)  7.75 us
    all_to_all x1, starting transfers between devices, shards(): rows_all = lax.all_to_all(rows_here, 'dp', 0, 0, tiled=True)  5.17 us
    mul x3, local copies, waits for them, and re-layouts, block_consts(): tail_decay[:, :, None] * inputs_b.astype(jnp.float32)  4.17 us
    dot_general x3, matrix products, per_lane(): jnp.einsum('...h,hd->...d', a, spread_heads, precision=lax.Precision.HIGH...  3.73 us
    dot_general x1, matrix products, shards(): jnp.einsum('mlsjn,mlsjd->mlsnd', in_blk, xt_full, preferred_element_type=...  3.18 us
  transfers between devices with their start and end apart: 7, of which 6 were waited for; matrix products, arithmetic and copies ran while one was open for 18% of the time, Pallas kernels for 30%

profile of v10, /device:TPU:0, one launch (start us, length us, event | category | flops | bytes accessed | tf_op | source)
XLA Modules:
  0.0 128.0 jit_solution(3648121283174484659)
XLA Ops:
  0.6 2.2 %copy.32 = bf16[1,1,128,2560]{2,3,1,0:T(8,128)(2,1)} copy(bf16[1,1,128,2560]{3,2,1,0:T(8,128)(2,1)} %param.6) | data formatting | bytes 1310720 | tf_op args[0]
  2.8 5.2 %all-to-all-start = ((bf16[8,1,128,320]{2,3,1,0:T(8,128)(2,1)}), bf16[8,1,128,320]{2,3,1,0:T(8,128)(2,1)}, u32[]{:S(2)}, u32[]{:S(2)}) async-start(bf16[8,1,128,320]{2,3,1,0:T(8,128)(2,1)} %bitcast.28), calls=%async_computation | async-start | bytes 1310720 | tf_op jit(solution)/shard_map/all_to_all | solution.py:392
  8.9 1.7 %mul.114 = f32[4,32,2560]{2,1,0:T(8,128)} reshape(f32[4,32,40,64]{3,2,1,0:T(8,128)S(1)} %mul.108) | data formatting | bytes 2621440 | tf_op jit(solution)/shard_map/vmap(vmap(vmap()))/mul | solution.py:129
  10.6 1.8 %mul.109 = f32[4,1,1,32,2560]{4,3,2,1,0:T(8,128)} reshape(f32[4,32,40,64]{3,2,1,0:T(8,128)S(1)} %mul.108) | data formatting | bytes 2621440 | tf_op jit(solution)/shard_map/vmap(vmap(vmap()))/mul | solution.py:129
  12.6 1.8 %convolution_bitcast_fusion.1.tail_ref = f32[4,1,1,32,2560]{4,3,2,1,0:T(8,128)} fusion(f32[4,32,40]{2,1,0:T(8,128)S(1)} %subtract_exponential_fusion, s32[2560]{0:T(1024)S(1)} %add_select_fusion), kind=kOutput, calls=%fused_computation.1 | convolution fusion | flops 157388800 | bytes 1341440 | tf_op jit(solution)/shard_map/...h,hd->...d/dot_general | solution.py:322
  14.4 1.7 %convolution_bitcast_fusion.lead_ref = f32[4,1,1,32,2560]{4,3,2,1,0:T(8,128)} fusion(s32[2560]{0:T(1024)S(1)} %add_select_fusion, f32[4,1,1,32,40]{4,3,2,1,0:T(8,128)S(1)} %reduce_window_sum.11), kind=kOutput, calls=%fused_computation | convolution fusion | flops 157388800 | bytes 1341440 | tf_op jit(solution)/shard_map/...h,hd->...d/dot_general | solution.py:322
  17.6 3.2 %fusion.13 = f32[4,128,2560]{2,1,0:T(8,128)} fusion(f32[4,32,2560]{2,1,0:T(8,128)S(1)} %copy-done.2, bf16[4,32,2560]{2,1,0:T(8,128)(2,1)S(1)} %bitcast.106, bf16[4,1,1,32,256]{4,3,2,1,0:T(8,128)(2,1)S(1)} %bitcast.116), kind=kOutput, calls=%fused_computation.23 | convolution fusion | flops 84869120 | bytes 7241728 | tf_op jit(solution)/shard_map/mlsjn,mlsjd->mlsnd/dot_general | solution.py:331
  22.5 1.8 %multiply_convert_fusion.wt_ref = bf16[4,1,1,40,32,32]{5,4,3,2,1,0:T(8,128)(2,1)} fusion(f32[4,32,32]{2,1,0:T(8,128)S(1)} %convolution_multiply_fusion, f32[4,40,32]{2,1,0:T(8,128)S(1)} %copy.28, pred[32,32]{1,0:T(8,128)(4,1)S(1)} %iota_compare_fusion.3), kind=kLoop, calls=%fused_computation.4 | loop fusion | flops 819200 | bytes 365568 | tf_op jit(solution)/shard_map/vmap(vmap(vmap()))/convert_element_type | solution.py:128
  24.3 2.5 %fusion.22 = (bf16[1,1,1,128,2560]{4,3,2,1,0:T(8,128)(2,1)S(1)}, bf16[1,1,1,128,2560]{4,3,2,1,0:T(8,128)(2,1)S(1)}, bf16[1,1,1,128,2560]{4,3,2,1,0:T(8,128)(2,1)S(1)}) fusion(f32[4,128,2560]{2,1,0:T(8,128)} %fusion.13, f32[2560]{0:T(1024)S(1)} %get-tuple-element.296, f32[2560]{0:T(1024)S(1)} %get-tuple-element.294, f32[2560]{0:T(1024)S(1)} %get-tuple-element.295), kind=kLoop, calls=%fused_computation.30 | loop fusion | flops 2621440 | bytes 5928960 | tf_op jit(solution)/shard_map/convert_element_type | solution.py:337
  26.8 1.8 %pad_maximum_fusion.sb_ref = bf16[4,1,1,128,2560]{4,3,2,1,0:T(8,128)(2,1)} fusion(bf16[1,1,1,128,2560]{4,3,2,1,0:T(8,128)(2,1)S(1)} %get-tuple-element.334, bf16[1,1,1,128,2560]{4,3,2,1,0:T(8,128)(2,1)S(1)} %get-tuple-element.333, bf16[1,1,1,128,2560]{4,3,2,1,0:T(8,128)(2,1)S(1)} %get-tuple-element.335, bf16[4]{0:T(256)(128)(2,1)S(1)} %pad.clone), kind=kLoop, calls=%fused_computation.2 | loop fusion | flops 3932160 | bytes 4587528 | tf_op jit(solution)/shard_map/stack | solution.py:339
  31.1 79.4 %while.19 = (s32[]{:T(128)}, bf16[1,32,2560]{2,1,0:T(8,128)(2,1)S(1)}, f32[1,1,128,2560]{3,2,1,0:T(8,128)}, bf16[4,1,1,32,2560]{4,3,2,1,0:T(8,128)(2,1)}, bf16[4...) while((s32[]{:T(128)}, ...), condition=%wide.region_2.3_spmd, body=%wide.region_1.2_spmd.sunk | while | flops 146800640 | bytes 8192213 | solution.py:381
  31.1 5.5 %eval_jaxpr.5 = (bf16[32,2560]{1,0:T(8,128)(2,1)}, f32[1,1,128,2560]{3,2,1,0:T(8,128)}, bf16[32,256]{1,0:T(8,128)(2,1)}, bf16[4,1,1,32,2560]{4,3,2,1,0:T(8,128)(2,1)}, bf16[4,1,1,32,256]{4,3,2,1,0:T(8,128)(2,1)S(1)}) custom-call(s32[1]{0:T(128)} %bitcast.103.step_ref, ...), custom_call_target="tpu_custom_call", output_to_operand_aliasing={{1}: (13, {}), {3}: (16, {}), {4}: (17, {})} | custom-call | flops 146800640 | bytes 7536640 | tf_op jit(solution)/shard_map/while/body/eval_jaxpr/pallas_call | solution.py:250
  36.6 1.3 %collective-permute-start = (bf16[1,32,2560]{2,1,0:T(8,128)(2,1)}, bf16[1,32,2560]{2,1,0:T(8,128)(2,1)S(1)}, u32[]{:S(2)}, u32[]{:S(2)}) collective-permute-start(bf16[1,32,2560]{2,1,0:T(8,128)(2,1)} %bitcast.120), channel_id=1, source_target_pairs={{8,0},{16,8},{24,16},{9,1},{17,9},{25,17},{10,2},{18,10},{26,18},{... | collective-permute-start | bytes 491528 | tf_op jit(solution)/shard_map/while/body/eval_jaxpr/ppermute | solution.py:20
  37.9 7.6 %collective-permute-done = bf16[1,32,2560]{2,1,0:T(8,128)(2,1)S(1)} collective-permute-done((bf16[1,32,2560]{2,1,0:T(8,128)(2,1)}, bf16[1,32,2560]{2,1,0:T(8,128)(2,1)S(1)}, u32[]{:S(2)}, u32[]{:S(2)}) %collective-permute-start) | collective-permute-done | bytes 163872 | tf_op jit(solution)/shard_map/while/body/eval_jaxpr/ppermute | solution.py:20
  45.5 5.5 %eval_jaxpr.5 = (bf16[32,2560]{1,0:T(8,128)(2,1)}, f32[1,1,128,2560]{3,2,1,0:T(8,128)}, bf16[32,256]{1,0:T(8,128)(2,1)}, bf16[4,1,1,32,2560]{4,3,2,1,0:T(8,128)(2,1)}, bf16[4,1,1,32,256]{4,3,2,1,0:T(8,128)(2,1)S(1)}) custom-call(s32[1]{0:T(128)} %bitcast.103.step_ref, ...), custom_call_target="tpu_custom_call", output_to_operand_aliasing={{1}: (13, {}), {3}: (16, {}), {4}: (17, {})} | custom-call | flops 146800640 | bytes 7536640 | tf_op jit(solution)/shard_map/while/body/eval_jaxpr/pallas_call | solution.py:250
  51.0 1.3 %collective-permute-start = (bf16[1,32,2560]{2,1,0:T(8,128)(2,1)}, bf16[1,32,2560]{2,1,0:T(8,128)(2,1)S(1)}, u32[]{:S(2)}, u32[]{:S(2)}) collective-permute-start(bf16[1,32,2560]{2,1,0:T(8,128)(2,1)} %bitcast.120), channel_id=1, source_target_pairs={{8,0},{16,8},{24,16},{9,1},{17,9},{25,17},{10,2},{18,10},{26,18},{... | collective-permute-start | bytes 491528 | tf_op jit(solution)/shard_map/while/body/eval_jaxpr/ppermute | solution.py:20
  52.3 6.7 %collective-permute-done = bf16[1,32,2560]{2,1,0:T(8,128)(2,1)S(1)} collective-permute-done((bf16[1,32,2560]{2,1,0:T(8,128)(2,1)}, bf16[1,32,2560]{2,1,0:T(8,128)(2,1)S(1)}, u32[]{:S(2)}, u32[]{:S(2)}) %collective-permute-start) | collective-permute-done | bytes 163872 | tf_op jit(solution)/shard_map/while/body/eval_jaxpr/ppermute | solution.py:20
  59.0 5.5 %eval_jaxpr.5 = (bf16[32,2560]{1,0:T(8,128)(2,1)}, f32[1,1,128,2560]{3,2,1,0:T(8,128)}, bf16[32,256]{1,0:T(8,128)(2,1)}, bf16[4,1,1,32,2560]{4,3,2,1,0:T(8,128)(2,1)}, bf16[4,1,1,32,256]{4,3,2,1,0:T(8,128)(2,1)S(1)}) custom-call(s32[1]{0:T(128)} %bitcast.103.step_ref, ...), custom_call_target="tpu_custom_call", output_to_operand_aliasing={{1}: (13, {}), {3}: (16, {}), {4}: (17, {})} | custom-call | flops 146800640 | bytes 7536640 | tf_op jit(solution)/shard_map/while/body/eval_jaxpr/pallas_call | solution.py:250
  64.4 1.3 %collective-permute-start = (bf16[1,32,2560]{2,1,0:T(8,128)(2,1)}, bf16[1,32,2560]{2,1,0:T(8,128)(2,1)S(1)}, u32[]{:S(2)}, u32[]{:S(2)}) collective-permute-start(bf16[1,32,2560]{2,1,0:T(8,128)(2,1)} %bitcast.120), channel_id=1, source_target_pairs={{8,0},{16,8},{24,16},{9,1},{17,9},{25,17},{10,2},{18,10},{26,18},{... | collective-permute-start | bytes 491528 | tf_op jit(solution)/shard_map/while/body/eval_jaxpr/ppermute | solution.py:20
  65.7 6.1 %collective-permute-done = bf16[1,32,2560]{2,1,0:T(8,128)(2,1)S(1)} collective-permute-done((bf16[1,32,2560]{2,1,0:T(8,128)(2,1)}, bf16[1,32,2560]{2,1,0:T(8,128)(2,1)S(1)}, u32[]{:S(2)}, u32[]{:S(2)}) %collective-permute-start) | collective-permute-done | bytes 163872 | tf_op jit(solution)/shard_map/while/body/eval_jaxpr/ppermute | solution.py:20
  71.9 5.5 %eval_jaxpr.5 = (bf16[32,2560]{1,0:T(8,128)(2,1)}, f32[1,1,128,2560]{3,2,1,0:T(8,128)}, bf16[32,256]{1,0:T(8,128)(2,1)}, bf16[4,1,1,32,2560]{4,3,2,1,0:T(8,128)(2,1)}, bf16[4,1,1,32,256]{4,3,2,1,0:T(8,128)(2,1)S(1)}) custom-call(s32[1]{0:T(128)} %bitcast.103.step_ref, ...), custom_call_target="tpu_custom_call", output_to_operand_aliasing={{1}: (13, {}), {3}: (16, {}), {4}: (17, {})} | custom-call | flops 146800640 | bytes 7536640 | tf_op jit(solution)/shard_map/while/body/eval_jaxpr/pallas_call | solution.py:250
  77.3 1.3 %collective-permute-start = (bf16[1,32,2560]{2,1,0:T(8,128)(2,1)}, bf16[1,32,2560]{2,1,0:T(8,128)(2,1)S(1)}, u32[]{:S(2)}, u32[]{:S(2)}) collective-permute-start(bf16[1,32,2560]{2,1,0:T(8,128)(2,1)} %bitcast.120), channel_id=1, source_target_pairs={{8,0},{16,8},{24,16},{9,1},{17,9},{25,17},{10,2},{18,10},{26,18},{... | collective-permute-start | bytes 491528 | tf_op jit(solution)/shard_map/while/body/eval_jaxpr/ppermute | solution.py:20
  78.6 6.1 %collective-permute-done = bf16[1,32,2560]{2,1,0:T(8,128)(2,1)S(1)} collective-permute-done((bf16[1,32,2560]{2,1,0:T(8,128)(2,1)}, bf16[1,32,2560]{2,1,0:T(8,128)(2,1)S(1)}, u32[]{:S(2)}, u32[]{:S(2)}) %collective-permute-start) | collective-permute-done | bytes 163872 | tf_op jit(solution)/shard_map/while/body/eval_jaxpr/ppermute | solution.py:20
  84.7 5.5 %eval_jaxpr.5 = (bf16[32,2560]{1,0:T(8,128)(2,1)}, f32[1,1,128,2560]{3,2,1,0:T(8,128)}, bf16[32,256]{1,0:T(8,128)(2,1)}, bf16[4,1,1,32,2560]{4,3,2,1,0:T(8,128)(2,1)}, bf16[4,1,1,32,256]{4,3,2,1,0:T(8,128)(2,1)S(1)}) custom-call(s32[1]{0:T(128)} %bitcast.103.step_ref, ...), custom_call_target="tpu_custom_call", output_to_operand_aliasing={{1}: (13, {}), {3}: (16, {}), {4}: (17, {})} | custom-call | flops 146800640 | bytes 7536640 | tf_op jit(solution)/shard_map/while/body/eval_jaxpr/pallas_call | solution.py:250
  90.2 1.3 %collective-permute-start = (bf16[1,32,2560]{2,1,0:T(8,128)(2,1)}, bf16[1,32,2560]{2,1,0:T(8,128)(2,1)S(1)}, u32[]{:S(2)}, u32[]{:S(2)}) collective-permute-start(bf16[1,32,2560]{2,1,0:T(8,128)(2,1)} %bitcast.120), channel_id=1, source_target_pairs={{8,0},{16,8},{24,16},{9,1},{17,9},{25,17},{10,2},{18,10},{26,18},{... | collective-permute-start | bytes 491528 | tf_op jit(solution)/shard_map/while/body/eval_jaxpr/ppermute | solution.py:20
  91.5 6.1 %collective-permute-done = bf16[1,32,2560]{2,1,0:T(8,128)(2,1)S(1)} collective-permute-done((bf16[1,32,2560]{2,1,0:T(8,128)(2,1)}, bf16[1,32,2560]{2,1,0:T(8,128)(2,1)S(1)}, u32[]{:S(2)}, u32[]{:S(2)}) %collective-permute-start) | collective-permute-done | bytes 163872 | tf_op jit(solution)/shard_map/while/body/eval_jaxpr/ppermute | solution.py:20
  97.6 5.5 %eval_jaxpr.5 = (bf16[32,2560]{1,0:T(8,128)(2,1)}, f32[1,1,128,2560]{3,2,1,0:T(8,128)}, bf16[32,256]{1,0:T(8,128)(2,1)}, bf16[4,1,1,32,2560]{4,3,2,1,0:T(8,128)(2,1)}, bf16[4,1,1,32,256]{4,3,2,1,0:T(8,128)(2,1)S(1)}) custom-call(s32[1]{0:T(128)} %bitcast.103.step_ref, ...), custom_call_target="tpu_custom_call", output_to_operand_aliasing={{1}: (13, {}), {3}: (16, {}), {4}: (17, {})} | custom-call | flops 146800640 | bytes 7536640 | tf_op jit(solution)/shard_map/while/body/eval_jaxpr/pallas_call | solution.py:250
  103.1 1.3 %collective-permute-start = (bf16[1,32,2560]{2,1,0:T(8,128)(2,1)}, bf16[1,32,2560]{2,1,0:T(8,128)(2,1)S(1)}, u32[]{:S(2)}, u32[]{:S(2)}) collective-permute-start(bf16[1,32,2560]{2,1,0:T(8,128)(2,1)} %bitcast.120), channel_id=1, source_target_pairs={{8,0},{16,8},{24,16},{9,1},{17,9},{25,17},{10,2},{18,10},{26,18},{... | collective-permute-start | bytes 491528 | tf_op jit(solution)/shard_map/while/body/eval_jaxpr/ppermute | solution.py:20
  104.4 6.1 %collective-permute-done = bf16[1,32,2560]{2,1,0:T(8,128)(2,1)S(1)} collective-permute-done((bf16[1,32,2560]{2,1,0:T(8,128)(2,1)}, bf16[1,32,2560]{2,1,0:T(8,128)(2,1)S(1)}, u32[]{:S(2)}, u32[]{:S(2)}) %collective-permute-start) | collective-permute-done | bytes 163872 | tf_op jit(solution)/shard_map/while/body/eval_jaxpr/ppermute | solution.py:20
  110.5 5.5 %shard_map.59 = (bf16[32,2560]{1,0:T(8,128)(2,1)}, f32[1,1,128,2560]{3,2,1,0:T(8,128)}, bf16[32,256]{1,0:T(8,128)(2,1)}, bf16[4,1,1,32,2560]{4,3,2,1,0:T(8,128)(2,1)}, bf16[4,1,1,32,256]{4,3,2,1,0:T(8,128)(2,1)S(1)}) custom-call(s32[1]{0:T(128)} %constant.45.clone.1.step_ref, ...), custom_call_target="tpu_custom_call", output_to_operand_aliasing={{1}: (13, {}), {3}: (16, {}), {4}: (17, {})} | custom-call | flops 146800640 | bytes 7536640 | tf_op jit(solution)/shard_map/pallas_call | solution.py:250
  116.0 9.8 %all_gather.3 = bf16[8,1,128,256]{3,2,1,0:T(8,128)(2,1)S(1)} all-gather(bf16[1,1,128,256]{3,2,1,0:T(8,128)(2,1)S(1)} %bitcast.111), channel_id=1, replica_groups=mesh['section'=4,'dp'=8] {'dp'}, dimensions={0}, use_global_device_ids=true | all-gather | bytes 589824 | tf_op jit(solution)/shard_map/all_gather | solution.py:394
  125.8 2.1 %fusion.8 = f32[1,320,256]{2,1,0:T(8,128)} fusion(bf16[8,1,128,320]{2,3,1,0:T(8,128)(2,1)} %all-to-all-done, bf16[8,1,128,256]{3,2,1,0:T(8,128)(2,1)S(1)} %all_gather.3), kind=kOutput, calls=%fused_computation.19 | convolution fusion | flops 167854080 | bytes 1507328 | tf_op jit(solution)/shard_map/glrd,glrc->ldc/dot_general | solution.py:395
  (44 shorter events, 6.8 us)
Async XLA Ops:
  0.6 7.3 %copy-start.6 = (f32[1,1,128,40]{2,3,1,0:T(8,128)S(1)}, f32[1,1,128,40]{2,3,1,0:T(8,128)}, u32[]{:S(2)}) copy-start(f32[1,1,128,40]{2,3,1,0:T(8,128)} %param.8) | copy-start | bytes 61444
  2.8 123.0 %all-to-all-start = ((bf16[8,1,128,320]{2,3,1,0:T(8,128)(2,1)}), bf16[8,1,128,320]{2,3,1,0:T(8,128)(2,1)}, u32[]{:S(2)}, u32[]{:S(2)}) async-start(bf16[8,1,128,320]{2,3,1,0:T(8,128)(2,1)} %bitcast.28), calls=%async_computation | async-start | bytes 1310720 | tf_op jit(solution)/shard_map/all_to_all | solution.py:392
  12.6 4.7 %copy-start.4 = (f32[4,2560]{1,0:T(4,128)}, f32[4,2560]{1,0:T(4,128)S(1)}, u32[]{:S(2)}) copy-start(f32[4,2560]{1,0:T(4,128)S(1)} %fusion.18) | copy-start | bytes 122884
  12.6 3.5 %copy-start = (bf16[1,1,128,2560]{3,2,1,0:T(8,128)(2,1)S(1)}, bf16[1,1,128,2560]{3,2,1,0:T(8,128)(2,1)}, u32[]{:S(2)}) copy-start(bf16[1,1,128,2560]{3,2,1,0:T(8,128)(2,1)} %param.6) | copy-start | bytes 1966084
  12.6 3.5 %copy-start.1 = (bf16[1,2560,256]{2,1,0:T(8,128)(2,1)S(1)}, bf16[1,2560,256]{2,1,0:T(8,128)(2,1)}, u32[]{:S(2)}) copy-start(bf16[1,2560,256]{2,1,0:T(8,128)(2,1)} %w_ref.1) | copy-start | bytes 3932164
  16.2 1.4 %copy-start.2 = (f32[4,32,2560]{2,1,0:T(8,128)S(1)}, f32[4,32,2560]{2,1,0:T(8,128)}, u32[]{:S(2)}) copy-start(f32[4,32,2560]{2,1,0:T(8,128)} %mul.114) | copy-start | bytes 3932164
  17.6 3.2 %copy-start.3 = (f32[4,1,1,32,2560]{4,3,2,1,0:T(8,128)S(1)}, f32[4,1,1,32,2560]{4,3,2,1,0:T(8,128)}, u32[]{:S(2)}) copy-start(f32[4,1,1,32,2560]{4,3,2,1,0:T(8,128)} %mul.109) | copy-start | bytes 3932164
  26.8 1.8 %copy-start.5 = (f32[4,2560]{1,0:T(4,128)S(1)}, f32[4,2560]{1,0:T(4,128)}, u32[]{:S(2)}) copy-start(f32[4,2560]{1,0:T(4,128)} %copy-done.4) | copy-start | bytes 122884
  36.6 8.9 %collective-permute-start = (bf16[1,32,2560]{2,1,0:T(8,128)(2,1)}, bf16[1,32,2560]{2,1,0:T(8,128)(2,1)S(1)}, u32[]{:S(2)}, u32[]{:S(2)}) collective-permute-start(bf16[1,32,2560]{2,1,0:T(8,128)(2,1)} %bitcast.120), channel_id=1, source_target_pairs={{8,0},{16,8},{24,16},{9,1},{17,9},{25,17},{10,2},{18,10},{26,18},{... | collective-permute-start | bytes 491528 | tf_op jit(solution)/shard_map/while/body/eval_jaxpr/ppermute | solution.py:20
  51.0 8.0 %collective-permute-start = (bf16[1,32,2560]{2,1,0:T(8,128)(2,1)}, bf16[1,32,2560]{2,1,0:T(8,128)(2,1)S(1)}, u32[]{:S(2)}, u32[]{:S(2)}) collective-permute-start(bf16[1,32,2560]{2,1,0:T(8,128)(2,1)} %bitcast.120), channel_id=1, source_target_pairs={{8,0},{16,8},{24,16},{9,1},{17,9},{25,17},{10,2},{18,10},{26,18},{... | collective-permute-start | bytes 491528 | tf_op jit(solution)/shard_map/while/body/eval_jaxpr/ppermute | solution.py:20
  64.4 7.4 %collective-permute-start = (bf16[1,32,2560]{2,1,0:T(8,128)(2,1)}, bf16[1,32,2560]{2,1,0:T(8,128)(2,1)S(1)}, u32[]{:S(2)}, u32[]{:S(2)}) collective-permute-start(bf16[1,32,2560]{2,1,0:T(8,128)(2,1)} %bitcast.120), channel_id=1, source_target_pairs={{8,0},{16,8},{24,16},{9,1},{17,9},{25,17},{10,2},{18,10},{26,18},{... | collective-permute-start | bytes 491528 | tf_op jit(solution)/shard_map/while/body/eval_jaxpr/ppermute | solution.py:20
  77.3 7.4 %collective-permute-start = (bf16[1,32,2560]{2,1,0:T(8,128)(2,1)}, bf16[1,32,2560]{2,1,0:T(8,128)(2,1)S(1)}, u32[]{:S(2)}, u32[]{:S(2)}) collective-permute-start(bf16[1,32,2560]{2,1,0:T(8,128)(2,1)} %bitcast.120), channel_id=1, source_target_pairs={{8,0},{16,8},{24,16},{9,1},{17,9},{25,17},{10,2},{18,10},{26,18},{... | collective-permute-start | bytes 491528 | tf_op jit(solution)/shard_map/while/body/eval_jaxpr/ppermute | solution.py:20
  90.2 7.4 %collective-permute-start = (bf16[1,32,2560]{2,1,0:T(8,128)(2,1)}, bf16[1,32,2560]{2,1,0:T(8,128)(2,1)S(1)}, u32[]{:S(2)}, u32[]{:S(2)}) collective-permute-start(bf16[1,32,2560]{2,1,0:T(8,128)(2,1)} %bitcast.120), channel_id=1, source_target_pairs={{8,0},{16,8},{24,16},{9,1},{17,9},{25,17},{10,2},{18,10},{26,18},{... | collective-permute-start | bytes 491528 | tf_op jit(solution)/shard_map/while/body/eval_jaxpr/ppermute | solution.py:20
  103.1 7.4 %collective-permute-start = (bf16[1,32,2560]{2,1,0:T(8,128)(2,1)}, bf16[1,32,2560]{2,1,0:T(8,128)(2,1)S(1)}, u32[]{:S(2)}, u32[]{:S(2)}) collective-permute-start(bf16[1,32,2560]{2,1,0:T(8,128)(2,1)} %bitcast.120), channel_id=1, source_target_pairs={{8,0},{16,8},{24,16},{9,1},{17,9},{25,17},{10,2},{18,10},{26,18},{... | collective-permute-start | bytes 491528 | tf_op jit(solution)/shard_map/while/body/eval_jaxpr/ppermute | solution.py:20

commit v11 on v10

--- a/solution.py
+++ b/solution.py
@@ -126,13 +126,11 @@
     decays_t = jnp.where(upper, jnp.exp(spread_t), 0.0)
     scores_t = jnp.dot(in_b, out_b.T, preferred_element_type=jnp.float32)
     weighted = (factor * decays_t * scores_t[None]).astype(jnp.bfloat16)
-    tail_inputs = (tail_decay[:, :, None] * inputs_b.astype(jnp.float32)).astype(jnp.bfloat16)
     return dict(
         decays=decays,
         tail=tail_decay,
         lead=leading,
         weighted=weighted,
-        tail_inputs=tail_inputs,
         ending=jnp.exp(ending),
     )
 
@@ -326,7 +324,8 @@
 
     tail_full = per_lane(consts["tail"])
     lead_full = per_lane(consts["lead"])
-    xt_full = consts["tail_inputs"].reshape(lead_dims + (block_len, features))
+    x_flat = x_blk.reshape(lead_dims + (block_len, features))
+    xt_full = (tail_full * x_flat.astype(jnp.float32)).astype(jnp.bfloat16)
     end_row = per_lane(consts["ending"])[..., None, :]
     fresh_t = jnp.einsum(
         "mlsjn,mlsjd->mlsnd", in_blk, xt_full, preferred_element_type=jnp.float32
@@ -337,7 +336,6 @@
         saved.append(state_now.astype(jnp.bfloat16))
         state_now = end_row[block_no] * state_now + fresh_t[block_no]
     states_t = jnp.stack(saved)
-    x_flat = x_blk.reshape(lead_dims + (block_len, features))
     per_block = (wt2, dec2, x_flat, in_blk, out_blk, tail_full, lead_full, xt_full, states_t, end_row)
     per_block = lax.optimization_barrier(per_block)
 

time: 129 us -> 123 us (0.953)
  local copies, waits for them, and re-layouts: 9.65 us -> 5.46 us
    mul x3 -> x0, local copies, waits for them, and re-layouts: 4.17 us -> none  [block_consts(): tail_decay[:, :, None] * inputs_b.astype(jnp.float32)]
  transfers between devices with their start and end apart: 7 -> 7, of which waited for: 6 -> 6; matrix products, arithmetic and copies ran while one was open for 18% -> 14% of each run, Pallas kernels for 30% -> 31%
where the time goes in v11:
time: 123 us
  waiting for transfers between devices  38.8 us (32%)
  Pallas kernels  38.3 us (31%)
  starting transfers between devices  13.1 us (11%)
  blocking collectives  9.83 us (8%)
  matrix products  8.53 us (7%)
  other arithmetic  7.99 us (6%)
  local copies, waits for them, and re-layouts  5.46 us (4%)
    ppermute x6, waiting for transfers between devices, passed_along(): return lax.ppermute(block, axis, route)  38.8 us
    pallas_call x7, Pallas kernels, fused_step(): pl.pallas_call(functools.partial(step_kernel, factor=factor, width=width,...  38.3 us
    all_gather x1, blocking collectives, shards(): maps_all = lax.all_gather(maps_here, 'dp', axis=0, tiled=True)  9.83 us
    ppermute x6, starting transfers between devices, passed_along(): return lax.ppermute(block, axis, route)  7.75 us
    all_to_all x1, starting transfers between devices, shards(): rows_all = lax.all_to_all(rows_here, 'dp', 0, 0, tiled=True)  5.3 us
    dot_general x1, matrix products, shards(): jnp.einsum('mlsjn,mlsjd->mlsnd', in_blk, xt_full, preferred_element_type=...  3.18 us
    dot_general x3, matrix products, per_lane(): jnp.einsum('...h,hd->...d', a, spread_heads, precision=lax.Precision.HIGH...  2.73 us
    convert_element_type x1, other arithmetic, shards(): saved.append(state_now.astype(jnp.bfloat16))  2.49 us
  transfers between devices with their start and end apart: 7, of which 6 were waited for; matrix products, arithmetic and copies ran while one was open for 14% of the time, Pallas kernels for 31%

profile of v11, /device:TPU:0, one launch (start us, length us, event | category | flops | bytes accessed | tf_op | source)
XLA Modules:
  0.0 122.8 jit_solution(9869283532778573334)
XLA Ops:
  0.6 2.2 %copy.32 = bf16[1,1,128,2560]{2,3,1,0:T(8,128)(2,1)} copy(bf16[1,1,128,2560]{3,2,1,0:T(8,128)(2,1)} %param.6) | data formatting | bytes 1310720 | tf_op args[0]
  2.8 5.3 %all-to-all-start = ((bf16[8,1,128,320]{2,3,1,0:T(8,128)(2,1)}), bf16[8,1,128,320]{2,3,1,0:T(8,128)(2,1)}, u32[]{:S(2)}, u32[]{:S(2)}) async-start(bf16[8,1,128,320]{2,3,1,0:T(8,128)(2,1)} %bitcast.29), calls=%async_computation | async-start | bytes 1310720 | tf_op jit(solution)/shard_map/all_to_all | solution.py:390
  9.6 1.0 fusion.44.xt_ref
  10.6 3.2 %fusion.29 = f32[4,128,2560]{2,1,0:T(8,128)} fusion(bf16[4,1,1,32,256]{4,3,2,1,0:T(8,128)(2,1)S(1)} %bitcast.114, f32[4,32,2560]{2,1,0:T(8,128)S(1)} %fusion.19, bf16[4,32,2560]{2,1,0:T(8,128)(2,1)S(1)} %bitcast.107), kind=kOutput, calls=%fused_computation.36 | convolution fusion | flops 84869120 | bytes 7241728 | tf_op jit(solution)/shard_map/mlsjn,mlsjd->mlsnd/dot_general | solution.py:330
  13.9 1.8 %convolution_bitcast_fusion.lead_ref = f32[4,1,1,32,2560]{4,3,2,1,0:T(8,128)} fusion(s32[2560]{0:T(1024)S(1)} %add_select_fusion, f32[4,1,1,32,40]{4,3,2,1,0:T(8,128)S(1)} %reduce_window_sum.11), kind=kOutput, calls=%fused_computation | convolution fusion | flops 157388800 | bytes 1341440 | tf_op jit(solution)/shard_map/...h,hd->...d/dot_general | solution.py:320
  17.4 1.7 %multiply_convert_fusion.wt_ref = bf16[4,1,1,40,32,32]{5,4,3,2,1,0:T(8,128)(2,1)} fusion(f32[4,32,32]{2,1,0:T(8,128)S(1)} %convolution_multiply_fusion, f32[4,40,32]{2,1,0:T(8,128)S(1)} %copy.28, pred[32,32]{1,0:T(8,128)(4,1)S(1)} %iota_compare_fusion.3), kind=kLoop, calls=%fused_computation.3 | loop fusion | flops 819200 | bytes 365568 | tf_op jit(solution)/shard_map/vmap(vmap(vmap()))/convert_element_type | solution.py:128
  19.1 2.5 %fusion.21 = (bf16[1,1,1,128,2560]{4,3,2,1,0:T(8,128)(2,1)S(1)}, bf16[1,1,1,128,2560]{4,3,2,1,0:T(8,128)(2,1)S(1)}, bf16[1,1,1,128,2560]{4,3,2,1,0:T(8,128)(2,1)S(1)}) fusion(f32[4,128,2560]{2,1,0:T(8,128)} %fusion.29, f32[2560]{0:T(1024)S(1)} %get-tuple-element.296, f32[2560]{0:T(1024)S(1)} %get-tuple-element.294, f32[2560]{0:T(1024)S(1)} %get-tuple-element.295), kind=kLoop, calls=%fused_computation.28 | loop fusion | flops 2621440 | bytes 5928960 | tf_op jit(solution)/shard_map/convert_element_type | solution.py:336
  21.6 1.8 %pad_maximum_fusion.sb_ref = bf16[4,1,1,128,2560]{4,3,2,1,0:T(8,128)(2,1)} fusion(bf16[1,1,1,128,2560]{4,3,2,1,0:T(8,128)(2,1)S(1)} %get-tuple-element.334, bf16[1,1,1,128,2560]{4,3,2,1,0:T(8,128)(2,1)S(1)} %get-tuple-element.333, bf16[1,1,1,128,2560]{4,3,2,1,0:T(8,128)(2,1)S(1)} %get-tuple-element.335, bf16[4]{0:T(256)(128)(2,1)S(1)} %pad.clone), kind=kLoop, calls=%fused_computation.1 | loop fusion | flops 3932160 | bytes 4587528 | tf_op jit(solution)/shard_map/stack | solution.py:338
  23.8 1.2 broadcast.401
  25.0 0.9 broadcast_in_dim.92
  25.9 79.4 %while.19 = (s32[]{:T(128)}, bf16[1,32,2560]{2,1,0:T(8,128)(2,1)S(1)}, f32[1,1,128,2560]{3,2,1,0:T(8,128)}, bf16[4,1,1,32,2560]{4,3,2,1,0:T(8,128)(2,1)}, bf16[4...) while((s32[]{:T(128)}, ...), condition=%wide.region_2.3_spmd, body=%wide.region_1.2_spmd.sunk | while | flops 146800640 | bytes 8192213 | solution.py:379
  25.9 5.5 %eval_jaxpr.5 = (bf16[32,2560]{1,0:T(8,128)(2,1)}, f32[1,1,128,2560]{3,2,1,0:T(8,128)}, bf16[32,256]{1,0:T(8,128)(2,1)}, bf16[4,1,1,32,2560]{4,3,2,1,0:T(8,128)(2,1)}, bf16[4,1,1,32,256]{4,3,2,1,0:T(8,128)(2,1)S(1)}) custom-call(s32[1]{0:T(128)} %bitcast.102.step_ref, ...), custom_call_target="tpu_custom_call", output_to_operand_aliasing={{1}: (13, {}), {3}: (16, {}), {4}: (17, {})} | custom-call | flops 146800640 | bytes 7536640 | tf_op jit(solution)/shard_map/while/body/eval_jaxpr/pallas_call | solution.py:248
  31.4 1.3 %collective-permute-start = (bf16[1,32,2560]{2,1,0:T(8,128)(2,1)}, bf16[1,32,2560]{2,1,0:T(8,128)(2,1)S(1)}, u32[]{:S(2)}, u32[]{:S(2)}) collective-permute-start(bf16[1,32,2560]{2,1,0:T(8,128)(2,1)} %bitcast.120), channel_id=1, source_target_pairs={{8,0},{16,8},{24,16},{9,1},{17,9},{25,17},{10,2},{18,10},{26,18},{... | collective-permute-start | bytes 491528 | tf_op jit(solution)/shard_map/while/body/eval_jaxpr/ppermute | solution.py:20
  32.7 7.6 %collective-permute-done = bf16[1,32,2560]{2,1,0:T(8,128)(2,1)S(1)} collective-permute-done((bf16[1,32,2560]{2,1,0:T(8,128)(2,1)}, bf16[1,32,2560]{2,1,0:T(8,128)(2,1)S(1)}, u32[]{:S(2)}, u32[]{:S(2)}) %collective-permute-start) | collective-permute-done | bytes 163872 | tf_op jit(solution)/shard_map/while/body/eval_jaxpr/ppermute | solution.py:20
  40.3 5.5 %eval_jaxpr.5 = (bf16[32,2560]{1,0:T(8,128)(2,1)}, f32[1,1,128,2560]{3,2,1,0:T(8,128)}, bf16[32,256]{1,0:T(8,128)(2,1)}, bf16[4,1,1,32,2560]{4,3,2,1,0:T(8,128)(2,1)}, bf16[4,1,1,32,256]{4,3,2,1,0:T(8,128)(2,1)S(1)}) custom-call(s32[1]{0:T(128)} %bitcast.102.step_ref, ...), custom_call_target="tpu_custom_call", output_to_operand_aliasing={{1}: (13, {}), {3}: (16, {}), {4}: (17, {})} | custom-call | flops 146800640 | bytes 7536640 | tf_op jit(solution)/shard_map/while/body/eval_jaxpr/pallas_call | solution.py:248
  45.8 1.3 %collective-permute-start = (bf16[1,32,2560]{2,1,0:T(8,128)(2,1)}, bf16[1,32,2560]{2,1,0:T(8,128)(2,1)S(1)}, u32[]{:S(2)}, u32[]{:S(2)}) collective-permute-start(bf16[1,32,2560]{2,1,0:T(8,128)(2,1)} %bitcast.120), channel_id=1, source_target_pairs={{8,0},{16,8},{24,16},{9,1},{17,9},{25,17},{10,2},{18,10},{26,18},{... | collective-permute-start | bytes 491528 | tf_op jit(solution)/shard_map/while/body/eval_jaxpr/ppermute | solution.py:20
  47.1 6.7 %collective-permute-done = bf16[1,32,2560]{2,1,0:T(8,128)(2,1)S(1)} collective-permute-done((bf16[1,32,2560]{2,1,0:T(8,128)(2,1)}, bf16[1,32,2560]{2,1,0:T(8,128)(2,1)S(1)}, u32[]{:S(2)}, u32[]{:S(2)}) %collective-permute-start) | collective-permute-done | bytes 163872 | tf_op jit(solution)/shard_map/while/body/eval_jaxpr/ppermute | solution.py:20
  53.8 5.5 %eval_jaxpr.5 = (bf16[32,2560]{1,0:T(8,128)(2,1)}, f32[1,1,128,2560]{3,2,1,0:T(8,128)}, bf16[32,256]{1,0:T(8,128)(2,1)}, bf16[4,1,1,32,2560]{4,3,2,1,0:T(8,128)(2,1)}, bf16[4,1,1,32,256]{4,3,2,1,0:T(8,128)(2,1)S(1)}) custom-call(s32[1]{0:T(128)} %bitcast.102.step_ref, ...), custom_call_target="tpu_custom_call", output_to_operand_aliasing={{1}: (13, {}), {3}: (16, {}), {4}: (17, {})} | custom-call | flops 146800640 | bytes 7536640 | tf_op jit(solution)/shard_map/while/body/eval_jaxpr/pallas_call | solution.py:248
  59.3 1.3 %collective-permute-start = (bf16[1,32,2560]{2,1,0:T(8,128)(2,1)}, bf16[1,32,2560]{2,1,0:T(8,128)(2,1)S(1)}, u32[]{:S(2)}, u32[]{:S(2)}) collective-permute-start(bf16[1,32,2560]{2,1,0:T(8,128)(2,1)} %bitcast.120), channel_id=1, source_target_pairs={{8,0},{16,8},{24,16},{9,1},{17,9},{25,17},{10,2},{18,10},{26,18},{... | collective-permute-start | bytes 491528 | tf_op jit(solution)/shard_map/while/body/eval_jaxpr/ppermute | solution.py:20
  60.6 6.1 %collective-permute-done = bf16[1,32,2560]{2,1,0:T(8,128)(2,1)S(1)} collective-permute-done((bf16[1,32,2560]{2,1,0:T(8,128)(2,1)}, bf16[1,32,2560]{2,1,0:T(8,128)(2,1)S(1)}, u32[]{:S(2)}, u32[]{:S(2)}) %collective-permute-start) | collective-permute-done | bytes 163872 | tf_op jit(solution)/shard_map/while/body/eval_jaxpr/ppermute | solution.py:20
  66.7 5.5 %eval_jaxpr.5 = (bf16[32,2560]{1,0:T(8,128)(2,1)}, f32[1,1,128,2560]{3,2,1,0:T(8,128)}, bf16[32,256]{1,0:T(8,128)(2,1)}, bf16[4,1,1,32,2560]{4,3,2,1,0:T(8,128)(2,1)}, bf16[4,1,1,32,256]{4,3,2,1,0:T(8,128)(2,1)S(1)}) custom-call(s32[1]{0:T(128)} %bitcast.102.step_ref, ...), custom_call_target="tpu_custom_call", output_to_operand_aliasing={{1}: (13, {}), {3}: (16, {}), {4}: (17, {})} | custom-call | flops 146800640 | bytes 7536640 | tf_op jit(solution)/shard_map/while/body/eval_jaxpr/pallas_call | solution.py:248
  72.2 1.3 %collective-permute-start = (bf16[1,32,2560]{2,1,0:T(8,128)(2,1)}, bf16[1,32,2560]{2,1,0:T(8,128)(2,1)S(1)}, u32[]{:S(2)}, u32[]{:S(2)}) collective-permute-start(bf16[1,32,2560]{2,1,0:T(8,128)(2,1)} %bitcast.120), channel_id=1, source_target_pairs={{8,0},{16,8},{24,16},{9,1},{17,9},{25,17},{10,2},{18,10},{26,18},{... | collective-permute-start | bytes 491528 | tf_op jit(solution)/shard_map/while/body/eval_jaxpr/ppermute | solution.py:20
  73.5 6.1 %collective-permute-done = bf16[1,32,2560]{2,1,0:T(8,128)(2,1)S(1)} collective-permute-done((bf16[1,32,2560]{2,1,0:T(8,128)(2,1)}, bf16[1,32,2560]{2,1,0:T(8,128)(2,1)S(1)}, u32[]{:S(2)}, u32[]{:S(2)}) %collective-permute-start) | collective-permute-done | bytes 163872 | tf_op jit(solution)/shard_map/while/body/eval_jaxpr/ppermute | solution.py:20
  79.6 5.5 %eval_jaxpr.5 = (bf16[32,2560]{1,0:T(8,128)(2,1)}, f32[1,1,128,2560]{3,2,1,0:T(8,128)}, bf16[32,256]{1,0:T(8,128)(2,1)}, bf16[4,1,1,32,2560]{4,3,2,1,0:T(8,128)(2,1)}, bf16[4,1,1,32,256]{4,3,2,1,0:T(8,128)(2,1)S(1)}) custom-call(s32[1]{0:T(128)} %bitcast.102.step_ref, ...), custom_call_target="tpu_custom_call", output_to_operand_aliasing={{1}: (13, {}), {3}: (16, {}), {4}: (17, {})} | custom-call | flops 146800640 | bytes 7536640 | tf_op jit(solution)/shard_map/while/body/eval_jaxpr/pallas_call | solution.py:248
  85.0 1.3 %collective-permute-start = (bf16[1,32,2560]{2,1,0:T(8,128)(2,1)}, bf16[1,32,2560]{2,1,0:T(8,128)(2,1)S(1)}, u32[]{:S(2)}, u32[]{:S(2)}) collective-permute-start(bf16[1,32,2560]{2,1,0:T(8,128)(2,1)} %bitcast.120), channel_id=1, source_target_pairs={{8,0},{16,8},{24,16},{9,1},{17,9},{25,17},{10,2},{18,10},{26,18},{... | collective-permute-start | bytes 491528 | tf_op jit(solution)/shard_map/while/body/eval_jaxpr/ppermute | solution.py:20
  86.3 6.1 %collective-permute-done = bf16[1,32,2560]{2,1,0:T(8,128)(2,1)S(1)} collective-permute-done((bf16[1,32,2560]{2,1,0:T(8,128)(2,1)}, bf16[1,32,2560]{2,1,0:T(8,128)(2,1)S(1)}, u32[]{:S(2)}, u32[]{:S(2)}) %collective-permute-start) | collective-permute-done | bytes 163872 | tf_op jit(solution)/shard_map/while/body/eval_jaxpr/ppermute | solution.py:20
  92.5 5.5 %eval_jaxpr.5 = (bf16[32,2560]{1,0:T(8,128)(2,1)}, f32[1,1,128,2560]{3,2,1,0:T(8,128)}, bf16[32,256]{1,0:T(8,128)(2,1)}, bf16[4,1,1,32,2560]{4,3,2,1,0:T(8,128)(2,1)}, bf16[4,1,1,32,256]{4,3,2,1,0:T(8,128)(2,1)S(1)}) custom-call(s32[1]{0:T(128)} %bitcast.102.step_ref, ...), custom_call_target="tpu_custom_call", output_to_operand_aliasing={{1}: (13, {}), {3}: (16, {}), {4}: (17, {})} | custom-call | flops 146800640 | bytes 7536640 | tf_op jit(solution)/shard_map/while/body/eval_jaxpr/pallas_call | solution.py:248
  97.9 1.3 %collective-permute-start = (bf16[1,32,2560]{2,1,0:T(8,128)(2,1)}, bf16[1,32,2560]{2,1,0:T(8,128)(2,1)S(1)}, u32[]{:S(2)}, u32[]{:S(2)}) collective-permute-start(bf16[1,32,2560]{2,1,0:T(8,128)(2,1)} %bitcast.120), channel_id=1, source_target_pairs={{8,0},{16,8},{24,16},{9,1},{17,9},{25,17},{10,2},{18,10},{26,18},{... | collective-permute-start | bytes 491528 | tf_op jit(solution)/shard_map/while/body/eval_jaxpr/ppermute | solution.py:20
  99.2 6.1 %collective-permute-done = bf16[1,32,2560]{2,1,0:T(8,128)(2,1)S(1)} collective-permute-done((bf16[1,32,2560]{2,1,0:T(8,128)(2,1)}, bf16[1,32,2560]{2,1,0:T(8,128)(2,1)S(1)}, u32[]{:S(2)}, u32[]{:S(2)}) %collective-permute-start) | collective-permute-done | bytes 163872 | tf_op jit(solution)/shard_map/while/body/eval_jaxpr/ppermute | solution.py:20
  105.4 5.5 %shard_map.59 = (bf16[32,2560]{1,0:T(8,128)(2,1)}, f32[1,1,128,2560]{3,2,1,0:T(8,128)}, bf16[32,256]{1,0:T(8,128)(2,1)}, bf16[4,1,1,32,2560]{4,3,2,1,0:T(8,128)(2,1)}, bf16[4,1,1,32,256]{4,3,2,1,0:T(8,128)(2,1)S(1)}) custom-call(s32[1]{0:T(128)} %constant.45.clone.1.step_ref, ...), custom_call_target="tpu_custom_call", output_to_operand_aliasing={{1}: (13, {}), {3}: (16, {}), {4}: (17, {})} | custom-call | flops 146800640 | bytes 7536640 | tf_op jit(solution)/shard_map/pallas_call | solution.py:248
  110.8 9.8 %all_gather.3 = bf16[8,1,128,256]{3,2,1,0:T(8,128)(2,1)S(1)} all-gather(bf16[1,1,128,256]{3,2,1,0:T(8,128)(2,1)S(1)} %bitcast.111), channel_id=1, replica_groups=mesh['section'=4,'dp'=8] {'dp'}, dimensions={0}, use_global_device_ids=true | all-gather | bytes 589824 | tf_op jit(solution)/shard_map/all_gather | solution.py:392
  120.7 2.1 %fusion.8 = f32[1,320,256]{2,1,0:T(8,128)} fusion(bf16[8,1,128,320]{2,3,1,0:T(8,128)(2,1)} %all-to-all-done, bf16[8,1,128,256]{3,2,1,0:T(8,128)(2,1)S(1)} %all_gather.3), kind=kOutput, calls=%fused_computation.17 | convolution fusion | flops 167854080 | bytes 1507328 | tf_op jit(solution)/shard_map/glrd,glrc->ldc/dot_general | solution.py:393
  (38 shorter events, 3.6 us)
Async XLA Ops:
  0.6 7.5 %copy-start.5 = (f32[1,1,128,40]{2,3,1,0:T(8,128)S(1)}, f32[1,1,128,40]{2,3,1,0:T(8,128)}, u32[]{:S(2)}) copy-start(f32[1,1,128,40]{2,3,1,0:T(8,128)} %param.8) | copy-start | bytes 61444
  2.8 6.4 %copy-start.1 = (bf16[1,1,128,2560]{3,2,1,0:T(8,128)(2,1)S(1)}, bf16[1,1,128,2560]{3,2,1,0:T(8,128)(2,1)}, u32[]{:S(2)}) copy-start(bf16[1,1,128,2560]{3,2,1,0:T(8,128)(2,1)} %param.6) | copy-start | bytes 1966084
  2.8 6.4 %copy-start.2 = (bf16[1,2560,256]{2,1,0:T(8,128)(2,1)S(1)}, bf16[1,2560,256]{2,1,0:T(8,128)(2,1)}, u32[]{:S(2)}) copy-start(bf16[1,2560,256]{2,1,0:T(8,128)(2,1)} %w_ref.1) | copy-start | bytes 3932164
  2.8 117.9 %all-to-all-start = ((bf16[8,1,128,320]{2,3,1,0:T(8,128)(2,1)}), bf16[8,1,128,320]{2,3,1,0:T(8,128)(2,1)}, u32[]{:S(2)}, u32[]{:S(2)}) async-start(bf16[8,1,128,320]{2,3,1,0:T(8,128)(2,1)} %bitcast.29), calls=%async_computation | async-start | bytes 1310720 | tf_op jit(solution)/shard_map/all_to_all | solution.py:390
  9.0 1.6 %copy-start = (f32[4,32,2560]{2,1,0:T(8,128)}, f32[4,32,2560]{2,1,0:T(8,128)S(1)}, u32[]{:S(2)}) copy-start(f32[4,32,2560]{2,1,0:T(8,128)S(1)} %fusion.19) | copy-start | bytes 3932164
  9.2 7.1 %copy-start.3 = (f32[4,2560]{1,0:T(4,128)}, f32[4,2560]{1,0:T(4,128)S(1)}, u32[]{:S(2)}) copy-start(f32[4,2560]{1,0:T(4,128)S(1)} %fusion.16) | copy-start | bytes 122884
  21.6 1.8 %copy-start.4 = (f32[4,2560]{1,0:T(4,128)S(1)}, f32[4,2560]{1,0:T(4,128)}, u32[]{:S(2)}) copy-start(f32[4,2560]{1,0:T(4,128)} %copy-done.3) | copy-start | bytes 122884
  31.4 8.9 %collective-permute-start = (bf16[1,32,2560]{2,1,0:T(8,128)(2,1)}, bf16[1,32,2560]{2,1,0:T(8,128)(2,1)S(1)}, u32[]{:S(2)}, u32[]{:S(2)}) collective-permute-start(bf16[1,32,2560]{2,1,0:T(8,128)(2,1)} %bitcast.120), channel_id=1, source_target_pairs={{8,0},{16,8},{24,16},{9,1},{17,9},{25,17},{10,2},{18,10},{26,18},{... | collective-permute-start | bytes 491528 | tf_op jit(solution)/shard_map/while/body/eval_jaxpr/ppermute | solution.py:20
  45.8 8.0 %collective-permute-start = (bf16[1,32,2560]{2,1,0:T(8,128)(2,1)}, bf16[1,32,2560]{2,1,0:T(8,128)(2,1)S(1)}, u32[]{:S(2)}, u32[]{:S(2)}) collective-permute-start(bf16[1,32,2560]{2,1,0:T(8,128)(2,1)} %bitcast.120), channel_id=1, source_target_pairs={{8,0},{16,8},{24,16},{9,1},{17,9},{25,17},{10,2},{18,10},{26,18},{... | collective-permute-start | bytes 491528 | tf_op jit(solution)/shard_map/while/body/eval_jaxpr/ppermute | solution.py:20
  59.3 7.4 %collective-permute-start = (bf16[1,32,2560]{2,1,0:T(8,128)(2,1)}, bf16[1,32,2560]{2,1,0:T(8,128)(2,1)S(1)}, u32[]{:S(2)}, u32[]{:S(2)}) collective-permute-start(bf16[1,32,2560]{2,1,0:T(8,128)(2,1)} %bitcast.120), channel_id=1, source_target_pairs={{8,0},{16,8},{24,16},{9,1},{17,9},{25,17},{10,2},{18,10},{26,18},{... | collective-permute-start | bytes 491528 | tf_op jit(solution)/shard_map/while/body/eval_jaxpr/ppermute | solution.py:20
  72.2 7.4 %collective-permute-start = (bf16[1,32,2560]{2,1,0:T(8,128)(2,1)}, bf16[1,32,2560]{2,1,0:T(8,128)(2,1)S(1)}, u32[]{:S(2)}, u32[]{:S(2)}) collective-permute-start(bf16[1,32,2560]{2,1,0:T(8,128)(2,1)} %bitcast.120), channel_id=1, source_target_pairs={{8,0},{16,8},{24,16},{9,1},{17,9},{25,17},{10,2},{18,10},{26,18},{... | collective-permute-start | bytes 491528 | tf_op jit(solution)/shard_map/while/body/eval_jaxpr/ppermute | solution.py:20
  85.0 7.4 %collective-permute-start = (bf16[1,32,2560]{2,1,0:T(8,128)(2,1)}, bf16[1,32,2560]{2,1,0:T(8,128)(2,1)S(1)}, u32[]{:S(2)}, u32[]{:S(2)}) collective-permute-start(bf16[1,32,2560]{2,1,0:T(8,128)(2,1)} %bitcast.120), channel_id=1, source_target_pairs={{8,0},{16,8},{24,16},{9,1},{17,9},{25,17},{10,2},{18,10},{26,18},{... | collective-permute-start | bytes 491528 | tf_op jit(solution)/shard_map/while/body/eval_jaxpr/ppermute | solution.py:20
  97.9 7.4 %collective-permute-start = (bf16[1,32,2560]{2,1,0:T(8,128)(2,1)}, bf16[1,32,2560]{2,1,0:T(8,128)(2,1)S(1)}, u32[]{:S(2)}, u32[]{:S(2)}) collective-permute-start(bf16[1,32,2560]{2,1,0:T(8,128)(2,1)} %bitcast.120), channel_id=1, source_target_pairs={{8,0},{16,8},{24,16},{9,1},{17,9},{25,17},{10,2},{18,10},{26,18},{... | collective-permute-start | bytes 491528 | tf_op jit(solution)/shard_map/while/body/eval_jaxpr/ppermute | solution.py:20

commit v12 on v11

--- a/solution.py
+++ b/solution.py
@@ -376,17 +376,23 @@
         jnp.zeros((MICRO, lay_dev, seq_dev, block_len, features), jnp.bfloat16),
         jnp.zeros((MICRO, lay_dev, seq_dev, block_len, 2 * state_size), jnp.bfloat16),
     )
-    final_state = lax.fori_loop(0, steps - 1, advance, initial)
-    final_state = advance(steps - 1, final_state, send=False)
+    ways = lax.axis_size("dp")
+    rows_here = layer_inputs.reshape(lay_dev, seq_dev * tok_len, ways, features // ways)
+    rows_here = jnp.transpose(rows_here, (2, 0, 1, 3))
+    final_state = initial
+    for counter in range(steps):
+        final_state = advance(
+            jnp.full((), counter, jnp.int32), final_state, send=counter < steps - 1
+        )
+        if counter == min(1, steps - 1):
+            rows_here, held = lax.optimization_barrier((rows_here, final_state[1]))
+            final_state = (final_state[0], held) + final_state[2:]
     grad_store = final_state[2]
     map_store = final_state[3]
 
     grad_inputs = jnp.moveaxis(grad_store, 0, 2).reshape(layer_inputs.shape)
     map_store = jnp.moveaxis(map_store, 0, 2).reshape(bc_all.shape)
-    ways = lax.axis_size("dp")
     divisor = ways * seq_dev
-    rows_here = layer_inputs.reshape(lay_dev, seq_dev * tok_len, ways, features // ways)
-    rows_here = jnp.transpose(rows_here, (2, 0, 1, 3))
     rows_all = lax.all_to_all(rows_here, "dp", 0, 0, tiled=True)
     maps_here = map_store.reshape(1, lay_dev, seq_dev * tok_len, map_store.shape[-1])
     maps_all = lax.all_gather(maps_here, "dp", axis=0, tiled=True)

time: 123 us -> 127 us (1.033)
  local copies, waits for them, and re-layouts: 5.46 us -> 11.7 us
  waiting for transfers between devices: 38.8 us -> 33.7 us
  Pallas kernels: 38.3 us -> 40.8 us
  starting transfers between devices: 13.1 us -> 11.6 us
    ppermute x6, waiting for transfers between devices: 38.8 us -> 33.7 us  [passed_along(): return lax.ppermute(block, axis, route)]
    unnamed x13 -> x21, local copies, waits for them, and re-layouts: 2.18 us -> 5.11 us
    pallas_call x7, Pallas kernels: 38.3 us -> 40.8 us  [fused_step(): pl.pallas_call(functools.partial(step_kernel, factor=factor, width=width,...]
    all_to_all x1, starting transfers between devices: 5.3 us -> 3.84 us  [shards(): rows_all = lax.all_to_all(rows_here, 'dp', 0, 0, tiled=True)]
  transfers between devices with their start and end apart: 7 -> 7, of which waited for: 6 -> 6; matrix products, arithmetic and copies ran while one was open for 14% -> 1% of each run, Pallas kernels for 31% -> 14%
where the time goes in v12:
time: 127 us
  Pallas kernels  40.8 us (32%)
  waiting for transfers between devices  33.7 us (27%)
  local copies, waits for them, and re-layouts  11.7 us (9%)
  starting transfers between devices  11.6 us (9%)
  blocking collectives  10.3 us (8%)
  other arithmetic  9.14 us (7%)
  matrix products  8.45 us (7%)
    pallas_call x7, Pallas kernels, fused_step(): pl.pallas_call(functools.partial(step_kernel, factor=factor, width=width,...  40.8 us
    ppermute x6, waiting for transfers between devices, passed_along(): return lax.ppermute(block, axis, route)  33.7 us
    all_gather x1, blocking collectives, shards(): maps_all = lax.all_gather(maps_here, 'dp', axis=0, tiled=True)  10.3 us
    ppermute x6, starting transfers between devices, passed_along(): return lax.ppermute(block, axis, route)  7.75 us
    unnamed x21, local copies, waits for them, and re-layouts  5.11 us
    all_to_all x1, starting transfers between devices, shards(): rows_all = lax.all_to_all(rows_here, 'dp', 0, 0, tiled=True)  3.84 us
    dot_general x1, matrix products, shards(): jnp.einsum('mlsjn,mlsjd->mlsnd', in_blk, xt_full, preferred_element_type=...  3.19 us
    dot_general x3, matrix products, per_lane(): jnp.einsum('...h,hd->...d', a, spread_heads, precision=lax.Precision.HIGH...  2.65 us
  transfers between devices with their start and end apart: 7, of which 6 were waited for; matrix products, arithmetic and copies ran while one was open for 1% of the time, Pallas kernels for 14%

profile of v12, /device:TPU:0, one launch (start us, length us, event | category | flops | bytes accessed | tf_op | source)
XLA Modules:
  0.0 126.6 jit_solution(626519103238135698)
XLA Ops:
  3.3 1.4 %fusion.9 = bf16[128,256]{1,0:T(8,128)(2,1)S(1)} fusion(bf16[1,2560,256]{2,1,0:T(8,128)(2,1)S(1)} %copy-done.1, bf16[1,1,128,2560]{3,2,1,0:T(8,128)(2,1)} %param.4), kind=kOutput, calls=%fused_computation.18 | convolution fusion | flops 167804928 | bytes 2031616 | tf_op jit(solution)/shard_map/lstd,ldc->lstc/dot_general | solution.py:290
  4.8 1.0 fusion.44.xt_ref
  5.8 3.2 %fusion.29 = f32[4,128,2560]{2,1,0:T(8,128)} fusion(bf16[4,1,1,32,256]{4,3,2,1,0:T(8,128)(2,1)S(1)} %bitcast.136, f32[4,32,2560]{2,1,0:T(8,128)S(1)} %fusion.19, bf16[4,32,2560]{2,1,0:T(8,128)(2,1)S(1)} %bitcast.124), kind=kOutput, calls=%fused_computation.36 | convolution fusion | flops 84869120 | bytes 7241728 | tf_op jit(solution)/shard_map/mlsjn,mlsjd->mlsnd/dot_general | solution.py:330
  9.1 1.7 %convolution_bitcast_fusion.lead_ref = f32[4,1,1,32,2560]{4,3,2,1,0:T(8,128)} fusion(s32[2560]{0:T(1024)S(1)} %add_select_fusion, f32[4,1,1,32,40]{4,3,2,1,0:T(8,128)S(1)} %reduce_window_sum.11), kind=kOutput, calls=%fused_computation | convolution fusion | flops 157388800 | bytes 1341440 | tf_op jit(solution)/shard_map/...h,hd->...d/dot_general | solution.py:320
  11.7 1.9 %exponential_select_fusion = f32[4,1,1,32,32,40]{4,3,5,0,2,1:T(8,128)} fusion(f32[4,32,40]{1,2,0:T(8,128)S(1)} %copy.45, pred[32,32]{1,0:T(8,128)(4,1)S(1)} %iota_compare_fusion.2), kind=kLoop, calls=%fused_computation.2 | loop fusion | flops 491520 | bytes 676864 | tf_op jit(solution)/shard_map/vmap(vmap(vmap(jit(_where))))/select_n | solution.py:119
  13.6 1.7 %multiply_convert_fusion.wt_ref = bf16[4,1,1,40,32,32]{5,4,3,2,1,0:T(8,128)(2,1)} fusion(f32[4,32,32]{2,1,0:T(8,128)S(1)} %convolution_multiply_fusion, f32[4,40,32]{2,1,0:T(8,128)S(1)} %copy.43, pred[32,32]{1,0:T(8,128)(4,1)S(1)} %iota_compare_fusion.3), kind=kLoop, calls=%fused_computation.3 | loop fusion | flops 819200 | bytes 365568 | tf_op jit(solution)/shard_map/vmap(vmap(vmap()))/convert_element_type | solution.py:128
  15.3 2.5 %fusion.21 = (bf16[1,1,1,128,2560]{4,3,2,1,0:T(8,128)(2,1)S(1)}, bf16[1,1,1,128,2560]{4,3,2,1,0:T(8,128)(2,1)S(1)}, bf16[1,1,1,128,2560]{4,3,2,1,0:T(8,128)(2,1)S(1)}) fusion(f32[4,128,2560]{2,1,0:T(8,128)} %fusion.29, f32[2560]{0:T(1024)S(1)} %get-tuple-element.80, f32[2560]{0:T(1024)S(1)} %get-tuple-element.78, f32[2560]{0:T(1024)S(1)} %get-tuple-element.79), kind=kLoop, calls=%fused_computation.28 | loop fusion | flops 2621440 | bytes 5928960 | tf_op jit(solution)/shard_map/convert_element_type | solution.py:336
  17.8 1.8 %pad_maximum_fusion.sb_ref = bf16[4,1,1,128,2560]{4,3,2,1,0:T(8,128)(2,1)} fusion(bf16[1,1,1,128,2560]{4,3,2,1,0:T(8,128)(2,1)S(1)} %get-tuple-element.82, bf16[1,1,1,128,2560]{4,3,2,1,0:T(8,128)(2,1)S(1)} %get-tuple-element.81, bf16[1,1,1,128,2560]{4,3,2,1,0:T(8,128)(2,1)S(1)} %get-tuple-element.83, bf16[4]{0:T(256)(128)(2,1)S(1)} %pad.clone), kind=kLoop, calls=%fused_computation.1 | loop fusion | flops 3932160 | bytes 4587528 | tf_op jit(solution)/shard_map/stack | solution.py:338
  20.4 1.2 broadcast_7_r_ref.2.r_ref
  23.8 5.8 %shard_map.59 = (bf16[32,2560]{1,0:T(8,128)(2,1)}, f32[1,1,128,2560]{3,2,1,0:T(8,128)}, bf16[32,256]{1,0:T(8,128)(2,1)}, bf16[4,1,1,32,2560]{4,3,2,1,0:T(8,128)(2,1)}, bf16[4,1,1,32,256]{4,3,2,1,0:T(8,128)(2,1)}) custom-call(s32[1]{0:T(128)} %constant.58.clone.1.step_ref, ...), custom_call_target="tpu_custom_call", output_to_operand_aliasing={{1}: (13, {}), {3}: (16, {}), {4}: (17, {})} | custom-call | flops 146800640 | bytes 7536640 | tf_op jit(solution)/shard_map/pallas_call | solution.py:248
  29.7 1.3 %collective-permute-start = (bf16[1,32,2560]{2,1,0:T(8,128)(2,1)}, bf16[1,32,2560]{2,1,0:T(8,128)(2,1)S(1)}, u32[]{:S(2)}, u32[]{:S(2)}) collective-permute-start(bf16[1,32,2560]{2,1,0:T(8,128)(2,1)} %bitcast.144), channel_id=1, source_target_pairs={{8,0},{16,8},{24,16},{9,1},{17,9},{25,17},{10,2},{18,10},{26,18},{... | collective-permute-start | bytes 491528 | tf_op jit(solution)/shard_map/ppermute | solution.py:20
  31.0 8.0 %collective-permute-done.inc_ref = bf16[1,32,2560]{2,1,0:T(8,128)(2,1)S(1)} collective-permute-done((bf16[1,32,2560]{2,1,0:T(8,128)(2,1)}, bf16[1,32,2560]{2,1,0:T(8,128)(2,1)S(1)}, u32[]{:S(2)}, u32[]{:S(2)}) %collective-permute-start) | collective-permute-done | bytes 163872 | tf_op jit(solution)/shard_map/ppermute | solution.py:20
  39.7 6.0 %shard_map.60 = (bf16[32,2560]{1,0:T(8,128)(2,1)}, f32[1,1,128,2560]{3,2,1,0:T(8,128)}, bf16[32,256]{1,0:T(8,128)(2,1)}, bf16[4,1,1,32,2560]{4,3,2,1,0:T(8,128)(2,1)}, bf16[4,1,1,32,256]{4,3,2,1,0:T(8,128)(2,1)}) custom-call(s32[1]{0:T(128)} %constant.57.clone.1.step_ref, ...), custom_call_target="tpu_custom_call", output_to_operand_aliasing={{1}: (13, {}), {3}: (16, {}), {4}: (17, {})} | custom-call | flops 146800640 | bytes 7536640 | tf_op jit(solution)/shard_map/pallas_call | solution.py:248
  45.6 1.3 %collective-permute-start.1 = (bf16[1,32,2560]{2,1,0:T(8,128)(2,1)}, bf16[1,32,2560]{2,1,0:T(8,128)(2,1)S(1)}, u32[]{:S(2)}, u32[]{:S(2)}) collective-permute-start(bf16[1,32,2560]{2,1,0:T(8,128)(2,1)} %bitcast.143), channel_id=1, source_target_pairs={{8,0},{16,8},{24,16},{9,1},{17,9},{25,17},{10,2},{18,10},{26,18},{... | collective-permute-start | bytes 491528 | tf_op jit(solution)/shard_map/ppermute | solution.py:20
  46.9 1.1 copy.47
  48.0 5.1 %collective-permute-done.1.inc_ref = bf16[1,32,2560]{2,1,0:T(8,128)(2,1)S(1)} collective-permute-done((bf16[1,32,2560]{2,1,0:T(8,128)(2,1)}, bf16[1,32,2560]{2,1,0:T(8,128)(2,1)S(1)}, u32[]{:S(2)}, u32[]{:S(2)}) %collective-permute-start.1) | collective-permute-done | bytes 163872 | tf_op jit(solution)/shard_map/ppermute | solution.py:20
  53.8 5.8 %shard_map.61 = (bf16[32,2560]{1,0:T(8,128)(2,1)}, f32[1,1,128,2560]{3,2,1,0:T(8,128)}, bf16[32,256]{1,0:T(8,128)(2,1)}, bf16[4,1,1,32,2560]{4,3,2,1,0:T(8,128)(2,1)}, bf16[4,1,1,32,256]{4,3,2,1,0:T(8,128)(2,1)}) custom-call(s32[1]{0:T(128)} %constant.56.clone.1.step_ref, ...), custom_call_target="tpu_custom_call", output_to_operand_aliasing={{1}: (13, {}), {3}: (16, {}), {4}: (17, {})} | custom-call | flops 146800640 | bytes 7536640 | tf_op jit(solution)/shard_map/pallas_call | solution.py:248
  59.6 1.3 %collective-permute-start.2 = (bf16[1,32,2560]{2,1,0:T(8,128)(2,1)}, bf16[1,32,2560]{2,1,0:T(8,128)(2,1)S(1)}, u32[]{:S(2)}, u32[]{:S(2)}) collective-permute-start(bf16[1,32,2560]{2,1,0:T(8,128)(2,1)} %bitcast.145), channel_id=1, source_target_pairs={{8,0},{16,8},{24,16},{9,1},{17,9},{25,17},{10,2},{18,10},{26,18},{... | collective-permute-start | bytes 491528 | tf_op jit(solution)/shard_map/ppermute | solution.py:20
  60.9 6.1 %collective-permute-done.2.inc_ref = bf16[1,32,2560]{2,1,0:T(8,128)(2,1)S(1)} collective-permute-done((bf16[1,32,2560]{2,1,0:T(8,128)(2,1)}, bf16[1,32,2560]{2,1,0:T(8,128)(2,1)S(1)}, u32[]{:S(2)}, u32[]{:S(2)}) %collective-permute-start.2) | collective-permute-done | bytes 163872 | tf_op jit(solution)/shard_map/ppermute | solution.py:20
  67.7 5.8 %shard_map.62 = (bf16[32,2560]{1,0:T(8,128)(2,1)}, f32[1,1,128,2560]{3,2,1,0:T(8,128)}, bf16[32,256]{1,0:T(8,128)(2,1)}, bf16[4,1,1,32,2560]{4,3,2,1,0:T(8,128)(2,1)}, bf16[4,1,1,32,256]{4,3,2,1,0:T(8,128)(2,1)}) custom-call(s32[1]{0:T(128)} %constant.55.clone.1.step_ref, ...), custom_call_target="tpu_custom_call", output_to_operand_aliasing={{1}: (13, {}), {3}: (16, {}), {4}: (17, {})} | custom-call | flops 146800640 | bytes 7536640 | tf_op jit(solution)/shard_map/pallas_call | solution.py:248
  73.5 1.3 %collective-permute-start.3 = (bf16[1,32,2560]{2,1,0:T(8,128)(2,1)}, bf16[1,32,2560]{2,1,0:T(8,128)(2,1)S(1)}, u32[]{:S(2)}, u32[]{:S(2)}) collective-permute-start(bf16[1,32,2560]{2,1,0:T(8,128)(2,1)} %bitcast.142), channel_id=1, source_target_pairs={{8,0},{16,8},{24,16},{9,1},{17,9},{25,17},{10,2},{18,10},{26,18},{... | collective-permute-start | bytes 491528 | tf_op jit(solution)/shard_map/ppermute | solution.py:20
  74.8 3.8 %all-to-all-start = ((bf16[8,1,128,320]{2,3,1,0:T(8,128)(2,1)}), bf16[8,1,128,320]{2,3,1,0:T(8,128)(2,1)S(1)}, u32[]{:S(2)}, u32[]{:S(2)}) async-start(bf16[8,1,128,320]{2,3,1,0:T(8,128)(2,1)} %bitcast.26), calls=%async_computation | async-start | bytes 1310720 | tf_op jit(solution)/shard_map/all_to_all | solution.py:396
  78.6 2.3 %collective-permute-done.3.inc_ref = bf16[1,32,2560]{2,1,0:T(8,128)(2,1)S(1)} collective-permute-done((bf16[1,32,2560]{2,1,0:T(8,128)(2,1)}, bf16[1,32,2560]{2,1,0:T(8,128)(2,1)S(1)}, u32[]{:S(2)}, u32[]{:S(2)}) %collective-permute-start.3) | collective-permute-done | bytes 163872 | tf_op jit(solution)/shard_map/ppermute | solution.py:20
  81.6 5.8 %shard_map.63 = (bf16[32,2560]{1,0:T(8,128)(2,1)}, f32[1,1,128,2560]{3,2,1,0:T(8,128)}, bf16[32,256]{1,0:T(8,128)(2,1)}, bf16[4,1,1,32,2560]{4,3,2,1,0:T(8,128)(2,1)}, bf16[4,1,1,32,256]{4,3,2,1,0:T(8,128)(2,1)}) custom-call(s32[1]{0:T(128)} %constant.54.clone.1.step_ref, ...), custom_call_target="tpu_custom_call", output_to_operand_aliasing={{1}: (13, {}), {3}: (16, {}), {4}: (17, {})} | custom-call | flops 146800640 | bytes 7536640 | tf_op jit(solution)/shard_map/pallas_call | solution.py:248
  87.4 1.3 %collective-permute-start.4 = (bf16[1,32,2560]{2,1,0:T(8,128)(2,1)}, bf16[1,32,2560]{2,1,0:T(8,128)(2,1)S(1)}, u32[]{:S(2)}, u32[]{:S(2)}) collective-permute-start(bf16[1,32,2560]{2,1,0:T(8,128)(2,1)} %bitcast.146), channel_id=1, source_target_pairs={{8,0},{16,8},{24,16},{9,1},{17,9},{25,17},{10,2},{18,10},{26,18},{... | collective-permute-start | bytes 491528 | tf_op jit(solution)/shard_map/ppermute | solution.py:20
  88.7 6.1 %collective-permute-done.4.inc_ref = bf16[1,32,2560]{2,1,0:T(8,128)(2,1)S(1)} collective-permute-done((bf16[1,32,2560]{2,1,0:T(8,128)(2,1)}, bf16[1,32,2560]{2,1,0:T(8,128)(2,1)S(1)}, u32[]{:S(2)}, u32[]{:S(2)}) %collective-permute-start.4) | collective-permute-done | bytes 163872 | tf_op jit(solution)/shard_map/ppermute | solution.py:20
  95.5 5.8 %shard_map.64 = (bf16[32,2560]{1,0:T(8,128)(2,1)}, f32[1,1,128,2560]{3,2,1,0:T(8,128)}, bf16[32,256]{1,0:T(8,128)(2,1)}, bf16[4,1,1,32,2560]{4,3,2,1,0:T(8,128)(2,1)}, bf16[4,1,1,32,256]{4,3,2,1,0:T(8,128)(2,1)}) custom-call(s32[1]{0:T(128)} %constant.53.clone.1.step_ref, ...), custom_call_target="tpu_custom_call", output_to_operand_aliasing={{1}: (13, {}), {3}: (16, {}), {4}: (17, {})} | custom-call | flops 146800640 | bytes 7536640 | tf_op jit(solution)/shard_map/pallas_call | solution.py:248
  101.3 1.3 %collective-permute-start.5 = (bf16[1,32,2560]{2,1,0:T(8,128)(2,1)}, bf16[1,32,2560]{2,1,0:T(8,128)(2,1)S(1)}, u32[]{:S(2)}, u32[]{:S(2)}) collective-permute-start(bf16[1,32,2560]{2,1,0:T(8,128)(2,1)} %bitcast.147), channel_id=1, source_target_pairs={{8,0},{16,8},{24,16},{9,1},{17,9},{25,17},{10,2},{18,10},{26,18},{... | collective-permute-start | bytes 491528 | tf_op jit(solution)/shard_map/ppermute | solution.py:20
  102.6 6.1 %collective-permute-done.5.inc_ref = bf16[1,32,2560]{2,1,0:T(8,128)(2,1)S(1)} collective-permute-done((bf16[1,32,2560]{2,1,0:T(8,128)(2,1)}, bf16[1,32,2560]{2,1,0:T(8,128)(2,1)S(1)}, u32[]{:S(2)}, u32[]{:S(2)}) %collective-permute-start.5) | collective-permute-done | bytes 163872 | tf_op jit(solution)/shard_map/ppermute | solution.py:20
  109.4 5.8 %shard_map.65 = (bf16[32,2560]{1,0:T(8,128)(2,1)}, f32[1,1,128,2560]{3,2,1,0:T(8,128)}, bf16[32,256]{1,0:T(8,128)(2,1)}, bf16[4,1,1,32,2560]{4,3,2,1,0:T(8,128)(2,1)}, bf16[4,1,1,32,256]{4,3,2,1,0:T(8,128)(2,1)}) custom-call(s32[1]{0:T(128)} %constant.19.clone.1.step_ref, ...), custom_call_target="tpu_custom_call", output_to_operand_aliasing={{1}: (13, {}), {3}: (16, {}), {4}: (17, {})} | custom-call | flops 146800640 | bytes 7536640 | tf_op jit(solution)/shard_map/pallas_call | solution.py:248
  115.2 10.3 %all_gather.3 = bf16[8,1,128,256]{3,2,1,0:T(8,128)(2,1)S(1)} all-gather(bf16[1,1,128,256]{3,2,1,0:T(8,128)(2,1)} %bitcast.133), channel_id=1, replica_groups=mesh['section'=4,'dp'=8] {'dp'}, dimensions={0}, use_global_device_ids=true | all-gather | bytes 589824 | tf_op jit(solution)/shard_map/all_gather | solution.py:398
  125.5 1.1 fusion.8
  (45 shorter events, 10.7 us)
Async XLA Ops:
  0.6 2.7 %copy-start.1 = (bf16[1,2560,256]{2,1,0:T(8,128)(2,1)S(1)}, bf16[1,2560,256]{2,1,0:T(8,128)(2,1)}, u32[]{:S(2)}) copy-start(bf16[1,2560,256]{2,1,0:T(8,128)(2,1)} %w_ref.13) | copy-start | bytes 3932164
  2.3 3.4 %copy-start = (f32[4,32,2560]{2,1,0:T(8,128)}, f32[4,32,2560]{2,1,0:T(8,128)S(1)}, u32[]{:S(2)}) copy-start(f32[4,32,2560]{2,1,0:T(8,128)S(1)} %fusion.19) | copy-start | bytes 3932164
  2.4 2.4 %copy-start.2 = (bf16[1,1,128,2560]{3,2,1,0:T(8,128)(2,1)S(1)}, bf16[1,1,128,2560]{3,2,1,0:T(8,128)(2,1)}, u32[]{:S(2)}) copy-start(bf16[1,1,128,2560]{3,2,1,0:T(8,128)(2,1)} %param.4) | copy-start | bytes 1966084
  29.7 9.3 %collective-permute-start = (bf16[1,32,2560]{2,1,0:T(8,128)(2,1)}, bf16[1,32,2560]{2,1,0:T(8,128)(2,1)S(1)}, u32[]{:S(2)}, u32[]{:S(2)}) collective-permute-start(bf16[1,32,2560]{2,1,0:T(8,128)(2,1)} %bitcast.144), channel_id=1, source_target_pairs={{8,0},{16,8},{24,16},{9,1},{17,9},{25,17},{10,2},{18,10},{26,18},{... | collective-permute-start | bytes 491528 | tf_op jit(solution)/shard_map/ppermute | solution.py:20
  39.0 0.7 copy-start.7
  39.7 7.3 %copy-start.3 = (bf16[1,1,128,2560]{3,2,1,0:T(8,128)(2,1)S(1)}, bf16[1,1,128,2560]{3,2,1,0:T(8,128)(2,1)}, u32[]{:S(2)}) copy-start(bf16[1,1,128,2560]{3,2,1,0:T(8,128)(2,1)} %param.4) | copy-start | bytes 1966084
  45.6 7.5 %collective-permute-start.1 = (bf16[1,32,2560]{2,1,0:T(8,128)(2,1)}, bf16[1,32,2560]{2,1,0:T(8,128)(2,1)S(1)}, u32[]{:S(2)}, u32[]{:S(2)}) collective-permute-start(bf16[1,32,2560]{2,1,0:T(8,128)(2,1)} %bitcast.143), channel_id=1, source_target_pairs={{8,0},{16,8},{24,16},{9,1},{17,9},{25,17},{10,2},{18,10},{26,18},{... | collective-permute-start | bytes 491528 | tf_op jit(solution)/shard_map/ppermute | solution.py:20
  53.1 0.7 copy-start.6
  59.6 7.4 %collective-permute-start.2 = (bf16[1,32,2560]{2,1,0:T(8,128)(2,1)}, bf16[1,32,2560]{2,1,0:T(8,128)(2,1)S(1)}, u32[]{:S(2)}, u32[]{:S(2)}) collective-permute-start(bf16[1,32,2560]{2,1,0:T(8,128)(2,1)} %bitcast.145), channel_id=1, source_target_pairs={{8,0},{16,8},{24,16},{9,1},{17,9},{25,17},{10,2},{18,10},{26,18},{... | collective-permute-start | bytes 491528 | tf_op jit(solution)/shard_map/ppermute | solution.py:20
  67.0 0.7 copy-start.8
  73.5 7.4 %collective-permute-start.3 = (bf16[1,32,2560]{2,1,0:T(8,128)(2,1)}, bf16[1,32,2560]{2,1,0:T(8,128)(2,1)S(1)}, u32[]{:S(2)}, u32[]{:S(2)}) collective-permute-start(bf16[1,32,2560]{2,1,0:T(8,128)(2,1)} %bitcast.142), channel_id=1, source_target_pairs={{8,0},{16,8},{24,16},{9,1},{17,9},{25,17},{10,2},{18,10},{26,18},{... | collective-permute-start | bytes 491528 | tf_op jit(solution)/shard_map/ppermute | solution.py:20
  74.8 50.7 %all-to-all-start = ((bf16[8,1,128,320]{2,3,1,0:T(8,128)(2,1)}), bf16[8,1,128,320]{2,3,1,0:T(8,128)(2,1)S(1)}, u32[]{:S(2)}, u32[]{:S(2)}) async-start(bf16[8,1,128,320]{2,3,1,0:T(8,128)(2,1)} %bitcast.26), calls=%async_computation | async-start | bytes 1310720 | tf_op jit(solution)/shard_map/all_to_all | solution.py:396
  80.9 0.7 copy-start.5
  87.4 7.4 %collective-permute-start.4 = (bf16[1,32,2560]{2,1,0:T(8,128)(2,1)}, bf16[1,32,2560]{2,1,0:T(8,128)(2,1)S(1)}, u32[]{:S(2)}, u32[]{:S(2)}) collective-permute-start(bf16[1,32,2560]{2,1,0:T(8,128)(2,1)} %bitcast.146), channel_id=1, source_target_pairs={{8,0},{16,8},{24,16},{9,1},{17,9},{25,17},{10,2},{18,10},{26,18},{... | collective-permute-start | bytes 491528 | tf_op jit(solution)/shard_map/ppermute | solution.py:20
  94.8 0.7 copy-start.9
  101.3 7.4 %collective-permute-start.5 = (bf16[1,32,2560]{2,1,0:T(8,128)(2,1)}, bf16[1,32,2560]{2,1,0:T(8,128)(2,1)S(1)}, u32[]{:S(2)}, u32[]{:S(2)}) collective-permute-start(bf16[1,32,2560]{2,1,0:T(8,128)(2,1)} %bitcast.147), channel_id=1, source_target_pairs={{8,0},{16,8},{24,16},{9,1},{17,9},{25,17},{10,2},{18,10},{26,18},{... | collective-permute-start | bytes 491528 | tf_op jit(solution)/shard_map/ppermute | solution.py:20
  108.8 0.7 copy-start.4

commit v13 on v11

--- a/solution.py
+++ b/solution.py
@@ -137,7 +137,7 @@
 
 def step_kernel(
     step_ref, tab_ref, wt_ref, dec_ref, inc_ref, top_ref, x_ref, b_ref, c_ref, tail_ref, lead_ref, xt_ref,
-    sb_ref, r_ref, end_ref, w_ref, gs_ref, ms_ref, out_ref, rnew_ref, dbc_ref, gstore_ref, mstore_ref,
+    sb_ref, r_ref, end_ref, w_ref, gs_ref, ms_ref, out_ref, dbc_ref, gstore_ref, mstore_ref,
     v_ref, gx_ref, tail_buf, lead_buf, xt_buf, sb_buf, r_buf, w_buf, sems, *, factor, width,
     level_pos, levels, level_no, seq_no
 ):
@@ -203,8 +203,6 @@
         jnp.dot(mixing, in_map, preferred_element_type=f32)
         + lax.dot_general(lead_grads, sb_buf[...], nt, preferred_element_type=f32)
     )
-    carry = factor * lax.dot_general(out_map, lead_grads, tn, preferred_element_type=f32)
-    rnew_ref[...] = carry + end_ref[...] * r_buf[...]
     grad_bc = jnp.concatenate([grad_inmap, grad_outmap], axis=1).astype(bf16)
     dbc_ref[...] = grad_bc
     mstore_ref[...] = jnp.where(tab_ref[base + 2] > 0, grad_bc, ms_ref[...])
@@ -213,6 +211,20 @@
     summed = (v.astype(f32) + gx_ref[...] + back).astype(out_ref.dtype)
     out_ref[...] = summed
     gstore_ref[...] = jnp.where(tab_ref[base + 2] > 0, summed, gs_ref[...])
+
+
+def carry_kernel(
+    step_ref, tab_ref, inc_ref, top_ref, c_ref, lead_ref, end_ref, r_ref, rnew_ref, *, factor,
+    level_pos, levels
+):
+    base = (step_ref[0] * levels + level_pos) * 3
+    tn = (((0,), (0,)), ((), ()))
+    v = jnp.where(tab_ref[base + 1] > 0, top_ref[...], inc_ref[...])
+    lead_grads = (lead_ref[...] * v.astype(jnp.float32)).astype(jnp.bfloat16)
+    carry = factor * lax.dot_general(
+        c_ref[...], lead_grads, tn, preferred_element_type=jnp.float32
+    )
+    rnew_ref[...] = carry + end_ref[...] * r_ref[...]
 
 
 def fused_step(step_arr, table, level_pos, levels, per_block, incoming, top_blk, carried, w_bc, grad_store, map_store, level_no, seq_no, factor, width):
@@ -238,21 +250,19 @@
     in_specs += [store_g, store_m]
     out_specs = (
         pl.BlockSpec((length, features), lambda i, c, t: (0, 0)),
-        pl.BlockSpec((None, None) + carried.shape[2:], lambda i, c, t: (level_no, seq_no, 0, 0)),
         pl.BlockSpec((length, 2 * state_size), lambda i, c, t: (0, 0)),
         store_g,
         store_m,
     )
     flops = 2 * length * features * (6 * state_size + 4 * length)
     moved = 2 * (4 * features * state_size * 2 + 6 * length * features) + 4 * 4 * length * features
-    return pl.pallas_call(
+    outs = pl.pallas_call(
         functools.partial(
             step_kernel, factor=factor, width=width, level_pos=level_pos, levels=levels,
             level_no=level_no, seq_no=seq_no,
         ),
         out_shape=(
             jax.ShapeDtypeStruct((length, features), jnp.bfloat16),
-            jax.ShapeDtypeStruct(carried.shape, jnp.float32),
             jax.ShapeDtypeStruct((length, 2 * state_size), jnp.bfloat16),
             jax.ShapeDtypeStruct(grad_store.shape, grad_store.dtype),
             jax.ShapeDtypeStruct(map_store.shape, map_store.dtype),
@@ -274,9 +284,34 @@
                 pltpu.SemaphoreType.DMA((6,)),
             ],
         ),
-        input_output_aliases={13: 1, 16: 3, 17: 4},
+        input_output_aliases={16: 2, 17: 3},
         cost_estimate=pl.CostEstimate(flops=flops, bytes_accessed=moved, transcendentals=0),
     )(step_arr, table, wt2, dec2, incoming, top_blk, x_flat, in_blk, out_blk, tail_full, lead_full, xt_full, states_t, carried, end_row, w_bc, grad_store, map_store)
+    carry_specs = [
+        pl.BlockSpec((None, length, features), lambda i, c, t: (seq_no, 0, 0)),
+        pl.BlockSpec((None, None, length, features), lambda i, c, t: (t[(c[0] * levels + level_pos) * 3], seq_no, 0, 0)),
+        lead_block(out_blk),
+        lead_block(lead_full),
+        lead_block(end_row),
+        pl.BlockSpec((None, None) + carried.shape[2:], lambda i, c, t: (level_no, seq_no, 0, 0)),
+    ]
+    carried = pl.pallas_call(
+        functools.partial(carry_kernel, factor=factor, level_pos=level_pos, levels=levels),
+        out_shape=jax.ShapeDtypeStruct(carried.shape, jnp.float32),
+        grid_spec=pltpu.PrefetchScalarGridSpec(
+            num_scalar_prefetch=2,
+            grid=(1,),
+            in_specs=carry_specs,
+            out_specs=carry_specs[-1],
+        ),
+        input_output_aliases={7: 0},
+        cost_estimate=pl.CostEstimate(
+            flops=2 * length * features * state_size,
+            bytes_accessed=8 * features * state_size + 10 * length * features,
+            transcendentals=0,
+        ),
+    )(step_arr, table, incoming, top_blk, out_blk, lead_full, end_row, carried)
+    return (outs[0], carried, outs[1], outs[2], outs[3])
 
 
 def shards(layer_inputs, w_bc, log_decay, top_grad):

time: 123 us -> 130 us (1.057)
  waiting for transfers between devices: 38.8 us -> 32.8 us
  Pallas kernels: 38.3 us -> 43.7 us
  local copies, waits for them, and re-layouts: 5.46 us -> 9.91 us
    pallas_call x0 -> x6, Pallas kernels: none -> 6.63 us  [fused_step(): pl.pallas_call(functools.partial(carry_kernel, factor=factor, level_pos=l...]
    ppermute x6, waiting for transfers between devices: 38.8 us -> 32.8 us  [passed_along(): return lax.ppermute(block, axis, route)]
    while x0 -> x6, local copies, waits for them, and re-layouts: none -> 5.5 us
    dot_general x1, matrix products: 0.34 us -> 1.87 us  [shards(): jnp.einsum('lstd,ldc->lstc', layer_inputs, w_bc, preferred_element_type=j...]
  transfers between devices with their start and end apart: 7 -> 7, of which waited for: 6 -> 6; matrix products, arithmetic and copies ran while one was open for 14% -> 18% of each run, Pallas kernels for 31% -> 34%
where the time goes in v13:
time: 130 us; the launch traced here: 129 us
  Pallas kernels  43.7 us (34%)
  waiting for transfers between devices  32.8 us (25%)
  starting transfers between devices  13.1 us (10%)
  blocking collectives  10.1 us (8%)
  local copies, waits for them, and re-layouts  9.91 us (8%)
  other arithmetic  9.14 us (7%)
  matrix products  8.91 us (7%)
    pallas_call x7, Pallas kernels, fused_step(): pl.pallas_call(functools.partial(step_kernel, factor=factor, width=width,...  37.1 us
    ppermute x6, waiting for transfers between devices, passed_along(): return lax.ppermute(block, axis, route)  32.8 us
    all_gather x1, blocking collectives, shards(): maps_all = lax.all_gather(maps_here, 'dp', axis=0, tiled=True)  10.1 us
    ppermute x6, starting transfers between devices, passed_along(): return lax.ppermute(block, axis, route)  7.75 us
    pallas_call x6, Pallas kernels, fused_step(): pl.pallas_call(functools.partial(carry_kernel, factor=factor, level_pos=l...  6.63 us
    while x6, local copies, waits for them, and re-layouts  5.5 us
    all_to_all x1, starting transfers between devices, shards(): rows_all = lax.all_to_all(rows_here, 'dp', 0, 0, tiled=True)  5.3 us
    dot_general x1, matrix products, shards(): jnp.einsum('mlsjn,mlsjd->mlsnd', in_blk, xt_full, preferred_element_type=...  3.19 us
  transfers between devices with their start and end apart: 7, of which 6 were waited for; matrix products, arithmetic and copies ran while one was open for 18% of the time, Pallas kernels for 34%

profile of v13, /device:TPU:0, one launch (start us, length us, event | category | flops | bytes accessed | tf_op | source)
XLA Modules:
  0.0 128.6 jit_solution(15321647231360564073)
XLA Ops:
  0.6 2.2 %copy.31 = bf16[1,1,128,2560]{2,3,1,0:T(8,128)(2,1)} copy(bf16[1,1,128,2560]{3,2,1,0:T(8,128)(2,1)} %param.6) | data formatting | bytes 1310720 | tf_op args[0]
  2.8 5.3 %all-to-all-start = ((bf16[8,1,128,320]{2,3,1,0:T(8,128)(2,1)}), bf16[8,1,128,320]{2,3,1,0:T(8,128)(2,1)}, u32[]{:S(2)}, u32[]{:S(2)}) async-start(bf16[8,1,128,320]{2,3,1,0:T(8,128)(2,1)} %bitcast.29), calls=%async_computation | async-start | bytes 1310720 | tf_op jit(solution)/shard_map/all_to_all | solution.py:425
  9.3 1.9 %fusion.9 = bf16[128,256]{1,0:T(8,128)(2,1)S(1)} fusion(bf16[1,2560,256]{2,1,0:T(8,128)(2,1)} %w_ref.1, bf16[1,1,128,2560]{3,2,1,0:T(8,128)(2,1)S(1)} %copy-done.2), kind=kOutput, calls=%fused_computation.18 | convolution fusion | flops 167804928 | bytes 2031616 | tf_op jit(solution)/shard_map/lstd,ldc->lstc/dot_general | solution.py:325
  12.1 3.2 %fusion.29 = f32[4,128,2560]{2,1,0:T(8,128)} fusion(bf16[4,1,1,32,256]{4,3,2,1,0:T(8,128)(2,1)S(1)} %bitcast.114, f32[4,32,2560]{2,1,0:T(8,128)S(1)} %fusion.19, bf16[4,32,2560]{2,1,0:T(8,128)(2,1)S(1)} %bitcast.109), kind=kOutput, calls=%fused_computation.36 | convolution fusion | flops 84869120 | bytes 7241728 | tf_op jit(solution)/shard_map/mlsjn,mlsjd->mlsnd/dot_general | solution.py:365
  16.4 1.9 %exponential_select_fusion = f32[4,1,1,32,32,40]{4,3,5,0,2,1:T(8,128)} fusion(f32[4,32,40]{1,2,0:T(8,128)S(1)} %copy.29, pred[32,32]{1,0:T(8,128)(4,1)S(1)} %iota_compare_fusion.2), kind=kLoop, calls=%fused_computation.2 | loop fusion | flops 491520 | bytes 676864 | tf_op jit(solution)/shard_map/vmap(vmap(vmap(jit(_where))))/select_n | solution.py:119
  18.4 1.7 %multiply_convert_fusion.wt_ref = bf16[4,1,1,40,32,32]{5,4,3,2,1,0:T(8,128)(2,1)} fusion(f32[4,32,32]{2,1,0:T(8,128)S(1)} %convolution_multiply_fusion, f32[4,40,32]{2,1,0:T(8,128)S(1)} %copy.27, pred[32,32]{1,0:T(8,128)(4,1)S(1)} %iota_compare_fusion.3), kind=kLoop, calls=%fused_computation.3 | loop fusion | flops 819200 | bytes 365568 | tf_op jit(solution)/shard_map/vmap(vmap(vmap()))/convert_element_type | solution.py:128
  20.1 2.5 %fusion.21 = (bf16[1,1,1,128,2560]{4,3,2,1,0:T(8,128)(2,1)S(1)}, bf16[1,1,1,128,2560]{4,3,2,1,0:T(8,128)(2,1)S(1)}, bf16[1,1,1,128,2560]{4,3,2,1,0:T(8,128)(2,1)S(1)}) fusion(f32[4,128,2560]{2,1,0:T(8,128)} %fusion.29, f32[2560]{0:T(1024)S(1)} %get-tuple-element.293, f32[2560]{0:T(1024)S(1)} %get-tuple-element.291, f32[2560]{0:T(1024)S(1)} %get-tuple-element.292), kind=kLoop, calls=%fused_computation.28 | loop fusion | flops 2621440 | bytes 5928960 | tf_op jit(solution)/shard_map/convert_element_type | solution.py:371
  22.5 1.8 %pad_maximum_fusion.sb_ref = bf16[4,1,1,128,2560]{4,3,2,1,0:T(8,128)(2,1)} fusion(bf16[1,1,1,128,2560]{4,3,2,1,0:T(8,128)(2,1)S(1)} %get-tuple-element.331, bf16[1,1,1,128,2560]{4,3,2,1,0:T(8,128)(2,1)S(1)} %get-tuple-element.330, bf16[1,1,1,128,2560]{4,3,2,1,0:T(8,128)(2,1)S(1)} %get-tuple-element.332, bf16[4]{0:T(256)(128)(2,1)S(1)} %pad.clone), kind=kLoop, calls=%fused_computation.1 | loop fusion | flops 3932160 | bytes 4587528 | tf_op jit(solution)/shard_map/stack | solution.py:373
  26.4 84.6 %while.19 = (s32[]{:T(128)}, bf16[1,32,2560]{2,1,0:T(8,128)(2,1)S(1)}, f32[1,1,128,2560]{3,2,1,0:T(8,128)S(1)}, bf16[4,1,1,32,2560]{4,3,2,1,0:T(8,128)(2,1)}, bf...) while((s32[]{:T(128)}, ...), condition=%wide.region_2.3_spmd, body=%wide.region_1.2_spmd.sunk | while | flops 167772160 | bytes 11960541 | solution.py:414
  26.4 5.3 %eval_jaxpr.10 = (bf16[32,2560]{1,0:T(8,128)(2,1)}, bf16[32,256]{1,0:T(8,128)(2,1)}, bf16[4,1,1,32,2560]{4,3,2,1,0:T(8,128)(2,1)}, bf16[4,1,1,32,256]{4,3,2,1,0:T(8,128)(2,1)}) custom-call(s32[1]{0:T(128)} %bitcast.102.step_ref, s32[21]{0:T(128)S(1)} %get-tuple-element.493.tab_ref, ...), custom_call_target="tpu_custom_call", output_to_operand_aliasing={{2}: (16, {}), {3}: (17, {})} | custom-call | flops 146800640 | bytes 7536640 | tf_op jit(solution)/shard_map/while/body/eval_jaxpr/pallas_call | solution.py:259
  31.7 1.3 %collective-permute-start = (bf16[1,32,2560]{2,1,0:T(8,128)(2,1)}, bf16[1,32,2560]{2,1,0:T(8,128)(2,1)}, u32[]{:S(2)}, u32[]{:S(2)}) collective-permute-start(bf16[1,32,2560]{2,1,0:T(8,128)(2,1)} %bitcast.120), channel_id=1, source_target_pairs={{8,0},{16,8},{24,16},{9,1},{17,9},{25,17},{10,2},{18,10},{26,18},{... | collective-permute-start | bytes 491528 | tf_op jit(solution)/shard_map/while/body/eval_jaxpr/ppermute | solution.py:20
  34.1 6.6 %collective-permute-done = bf16[1,32,2560]{2,1,0:T(8,128)(2,1)} collective-permute-done((bf16[1,32,2560]{2,1,0:T(8,128)(2,1)}, bf16[1,32,2560]{2,1,0:T(8,128)(2,1)}, u32[]{:S(2)}, u32[]{:S(2)}) %collective-permute-start) | collective-permute-done | bytes 163872 | tf_op jit(solution)/shard_map/while/body/eval_jaxpr/ppermute | solution.py:20
  41.6 5.3 %eval_jaxpr.10 = (bf16[32,2560]{1,0:T(8,128)(2,1)}, bf16[32,256]{1,0:T(8,128)(2,1)}, bf16[4,1,1,32,2560]{4,3,2,1,0:T(8,128)(2,1)}, bf16[4,1,1,32,256]{4,3,2,1,0:T(8,128)(2,1)}) custom-call(s32[1]{0:T(128)} %bitcast.102.step_ref, s32[21]{0:T(128)S(1)} %get-tuple-element.493.tab_ref, ...), custom_call_target="tpu_custom_call", output_to_operand_aliasing={{2}: (16, {}), {3}: (17, {})} | custom-call | flops 146800640 | bytes 7536640 | tf_op jit(solution)/shard_map/while/body/eval_jaxpr/pallas_call | solution.py:259
  47.0 1.3 %collective-permute-start = (bf16[1,32,2560]{2,1,0:T(8,128)(2,1)}, bf16[1,32,2560]{2,1,0:T(8,128)(2,1)}, u32[]{:S(2)}, u32[]{:S(2)}) collective-permute-start(bf16[1,32,2560]{2,1,0:T(8,128)(2,1)} %bitcast.120), channel_id=1, source_target_pairs={{8,0},{16,8},{24,16},{9,1},{17,9},{25,17},{10,2},{18,10},{26,18},{... | collective-permute-start | bytes 491528 | tf_op jit(solution)/shard_map/while/body/eval_jaxpr/ppermute | solution.py:20
  49.4 5.7 %collective-permute-done = bf16[1,32,2560]{2,1,0:T(8,128)(2,1)} collective-permute-done((bf16[1,32,2560]{2,1,0:T(8,128)(2,1)}, bf16[1,32,2560]{2,1,0:T(8,128)(2,1)}, u32[]{:S(2)}, u32[]{:S(2)}) %collective-permute-start) | collective-permute-done | bytes 163872 | tf_op jit(solution)/shard_map/while/body/eval_jaxpr/ppermute | solution.py:20
  56.0 5.3 %eval_jaxpr.10 = (bf16[32,2560]{1,0:T(8,128)(2,1)}, bf16[32,256]{1,0:T(8,128)(2,1)}, bf16[4,1,1,32,2560]{4,3,2,1,0:T(8,128)(2,1)}, bf16[4,1,1,32,256]{4,3,2,1,0:T(8,128)(2,1)}) custom-call(s32[1]{0:T(128)} %bitcast.102.step_ref, s32[21]{0:T(128)S(1)} %get-tuple-element.493.tab_ref, ...), custom_call_target="tpu_custom_call", output_to_operand_aliasing={{2}: (16, {}), {3}: (17, {})} | custom-call | flops 146800640 | bytes 7536640 | tf_op jit(solution)/shard_map/while/body/eval_jaxpr/pallas_call | solution.py:259
  61.3 1.3 %collective-permute-start = (bf16[1,32,2560]{2,1,0:T(8,128)(2,1)}, bf16[1,32,2560]{2,1,0:T(8,128)(2,1)}, u32[]{:S(2)}, u32[]{:S(2)}) collective-permute-start(bf16[1,32,2560]{2,1,0:T(8,128)(2,1)} %bitcast.120), channel_id=1, source_target_pairs={{8,0},{16,8},{24,16},{9,1},{17,9},{25,17},{10,2},{18,10},{26,18},{... | collective-permute-start | bytes 491528 | tf_op jit(solution)/shard_map/while/body/eval_jaxpr/ppermute | solution.py:20
  63.7 5.1 %collective-permute-done = bf16[1,32,2560]{2,1,0:T(8,128)(2,1)} collective-permute-done((bf16[1,32,2560]{2,1,0:T(8,128)(2,1)}, bf16[1,32,2560]{2,1,0:T(8,128)(2,1)}, u32[]{:S(2)}, u32[]{:S(2)}) %collective-permute-start) | collective-permute-done | bytes 163872 | tf_op jit(solution)/shard_map/while/body/eval_jaxpr/ppermute | solution.py:20
  69.7 5.3 %eval_jaxpr.10 = (bf16[32,2560]{1,0:T(8,128)(2,1)}, bf16[32,256]{1,0:T(8,128)(2,1)}, bf16[4,1,1,32,2560]{4,3,2,1,0:T(8,128)(2,1)}, bf16[4,1,1,32,256]{4,3,2,1,0:T(8,128)(2,1)}) custom-call(s32[1]{0:T(128)} %bitcast.102.step_ref, s32[21]{0:T(128)S(1)} %get-tuple-element.493.tab_ref, ...), custom_call_target="tpu_custom_call", output_to_operand_aliasing={{2}: (16, {}), {3}: (17, {})} | custom-call | flops 146800640 | bytes 7536640 | tf_op jit(solution)/shard_map/while/body/eval_jaxpr/pallas_call | solution.py:259
  75.0 1.3 %collective-permute-start = (bf16[1,32,2560]{2,1,0:T(8,128)(2,1)}, bf16[1,32,2560]{2,1,0:T(8,128)(2,1)}, u32[]{:S(2)}, u32[]{:S(2)}) collective-permute-start(bf16[1,32,2560]{2,1,0:T(8,128)(2,1)} %bitcast.120), channel_id=1, source_target_pairs={{8,0},{16,8},{24,16},{9,1},{17,9},{25,17},{10,2},{18,10},{26,18},{... | collective-permute-start | bytes 491528 | tf_op jit(solution)/shard_map/while/body/eval_jaxpr/ppermute | solution.py:20
  77.5 5.1 %collective-permute-done = bf16[1,32,2560]{2,1,0:T(8,128)(2,1)} collective-permute-done((bf16[1,32,2560]{2,1,0:T(8,128)(2,1)}, bf16[1,32,2560]{2,1,0:T(8,128)(2,1)}, u32[]{:S(2)}, u32[]{:S(2)}) %collective-permute-start) | collective-permute-done | bytes 163872 | tf_op jit(solution)/shard_map/while/body/eval_jaxpr/ppermute | solution.py:20
  83.5 5.3 %eval_jaxpr.10 = (bf16[32,2560]{1,0:T(8,128)(2,1)}, bf16[32,256]{1,0:T(8,128)(2,1)}, bf16[4,1,1,32,2560]{4,3,2,1,0:T(8,128)(2,1)}, bf16[4,1,1,32,256]{4,3,2,1,0:T(8,128)(2,1)}) custom-call(s32[1]{0:T(128)} %bitcast.102.step_ref, s32[21]{0:T(128)S(1)} %get-tuple-element.493.tab_ref, ...), custom_call_target="tpu_custom_call", output_to_operand_aliasing={{2}: (16, {}), {3}: (17, {})} | custom-call | flops 146800640 | bytes 7536640 | tf_op jit(solution)/shard_map/while/body/eval_jaxpr/pallas_call | solution.py:259
  88.8 1.3 %collective-permute-start = (bf16[1,32,2560]{2,1,0:T(8,128)(2,1)}, bf16[1,32,2560]{2,1,0:T(8,128)(2,1)}, u32[]{:S(2)}, u32[]{:S(2)}) collective-permute-start(bf16[1,32,2560]{2,1,0:T(8,128)(2,1)} %bitcast.120), channel_id=1, source_target_pairs={{8,0},{16,8},{24,16},{9,1},{17,9},{25,17},{10,2},{18,10},{26,18},{... | collective-permute-start | bytes 491528 | tf_op jit(solution)/shard_map/while/body/eval_jaxpr/ppermute | solution.py:20
  90.1 1.1 eval_jaxpr.11
  91.2 5.1 %collective-permute-done = bf16[1,32,2560]{2,1,0:T(8,128)(2,1)} collective-permute-done((bf16[1,32,2560]{2,1,0:T(8,128)(2,1)}, bf16[1,32,2560]{2,1,0:T(8,128)(2,1)}, u32[]{:S(2)}, u32[]{:S(2)}) %collective-permute-start) | collective-permute-done | bytes 163872 | tf_op jit(solution)/shard_map/while/body/eval_jaxpr/ppermute | solution.py:20
  97.3 5.3 %eval_jaxpr.10 = (bf16[32,2560]{1,0:T(8,128)(2,1)}, bf16[32,256]{1,0:T(8,128)(2,1)}, bf16[4,1,1,32,2560]{4,3,2,1,0:T(8,128)(2,1)}, bf16[4,1,1,32,256]{4,3,2,1,0:T(8,128)(2,1)}) custom-call(s32[1]{0:T(128)} %bitcast.102.step_ref, s32[21]{0:T(128)S(1)} %get-tuple-element.493.tab_ref, ...), custom_call_target="tpu_custom_call", output_to_operand_aliasing={{2}: (16, {}), {3}: (17, {})} | custom-call | flops 146800640 | bytes 7536640 | tf_op jit(solution)/shard_map/while/body/eval_jaxpr/pallas_call | solution.py:259
  102.6 1.3 %collective-permute-start = (bf16[1,32,2560]{2,1,0:T(8,128)(2,1)}, bf16[1,32,2560]{2,1,0:T(8,128)(2,1)}, u32[]{:S(2)}, u32[]{:S(2)}) collective-permute-start(bf16[1,32,2560]{2,1,0:T(8,128)(2,1)} %bitcast.120), channel_id=1, source_target_pairs={{8,0},{16,8},{24,16},{9,1},{17,9},{25,17},{10,2},{18,10},{26,18},{... | collective-permute-start | bytes 491528 | tf_op jit(solution)/shard_map/while/body/eval_jaxpr/ppermute | solution.py:20
  103.9 1.1 eval_jaxpr.11
  105.0 5.1 %collective-permute-done = bf16[1,32,2560]{2,1,0:T(8,128)(2,1)} collective-permute-done((bf16[1,32,2560]{2,1,0:T(8,128)(2,1)}, bf16[1,32,2560]{2,1,0:T(8,128)(2,1)}, u32[]{:S(2)}, u32[]{:S(2)}) %collective-permute-start) | collective-permute-done | bytes 163872 | tf_op jit(solution)/shard_map/while/body/eval_jaxpr/ppermute | solution.py:20
  111.0 5.3 %shard_map.59 = (bf16[32,2560]{1,0:T(8,128)(2,1)}, bf16[32,256]{1,0:T(8,128)(2,1)}, bf16[4,1,1,32,2560]{4,3,2,1,0:T(8,128)(2,1)}, bf16[4,1,1,32,256]{4,3,2,1,0:T(8,128)(2,1)}) custom-call(s32[1]{0:T(128)} %constant.45.clone.1.step_ref, s32[21]{0:T(128)S(1)} %get-tuple-element.519, ...), custom_call_target="tpu_custom_call", output_to_operand_aliasing={{2}: (16, {}), {3}: (17, {})} | custom-call | flops 146800640 | bytes 7536640 | tf_op jit(solution)/shard_map/pallas_call | solution.py:259
  116.3 10.1 %all_gather.3 = bf16[8,1,128,256]{3,2,1,0:T(8,128)(2,1)S(1)} all-gather(bf16[1,1,128,256]{3,2,1,0:T(8,128)(2,1)} %bitcast.111), channel_id=1, replica_groups=mesh['section'=4,'dp'=8] {'dp'}, dimensions={0}, use_global_device_ids=true | all-gather | bytes 589824 | tf_op jit(solution)/shard_map/all_gather | solution.py:427
  126.4 2.1 %fusion.8 = f32[1,320,256]{2,1,0:T(8,128)} fusion(bf16[8,1,128,320]{2,3,1,0:T(8,128)(2,1)} %all-to-all-done, bf16[8,1,128,256]{3,2,1,0:T(8,128)(2,1)S(1)} %all_gather.3), kind=kOutput, calls=%fused_computation.17 | convolution fusion | flops 167854080 | bytes 1507328 | tf_op jit(solution)/shard_map/glrd,glrc->ldc/dot_general | solution.py:428
  (46 shorter events, 15.1 us)
Async XLA Ops:
  0.6 7.5 %copy-start.3 = (f32[1,1,128,40]{2,3,1,0:T(8,128)S(1)}, f32[1,1,128,40]{2,3,1,0:T(8,128)}, u32[]{:S(2)}) copy-start(f32[1,1,128,40]{2,3,1,0:T(8,128)} %param.8) | copy-start | bytes 61444
  2.8 6.4 %copy-start.2 = (bf16[1,1,128,2560]{3,2,1,0:T(8,128)(2,1)S(1)}, bf16[1,1,128,2560]{3,2,1,0:T(8,128)(2,1)}, u32[]{:S(2)}) copy-start(bf16[1,1,128,2560]{3,2,1,0:T(8,128)(2,1)} %param.6) | copy-start | bytes 1966084
  2.8 123.6 %all-to-all-start = ((bf16[8,1,128,320]{2,3,1,0:T(8,128)(2,1)}), bf16[8,1,128,320]{2,3,1,0:T(8,128)(2,1)}, u32[]{:S(2)}, u32[]{:S(2)}) async-start(bf16[8,1,128,320]{2,3,1,0:T(8,128)(2,1)} %bitcast.29), calls=%async_computation | async-start | bytes 1310720 | tf_op jit(solution)/shard_map/all_to_all | solution.py:425
  9.0 3.1 %copy-start = (f32[4,32,2560]{2,1,0:T(8,128)}, f32[4,32,2560]{2,1,0:T(8,128)S(1)}, u32[]{:S(2)}) copy-start(f32[4,32,2560]{2,1,0:T(8,128)S(1)} %fusion.19) | copy-start | bytes 3932164
  24.4 2.1 %copy-start.1 = (bf16[1,128,2560]{2,1,0:T(8,128)(2,1)S(1)}, bf16[1,128,2560]{2,1,0:T(8,128)(2,1)}, u32[]{:S(2)}) copy-start(bf16[1,128,2560]{2,1,0:T(8,128)(2,1)} %param.9) | copy-start | bytes 1966084
  31.7 9.0 %collective-permute-start = (bf16[1,32,2560]{2,1,0:T(8,128)(2,1)}, bf16[1,32,2560]{2,1,0:T(8,128)(2,1)}, u32[]{:S(2)}, u32[]{:S(2)}) collective-permute-start(bf16[1,32,2560]{2,1,0:T(8,128)(2,1)} %bitcast.120), channel_id=1, source_target_pairs={{8,0},{16,8},{24,16},{9,1},{17,9},{25,17},{10,2},{18,10},{26,18},{... | collective-permute-start | bytes 491528 | tf_op jit(solution)/shard_map/while/body/eval_jaxpr/ppermute | solution.py:20
  47.0 8.1 %collective-permute-start = (bf16[1,32,2560]{2,1,0:T(8,128)(2,1)}, bf16[1,32,2560]{2,1,0:T(8,128)(2,1)}, u32[]{:S(2)}, u32[]{:S(2)}) collective-permute-start(bf16[1,32,2560]{2,1,0:T(8,128)(2,1)} %bitcast.120), channel_id=1, source_target_pairs={{8,0},{16,8},{24,16},{9,1},{17,9},{25,17},{10,2},{18,10},{26,18},{... | collective-permute-start | bytes 491528 | tf_op jit(solution)/shard_map/while/body/eval_jaxpr/ppermute | solution.py:20
  61.3 7.5 %collective-permute-start = (bf16[1,32,2560]{2,1,0:T(8,128)(2,1)}, bf16[1,32,2560]{2,1,0:T(8,128)(2,1)}, u32[]{:S(2)}, u32[]{:S(2)}) collective-permute-start(bf16[1,32,2560]{2,1,0:T(8,128)(2,1)} %bitcast.120), channel_id=1, source_target_pairs={{8,0},{16,8},{24,16},{9,1},{17,9},{25,17},{10,2},{18,10},{26,18},{... | collective-permute-start | bytes 491528 | tf_op jit(solution)/shard_map/while/body/eval_jaxpr/ppermute | solution.py:20
  75.0 7.5 %collective-permute-start = (bf16[1,32,2560]{2,1,0:T(8,128)(2,1)}, bf16[1,32,2560]{2,1,0:T(8,128)(2,1)}, u32[]{:S(2)}, u32[]{:S(2)}) collective-permute-start(bf16[1,32,2560]{2,1,0:T(8,128)(2,1)} %bitcast.120), channel_id=1, source_target_pairs={{8,0},{16,8},{24,16},{9,1},{17,9},{25,17},{10,2},{18,10},{26,18},{... | collective-permute-start | bytes 491528 | tf_op jit(solution)/shard_map/while/body/eval_jaxpr/ppermute | solution.py:20
  88.8 7.5 %collective-permute-start = (bf16[1,32,2560]{2,1,0:T(8,128)(2,1)}, bf16[1,32,2560]{2,1,0:T(8,128)(2,1)}, u32[]{:S(2)}, u32[]{:S(2)}) collective-permute-start(bf16[1,32,2560]{2,1,0:T(8,128)(2,1)} %bitcast.120), channel_id=1, source_target_pairs={{8,0},{16,8},{24,16},{9,1},{17,9},{25,17},{10,2},{18,10},{26,18},{... | collective-permute-start | bytes 491528 | tf_op jit(solution)/shard_map/while/body/eval_jaxpr/ppermute | solution.py:20
  102.6 7.5 %collective-permute-start = (bf16[1,32,2560]{2,1,0:T(8,128)(2,1)}, bf16[1,32,2560]{2,1,0:T(8,128)(2,1)}, u32[]{:S(2)}, u32[]{:S(2)}) collective-permute-start(bf16[1,32,2560]{2,1,0:T(8,128)(2,1)} %bitcast.120), channel_id=1, source_target_pairs={{8,0},{16,8},{24,16},{9,1},{17,9},{25,17},{10,2},{18,10},{26,18},{... | collective-permute-start | bytes 491528 | tf_op jit(solution)/shard_map/while/body/eval_jaxpr/ppermute | solution.py:20

commit v14 on v11

--- a/solution.py
+++ b/solution.py
@@ -328,14 +328,17 @@
     xt_full = (tail_full * x_flat.astype(jnp.float32)).astype(jnp.bfloat16)
     end_row = per_lane(consts["ending"])[..., None, :]
     fresh_t = jnp.einsum(
-        "mlsjn,mlsjd->mlsnd", in_blk, xt_full, preferred_element_type=jnp.float32
+        "mlsnj,mlsjd->mlsnd",
+        jnp.swapaxes(in_blk[: MICRO - 1], -1, -2),
+        xt_full[: MICRO - 1],
+        preferred_element_type=jnp.float32,
     )
     state_now = jnp.zeros(fresh_t.shape[1:], jnp.float32)
-    saved = []
-    for block_no in range(MICRO):
-        saved.append(state_now.astype(jnp.bfloat16))
+    saved = [state_now.astype(jnp.bfloat16)[None]]
+    for block_no in range(MICRO - 1):
         state_now = end_row[block_no] * state_now + fresh_t[block_no]
-    states_t = jnp.stack(saved)
+        saved.append(state_now.astype(jnp.bfloat16)[None])
+    states_t = jnp.concatenate(saved, axis=0)
     per_block = (wt2, dec2, x_flat, in_blk, out_blk, tail_full, lead_full, xt_full, states_t, end_row)
     per_block = lax.optimization_barrier(per_block)
 

time: 123 us -> 123 us (level)
    another operation x1 -> x0, other arithmetic: 1.79 us -> none  [shards(): states_t = jnp.stack(saved)]
    concatenate x0 -> x1, other arithmetic: none -> 1.79 us  [shards(): states_t = jnp.concatenate(saved, axis=0)]
    convert_element_type x2 -> x1, other arithmetic: 3.49 us -> 2.49 us  [shards(): saved.append(state_now.astype(jnp.bfloat16)[None])]
where the time goes in v14:
time: 123 us; the launch traced here: 122 us
  waiting for transfers between devices  38.8 us (32%)
  Pallas kernels  38.3 us (31%)
  starting transfers between devices  12.9 us (10%)
  blocking collectives  9.81 us (8%)
  matrix products  8.99 us (7%)
  other arithmetic  6.98 us (6%)
  local copies, waits for them, and re-layouts  5.69 us (5%)
    ppermute x6, waiting for transfers between devices, passed_along(): return lax.ppermute(block, axis, route)  38.8 us
    pallas_call x7, Pallas kernels, fused_step(): pl.pallas_call(functools.partial(step_kernel, factor=factor, width=width,...  38.3 us
    all_gather x1, blocking collectives, shards(): maps_all = lax.all_gather(maps_here, 'dp', axis=0, tiled=True)  9.81 us
    ppermute x6, starting transfers between devices, passed_along(): return lax.ppermute(block, axis, route)  7.75 us
    all_to_all x1, starting transfers between devices, shards(): rows_all = lax.all_to_all(rows_here, 'dp', 0, 0, tiled=True)  5.17 us
    dot_general x3, matrix products, per_lane(): jnp.einsum('...h,hd->...d', a, spread_heads, precision=lax.Precision.HIGH...  3.81 us
    dot_general x1, matrix products, shards(): jnp.einsum('mlsnj,mlsjd->mlsnd', jnp.swapaxes(in_blk[:MICRO - 1], -1, -2)...  2.57 us
    convert_element_type x1, other arithmetic, shards(): saved.append(state_now.astype(jnp.bfloat16)[None])  2.49 us
  transfers between devices with their start and end apart: 7, of which 6 were waited for; matrix products, arithmetic and copies ran while one was open for 14% of the time, Pallas kernels for 31%

profile of v14, /device:TPU:0, one launch (start us, length us, event | category | flops | bytes accessed | tf_op | source)
XLA Modules:
  0.0 122.3 jit_solution(5779202470042449821)
XLA Ops:
  0.7 2.4 %copy.32 = bf16[1,1,128,2560]{2,3,1,0:T(8,128)(2,1)} copy(bf16[1,1,128,2560]{3,2,1,0:T(8,128)(2,1)} %param.6) | data formatting | bytes 1310720 | tf_op args[0]
  3.0 5.2 %all-to-all-start = ((bf16[8,1,128,320]{2,3,1,0:T(8,128)(2,1)}), bf16[8,1,128,320]{2,3,1,0:T(8,128)(2,1)}, u32[]{:S(2)}, u32[]{:S(2)}) async-start(bf16[8,1,128,320]{2,3,1,0:T(8,128)(2,1)} %bitcast.30), calls=%async_computation | async-start | bytes 1310720 | tf_op jit(solution)/shard_map/all_to_all | solution.py:393
  9.6 1.8 %convolution_bitcast_fusion.lead_ref = f32[4,1,1,32,2560]{4,3,2,1,0:T(8,128)} fusion(s32[2560]{0:T(1024)S(1)} %add_select_fusion, f32[4,1,1,32,40]{4,3,2,1,0:T(8,128)S(1)} %reduce_window_sum.11), kind=kOutput, calls=%fused_computation | convolution fusion | flops 157388800 | bytes 1341440 | tf_op jit(solution)/shard_map/...h,hd->...d/dot_general | solution.py:320
  11.6 1.8 %fusion.4 = (bf16[4,32,2560]{2,1,0:T(8,128)(2,1)S(1)}, f32[4,32,2560]{2,1,0:T(8,128)}) fusion(bf16[4,32,2560]{2,1,0:T(8,128)(2,1)S(1)} %bitcast.110, s32[2560]{0:T(1024)S(1)} %add_select_fusion, f32[4,40]{1,0:T(4,128)S(1)} %bitcast.123, f32[4,1,1,32,40]{4,3,2,1,0:T(8,128)S(1)} %reduce_window_sum.11), kind=kOutput, calls=%fused_computation.12 | convolution fusion | flops 158376960 | bytes 2652800 | tf_op jit(solution)/shard_map/...h,hd->...d/dot_general | solution.py:320
  13.4 2.6 %fusion.16 = f32[3,128,2560]{2,1,0:T(8,128)} fusion(bf16[4,32,2560]{2,1,0:T(8,128)(2,1)S(1)} %get-tuple-element.338, bf16[4,1,1,32,256]{4,3,2,1,0:T(8,128)(2,1)S(1)} %bitcast.120), kind=kOutput, calls=%fused_computation.24 | convolution fusion | flops 62914560 | bytes 4448256 | tf_op jit(solution)/shard_map/mlsnj,mlsjd->mlsnd/dot_general | solution.py:330
  17.0 1.7 %multiply_convert_fusion.wt_ref = bf16[4,1,1,40,32,32]{5,4,3,2,1,0:T(8,128)(2,1)} fusion(f32[4,32,32]{2,1,0:T(8,128)S(1)} %convolution_multiply_fusion, f32[4,40,32]{2,1,0:T(8,128)S(1)} %copy.28, pred[32,32]{1,0:T(8,128)(4,1)S(1)} %iota_compare_fusion.3), kind=kLoop, calls=%fused_computation.3 | loop fusion | flops 819200 | bytes 365568 | tf_op jit(solution)/shard_map/vmap(vmap(vmap()))/convert_element_type | solution.py:128
  18.7 2.5 %fusion.23 = (bf16[1,1,1,128,2560]{4,3,2,1,0:T(8,128)(2,1)S(1)}, bf16[1,1,1,128,2560]{4,3,2,1,0:T(8,128)(2,1)S(1)}, bf16[1,1,1,128,2560]{4,3,2,1,0:T(8,128)(2,1)S(1)}) fusion(f32[3,128,2560]{2,1,0:T(8,128)} %fusion.16, f32[2560]{0:T(1024)S(1)} %get-tuple-element.296, f32[2560]{0:T(1024)S(1)} %get-tuple-element.294, f32[2560]{0:T(1024)S(1)} %get-tuple-element.295), kind=kLoop, calls=%fused_computation.30 | loop fusion | flops 2621440 | bytes 5928960 | tf_op jit(solution)/shard_map/convert_element_type | solution.py:340
  21.2 1.8 %pad_maximum_fusion.sb_ref = bf16[4,1,1,128,2560]{4,3,2,1,0:T(8,128)(2,1)} fusion(bf16[1,1,1,128,2560]{4,3,2,1,0:T(8,128)(2,1)S(1)} %get-tuple-element.334, bf16[1,1,1,128,2560]{4,3,2,1,0:T(8,128)(2,1)S(1)} %get-tuple-element.333, bf16[1,1,1,128,2560]{4,3,2,1,0:T(8,128)(2,1)S(1)} %get-tuple-element.335, bf16[4]{0:T(256)(128)(2,1)S(1)} %pad.clone), kind=kLoop, calls=%fused_computation.1 | loop fusion | flops 3932160 | bytes 4587528 | tf_op jit(solution)/shard_map/concatenate | solution.py:341
  23.4 1.2 broadcast.401
  24.6 0.9 broadcast_in_dim.99
  25.5 79.4 %while.19 = (s32[]{:T(128)}, bf16[1,32,2560]{2,1,0:T(8,128)(2,1)S(1)}, f32[1,1,128,2560]{3,2,1,0:T(8,128)}, bf16[4,1,1,32,2560]{4,3,2,1,0:T(8,128)(2,1)}, bf16[4...) while((s32[]{:T(128)}, ...), condition=%wide.region_2.3_spmd, body=%wide.region_1.2_spmd.sunk | while | flops 146800640 | bytes 8192213 | solution.py:382
  25.5 5.5 %eval_jaxpr.5 = (bf16[32,2560]{1,0:T(8,128)(2,1)}, f32[1,1,128,2560]{3,2,1,0:T(8,128)}, bf16[32,256]{1,0:T(8,128)(2,1)}, bf16[4,1,1,32,2560]{4,3,2,1,0:T(8,128)(2,1)}, bf16[4,1,1,32,256]{4,3,2,1,0:T(8,128)(2,1)S(1)}) custom-call(s32[1]{0:T(128)} %bitcast.106.step_ref, ...), custom_call_target="tpu_custom_call", output_to_operand_aliasing={{1}: (13, {}), {3}: (16, {}), {4}: (17, {})} | custom-call | flops 146800640 | bytes 7536640 | tf_op jit(solution)/shard_map/while/body/eval_jaxpr/pallas_call | solution.py:248
  31.0 1.3 %collective-permute-start = (bf16[1,32,2560]{2,1,0:T(8,128)(2,1)}, bf16[1,32,2560]{2,1,0:T(8,128)(2,1)S(1)}, u32[]{:S(2)}, u32[]{:S(2)}) collective-permute-start(bf16[1,32,2560]{2,1,0:T(8,128)(2,1)} %bitcast.124), channel_id=1, source_target_pairs={{8,0},{16,8},{24,16},{9,1},{17,9},{25,17},{10,2},{18,10},{26,18},{... | collective-permute-start | bytes 491528 | tf_op jit(solution)/shard_map/while/body/eval_jaxpr/ppermute | solution.py:20
  32.3 7.6 %collective-permute-done = bf16[1,32,2560]{2,1,0:T(8,128)(2,1)S(1)} collective-permute-done((bf16[1,32,2560]{2,1,0:T(8,128)(2,1)}, bf16[1,32,2560]{2,1,0:T(8,128)(2,1)S(1)}, u32[]{:S(2)}, u32[]{:S(2)}) %collective-permute-start) | collective-permute-done | bytes 163872 | tf_op jit(solution)/shard_map/while/body/eval_jaxpr/ppermute | solution.py:20
  39.9 5.5 %eval_jaxpr.5 = (bf16[32,2560]{1,0:T(8,128)(2,1)}, f32[1,1,128,2560]{3,2,1,0:T(8,128)}, bf16[32,256]{1,0:T(8,128)(2,1)}, bf16[4,1,1,32,2560]{4,3,2,1,0:T(8,128)(2,1)}, bf16[4,1,1,32,256]{4,3,2,1,0:T(8,128)(2,1)S(1)}) custom-call(s32[1]{0:T(128)} %bitcast.106.step_ref, ...), custom_call_target="tpu_custom_call", output_to_operand_aliasing={{1}: (13, {}), {3}: (16, {}), {4}: (17, {})} | custom-call | flops 146800640 | bytes 7536640 | tf_op jit(solution)/shard_map/while/body/eval_jaxpr/pallas_call | solution.py:248
  45.3 1.3 %collective-permute-start = (bf16[1,32,2560]{2,1,0:T(8,128)(2,1)}, bf16[1,32,2560]{2,1,0:T(8,128)(2,1)S(1)}, u32[]{:S(2)}, u32[]{:S(2)}) collective-permute-start(bf16[1,32,2560]{2,1,0:T(8,128)(2,1)} %bitcast.124), channel_id=1, source_target_pairs={{8,0},{16,8},{24,16},{9,1},{17,9},{25,17},{10,2},{18,10},{26,18},{... | collective-permute-start | bytes 491528 | tf_op jit(solution)/shard_map/while/body/eval_jaxpr/ppermute | solution.py:20
  46.7 6.7 %collective-permute-done = bf16[1,32,2560]{2,1,0:T(8,128)(2,1)S(1)} collective-permute-done((bf16[1,32,2560]{2,1,0:T(8,128)(2,1)}, bf16[1,32,2560]{2,1,0:T(8,128)(2,1)S(1)}, u32[]{:S(2)}, u32[]{:S(2)}) %collective-permute-start) | collective-permute-done | bytes 163872 | tf_op jit(solution)/shard_map/while/body/eval_jaxpr/ppermute | solution.py:20
  53.3 5.5 %eval_jaxpr.5 = (bf16[32,2560]{1,0:T(8,128)(2,1)}, f32[1,1,128,2560]{3,2,1,0:T(8,128)}, bf16[32,256]{1,0:T(8,128)(2,1)}, bf16[4,1,1,32,2560]{4,3,2,1,0:T(8,128)(2,1)}, bf16[4,1,1,32,256]{4,3,2,1,0:T(8,128)(2,1)S(1)}) custom-call(s32[1]{0:T(128)} %bitcast.106.step_ref, ...), custom_call_target="tpu_custom_call", output_to_operand_aliasing={{1}: (13, {}), {3}: (16, {}), {4}: (17, {})} | custom-call | flops 146800640 | bytes 7536640 | tf_op jit(solution)/shard_map/while/body/eval_jaxpr/pallas_call | solution.py:248
  58.8 1.3 %collective-permute-start = (bf16[1,32,2560]{2,1,0:T(8,128)(2,1)}, bf16[1,32,2560]{2,1,0:T(8,128)(2,1)S(1)}, u32[]{:S(2)}, u32[]{:S(2)}) collective-permute-start(bf16[1,32,2560]{2,1,0:T(8,128)(2,1)} %bitcast.124), channel_id=1, source_target_pairs={{8,0},{16,8},{24,16},{9,1},{17,9},{25,17},{10,2},{18,10},{26,18},{... | collective-permute-start | bytes 491528 | tf_op jit(solution)/shard_map/while/body/eval_jaxpr/ppermute | solution.py:20
  60.1 6.1 %collective-permute-done = bf16[1,32,2560]{2,1,0:T(8,128)(2,1)S(1)} collective-permute-done((bf16[1,32,2560]{2,1,0:T(8,128)(2,1)}, bf16[1,32,2560]{2,1,0:T(8,128)(2,1)S(1)}, u32[]{:S(2)}, u32[]{:S(2)}) %collective-permute-start) | collective-permute-done | bytes 163872 | tf_op jit(solution)/shard_map/while/body/eval_jaxpr/ppermute | solution.py:20
  66.2 5.5 %eval_jaxpr.5 = (bf16[32,2560]{1,0:T(8,128)(2,1)}, f32[1,1,128,2560]{3,2,1,0:T(8,128)}, bf16[32,256]{1,0:T(8,128)(2,1)}, bf16[4,1,1,32,2560]{4,3,2,1,0:T(8,128)(2,1)}, bf16[4,1,1,32,256]{4,3,2,1,0:T(8,128)(2,1)S(1)}) custom-call(s32[1]{0:T(128)} %bitcast.106.step_ref, ...), custom_call_target="tpu_custom_call", output_to_operand_aliasing={{1}: (13, {}), {3}: (16, {}), {4}: (17, {})} | custom-call | flops 146800640 | bytes 7536640 | tf_op jit(solution)/shard_map/while/body/eval_jaxpr/pallas_call | solution.py:248
  71.7 1.3 %collective-permute-start = (bf16[1,32,2560]{2,1,0:T(8,128)(2,1)}, bf16[1,32,2560]{2,1,0:T(8,128)(2,1)S(1)}, u32[]{:S(2)}, u32[]{:S(2)}) collective-permute-start(bf16[1,32,2560]{2,1,0:T(8,128)(2,1)} %bitcast.124), channel_id=1, source_target_pairs={{8,0},{16,8},{24,16},{9,1},{17,9},{25,17},{10,2},{18,10},{26,18},{... | collective-permute-start | bytes 491528 | tf_op jit(solution)/shard_map/while/body/eval_jaxpr/ppermute | solution.py:20
  73.0 6.1 %collective-permute-done = bf16[1,32,2560]{2,1,0:T(8,128)(2,1)S(1)} collective-permute-done((bf16[1,32,2560]{2,1,0:T(8,128)(2,1)}, bf16[1,32,2560]{2,1,0:T(8,128)(2,1)S(1)}, u32[]{:S(2)}, u32[]{:S(2)}) %collective-permute-start) | collective-permute-done | bytes 163872 | tf_op jit(solution)/shard_map/while/body/eval_jaxpr/ppermute | solution.py:20
  79.1 5.5 %eval_jaxpr.5 = (bf16[32,2560]{1,0:T(8,128)(2,1)}, f32[1,1,128,2560]{3,2,1,0:T(8,128)}, bf16[32,256]{1,0:T(8,128)(2,1)}, bf16[4,1,1,32,2560]{4,3,2,1,0:T(8,128)(2,1)}, bf16[4,1,1,32,256]{4,3,2,1,0:T(8,128)(2,1)S(1)}) custom-call(s32[1]{0:T(128)} %bitcast.106.step_ref, ...), custom_call_target="tpu_custom_call", output_to_operand_aliasing={{1}: (13, {}), {3}: (16, {}), {4}: (17, {})} | custom-call | flops 146800640 | bytes 7536640 | tf_op jit(solution)/shard_map/while/body/eval_jaxpr/pallas_call | solution.py:248
  84.6 1.3 %collective-permute-start = (bf16[1,32,2560]{2,1,0:T(8,128)(2,1)}, bf16[1,32,2560]{2,1,0:T(8,128)(2,1)S(1)}, u32[]{:S(2)}, u32[]{:S(2)}) collective-permute-start(bf16[1,32,2560]{2,1,0:T(8,128)(2,1)} %bitcast.124), channel_id=1, source_target_pairs={{8,0},{16,8},{24,16},{9,1},{17,9},{25,17},{10,2},{18,10},{26,18},{... | collective-permute-start | bytes 491528 | tf_op jit(solution)/shard_map/while/body/eval_jaxpr/ppermute | solution.py:20
  85.9 6.1 %collective-permute-done = bf16[1,32,2560]{2,1,0:T(8,128)(2,1)S(1)} collective-permute-done((bf16[1,32,2560]{2,1,0:T(8,128)(2,1)}, bf16[1,32,2560]{2,1,0:T(8,128)(2,1)S(1)}, u32[]{:S(2)}, u32[]{:S(2)}) %collective-permute-start) | collective-permute-done | bytes 163872 | tf_op jit(solution)/shard_map/while/body/eval_jaxpr/ppermute | solution.py:20
  92.0 5.5 %eval_jaxpr.5 = (bf16[32,2560]{1,0:T(8,128)(2,1)}, f32[1,1,128,2560]{3,2,1,0:T(8,128)}, bf16[32,256]{1,0:T(8,128)(2,1)}, bf16[4,1,1,32,2560]{4,3,2,1,0:T(8,128)(2,1)}, bf16[4,1,1,32,256]{4,3,2,1,0:T(8,128)(2,1)S(1)}) custom-call(s32[1]{0:T(128)} %bitcast.106.step_ref, ...), custom_call_target="tpu_custom_call", output_to_operand_aliasing={{1}: (13, {}), {3}: (16, {}), {4}: (17, {})} | custom-call | flops 146800640 | bytes 7536640 | tf_op jit(solution)/shard_map/while/body/eval_jaxpr/pallas_call | solution.py:248
  97.5 1.3 %collective-permute-start = (bf16[1,32,2560]{2,1,0:T(8,128)(2,1)}, bf16[1,32,2560]{2,1,0:T(8,128)(2,1)S(1)}, u32[]{:S(2)}, u32[]{:S(2)}) collective-permute-start(bf16[1,32,2560]{2,1,0:T(8,128)(2,1)} %bitcast.124), channel_id=1, source_target_pairs={{8,0},{16,8},{24,16},{9,1},{17,9},{25,17},{10,2},{18,10},{26,18},{... | collective-permute-start | bytes 491528 | tf_op jit(solution)/shard_map/while/body/eval_jaxpr/ppermute | solution.py:20
  98.8 6.1 %collective-permute-done = bf16[1,32,2560]{2,1,0:T(8,128)(2,1)S(1)} collective-permute-done((bf16[1,32,2560]{2,1,0:T(8,128)(2,1)}, bf16[1,32,2560]{2,1,0:T(8,128)(2,1)S(1)}, u32[]{:S(2)}, u32[]{:S(2)}) %collective-permute-start) | collective-permute-done | bytes 163872 | tf_op jit(solution)/shard_map/while/body/eval_jaxpr/ppermute | solution.py:20
  104.9 5.5 %shard_map.59 = (bf16[32,2560]{1,0:T(8,128)(2,1)}, f32[1,1,128,2560]{3,2,1,0:T(8,128)}, bf16[32,256]{1,0:T(8,128)(2,1)}, bf16[4,1,1,32,2560]{4,3,2,1,0:T(8,128)(2,1)}, bf16[4,1,1,32,256]{4,3,2,1,0:T(8,128)(2,1)S(1)}) custom-call(s32[1]{0:T(128)} %constant.45.clone.1.step_ref, ...), custom_call_target="tpu_custom_call", output_to_operand_aliasing={{1}: (13, {}), {3}: (16, {}), {4}: (17, {})} | custom-call | flops 146800640 | bytes 7536640 | tf_op jit(solution)/shard_map/pallas_call | solution.py:248
  110.4 9.8 %all_gather.3 = bf16[8,1,128,256]{3,2,1,0:T(8,128)(2,1)S(1)} all-gather(bf16[1,1,128,256]{3,2,1,0:T(8,128)(2,1)S(1)} %bitcast.115), channel_id=1, replica_groups=mesh['section'=4,'dp'=8] {'dp'}, dimensions={0}, use_global_device_ids=true | all-gather | bytes 589824 | tf_op jit(solution)/shard_map/all_gather | solution.py:395
  120.2 2.1 %fusion.8 = f32[1,320,256]{2,1,0:T(8,128)} fusion(bf16[8,1,128,320]{2,3,1,0:T(8,128)(2,1)} %all-to-all-done, bf16[8,1,128,256]{3,2,1,0:T(8,128)(2,1)S(1)} %all_gather.3), kind=kOutput, calls=%fused_computation.17 | convolution fusion | flops 167854080 | bytes 1507328 | tf_op jit(solution)/shard_map/glrd,glrc->ldc/dot_general | solution.py:396
  (37 shorter events, 3.0 us)
Async XLA Ops:
  0.6 7.6 %copy-start.1 = (bf16[1,1,128,2560]{3,2,1,0:T(8,128)(2,1)S(1)}, bf16[1,1,128,2560]{3,2,1,0:T(8,128)(2,1)}, u32[]{:S(2)}) copy-start(bf16[1,1,128,2560]{3,2,1,0:T(8,128)(2,1)} %param.6) | copy-start | bytes 1966084
  0.6 7.6 %copy-start = (bf16[1,2560,256]{2,1,0:T(8,128)(2,1)S(1)}, bf16[1,2560,256]{2,1,0:T(8,128)(2,1)}, u32[]{:S(2)}) copy-start(bf16[1,2560,256]{2,1,0:T(8,128)(2,1)} %w_ref.1) | copy-start | bytes 3932164
  3.0 117.2 %all-to-all-start = ((bf16[8,1,128,320]{2,3,1,0:T(8,128)(2,1)}), bf16[8,1,128,320]{2,3,1,0:T(8,128)(2,1)}, u32[]{:S(2)}, u32[]{:S(2)}) async-start(bf16[8,1,128,320]{2,3,1,0:T(8,128)(2,1)} %bitcast.30), calls=%async_computation | async-start | bytes 1310720 | tf_op jit(solution)/shard_map/all_to_all | solution.py:393
  8.2 1.2 copy-start.5
  11.6 4.4 %copy-start.3 = (f32[4,2560]{1,0:T(4,128)}, f32[4,2560]{1,0:T(4,128)S(1)}, u32[]{:S(2)}) copy-start(f32[4,2560]{1,0:T(4,128)S(1)} %fusion.18) | copy-start | bytes 122884
  13.4 2.6 %copy-start.2 = (bf16[4,32,2560]{2,1,0:T(8,128)(2,1)}, bf16[4,32,2560]{2,1,0:T(8,128)(2,1)S(1)}, u32[]{:S(2)}) copy-start(bf16[4,32,2560]{2,1,0:T(8,128)(2,1)S(1)} %get-tuple-element.338) | copy-start | bytes 1966084
  21.2 1.8 %copy-start.4 = (f32[4,2560]{1,0:T(4,128)S(1)}, f32[4,2560]{1,0:T(4,128)}, u32[]{:S(2)}) copy-start(f32[4,2560]{1,0:T(4,128)} %copy-done.3) | copy-start | bytes 122884
  31.0 8.9 %collective-permute-start = (bf16[1,32,2560]{2,1,0:T(8,128)(2,1)}, bf16[1,32,2560]{2,1,0:T(8,128)(2,1)S(1)}, u32[]{:S(2)}, u32[]{:S(2)}) collective-permute-start(bf16[1,32,2560]{2,1,0:T(8,128)(2,1)} %bitcast.124), channel_id=1, source_target_pairs={{8,0},{16,8},{24,16},{9,1},{17,9},{25,17},{10,2},{18,10},{26,18},{... | collective-permute-start | bytes 491528 | tf_op jit(solution)/shard_map/while/body/eval_jaxpr/ppermute | solution.py:20
  45.3 8.0 %collective-permute-start = (bf16[1,32,2560]{2,1,0:T(8,128)(2,1)}, bf16[1,32,2560]{2,1,0:T(8,128)(2,1)S(1)}, u32[]{:S(2)}, u32[]{:S(2)}) collective-permute-start(bf16[1,32,2560]{2,1,0:T(8,128)(2,1)} %bitcast.124), channel_id=1, source_target_pairs={{8,0},{16,8},{24,16},{9,1},{17,9},{25,17},{10,2},{18,10},{26,18},{... | collective-permute-start | bytes 491528 | tf_op jit(solution)/shard_map/while/body/eval_jaxpr/ppermute | solution.py:20
  58.8 7.4 %collective-permute-start = (bf16[1,32,2560]{2,1,0:T(8,128)(2,1)}, bf16[1,32,2560]{2,1,0:T(8,128)(2,1)S(1)}, u32[]{:S(2)}, u32[]{:S(2)}) collective-permute-start(bf16[1,32,2560]{2,1,0:T(8,128)(2,1)} %bitcast.124), channel_id=1, source_target_pairs={{8,0},{16,8},{24,16},{9,1},{17,9},{25,17},{10,2},{18,10},{26,18},{... | collective-permute-start | bytes 491528 | tf_op jit(solution)/shard_map/while/body/eval_jaxpr/ppermute | solution.py:20
  71.7 7.4 %collective-permute-start = (bf16[1,32,2560]{2,1,0:T(8,128)(2,1)}, bf16[1,32,2560]{2,1,0:T(8,128)(2,1)S(1)}, u32[]{:S(2)}, u32[]{:S(2)}) collective-permute-start(bf16[1,32,2560]{2,1,0:T(8,128)(2,1)} %bitcast.124), channel_id=1, source_target_pairs={{8,0},{16,8},{24,16},{9,1},{17,9},{25,17},{10,2},{18,10},{26,18},{... | collective-permute-start | bytes 491528 | tf_op jit(solution)/shard_map/while/body/eval_jaxpr/ppermute | solution.py:20
  84.6 7.4 %collective-permute-start = (bf16[1,32,2560]{2,1,0:T(8,128)(2,1)}, bf16[1,32,2560]{2,1,0:T(8,128)(2,1)S(1)}, u32[]{:S(2)}, u32[]{:S(2)}) collective-permute-start(bf16[1,32,2560]{2,1,0:T(8,128)(2,1)} %bitcast.124), channel_id=1, source_target_pairs={{8,0},{16,8},{24,16},{9,1},{17,9},{25,17},{10,2},{18,10},{26,18},{... | collective-permute-start | bytes 491528 | tf_op jit(solution)/shard_map/while/body/eval_jaxpr/ppermute | solution.py:20
  97.5 7.4 %collective-permute-start = (bf16[1,32,2560]{2,1,0:T(8,128)(2,1)}, bf16[1,32,2560]{2,1,0:T(8,128)(2,1)S(1)}, u32[]{:S(2)}, u32[]{:S(2)}) collective-permute-start(bf16[1,32,2560]{2,1,0:T(8,128)(2,1)} %bitcast.124), channel_id=1, source_target_pairs={{8,0},{16,8},{24,16},{9,1},{17,9},{25,17},{10,2},{18,10},{26,18},{... | collective-permute-start | bytes 491528 | tf_op jit(solution)/shard_map/while/body/eval_jaxpr/ppermute | solution.py:20

commit v15 on v14

--- a/solution.py
+++ b/solution.py
@@ -136,8 +136,8 @@
 
 
 def step_kernel(
-    step_ref, tab_ref, wt_ref, dec_ref, inc_ref, top_ref, x_ref, b_ref, c_ref, tail_ref, lead_ref, xt_ref,
-    sb_ref, r_ref, end_ref, w_ref, gs_ref, ms_ref, out_ref, rnew_ref, dbc_ref, gstore_ref, mstore_ref,
+    step_ref, tab_ref, wt_ref, dec_ref, inc_a_ref, inc_b_ref, top_ref, x_ref, b_ref, c_ref, tail_ref, lead_ref, xt_ref,
+    sb_ref, r_ref, end_ref, w_ref, gs_ref, ms_ref, out_a_ref, out_b_ref, rnew_ref, dbc_ref, gstore_ref, mstore_ref,
     v_ref, gx_ref, tail_buf, lead_buf, xt_buf, sb_buf, r_buf, w_buf, sems, *, factor, width,
     level_pos, levels, level_no, seq_no
 ):
@@ -160,7 +160,10 @@
     per_pair = lanes // width
     nt = (((1,), (1,)), ((), ()))
     tn = (((0,), (0,)), ((), ()))
-    v_ref[...] = jnp.where(tab_ref[base + 1] > 0, top_ref[...], inc_ref[...])
+    half = inc_a_ref.shape[0]
+    from_top = tab_ref[base + 1] > 0
+    v_ref[0:half] = jnp.where(from_top, top_ref[0:half], inc_a_ref[...])
+    v_ref[half:] = jnp.where(from_top, top_ref[half:], inc_b_ref[...])
     in_map = b_ref[...]
     out_map = c_ref[...]
     lane_id = lax.broadcasted_iota(jnp.int32, (length, lanes), 1)
@@ -210,14 +213,16 @@
     mstore_ref[...] = jnp.where(tab_ref[base + 2] > 0, grad_bc, ms_ref[...])
     fetches[5].wait()
     back = lax.dot_general(grad_bc, w_buf[...], nt, preferred_element_type=f32)
-    summed = (v.astype(f32) + gx_ref[...] + back).astype(out_ref.dtype)
-    out_ref[...] = summed
+    summed = (v.astype(f32) + gx_ref[...] + back).astype(out_a_ref.dtype)
+    out_a_ref[...] = summed[0:half]
+    out_b_ref[...] = summed[half:]
     gstore_ref[...] = jnp.where(tab_ref[base + 2] > 0, summed, gs_ref[...])
 
 
 def fused_step(step_arr, table, level_pos, levels, per_block, incoming, top_blk, carried, w_bc, grad_store, map_store, level_no, seq_no, factor, width):
     wt2, dec2, x_flat, in_blk, out_blk, tail_full, lead_full, xt_full, states_t, end_row = per_block
-    length, features = incoming.shape[1:]
+    half, features = incoming[0].shape[1:]
+    length = 2 * half
     state_size = in_blk.shape[-1]
 
     def lead_block(a):
@@ -226,7 +231,7 @@
         return pl.BlockSpec(shape, lambda i, c, t: (t[(c[0] * levels + level_pos) * 3], level_no, seq_no) + tail)
 
     in_specs = [lead_block(a) for a in (wt2, dec2)]
-    in_specs.append(pl.BlockSpec((None, length, features), lambda i, c, t: (seq_no, 0, 0)))
+    in_specs += [pl.BlockSpec((None, half, features), lambda i, c, t: (seq_no, 0, 0))] * 2
     in_specs.append(pl.BlockSpec((None, None, length, features), lambda i, c, t: (t[(c[0] * levels + level_pos) * 3], seq_no, 0, 0)))
     in_hbm = pl.BlockSpec(memory_space=pl.ANY)
     in_specs += [lead_block(a) for a in (x_flat, in_blk, out_blk)]
@@ -237,7 +242,8 @@
     store_m = pl.BlockSpec((None, None, None, length, 2 * state_size), lambda i, c, t: (t[(c[0] * levels + level_pos) * 3], level_no, seq_no, 0, 0))
     in_specs += [store_g, store_m]
     out_specs = (
-        pl.BlockSpec((length, features), lambda i, c, t: (0, 0)),
+        pl.BlockSpec((half, features), lambda i, c, t: (0, 0)),
+        pl.BlockSpec((half, features), lambda i, c, t: (0, 0)),
         pl.BlockSpec((None, None) + carried.shape[2:], lambda i, c, t: (level_no, seq_no, 0, 0)),
         pl.BlockSpec((length, 2 * state_size), lambda i, c, t: (0, 0)),
         store_g,
@@ -245,13 +251,14 @@
     )
     flops = 2 * length * features * (6 * state_size + 4 * length)
     moved = 2 * (4 * features * state_size * 2 + 6 * length * features) + 4 * 4 * length * features
-    return pl.pallas_call(
+    outs = pl.pallas_call(
         functools.partial(
             step_kernel, factor=factor, width=width, level_pos=level_pos, levels=levels,
             level_no=level_no, seq_no=seq_no,
         ),
         out_shape=(
-            jax.ShapeDtypeStruct((length, features), jnp.bfloat16),
+            jax.ShapeDtypeStruct((half, features), jnp.bfloat16),
+            jax.ShapeDtypeStruct((half, features), jnp.bfloat16),
             jax.ShapeDtypeStruct(carried.shape, jnp.float32),
             jax.ShapeDtypeStruct((length, 2 * state_size), jnp.bfloat16),
             jax.ShapeDtypeStruct(grad_store.shape, grad_store.dtype),
@@ -274,9 +281,10 @@
                 pltpu.SemaphoreType.DMA((6,)),
             ],
         ),
-        input_output_aliases={13: 1, 16: 3, 17: 4},
+        input_output_aliases={14: 2, 17: 4, 18: 5},
         cost_estimate=pl.CostEstimate(flops=flops, bytes_accessed=moved, transcendentals=0),
-    )(step_arr, table, wt2, dec2, incoming, top_blk, x_flat, in_blk, out_blk, tail_full, lead_full, xt_full, states_t, carried, end_row, w_bc, grad_store, map_store)
+    )(step_arr, table, wt2, dec2, incoming[0], incoming[1], top_blk, x_flat, in_blk, out_blk, tail_full, lead_full, xt_full, states_t, carried, end_row, w_bc, grad_store, map_store)
+    return ((outs[0], outs[1]),) + tuple(outs[2:])
 
 
 def shards(layer_inputs, w_bc, log_decay, top_grad):
@@ -368,13 +376,13 @@
                     w_bc, grad_store, map_store, level_no, seq_no, factor, width,
                 )
                 level_out.append(level_grads)
-            incoming = jnp.stack(level_out)
+            incoming = tuple(jnp.stack([g[e] for g in level_out]) for e in range(2))
         if send:
-            incoming = passed_along(incoming, "section", -1)
+            incoming = tuple(passed_along(part, "section", -1) for part in incoming)
         return (incoming, carried, grad_store, map_store)
 
     initial = (
-        jnp.zeros((seq_dev, block_len, features), jnp.bfloat16),
+        tuple(jnp.zeros((seq_dev, block_len // 2, features), jnp.bfloat16) for _ in range(2)),
         jnp.zeros(states_t.shape[1:], jnp.float32),
         jnp.zeros((MICRO, lay_dev, seq_dev, block_len, features), jnp.bfloat16),
         jnp.zeros((MICRO, lay_dev, seq_dev, block_len, 2 * state_size), jnp.bfloat16),

time: 123 us -> 131 us (1.065)
  starting transfers between devices: 12.9 us -> 20.7 us
  waiting for transfers between devices: 38.8 us -> 35.8 us
  Pallas kernels: 38.3 us -> 41.2 us
    ppermute x6 -> x12, starting transfers between devices: 7.75 us -> 15.5 us  [passed_along(): return lax.ppermute(block, axis, route)]
    pallas_call x7, Pallas kernels: 38.3 us -> 41.2 us  [fused_step(): pl.pallas_call(functools.partial(step_kernel, factor=factor, width=width,...]
    ppermute x6 -> x12, waiting for transfers between devices: 38.8 us -> 35.8 us  [passed_along(): return lax.ppermute(block, axis, route)]
  transfers between devices with their start and end apart: 7 -> 13, of which waited for: 6 -> 12; matrix products, arithmetic and copies ran while one was open for 14% -> 13% of each run, Pallas kernels for 31% -> 32%
where the time goes in v15:
time: 131 us; the launch traced here: 130 us
  Pallas kernels  41.2 us (31%)
  waiting for transfers between devices  35.8 us (27%)
  starting transfers between devices  20.7 us (16%)
  blocking collectives  10 us (8%)
  matrix products  8.98 us (7%)
  other arithmetic  6.99 us (5%)
  local copies, waits for them, and re-layouts  5.67 us (4%)
    pallas_call x7, Pallas kernels, fused_step(): pl.pallas_call(functools.partial(step_kernel, factor=factor, width=width,...  41.2 us
    ppermute x12, waiting for transfers between devices, passed_along(): return lax.ppermute(block, axis, route)  35.8 us
    ppermute x12, starting transfers between devices, passed_along(): return lax.ppermute(block, axis, route)  15.5 us
    all_gather x1, blocking collectives, shards(): maps_all = lax.all_gather(maps_here, 'dp', axis=0, tiled=True)  10 us
    all_to_all x1, starting transfers between devices, shards(): rows_all = lax.all_to_all(rows_here, 'dp', 0, 0, tiled=True)  5.17 us
    dot_general x3, matrix products, per_lane(): jnp.einsum('...h,hd->...d', a, spread_heads, precision=lax.Precision.HIGH...  3.79 us
  transfers between devices with their start and end apart: 13, of which 12 were waited for; matrix products, arithmetic and copies ran while one was open for 13% of the time, Pallas kernels for 32%

profile of v15, /device:TPU:0, one launch (start us, length us, event | category | flops | bytes accessed | tf_op | source)
XLA Modules:
  0.0 130.4 jit_solution(6201092368653911562)
XLA Ops:
  0.7 2.4 %copy.32 = bf16[1,1,128,2560]{2,3,1,0:T(8,128)(2,1)} copy(bf16[1,1,128,2560]{3,2,1,0:T(8,128)(2,1)} %param.6) | data formatting | bytes 1310720 | tf_op args[0]
  3.0 5.2 %all-to-all-start = ((bf16[8,1,128,320]{2,3,1,0:T(8,128)(2,1)}), bf16[8,1,128,320]{2,3,1,0:T(8,128)(2,1)}, u32[]{:S(2)}, u32[]{:S(2)}) async-start(bf16[8,1,128,320]{2,3,1,0:T(8,128)(2,1)} %bitcast.31), calls=%async_computation | async-start | bytes 1310720 | tf_op jit(solution)/shard_map/all_to_all | solution.py:401
  9.5 1.8 %convolution_bitcast_fusion.lead_ref = f32[4,1,1,32,2560]{4,3,2,1,0:T(8,128)} fusion(s32[2560]{0:T(1024)S(1)} %add_select_fusion, f32[4,1,1,32,40]{4,3,2,1,0:T(8,128)S(1)} %reduce_window_sum.11), kind=kOutput, calls=%fused_computation | convolution fusion | flops 157388800 | bytes 1341440 | tf_op jit(solution)/shard_map/...h,hd->...d/dot_general | solution.py:328
  11.6 1.8 %fusion.4 = (bf16[4,32,2560]{2,1,0:T(8,128)(2,1)S(1)}, f32[4,32,2560]{2,1,0:T(8,128)}) fusion(bf16[4,32,2560]{2,1,0:T(8,128)(2,1)S(1)} %bitcast.113, s32[2560]{0:T(1024)S(1)} %add_select_fusion, f32[4,40]{1,0:T(4,128)S(1)} %bitcast.126, f32[4,1,1,32,40]{4,3,2,1,0:T(8,128)S(1)} %reduce_window_sum.11), kind=kOutput, calls=%fused_computation.12 | convolution fusion | flops 158376960 | bytes 2652800 | tf_op jit(solution)/shard_map/...h,hd->...d/dot_general | solution.py:328
  13.4 2.6 %fusion.16 = f32[3,128,2560]{2,1,0:T(8,128)} fusion(bf16[4,32,2560]{2,1,0:T(8,128)(2,1)S(1)} %get-tuple-element.355, bf16[4,1,1,32,256]{4,3,2,1,0:T(8,128)(2,1)S(1)} %bitcast.123), kind=kOutput, calls=%fused_computation.24 | convolution fusion | flops 62914560 | bytes 4448256 | tf_op jit(solution)/shard_map/mlsnj,mlsjd->mlsnd/dot_general | solution.py:338
  17.0 1.7 %multiply_convert_fusion.wt_ref = bf16[4,1,1,40,32,32]{5,4,3,2,1,0:T(8,128)(2,1)} fusion(f32[4,32,32]{2,1,0:T(8,128)S(1)} %convolution_multiply_fusion, f32[4,40,32]{2,1,0:T(8,128)S(1)} %copy.28, pred[32,32]{1,0:T(8,128)(4,1)S(1)} %iota_compare_fusion.3), kind=kLoop, calls=%fused_computation.3 | loop fusion | flops 819200 | bytes 365568 | tf_op jit(solution)/shard_map/vmap(vmap(vmap()))/convert_element_type | solution.py:128
  18.7 2.5 %fusion.23 = (bf16[1,1,1,128,2560]{4,3,2,1,0:T(8,128)(2,1)S(1)}, bf16[1,1,1,128,2560]{4,3,2,1,0:T(8,128)(2,1)S(1)}, bf16[1,1,1,128,2560]{4,3,2,1,0:T(8,128)(2,1)S(1)}) fusion(f32[3,128,2560]{2,1,0:T(8,128)} %fusion.16, f32[2560]{0:T(1024)S(1)} %get-tuple-element.311, f32[2560]{0:T(1024)S(1)} %get-tuple-element.309, f32[2560]{0:T(1024)S(1)} %get-tuple-element.310), kind=kLoop, calls=%fused_computation.30 | loop fusion | flops 2621440 | bytes 5928960 | tf_op jit(solution)/shard_map/convert_element_type | solution.py:348
  21.2 1.8 %pad_maximum_fusion.sb_ref = bf16[4,1,1,128,2560]{4,3,2,1,0:T(8,128)(2,1)} fusion(bf16[1,1,1,128,2560]{4,3,2,1,0:T(8,128)(2,1)S(1)} %get-tuple-element.351, bf16[1,1,1,128,2560]{4,3,2,1,0:T(8,128)(2,1)S(1)} %get-tuple-element.350, bf16[1,1,1,128,2560]{4,3,2,1,0:T(8,128)(2,1)S(1)} %get-tuple-element.352, bf16[4]{0:T(256)(128)(2,1)S(1)} %pad.clone), kind=kLoop, calls=%fused_computation.1 | loop fusion | flops 3932160 | bytes 4587528 | tf_op jit(solution)/shard_map/concatenate | solution.py:349
  25.4 86.9 %while.21 = (s32[]{:T(128)}, bf16[1,16,2560]{2,1,0:T(8,128)(2,1)S(1)}, bf16[1,16,2560]{2,1,0:T(8,128)(2,1)S(1)}, f32[1,1,128,2560]{3,2,1,0:T(8,128)}, bf16[4,1,1...) while((s32[]{:T(128)}, ...), condition=%wide.region_2.3_spmd, body=%wide.region_1.2_spmd.sunk | while | flops 146800640 | bytes 8192261 | solution.py:390
  25.5 5.9 %eval_jaxpr.5 = (bf16[16,2560]{1,0:T(8,128)(2,1)}, bf16[16,2560]{1,0:T(8,128)(2,1)}, f32[1,1,128,2560]{3,2,1,0:T(8,128)}, bf16[32,256]{1,0:T(8,128)(2,1)}, bf16[...) custom-call(s32[1]{0:T(128)} %bitcast.108.step_ref, ...), custom_call_target="tpu_custom_call", output_to_operand_aliasing={{2}: (14, {}), {4}: (17, {}), {5}: (18, {})} | custom-call | flops 146800640 | bytes 7536640 | tf_op jit(solution)/shard_map/while/body/eval_jaxpr/pallas_call | solution.py:254
  31.4 1.3 collective-permute-start
  32.7 1.3 collective-permute-start.1
  34.0 4.6 %collective-permute-done = bf16[1,16,2560]{2,1,0:T(8,128)(2,1)S(1)} collective-permute-done((bf16[1,16,2560]{2,1,0:T(8,128)(2,1)}, bf16[1,16,2560]{2,1,0:T(8,128)(2,1)S(1)}, u32[]{:S(2)}, u32[]{:S(2)}) %collective-permute-start) | collective-permute-done | bytes 81952 | tf_op jit(solution)/shard_map/while/body/eval_jaxpr/ppermute | solution.py:20
  38.5 1.9 %collective-permute-done.1 = bf16[1,16,2560]{2,1,0:T(8,128)(2,1)S(1)} collective-permute-done((bf16[1,16,2560]{2,1,0:T(8,128)(2,1)}, bf16[1,16,2560]{2,1,0:T(8,128)(2,1)S(1)}, u32[]{:S(2)}, u32[]{:S(2)}) %collective-permute-start.1) | collective-permute-done | bytes 81952 | tf_op jit(solution)/shard_map/while/body/eval_jaxpr/ppermute | solution.py:20
  40.5 5.9 %eval_jaxpr.5 = (bf16[16,2560]{1,0:T(8,128)(2,1)}, bf16[16,2560]{1,0:T(8,128)(2,1)}, f32[1,1,128,2560]{3,2,1,0:T(8,128)}, bf16[32,256]{1,0:T(8,128)(2,1)}, bf16[...) custom-call(s32[1]{0:T(128)} %bitcast.108.step_ref, ...), custom_call_target="tpu_custom_call", output_to_operand_aliasing={{2}: (14, {}), {4}: (17, {}), {5}: (18, {})} | custom-call | flops 146800640 | bytes 7536640 | tf_op jit(solution)/shard_map/while/body/eval_jaxpr/pallas_call | solution.py:254
  49.0 4.1 %collective-permute-done = bf16[1,16,2560]{2,1,0:T(8,128)(2,1)S(1)} collective-permute-done((bf16[1,16,2560]{2,1,0:T(8,128)(2,1)}, bf16[1,16,2560]{2,1,0:T(8,128)(2,1)S(1)}, u32[]{:S(2)}, u32[]{:S(2)}) %collective-permute-start) | collective-permute-done | bytes 81952 | tf_op jit(solution)/shard_map/while/body/eval_jaxpr/ppermute | solution.py:20
  53.1 1.8 %collective-permute-done.1 = bf16[1,16,2560]{2,1,0:T(8,128)(2,1)S(1)} collective-permute-done((bf16[1,16,2560]{2,1,0:T(8,128)(2,1)}, bf16[1,16,2560]{2,1,0:T(8,128)(2,1)S(1)}, u32[]{:S(2)}, u32[]{:S(2)}) %collective-permute-start.1) | collective-permute-done | bytes 81952 | tf_op jit(solution)/shard_map/while/body/eval_jaxpr/ppermute | solution.py:20
  54.8 5.9 %eval_jaxpr.5 = (bf16[16,2560]{1,0:T(8,128)(2,1)}, bf16[16,2560]{1,0:T(8,128)(2,1)}, f32[1,1,128,2560]{3,2,1,0:T(8,128)}, bf16[32,256]{1,0:T(8,128)(2,1)}, bf16[...) custom-call(s32[1]{0:T(128)} %bitcast.108.step_ref, ...), custom_call_target="tpu_custom_call", output_to_operand_aliasing={{2}: (14, {}), {4}: (17, {}), {5}: (18, {})} | custom-call | flops 146800640 | bytes 7536640 | tf_op jit(solution)/shard_map/while/body/eval_jaxpr/pallas_call | solution.py:254
  63.3 4.6 %collective-permute-done = bf16[1,16,2560]{2,1,0:T(8,128)(2,1)S(1)} collective-permute-done((bf16[1,16,2560]{2,1,0:T(8,128)(2,1)}, bf16[1,16,2560]{2,1,0:T(8,128)(2,1)S(1)}, u32[]{:S(2)}, u32[]{:S(2)}) %collective-permute-start) | collective-permute-done | bytes 81952 | tf_op jit(solution)/shard_map/while/body/eval_jaxpr/ppermute | solution.py:20
  67.9 1.3 %collective-permute-done.1 = bf16[1,16,2560]{2,1,0:T(8,128)(2,1)S(1)} collective-permute-done((bf16[1,16,2560]{2,1,0:T(8,128)(2,1)}, bf16[1,16,2560]{2,1,0:T(8,128)(2,1)S(1)}, u32[]{:S(2)}, u32[]{:S(2)}) %collective-permute-start.1) | collective-permute-done | bytes 81952 | tf_op jit(solution)/shard_map/while/body/eval_jaxpr/ppermute | solution.py:20
  69.2 5.9 %eval_jaxpr.5 = (bf16[16,2560]{1,0:T(8,128)(2,1)}, bf16[16,2560]{1,0:T(8,128)(2,1)}, f32[1,1,128,2560]{3,2,1,0:T(8,128)}, bf16[32,256]{1,0:T(8,128)(2,1)}, bf16[...) custom-call(s32[1]{0:T(128)} %bitcast.108.step_ref, ...), custom_call_target="tpu_custom_call", output_to_operand_aliasing={{2}: (14, {}), {4}: (17, {}), {5}: (18, {})} | custom-call | flops 146800640 | bytes 7536640 | tf_op jit(solution)/shard_map/while/body/eval_jaxpr/pallas_call | solution.py:254
  77.7 4.3 %collective-permute-done = bf16[1,16,2560]{2,1,0:T(8,128)(2,1)S(1)} collective-permute-done((bf16[1,16,2560]{2,1,0:T(8,128)(2,1)}, bf16[1,16,2560]{2,1,0:T(8,128)(2,1)S(1)}, u32[]{:S(2)}, u32[]{:S(2)}) %collective-permute-start) | collective-permute-done | bytes 81952 | tf_op jit(solution)/shard_map/while/body/eval_jaxpr/ppermute | solution.py:20
  82.0 1.6 %collective-permute-done.1 = bf16[1,16,2560]{2,1,0:T(8,128)(2,1)S(1)} collective-permute-done((bf16[1,16,2560]{2,1,0:T(8,128)(2,1)}, bf16[1,16,2560]{2,1,0:T(8,128)(2,1)S(1)}, u32[]{:S(2)}, u32[]{:S(2)}) %collective-permute-start.1) | collective-permute-done | bytes 81952 | tf_op jit(solution)/shard_map/while/body/eval_jaxpr/ppermute | solution.py:20
  83.6 5.9 %eval_jaxpr.5 = (bf16[16,2560]{1,0:T(8,128)(2,1)}, bf16[16,2560]{1,0:T(8,128)(2,1)}, f32[1,1,128,2560]{3,2,1,0:T(8,128)}, bf16[32,256]{1,0:T(8,128)(2,1)}, bf16[...) custom-call(s32[1]{0:T(128)} %bitcast.108.step_ref, ...), custom_call_target="tpu_custom_call", output_to_operand_aliasing={{2}: (14, {}), {4}: (17, {}), {5}: (18, {})} | custom-call | flops 146800640 | bytes 7536640 | tf_op jit(solution)/shard_map/while/body/eval_jaxpr/pallas_call | solution.py:254
  92.1 3.9 %collective-permute-done = bf16[1,16,2560]{2,1,0:T(8,128)(2,1)S(1)} collective-permute-done((bf16[1,16,2560]{2,1,0:T(8,128)(2,1)}, bf16[1,16,2560]{2,1,0:T(8,128)(2,1)S(1)}, u32[]{:S(2)}, u32[]{:S(2)}) %collective-permute-start) | collective-permute-done | bytes 81952 | tf_op jit(solution)/shard_map/while/body/eval_jaxpr/ppermute | solution.py:20
  96.0 1.9 %collective-permute-done.1 = bf16[1,16,2560]{2,1,0:T(8,128)(2,1)S(1)} collective-permute-done((bf16[1,16,2560]{2,1,0:T(8,128)(2,1)}, bf16[1,16,2560]{2,1,0:T(8,128)(2,1)S(1)}, u32[]{:S(2)}, u32[]{:S(2)}) %collective-permute-start.1) | collective-permute-done | bytes 81952 | tf_op jit(solution)/shard_map/while/body/eval_jaxpr/ppermute | solution.py:20
  97.9 5.9 %eval_jaxpr.5 = (bf16[16,2560]{1,0:T(8,128)(2,1)}, bf16[16,2560]{1,0:T(8,128)(2,1)}, f32[1,1,128,2560]{3,2,1,0:T(8,128)}, bf16[32,256]{1,0:T(8,128)(2,1)}, bf16[...) custom-call(s32[1]{0:T(128)} %bitcast.108.step_ref, ...), custom_call_target="tpu_custom_call", output_to_operand_aliasing={{2}: (14, {}), {4}: (17, {}), {5}: (18, {})} | custom-call | flops 146800640 | bytes 7536640 | tf_op jit(solution)/shard_map/while/body/eval_jaxpr/pallas_call | solution.py:254
  106.5 3.9 %collective-permute-done = bf16[1,16,2560]{2,1,0:T(8,128)(2,1)S(1)} collective-permute-done((bf16[1,16,2560]{2,1,0:T(8,128)(2,1)}, bf16[1,16,2560]{2,1,0:T(8,128)(2,1)S(1)}, u32[]{:S(2)}, u32[]{:S(2)}) %collective-permute-start) | collective-permute-done | bytes 81952 | tf_op jit(solution)/shard_map/while/body/eval_jaxpr/ppermute | solution.py:20
  110.4 1.9 %collective-permute-done.1 = bf16[1,16,2560]{2,1,0:T(8,128)(2,1)S(1)} collective-permute-done((bf16[1,16,2560]{2,1,0:T(8,128)(2,1)}, bf16[1,16,2560]{2,1,0:T(8,128)(2,1)S(1)}, u32[]{:S(2)}, u32[]{:S(2)}) %collective-permute-start.1) | collective-permute-done | bytes 81952 | tf_op jit(solution)/shard_map/while/body/eval_jaxpr/ppermute | solution.py:20
  112.3 5.9 %shard_map.59 = (bf16[16,2560]{1,0:T(8,128)(2,1)}, bf16[16,2560]{1,0:T(8,128)(2,1)}, f32[1,1,128,2560]{3,2,1,0:T(8,128)}, bf16[32,256]{1,0:T(8,128)(2,1)}, bf16[...) custom-call(s32[1]{0:T(128)} %constant.45.clone.1.step_ref, ...), custom_call_target="tpu_custom_call", output_to_operand_aliasing={{2}: (14, {}), {4}: (17, {}), {5}: (18, {})} | custom-call | flops 146800640 | bytes 7536640 | tf_op jit(solution)/shard_map/pallas_call | solution.py:254
  118.2 10.0 %all_gather.3 = bf16[8,1,128,256]{3,2,1,0:T(8,128)(2,1)S(1)} all-gather(bf16[1,1,128,256]{3,2,1,0:T(8,128)(2,1)S(1)} %bitcast.118), channel_id=1, replica_groups=mesh['section'=4,'dp'=8] {'dp'}, dimensions={0}, use_global_device_ids=true | all-gather | bytes 589824 | tf_op jit(solution)/shard_map/all_gather | solution.py:403
  128.3 2.1 %fusion.8 = f32[1,320,256]{2,1,0:T(8,128)} fusion(bf16[8,1,128,320]{2,3,1,0:T(8,128)(2,1)} %all-to-all-done, bf16[8,1,128,256]{3,2,1,0:T(8,128)(2,1)S(1)} %all_gather.3), kind=kOutput, calls=%fused_computation.17 | convolution fusion | flops 167854080 | bytes 1507328 | tf_op jit(solution)/shard_map/glrd,glrc->ldc/dot_general | solution.py:404
  (50 shorter events, 18.0 us)
Async XLA Ops:
  0.6 7.6 %copy-start.1 = (bf16[1,1,128,2560]{3,2,1,0:T(8,128)(2,1)S(1)}, bf16[1,1,128,2560]{3,2,1,0:T(8,128)(2,1)}, u32[]{:S(2)}) copy-start(bf16[1,1,128,2560]{3,2,1,0:T(8,128)(2,1)} %param.6) | copy-start | bytes 1966084
  0.6 7.6 %copy-start = (bf16[1,2560,256]{2,1,0:T(8,128)(2,1)S(1)}, bf16[1,2560,256]{2,1,0:T(8,128)(2,1)}, u32[]{:S(2)}) copy-start(bf16[1,2560,256]{2,1,0:T(8,128)(2,1)} %w_ref.1) | copy-start | bytes 3932164
  3.0 125.3 %all-to-all-start = ((bf16[8,1,128,320]{2,3,1,0:T(8,128)(2,1)}), bf16[8,1,128,320]{2,3,1,0:T(8,128)(2,1)}, u32[]{:S(2)}, u32[]{:S(2)}) async-start(bf16[8,1,128,320]{2,3,1,0:T(8,128)(2,1)} %bitcast.31), calls=%async_computation | async-start | bytes 1310720 | tf_op jit(solution)/shard_map/all_to_all | solution.py:401
  8.2 1.2 copy-start.5
  11.6 4.4 %copy-start.3 = (f32[4,2560]{1,0:T(4,128)}, f32[4,2560]{1,0:T(4,128)S(1)}, u32[]{:S(2)}) copy-start(f32[4,2560]{1,0:T(4,128)S(1)} %fusion.18) | copy-start | bytes 122884
  13.4 2.6 %copy-start.2 = (bf16[4,32,2560]{2,1,0:T(8,128)(2,1)}, bf16[4,32,2560]{2,1,0:T(8,128)(2,1)S(1)}, u32[]{:S(2)}) copy-start(bf16[4,32,2560]{2,1,0:T(8,128)(2,1)S(1)} %get-tuple-element.355) | copy-start | bytes 1966084
  21.1 1.8 %copy-start.4 = (f32[4,2560]{1,0:T(4,128)S(1)}, f32[4,2560]{1,0:T(4,128)}, u32[]{:S(2)}) copy-start(f32[4,2560]{1,0:T(4,128)} %copy-done.3) | copy-start | bytes 122884
  31.4 7.2 %collective-permute-start = (bf16[1,16,2560]{2,1,0:T(8,128)(2,1)}, bf16[1,16,2560]{2,1,0:T(8,128)(2,1)S(1)}, u32[]{:S(2)}, u32[]{:S(2)}) collective-permute-start(bf16[1,16,2560]{2,1,0:T(8,128)(2,1)} %bitcast.128), channel_id=1, source_target_pairs={{8,0},{16,8},{24,16},{9,1},{17,9},{25,17},{10,2},{18,10},{26,18},{... | collective-permute-start | bytes 245768 | tf_op jit(solution)/shard_map/while/body/eval_jaxpr/ppermute | solution.py:20
  32.7 7.8 %collective-permute-start.1 = (bf16[1,16,2560]{2,1,0:T(8,128)(2,1)}, bf16[1,16,2560]{2,1,0:T(8,128)(2,1)S(1)}, u32[]{:S(2)}, u32[]{:S(2)}) collective-permute-start(bf16[1,16,2560]{2,1,0:T(8,128)(2,1)} %bitcast.127), channel_id=1, source_target_pairs={{8,0},{16,8},{24,16},{9,1},{17,9},{25,17},{10,2},{18,10},{26,18},{... | collective-permute-start | bytes 245768 | tf_op jit(solution)/shard_map/while/body/eval_jaxpr/ppermute | solution.py:20
  46.4 6.7 %collective-permute-start = (bf16[1,16,2560]{2,1,0:T(8,128)(2,1)}, bf16[1,16,2560]{2,1,0:T(8,128)(2,1)S(1)}, u32[]{:S(2)}, u32[]{:S(2)}) collective-permute-start(bf16[1,16,2560]{2,1,0:T(8,128)(2,1)} %bitcast.128), channel_id=1, source_target_pairs={{8,0},{16,8},{24,16},{9,1},{17,9},{25,17},{10,2},{18,10},{26,18},{... | collective-permute-start | bytes 245768 | tf_op jit(solution)/shard_map/while/body/eval_jaxpr/ppermute | solution.py:20
  47.7 7.2 %collective-permute-start.1 = (bf16[1,16,2560]{2,1,0:T(8,128)(2,1)}, bf16[1,16,2560]{2,1,0:T(8,128)(2,1)S(1)}, u32[]{:S(2)}, u32[]{:S(2)}) collective-permute-start(bf16[1,16,2560]{2,1,0:T(8,128)(2,1)} %bitcast.127), channel_id=1, source_target_pairs={{8,0},{16,8},{24,16},{9,1},{17,9},{25,17},{10,2},{18,10},{26,18},{... | collective-permute-start | bytes 245768 | tf_op jit(solution)/shard_map/while/body/eval_jaxpr/ppermute | solution.py:20
  60.7 7.2 %collective-permute-start = (bf16[1,16,2560]{2,1,0:T(8,128)(2,1)}, bf16[1,16,2560]{2,1,0:T(8,128)(2,1)S(1)}, u32[]{:S(2)}, u32[]{:S(2)}) collective-permute-start(bf16[1,16,2560]{2,1,0:T(8,128)(2,1)} %bitcast.128), channel_id=1, source_target_pairs={{8,0},{16,8},{24,16},{9,1},{17,9},{25,17},{10,2},{18,10},{26,18},{... | collective-permute-start | bytes 245768 | tf_op jit(solution)/shard_map/while/body/eval_jaxpr/ppermute | solution.py:20
  62.0 7.2 %collective-permute-start.1 = (bf16[1,16,2560]{2,1,0:T(8,128)(2,1)}, bf16[1,16,2560]{2,1,0:T(8,128)(2,1)S(1)}, u32[]{:S(2)}, u32[]{:S(2)}) collective-permute-start(bf16[1,16,2560]{2,1,0:T(8,128)(2,1)} %bitcast.127), channel_id=1, source_target_pairs={{8,0},{16,8},{24,16},{9,1},{17,9},{25,17},{10,2},{18,10},{26,18},{... | collective-permute-start | bytes 245768 | tf_op jit(solution)/shard_map/while/body/eval_jaxpr/ppermute | solution.py:20
  75.1 6.9 %collective-permute-start = (bf16[1,16,2560]{2,1,0:T(8,128)(2,1)}, bf16[1,16,2560]{2,1,0:T(8,128)(2,1)S(1)}, u32[]{:S(2)}, u32[]{:S(2)}) collective-permute-start(bf16[1,16,2560]{2,1,0:T(8,128)(2,1)} %bitcast.128), channel_id=1, source_target_pairs={{8,0},{16,8},{24,16},{9,1},{17,9},{25,17},{10,2},{18,10},{26,18},{... | collective-permute-start | bytes 245768 | tf_op jit(solution)/shard_map/while/body/eval_jaxpr/ppermute | solution.py:20
  76.4 7.2 %collective-permute-start.1 = (bf16[1,16,2560]{2,1,0:T(8,128)(2,1)}, bf16[1,16,2560]{2,1,0:T(8,128)(2,1)S(1)}, u32[]{:S(2)}, u32[]{:S(2)}) collective-permute-start(bf16[1,16,2560]{2,1,0:T(8,128)(2,1)} %bitcast.127), channel_id=1, source_target_pairs={{8,0},{16,8},{24,16},{9,1},{17,9},{25,17},{10,2},{18,10},{26,18},{... | collective-permute-start | bytes 245768 | tf_op jit(solution)/shard_map/while/body/eval_jaxpr/ppermute | solution.py:20
  89.5 6.5 %collective-permute-start = (bf16[1,16,2560]{2,1,0:T(8,128)(2,1)}, bf16[1,16,2560]{2,1,0:T(8,128)(2,1)S(1)}, u32[]{:S(2)}, u32[]{:S(2)}) collective-permute-start(bf16[1,16,2560]{2,1,0:T(8,128)(2,1)} %bitcast.128), channel_id=1, source_target_pairs={{8,0},{16,8},{24,16},{9,1},{17,9},{25,17},{10,2},{18,10},{26,18},{... | collective-permute-start | bytes 245768 | tf_op jit(solution)/shard_map/while/body/eval_jaxpr/ppermute | solution.py:20
  90.8 7.2 %collective-permute-start.1 = (bf16[1,16,2560]{2,1,0:T(8,128)(2,1)}, bf16[1,16,2560]{2,1,0:T(8,128)(2,1)S(1)}, u32[]{:S(2)}, u32[]{:S(2)}) collective-permute-start(bf16[1,16,2560]{2,1,0:T(8,128)(2,1)} %bitcast.127), channel_id=1, source_target_pairs={{8,0},{16,8},{24,16},{9,1},{17,9},{25,17},{10,2},{18,10},{26,18},{... | collective-permute-start | bytes 245768 | tf_op jit(solution)/shard_map/while/body/eval_jaxpr/ppermute | solution.py:20
  103.8 6.5 %collective-permute-start = (bf16[1,16,2560]{2,1,0:T(8,128)(2,1)}, bf16[1,16,2560]{2,1,0:T(8,128)(2,1)S(1)}, u32[]{:S(2)}, u32[]{:S(2)}) collective-permute-start(bf16[1,16,2560]{2,1,0:T(8,128)(2,1)} %bitcast.128), channel_id=1, source_target_pairs={{8,0},{16,8},{24,16},{9,1},{17,9},{25,17},{10,2},{18,10},{26,18},{... | collective-permute-start | bytes 245768 | tf_op jit(solution)/shard_map/while/body/eval_jaxpr/ppermute | solution.py:20
  105.1 7.2 %collective-permute-start.1 = (bf16[1,16,2560]{2,1,0:T(8,128)(2,1)}, bf16[1,16,2560]{2,1,0:T(8,128)(2,1)S(1)}, u32[]{:S(2)}, u32[]{:S(2)}) collective-permute-start(bf16[1,16,2560]{2,1,0:T(8,128)(2,1)} %bitcast.127), channel_id=1, source_target_pairs={{8,0},{16,8},{24,16},{9,1},{17,9},{25,17},{10,2},{18,10},{26,18},{... | collective-permute-start | bytes 245768 | tf_op jit(solution)/shard_map/while/body/eval_jaxpr/ppermute | solution.py:20

commit v16 on v14

--- a/solution.py
+++ b/solution.py
@@ -379,24 +379,27 @@
         jnp.zeros((MICRO, lay_dev, seq_dev, block_len, features), jnp.bfloat16),
         jnp.zeros((MICRO, lay_dev, seq_dev, block_len, 2 * state_size), jnp.bfloat16),
     )
-    final_state = lax.fori_loop(0, steps - 1, advance, initial)
-    final_state = advance(steps - 1, final_state, send=False)
+    final_state = lax.fori_loop(0, steps - 2, advance, initial)
+    final_state = advance(steps - 2, final_state)
+    early_all = lax.all_gather(final_state[3][None, 1:], "dp", axis=0, tiled=True)
+    received, early_all = lax.optimization_barrier((final_state[0], early_all))
+    final_state = advance(steps - 1, (received,) + final_state[1:], send=False)
+    late_all = lax.all_gather(final_state[3][None, :1], "dp", axis=0, tiled=True)
     grad_store = final_state[2]
-    map_store = final_state[3]
 
     grad_inputs = jnp.moveaxis(grad_store, 0, 2).reshape(layer_inputs.shape)
-    map_store = jnp.moveaxis(map_store, 0, 2).reshape(bc_all.shape)
     ways = lax.axis_size("dp")
     divisor = ways * seq_dev
     rows_here = layer_inputs.reshape(lay_dev, seq_dev * tok_len, ways, features // ways)
     rows_here = jnp.transpose(rows_here, (2, 0, 1, 3))
     rows_all = lax.all_to_all(rows_here, "dp", 0, 0, tiled=True)
-    maps_here = map_store.reshape(1, lay_dev, seq_dev * tok_len, map_store.shape[-1])
-    maps_all = lax.all_gather(maps_here, "dp", axis=0, tiled=True)
+    rows_all = rows_all.reshape((ways, lay_dev, seq_dev, MICRO, block_len, features // ways))
     grad_w = jnp.einsum(
-        "glrd,glrc->ldc", rows_all, maps_all, preferred_element_type=jnp.float32
-    ) / divisor
-    return (grad_inputs, grad_w)
+        "alsmjd,amlsjc->ldc", rows_all[:, :, :, 1:], early_all, preferred_element_type=jnp.float32
+    ) + jnp.einsum(
+        "alsmjd,amlsjc->ldc", rows_all[:, :, :, :1], late_all, preferred_element_type=jnp.float32
+    )
+    return (grad_inputs, grad_w / divisor)
 
 
 def solution(mesh):

time: 123 us -> 126 us (1.024)
  blocking collectives: 9.81 us -> 19.9 us
  waiting for transfers between devices: 38.8 us -> 32.6 us
  local copies, waits for them, and re-layouts: 5.69 us -> 7.81 us
  other arithmetic: 6.98 us -> 4.9 us
    all_gather x1 -> x2, blocking collectives: 9.81 us -> 19.9 us  [the longest x1 10.6 us: shards(): lax.all_gather(final_state[3][None, 1:], 'dp', axis=0, tiled=True)]
    ppermute x6, waiting for transfers between devices: 38.8 us -> 32.6 us  [passed_along(): return lax.ppermute(block, axis, route)]
    convert_element_type x1, other arithmetic: 2.49 us -> 0.39 us  [shards(): saved.append(state_now.astype(jnp.bfloat16)[None])]
    all_to_all x0 -> x1, local copies, waits for them, and re-layouts: none -> 1.44 us  [shards(): rows_all = lax.all_to_all(rows_here, 'dp', 0, 0, tiled=True)]
    unnamed x13 -> x19, local copies, waits for them, and re-layouts: 2.39 us -> 3.08 us
  transfers between devices with their start and end apart: 7 -> 7, of which waited for: 6 -> 5; matrix products, arithmetic and copies ran while one was open for 14% -> 12% of each run, Pallas kernels for 31% -> 30%
where the time goes in v16:
time: 126 us
  Pallas kernels  38.3 us (30%)
  waiting for transfers between devices  32.6 us (26%)
  blocking collectives  19.9 us (16%)
  starting transfers between devices  12.9 us (10%)
  matrix products  8.17 us (6%)
  local copies, waits for them, and re-layouts  7.81 us (6%)
  other arithmetic  4.9 us (4%)
    pallas_call x7, Pallas kernels, fused_step(): pl.pallas_call(functools.partial(step_kernel, factor=factor, width=width,...  38.3 us
    ppermute x6, waiting for transfers between devices, passed_along(): return lax.ppermute(block, axis, route)  32.6 us
    all_gather x1, blocking collectives, shards(): lax.all_gather(final_state[3][None, 1:], 'dp', axis=0, tiled=True)  10.6 us
    all_gather x1, blocking collectives, shards(): lax.all_gather(final_state[3][None, :1], 'dp', axis=0, tiled=True)  9.27 us
    ppermute x6, starting transfers between devices, passed_along(): return lax.ppermute(block, axis, route)  7.75 us
    all_to_all x1, starting transfers between devices, shards(): rows_all = lax.all_to_all(rows_here, 'dp', 0, 0, tiled=True)  5.17 us
    dot_general x3, matrix products, per_lane(): jnp.einsum('...h,hd->...d', a, spread_heads, precision=lax.Precision.HIGH...  3.78 us
    unnamed x19, local copies, waits for them, and re-layouts  3.08 us
  transfers between devices with their start and end apart: 7, of which 5 were waited for; matrix products, arithmetic and copies ran while one was open for 12% of the time, Pallas kernels for 30%

profile of v16, /device:TPU:0, one launch (start us, length us, event | category | flops | bytes accessed | tf_op | source)
XLA Modules:
  0.0 125.6 jit_solution(1161905950341645526)
XLA Ops:
  0.7 2.4 %copy.34 = bf16[1,1,128,2560]{2,3,1,0:T(8,128)(2,1)} copy(bf16[1,1,128,2560]{3,2,1,0:T(8,128)(2,1)} %param.6) | data formatting | bytes 1310720 | tf_op args[0]
  3.0 5.2 %all-to-all-start = ((bf16[8,1,128,320]{2,3,1,0:T(8,128)(2,1)}), bf16[8,1,128,320]{2,3,1,0:T(8,128)(2,1)}, u32[]{:S(2)}, u32[]{:S(2)}) async-start(bf16[8,1,128,320]{2,3,1,0:T(8,128)(2,1)} %bitcast.32), calls=%async_computation | async-start | bytes 1310720 | tf_op jit(solution)/shard_map/all_to_all | solution.py:395
  9.6 1.8 %convolution_bitcast_fusion.lead_ref = f32[4,1,1,32,2560]{4,3,2,1,0:T(8,128)} fusion(s32[2560]{0:T(1024)S(1)} %add_select_fusion, f32[4,1,1,32,40]{4,3,2,1,0:T(8,128)S(1)} %reduce_window_sum.11), kind=kOutput, calls=%fused_computation | convolution fusion | flops 157388800 | bytes 1341440 | tf_op jit(solution)/shard_map/...h,hd->...d/dot_general | solution.py:320
  11.6 1.8 %fusion.4 = (bf16[4,32,2560]{2,1,0:T(8,128)(2,1)S(1)}, f32[4,32,2560]{2,1,0:T(8,128)}) fusion(bf16[4,32,2560]{2,1,0:T(8,128)(2,1)S(1)} %bitcast.126, s32[2560]{0:T(1024)S(1)} %add_select_fusion, f32[4,40]{1,0:T(4,128)S(1)} %bitcast.141, f32[4,1,1,32,40]{4,3,2,1,0:T(8,128)S(1)} %reduce_window_sum.11), kind=kOutput, calls=%fused_computation.12 | convolution fusion | flops 158376960 | bytes 2652800 | tf_op jit(solution)/shard_map/...h,hd->...d/dot_general | solution.py:320
  13.4 2.6 %fusion.15 = f32[3,128,2560]{2,1,0:T(8,128)} fusion(bf16[4,32,2560]{2,1,0:T(8,128)(2,1)S(1)} %get-tuple-element.350, bf16[4,1,1,32,256]{4,3,2,1,0:T(8,128)(2,1)S(1)} %bitcast.138), kind=kOutput, calls=%fused_computation.25 | convolution fusion | flops 62914560 | bytes 4448256 | tf_op jit(solution)/shard_map/mlsnj,mlsjd->mlsnd/dot_general | solution.py:330
  17.0 1.7 %multiply_convert_fusion.wt_ref = bf16[4,1,1,40,32,32]{5,4,3,2,1,0:T(8,128)(2,1)} fusion(f32[4,32,32]{2,1,0:T(8,128)S(1)} %convolution_multiply_fusion, f32[4,40,32]{2,1,0:T(8,128)S(1)} %copy.30, pred[32,32]{1,0:T(8,128)(4,1)S(1)} %iota_compare_fusion.3), kind=kLoop, calls=%fused_computation.3 | loop fusion | flops 819200 | bytes 365568 | tf_op jit(solution)/shard_map/vmap(vmap(vmap()))/convert_element_type | solution.py:128
  19.1 1.8 %pad_maximum_fusion.sb_ref = bf16[4,1,1,128,2560]{4,3,2,1,0:T(8,128)(2,1)} fusion(bf16[1,1,1,128,2560]{4,3,2,1,0:T(8,128)(2,1)S(1)} %get-tuple-element.346, bf16[1,1,1,128,2560]{4,3,2,1,0:T(8,128)(2,1)S(1)} %get-tuple-element.345, bf16[1,1,1,128,2560]{4,3,2,1,0:T(8,128)(2,1)S(1)} %get-tuple-element.347, bf16[4]{0:T(256)(128)(2,1)S(1)} %pad.clone), kind=kLoop, calls=%fused_computation.1 | loop fusion | flops 3932160 | bytes 4587528 | tf_op jit(solution)/shard_map/concatenate | solution.py:341
  21.3 1.2 broadcast.401
  22.5 0.9 broadcast_in_dim.105
  23.4 66.5 %while.19 = (s32[]{:T(128)}, bf16[1,32,2560]{2,1,0:T(8,128)(2,1)S(1)}, f32[1,1,128,2560]{3,2,1,0:T(8,128)}, bf16[4,1,1,32,2560]{4,3,2,1,0:T(8,128)(2,1)}, bf16[4...) while((s32[]{:T(128)}, ...), condition=%wide.region_2.3_spmd, body=%wide.region_1.2_spmd.sunk | while | flops 146800640 | bytes 8192213 | solution.py:382
  23.4 5.5 %eval_jaxpr.5 = (bf16[32,2560]{1,0:T(8,128)(2,1)}, f32[1,1,128,2560]{3,2,1,0:T(8,128)}, bf16[32,256]{1,0:T(8,128)(2,1)}, bf16[4,1,1,32,2560]{4,3,2,1,0:T(8,128)(2,1)}, bf16[4,1,1,32,256]{4,3,2,1,0:T(8,128)(2,1)S(1)}) custom-call(s32[1]{0:T(128)} %bitcast.122.step_ref, ...), custom_call_target="tpu_custom_call", output_to_operand_aliasing={{1}: (13, {}), {3}: (16, {}), {4}: (17, {})} | custom-call | flops 146800640 | bytes 7536640 | tf_op jit(solution)/shard_map/while/body/eval_jaxpr/pallas_call | solution.py:248
  28.9 1.3 %collective-permute-start = (bf16[1,32,2560]{2,1,0:T(8,128)(2,1)}, bf16[1,32,2560]{2,1,0:T(8,128)(2,1)S(1)}, u32[]{:S(2)}, u32[]{:S(2)}) collective-permute-start(bf16[1,32,2560]{2,1,0:T(8,128)(2,1)} %bitcast.143), channel_id=1, source_target_pairs={{8,0},{16,8},{24,16},{9,1},{17,9},{25,17},{10,2},{18,10},{26,18},{... | collective-permute-start | bytes 491528 | tf_op jit(solution)/shard_map/while/body/eval_jaxpr/ppermute | solution.py:20
  30.2 7.6 %collective-permute-done = bf16[1,32,2560]{2,1,0:T(8,128)(2,1)S(1)} collective-permute-done((bf16[1,32,2560]{2,1,0:T(8,128)(2,1)}, bf16[1,32,2560]{2,1,0:T(8,128)(2,1)S(1)}, u32[]{:S(2)}, u32[]{:S(2)}) %collective-permute-start) | collective-permute-done | bytes 163872 | tf_op jit(solution)/shard_map/while/body/eval_jaxpr/ppermute | solution.py:20
  37.8 5.5 %eval_jaxpr.5 = (bf16[32,2560]{1,0:T(8,128)(2,1)}, f32[1,1,128,2560]{3,2,1,0:T(8,128)}, bf16[32,256]{1,0:T(8,128)(2,1)}, bf16[4,1,1,32,2560]{4,3,2,1,0:T(8,128)(2,1)}, bf16[4,1,1,32,256]{4,3,2,1,0:T(8,128)(2,1)S(1)}) custom-call(s32[1]{0:T(128)} %bitcast.122.step_ref, ...), custom_call_target="tpu_custom_call", output_to_operand_aliasing={{1}: (13, {}), {3}: (16, {}), {4}: (17, {})} | custom-call | flops 146800640 | bytes 7536640 | tf_op jit(solution)/shard_map/while/body/eval_jaxpr/pallas_call | solution.py:248
  43.3 1.3 %collective-permute-start = (bf16[1,32,2560]{2,1,0:T(8,128)(2,1)}, bf16[1,32,2560]{2,1,0:T(8,128)(2,1)S(1)}, u32[]{:S(2)}, u32[]{:S(2)}) collective-permute-start(bf16[1,32,2560]{2,1,0:T(8,128)(2,1)} %bitcast.143), channel_id=1, source_target_pairs={{8,0},{16,8},{24,16},{9,1},{17,9},{25,17},{10,2},{18,10},{26,18},{... | collective-permute-start | bytes 491528 | tf_op jit(solution)/shard_map/while/body/eval_jaxpr/ppermute | solution.py:20
  44.6 6.7 %collective-permute-done = bf16[1,32,2560]{2,1,0:T(8,128)(2,1)S(1)} collective-permute-done((bf16[1,32,2560]{2,1,0:T(8,128)(2,1)}, bf16[1,32,2560]{2,1,0:T(8,128)(2,1)S(1)}, u32[]{:S(2)}, u32[]{:S(2)}) %collective-permute-start) | collective-permute-done | bytes 163872 | tf_op jit(solution)/shard_map/while/body/eval_jaxpr/ppermute | solution.py:20
  51.3 5.5 %eval_jaxpr.5 = (bf16[32,2560]{1,0:T(8,128)(2,1)}, f32[1,1,128,2560]{3,2,1,0:T(8,128)}, bf16[32,256]{1,0:T(8,128)(2,1)}, bf16[4,1,1,32,2560]{4,3,2,1,0:T(8,128)(2,1)}, bf16[4,1,1,32,256]{4,3,2,1,0:T(8,128)(2,1)S(1)}) custom-call(s32[1]{0:T(128)} %bitcast.122.step_ref, ...), custom_call_target="tpu_custom_call", output_to_operand_aliasing={{1}: (13, {}), {3}: (16, {}), {4}: (17, {})} | custom-call | flops 146800640 | bytes 7536640 | tf_op jit(solution)/shard_map/while/body/eval_jaxpr/pallas_call | solution.py:248
  56.7 1.3 %collective-permute-start = (bf16[1,32,2560]{2,1,0:T(8,128)(2,1)}, bf16[1,32,2560]{2,1,0:T(8,128)(2,1)S(1)}, u32[]{:S(2)}, u32[]{:S(2)}) collective-permute-start(bf16[1,32,2560]{2,1,0:T(8,128)(2,1)} %bitcast.143), channel_id=1, source_target_pairs={{8,0},{16,8},{24,16},{9,1},{17,9},{25,17},{10,2},{18,10},{26,18},{... | collective-permute-start | bytes 491528 | tf_op jit(solution)/shard_map/while/body/eval_jaxpr/ppermute | solution.py:20
  58.0 6.1 %collective-permute-done = bf16[1,32,2560]{2,1,0:T(8,128)(2,1)S(1)} collective-permute-done((bf16[1,32,2560]{2,1,0:T(8,128)(2,1)}, bf16[1,32,2560]{2,1,0:T(8,128)(2,1)S(1)}, u32[]{:S(2)}, u32[]{:S(2)}) %collective-permute-start) | collective-permute-done | bytes 163872 | tf_op jit(solution)/shard_map/while/body/eval_jaxpr/ppermute | solution.py:20
  64.2 5.5 %eval_jaxpr.5 = (bf16[32,2560]{1,0:T(8,128)(2,1)}, f32[1,1,128,2560]{3,2,1,0:T(8,128)}, bf16[32,256]{1,0:T(8,128)(2,1)}, bf16[4,1,1,32,2560]{4,3,2,1,0:T(8,128)(2,1)}, bf16[4,1,1,32,256]{4,3,2,1,0:T(8,128)(2,1)S(1)}) custom-call(s32[1]{0:T(128)} %bitcast.122.step_ref, ...), custom_call_target="tpu_custom_call", output_to_operand_aliasing={{1}: (13, {}), {3}: (16, {}), {4}: (17, {})} | custom-call | flops 146800640 | bytes 7536640 | tf_op jit(solution)/shard_map/while/body/eval_jaxpr/pallas_call | solution.py:248
  69.6 1.3 %collective-permute-start = (bf16[1,32,2560]{2,1,0:T(8,128)(2,1)}, bf16[1,32,2560]{2,1,0:T(8,128)(2,1)S(1)}, u32[]{:S(2)}, u32[]{:S(2)}) collective-permute-start(bf16[1,32,2560]{2,1,0:T(8,128)(2,1)} %bitcast.143), channel_id=1, source_target_pairs={{8,0},{16,8},{24,16},{9,1},{17,9},{25,17},{10,2},{18,10},{26,18},{... | collective-permute-start | bytes 491528 | tf_op jit(solution)/shard_map/while/body/eval_jaxpr/ppermute | solution.py:20
  70.9 6.1 %collective-permute-done = bf16[1,32,2560]{2,1,0:T(8,128)(2,1)S(1)} collective-permute-done((bf16[1,32,2560]{2,1,0:T(8,128)(2,1)}, bf16[1,32,2560]{2,1,0:T(8,128)(2,1)S(1)}, u32[]{:S(2)}, u32[]{:S(2)}) %collective-permute-start) | collective-permute-done | bytes 163872 | tf_op jit(solution)/shard_map/while/body/eval_jaxpr/ppermute | solution.py:20
  77.0 5.5 %eval_jaxpr.5 = (bf16[32,2560]{1,0:T(8,128)(2,1)}, f32[1,1,128,2560]{3,2,1,0:T(8,128)}, bf16[32,256]{1,0:T(8,128)(2,1)}, bf16[4,1,1,32,2560]{4,3,2,1,0:T(8,128)(2,1)}, bf16[4,1,1,32,256]{4,3,2,1,0:T(8,128)(2,1)S(1)}) custom-call(s32[1]{0:T(128)} %bitcast.122.step_ref, ...), custom_call_target="tpu_custom_call", output_to_operand_aliasing={{1}: (13, {}), {3}: (16, {}), {4}: (17, {})} | custom-call | flops 146800640 | bytes 7536640 | tf_op jit(solution)/shard_map/while/body/eval_jaxpr/pallas_call | solution.py:248
  82.5 1.3 %collective-permute-start = (bf16[1,32,2560]{2,1,0:T(8,128)(2,1)}, bf16[1,32,2560]{2,1,0:T(8,128)(2,1)S(1)}, u32[]{:S(2)}, u32[]{:S(2)}) collective-permute-start(bf16[1,32,2560]{2,1,0:T(8,128)(2,1)} %bitcast.143), channel_id=1, source_target_pairs={{8,0},{16,8},{24,16},{9,1},{17,9},{25,17},{10,2},{18,10},{26,18},{... | collective-permute-start | bytes 491528 | tf_op jit(solution)/shard_map/while/body/eval_jaxpr/ppermute | solution.py:20
  83.8 6.1 %collective-permute-done = bf16[1,32,2560]{2,1,0:T(8,128)(2,1)S(1)} collective-permute-done((bf16[1,32,2560]{2,1,0:T(8,128)(2,1)}, bf16[1,32,2560]{2,1,0:T(8,128)(2,1)S(1)}, u32[]{:S(2)}, u32[]{:S(2)}) %collective-permute-start) | collective-permute-done | bytes 163872 | tf_op jit(solution)/shard_map/while/body/eval_jaxpr/ppermute | solution.py:20
  89.9 5.5 %shard_map.59 = (bf16[32,2560]{1,0:T(8,128)(2,1)}, f32[1,1,128,2560]{3,2,1,0:T(8,128)}, bf16[32,256]{1,0:T(8,128)(2,1)}, bf16[4,1,1,32,2560]{4,3,2,1,0:T(8,128)(2,1)}, bf16[4,1,1,32,256]{4,3,2,1,0:T(8,128)(2,1)S(1)}) custom-call(s32[1]{0:T(128)} %constant.58.clone.1.step_ref, ...), custom_call_target="tpu_custom_call", output_to_operand_aliasing={{1}: (13, {}), {3}: (16, {}), {4}: (17, {})} | custom-call | flops 146800640 | bytes 7536640 | tf_op jit(solution)/shard_map/pallas_call | solution.py:248
  95.4 1.3 %collective-permute-start.1 = (bf16[1,32,2560]{2,1,0:T(8,128)(2,1)}, bf16[1,32,2560]{2,1,0:T(8,128)(2,1)S(1)}, u32[]{:S(2)}, u32[]{:S(2)}) collective-permute-start(bf16[1,32,2560]{2,1,0:T(8,128)(2,1)} %bitcast.142), channel_id=1, source_target_pairs={{8,0},{16,8},{24,16},{9,1},{17,9},{25,17},{10,2},{18,10},{26,18},{... | collective-permute-start | bytes 491528 | tf_op jit(solution)/shard_map/ppermute | solution.py:20
  96.7 10.6 %all-gather = bf16[24,1,1,32,256]{4,3,2,1,0:T(8,128)(2,1)} all-gather(bf16[3,1,1,32,256]{4,3,2,1,0:T(8,128)(2,1)S(1)} %slice.64), channel_id=2, replica_groups=mesh['section'=4,'dp'=8] {'dp'}, dimensions={0}, use_global_device_ids=true | all-gather | bytes 442368 | tf_op jit(solution)/shard_map/all_gather | solution.py:384
  108.0 5.5 %shard_map.60 = (bf16[32,2560]{1,0:T(8,128)(2,1)}, f32[1,1,128,2560]{3,2,1,0:T(8,128)}, bf16[32,256]{1,0:T(8,128)(2,1)}, bf16[4,1,1,32,2560]{4,3,2,1,0:T(8,128)(2,1)}, bf16[4,1,1,32,256]{4,3,2,1,0:T(8,128)(2,1)S(1)}) custom-call(s32[1]{0:T(128)} %constant.46.clone.1.step_ref, ...), custom_call_target="tpu_custom_call", output_to_operand_aliasing={{1}: (13, {}), {3}: (16, {}), {4}: (17, {})} | custom-call | flops 146800640 | bytes 7536640 | tf_op jit(solution)/shard_map/pallas_call | solution.py:248
  113.5 9.3 %all-gather.1 = bf16[8,1,1,32,256]{4,3,2,1,0:T(8,128)(2,1)S(1)} all-gather(bf16[1,1,1,32,256]{4,3,2,1,0:T(8,128)(2,1)S(1)} %slice.66), channel_id=3, replica_groups=mesh['section'=4,'dp'=8] {'dp'}, dimensions={0}, use_global_device_ids=true | all-gather | bytes 147456 | tf_op jit(solution)/shard_map/all_gather | solution.py:387
  122.8 1.4 %copy.36 = bf16[8,1,128,320]{3,2,0,1:T(8,128)(2,1)S(1)} copy(bf16[8,1,128,320]{2,3,1,0:T(8,128)(2,1)} %all-to-all-done) | data formatting | bytes 1310720 | tf_op jit(solution)/shard_map/all_to_all | solution.py:395
  124.5 1.1 fusion.9
  (48 shorter events, 4.3 us)
Async XLA Ops:
  0.6 7.6 %copy-start.1 = (bf16[1,1,128,2560]{3,2,1,0:T(8,128)(2,1)S(1)}, bf16[1,1,128,2560]{3,2,1,0:T(8,128)(2,1)}, u32[]{:S(2)}) copy-start(bf16[1,1,128,2560]{3,2,1,0:T(8,128)(2,1)} %param.6) | copy-start | bytes 1966084
  0.6 7.6 %copy-start = (bf16[1,2560,256]{2,1,0:T(8,128)(2,1)S(1)}, bf16[1,2560,256]{2,1,0:T(8,128)(2,1)}, u32[]{:S(2)}) copy-start(bf16[1,2560,256]{2,1,0:T(8,128)(2,1)} %w_ref.3) | copy-start | bytes 3932164
  3.0 119.8 %all-to-all-start = ((bf16[8,1,128,320]{2,3,1,0:T(8,128)(2,1)}), bf16[8,1,128,320]{2,3,1,0:T(8,128)(2,1)}, u32[]{:S(2)}, u32[]{:S(2)}) async-start(bf16[8,1,128,320]{2,3,1,0:T(8,128)(2,1)} %bitcast.32), calls=%async_computation | async-start | bytes 1310720 | tf_op jit(solution)/shard_map/all_to_all | solution.py:395
  8.2 1.2 copy-start.8
  11.6 4.4 %copy-start.6 = (f32[4,2560]{1,0:T(4,128)}, f32[4,2560]{1,0:T(4,128)S(1)}, u32[]{:S(2)}) copy-start(f32[4,2560]{1,0:T(4,128)S(1)} %fusion.17) | copy-start | bytes 122884
  13.4 2.6 %copy-start.2 = (bf16[4,32,2560]{2,1,0:T(8,128)(2,1)}, bf16[4,32,2560]{2,1,0:T(8,128)(2,1)S(1)}, u32[]{:S(2)}) copy-start(bf16[4,32,2560]{2,1,0:T(8,128)(2,1)S(1)} %get-tuple-element.350) | copy-start | bytes 1966084
  16.2 2.5 %copy-start.3 = (f32[3,128,2560]{2,1,0:T(8,128)S(1)}, f32[3,128,2560]{2,1,0:T(8,128)}, u32[]{:S(2)}) copy-start(f32[3,128,2560]{2,1,0:T(8,128)} %fusion.15) | copy-start | bytes 11796484
  19.1 1.8 %copy-start.7 = (f32[4,2560]{1,0:T(4,128)S(1)}, f32[4,2560]{1,0:T(4,128)}, u32[]{:S(2)}) copy-start(f32[4,2560]{1,0:T(4,128)} %copy-done.6) | copy-start | bytes 122884
  28.9 8.9 %collective-permute-start = (bf16[1,32,2560]{2,1,0:T(8,128)(2,1)}, bf16[1,32,2560]{2,1,0:T(8,128)(2,1)S(1)}, u32[]{:S(2)}, u32[]{:S(2)}) collective-permute-start(bf16[1,32,2560]{2,1,0:T(8,128)(2,1)} %bitcast.143), channel_id=1, source_target_pairs={{8,0},{16,8},{24,16},{9,1},{17,9},{25,17},{10,2},{18,10},{26,18},{... | collective-permute-start | bytes 491528 | tf_op jit(solution)/shard_map/while/body/eval_jaxpr/ppermute | solution.py:20
  43.3 8.0 %collective-permute-start = (bf16[1,32,2560]{2,1,0:T(8,128)(2,1)}, bf16[1,32,2560]{2,1,0:T(8,128)(2,1)S(1)}, u32[]{:S(2)}, u32[]{:S(2)}) collective-permute-start(bf16[1,32,2560]{2,1,0:T(8,128)(2,1)} %bitcast.143), channel_id=1, source_target_pairs={{8,0},{16,8},{24,16},{9,1},{17,9},{25,17},{10,2},{18,10},{26,18},{... | collective-permute-start | bytes 491528 | tf_op jit(solution)/shard_map/while/body/eval_jaxpr/ppermute | solution.py:20
  56.7 7.4 %collective-permute-start = (bf16[1,32,2560]{2,1,0:T(8,128)(2,1)}, bf16[1,32,2560]{2,1,0:T(8,128)(2,1)S(1)}, u32[]{:S(2)}, u32[]{:S(2)}) collective-permute-start(bf16[1,32,2560]{2,1,0:T(8,128)(2,1)} %bitcast.143), channel_id=1, source_target_pairs={{8,0},{16,8},{24,16},{9,1},{17,9},{25,17},{10,2},{18,10},{26,18},{... | collective-permute-start | bytes 491528 | tf_op jit(solution)/shard_map/while/body/eval_jaxpr/ppermute | solution.py:20
  69.6 7.4 %collective-permute-start = (bf16[1,32,2560]{2,1,0:T(8,128)(2,1)}, bf16[1,32,2560]{2,1,0:T(8,128)(2,1)S(1)}, u32[]{:S(2)}, u32[]{:S(2)}) collective-permute-start(bf16[1,32,2560]{2,1,0:T(8,128)(2,1)} %bitcast.143), channel_id=1, source_target_pairs={{8,0},{16,8},{24,16},{9,1},{17,9},{25,17},{10,2},{18,10},{26,18},{... | collective-permute-start | bytes 491528 | tf_op jit(solution)/shard_map/while/body/eval_jaxpr/ppermute | solution.py:20
  82.5 7.4 %collective-permute-start = (bf16[1,32,2560]{2,1,0:T(8,128)(2,1)}, bf16[1,32,2560]{2,1,0:T(8,128)(2,1)S(1)}, u32[]{:S(2)}, u32[]{:S(2)}) collective-permute-start(bf16[1,32,2560]{2,1,0:T(8,128)(2,1)} %bitcast.143), channel_id=1, source_target_pairs={{8,0},{16,8},{24,16},{9,1},{17,9},{25,17},{10,2},{18,10},{26,18},{... | collective-permute-start | bytes 491528 | tf_op jit(solution)/shard_map/while/body/eval_jaxpr/ppermute | solution.py:20
  95.4 11.9 %collective-permute-start.1 = (bf16[1,32,2560]{2,1,0:T(8,128)(2,1)}, bf16[1,32,2560]{2,1,0:T(8,128)(2,1)S(1)}, u32[]{:S(2)}, u32[]{:S(2)}) collective-permute-start(bf16[1,32,2560]{2,1,0:T(8,128)(2,1)} %bitcast.142), channel_id=1, source_target_pairs={{8,0},{16,8},{24,16},{9,1},{17,9},{25,17},{10,2},{18,10},{26,18},{... | collective-permute-start | bytes 491528 | tf_op jit(solution)/shard_map/ppermute | solution.py:20
  107.3 0.7 copy-start.5
  113.5 11.0 %copy-start.4 = (bf16[24,1,1,32,256]{4,3,2,1,0:T(8,128)(2,1)S(1)}, bf16[24,1,1,32,256]{4,3,2,1,0:T(8,128)(2,1)}, u32[]{:S(2)}) copy-start(bf16[24,1,1,32,256]{4,3,2,1,0:T(8,128)(2,1)} %all-gather) | copy-start | bytes 1179652

commit v17 on v14

--- a/solution.py
+++ b/solution.py
@@ -139,7 +139,7 @@
     step_ref, tab_ref, wt_ref, dec_ref, inc_ref, top_ref, x_ref, b_ref, c_ref, tail_ref, lead_ref, xt_ref,
     sb_ref, r_ref, end_ref, w_ref, gs_ref, ms_ref, out_ref, rnew_ref, dbc_ref, gstore_ref, mstore_ref,
     v_ref, gx_ref, tail_buf, lead_buf, xt_buf, sb_buf, r_buf, w_buf, sems, *, factor, width,
-    level_pos, levels, level_no, seq_no
+    level_pos, levels, level_no, seq_no, need_carry
 ):
     base = (step_ref[0] * levels + level_pos) * 3
     blk = tab_ref[base]
@@ -203,8 +203,10 @@
         jnp.dot(mixing, in_map, preferred_element_type=f32)
         + lax.dot_general(lead_grads, sb_buf[...], nt, preferred_element_type=f32)
     )
-    carry = factor * lax.dot_general(out_map, lead_grads, tn, preferred_element_type=f32)
-    rnew_ref[...] = carry + end_ref[...] * r_buf[...]
+    if need_carry:
+        carry = factor * lax.dot_general(out_map, lead_grads, tn, preferred_element_type=f32)
+    if need_carry:
+        rnew_ref[...] = carry + end_ref[...] * r_buf[...]
     grad_bc = jnp.concatenate([grad_inmap, grad_outmap], axis=1).astype(bf16)
     dbc_ref[...] = grad_bc
     mstore_ref[...] = jnp.where(tab_ref[base + 2] > 0, grad_bc, ms_ref[...])
@@ -215,7 +217,7 @@
     gstore_ref[...] = jnp.where(tab_ref[base + 2] > 0, summed, gs_ref[...])
 
 
-def fused_step(step_arr, table, level_pos, levels, per_block, incoming, top_blk, carried, w_bc, grad_store, map_store, level_no, seq_no, factor, width):
+def fused_step(step_arr, table, level_pos, levels, per_block, incoming, top_blk, carried, w_bc, grad_store, map_store, level_no, seq_no, factor, width, need_carry=True):
     wt2, dec2, x_flat, in_blk, out_blk, tail_full, lead_full, xt_full, states_t, end_row = per_block
     length, features = incoming.shape[1:]
     state_size = in_blk.shape[-1]
@@ -248,7 +250,7 @@
     return pl.pallas_call(
         functools.partial(
             step_kernel, factor=factor, width=width, level_pos=level_pos, levels=levels,
-            level_no=level_no, seq_no=seq_no,
+            level_no=level_no, seq_no=seq_no, need_carry=need_carry,
         ),
         out_shape=(
             jax.ShapeDtypeStruct((length, features), jnp.bfloat16),
@@ -365,7 +367,7 @@
             for seq_no in range(seq_dev):
                 level_grads, carried, grad_bc, grad_store, map_store = fused_step(
                     step_arr, table, level_pos, lay_dev, per_block, incoming, top_blk, carried,
-                    w_bc, grad_store, map_store, level_no, seq_no, factor, width,
+                    w_bc, grad_store, map_store, level_no, seq_no, factor, width, send,
                 )
                 level_out.append(level_grads)
             incoming = jnp.stack(level_out)
@@ -377,7 +379,7 @@
         jnp.zeros((seq_dev, block_len, features), jnp.bfloat16),
         jnp.zeros(states_t.shape[1:], jnp.float32),
         jnp.zeros((MICRO, lay_dev, seq_dev, block_len, features), jnp.bfloat16),
-        jnp.zeros((MICRO, lay_dev, seq_dev, block_len, 2 * state_size), jnp.bfloat16),
+        bc_all.reshape((MICRO, lay_dev, seq_dev, block_len, 2 * state_size)),
     )
     final_state = lax.fori_loop(0, steps - 1, advance, initial)
     final_state = advance(steps - 1, final_state, send=False)

time: 123 us -> 125 us (1.016)
  transfers between devices with their start and end apart: 7 -> 7, of which waited for: 6 -> 6; matrix products, arithmetic and copies ran while one was open for 14% -> 16% of each run, Pallas kernels for 31% -> 31%
where the time goes in v17:
time: 125 us
  waiting for transfers between devices  38.8 us (31%)
  Pallas kernels  38.3 us (31%)
  starting transfers between devices  12.9 us (10%)
  blocking collectives  9.83 us (8%)
  matrix products  9.62 us (8%)
  other arithmetic  7.94 us (6%)
  local copies, waits for them, and re-layouts  6.28 us (5%)
    ppermute x6, waiting for transfers between devices, passed_along(): return lax.ppermute(block, axis, route)  38.8 us
    pallas_call x7, Pallas kernels, fused_step(): pl.pallas_call(functools.partial(step_kernel, factor=factor, width=width,...  38.3 us
    all_gather x1, blocking collectives, shards(): maps_all = lax.all_gather(maps_here, 'dp', axis=0, tiled=True)  9.83 us
    ppermute x6, starting transfers between devices, passed_along(): return lax.ppermute(block, axis, route)  7.75 us
    all_to_all x1, starting transfers between devices, shards(): rows_all = lax.all_to_all(rows_here, 'dp', 0, 0, tiled=True)  5.17 us
    dot_general x3, matrix products, per_lane(): jnp.einsum('...h,hd->...d', a, spread_heads, precision=lax.Precision.HIGH...  3.8 us
    dot_general x1, matrix products, shards(): jnp.einsum('mlsnj,mlsjd->mlsnd', jnp.swapaxes(in_blk[:MICRO - 1], -1, -2)...  2.57 us
  transfers between devices with their start and end apart: 7, of which 6 were waited for; matrix products, arithmetic and copies ran while one was open for 16% of the time, Pallas kernels for 31%

profile of v17, /device:TPU:0, one launch (start us, length us, event | category | flops | bytes accessed | tf_op | source)
XLA Modules:
  0.0 124.6 jit_solution(15274261775177118053)
XLA Ops:
  0.7 2.4 %copy.32 = bf16[1,1,128,2560]{2,3,1,0:T(8,128)(2,1)} copy(bf16[1,1,128,2560]{3,2,1,0:T(8,128)(2,1)} %param.6) | data formatting | bytes 1310720 | tf_op args[0]
  3.0 5.2 %all-to-all-start = ((bf16[8,1,128,320]{2,3,1,0:T(8,128)(2,1)}), bf16[8,1,128,320]{2,3,1,0:T(8,128)(2,1)}, u32[]{:S(2)}, u32[]{:S(2)}) async-start(bf16[8,1,128,320]{2,3,1,0:T(8,128)(2,1)} %bitcast.30), calls=%async_computation | async-start | bytes 1310720 | tf_op jit(solution)/shard_map/all_to_all | solution.py:395
  10.2 1.7 %convolution_bitcast_fusion.lead_ref = f32[4,1,1,32,2560]{4,3,2,1,0:T(8,128)} fusion(s32[2560]{0:T(1024)S(1)} %add_select_fusion, f32[4,1,1,32,40]{4,3,2,1,0:T(8,128)S(1)} %reduce_window_sum.11), kind=kOutput, calls=%fused_computation | convolution fusion | flops 157388800 | bytes 1341440 | tf_op jit(solution)/shard_map/...h,hd->...d/dot_general | solution.py:322
  12.2 1.8 %fusion.4 = (bf16[4,32,2560]{2,1,0:T(8,128)(2,1)S(1)}, f32[4,32,2560]{2,1,0:T(8,128)}) fusion(bf16[4,32,2560]{2,1,0:T(8,128)(2,1)S(1)} %bitcast.110, s32[2560]{0:T(1024)S(1)} %add_select_fusion, f32[4,40]{1,0:T(4,128)S(1)} %bitcast.124, f32[4,1,1,32,40]{4,3,2,1,0:T(8,128)S(1)} %reduce_window_sum.11), kind=kOutput, calls=%fused_computation.12 | convolution fusion | flops 158376960 | bytes 2652800 | tf_op jit(solution)/shard_map/...h,hd->...d/dot_general | solution.py:322
  14.0 2.6 %fusion.16 = f32[3,128,2560]{2,1,0:T(8,128)} fusion(bf16[4,32,2560]{2,1,0:T(8,128)(2,1)S(1)} %get-tuple-element.338, bf16[4,1,1,32,256]{4,3,2,1,0:T(8,128)(2,1)S(1)} %bitcast.117), kind=kOutput, calls=%fused_computation.24 | convolution fusion | flops 62914560 | bytes 4448256 | tf_op jit(solution)/shard_map/mlsnj,mlsjd->mlsnd/dot_general | solution.py:332
  17.5 1.7 %exponential_select_fusion = f32[4,1,1,32,32,40]{4,3,5,0,2,1:T(8,128)S(1)} fusion(f32[4,32,40]{1,2,0:T(8,128)} %copy.30, pred[32,32]{1,0:T(8,128)(4,1)S(1)} %iota_compare_fusion.2), kind=kLoop, calls=%fused_computation.2 | loop fusion | flops 491520 | bytes 676864 | tf_op jit(solution)/shard_map/vmap(vmap(vmap(jit(_where))))/select_n | solution.py:119
  19.2 1.7 %multiply_convert_fusion.wt_ref = bf16[4,1,1,40,32,32]{5,4,3,2,1,0:T(8,128)(2,1)} fusion(f32[4,32,32]{2,1,0:T(8,128)S(1)} %copy-done.3, f32[4,40,32]{2,1,0:T(8,128)S(1)} %copy.28, pred[32,32]{1,0:T(8,128)(4,1)S(1)} %iota_compare_fusion.3), kind=kLoop, calls=%fused_computation.3 | loop fusion | flops 819200 | bytes 365568 | tf_op jit(solution)/shard_map/vmap(vmap(vmap()))/convert_element_type | solution.py:128
  20.9 2.5 %fusion.23 = (bf16[1,1,1,128,2560]{4,3,2,1,0:T(8,128)(2,1)S(1)}, bf16[1,1,1,128,2560]{4,3,2,1,0:T(8,128)(2,1)S(1)}, bf16[1,1,1,128,2560]{4,3,2,1,0:T(8,128)(2,1)S(1)}) fusion(f32[3,128,2560]{2,1,0:T(8,128)} %fusion.16, f32[2560]{0:T(1024)S(1)} %get-tuple-element.296, f32[2560]{0:T(1024)S(1)} %get-tuple-element.294, f32[2560]{0:T(1024)S(1)} %get-tuple-element.295), kind=kLoop, calls=%fused_computation.30 | loop fusion | flops 2621440 | bytes 5928960 | tf_op jit(solution)/shard_map/convert_element_type | solution.py:342
  23.4 1.8 %pad_maximum_fusion.sb_ref = bf16[4,1,1,128,2560]{4,3,2,1,0:T(8,128)(2,1)} fusion(bf16[1,1,1,128,2560]{4,3,2,1,0:T(8,128)(2,1)S(1)} %get-tuple-element.334, bf16[1,1,1,128,2560]{4,3,2,1,0:T(8,128)(2,1)S(1)} %get-tuple-element.333, bf16[1,1,1,128,2560]{4,3,2,1,0:T(8,128)(2,1)S(1)} %get-tuple-element.335, bf16[4]{0:T(256)(128)(2,1)S(1)} %pad.clone), kind=kLoop, calls=%fused_computation.1 | loop fusion | flops 3932160 | bytes 4587528 | tf_op jit(solution)/shard_map/concatenate | solution.py:343
  25.6 1.2 broadcast.401
  27.6 79.5 %while.19 = (s32[]{:T(128)}, bf16[1,32,2560]{2,1,0:T(8,128)(2,1)S(1)}, f32[1,1,128,2560]{3,2,1,0:T(8,128)}, bf16[4,1,1,32,2560]{4,3,2,1,0:T(8,128)(2,1)}, bf16[4...) while((s32[]{:T(128)}, ...), condition=%wide.region_2.3_spmd, body=%wide.region_1.2_spmd.sunk | while | flops 146800640 | bytes 8192213 | solution.py:384
  27.7 5.5 %eval_jaxpr.5 = (bf16[32,2560]{1,0:T(8,128)(2,1)}, f32[1,1,128,2560]{3,2,1,0:T(8,128)}, bf16[32,256]{1,0:T(8,128)(2,1)}, bf16[4,1,1,32,2560]{4,3,2,1,0:T(8,128)(2,1)}, bf16[4,1,1,32,256]{4,3,2,1,0:T(8,128)(2,1)S(1)}) custom-call(s32[1]{0:T(128)} %bitcast.106.step_ref, ...), custom_call_target="tpu_custom_call", output_to_operand_aliasing={{1}: (13, {}), {3}: (16, {}), {4}: (17, {})} | custom-call | flops 146800640 | bytes 7536640 | tf_op jit(solution)/shard_map/while/body/eval_jaxpr/pallas_call | solution.py:250
  33.1 1.3 %collective-permute-start = (bf16[1,32,2560]{2,1,0:T(8,128)(2,1)}, bf16[1,32,2560]{2,1,0:T(8,128)(2,1)S(1)}, u32[]{:S(2)}, u32[]{:S(2)}) collective-permute-start(bf16[1,32,2560]{2,1,0:T(8,128)(2,1)} %bitcast.125), channel_id=1, source_target_pairs={{8,0},{16,8},{24,16},{9,1},{17,9},{25,17},{10,2},{18,10},{26,18},{... | collective-permute-start | bytes 491528 | tf_op jit(solution)/shard_map/while/body/eval_jaxpr/ppermute | solution.py:20
  34.4 7.6 %collective-permute-done = bf16[1,32,2560]{2,1,0:T(8,128)(2,1)S(1)} collective-permute-done((bf16[1,32,2560]{2,1,0:T(8,128)(2,1)}, bf16[1,32,2560]{2,1,0:T(8,128)(2,1)S(1)}, u32[]{:S(2)}, u32[]{:S(2)}) %collective-permute-start) | collective-permute-done | bytes 163872 | tf_op jit(solution)/shard_map/while/body/eval_jaxpr/ppermute | solution.py:20
  42.1 5.5 %eval_jaxpr.5 = (bf16[32,2560]{1,0:T(8,128)(2,1)}, f32[1,1,128,2560]{3,2,1,0:T(8,128)}, bf16[32,256]{1,0:T(8,128)(2,1)}, bf16[4,1,1,32,2560]{4,3,2,1,0:T(8,128)(2,1)}, bf16[4,1,1,32,256]{4,3,2,1,0:T(8,128)(2,1)S(1)}) custom-call(s32[1]{0:T(128)} %bitcast.106.step_ref, ...), custom_call_target="tpu_custom_call", output_to_operand_aliasing={{1}: (13, {}), {3}: (16, {}), {4}: (17, {})} | custom-call | flops 146800640 | bytes 7536640 | tf_op jit(solution)/shard_map/while/body/eval_jaxpr/pallas_call | solution.py:250
  47.5 1.3 %collective-permute-start = (bf16[1,32,2560]{2,1,0:T(8,128)(2,1)}, bf16[1,32,2560]{2,1,0:T(8,128)(2,1)S(1)}, u32[]{:S(2)}, u32[]{:S(2)}) collective-permute-start(bf16[1,32,2560]{2,1,0:T(8,128)(2,1)} %bitcast.125), channel_id=1, source_target_pairs={{8,0},{16,8},{24,16},{9,1},{17,9},{25,17},{10,2},{18,10},{26,18},{... | collective-permute-start | bytes 491528 | tf_op jit(solution)/shard_map/while/body/eval_jaxpr/ppermute | solution.py:20
  48.8 6.7 %collective-permute-done = bf16[1,32,2560]{2,1,0:T(8,128)(2,1)S(1)} collective-permute-done((bf16[1,32,2560]{2,1,0:T(8,128)(2,1)}, bf16[1,32,2560]{2,1,0:T(8,128)(2,1)S(1)}, u32[]{:S(2)}, u32[]{:S(2)}) %collective-permute-start) | collective-permute-done | bytes 163872 | tf_op jit(solution)/shard_map/while/body/eval_jaxpr/ppermute | solution.py:20
  55.5 5.5 %eval_jaxpr.5 = (bf16[32,2560]{1,0:T(8,128)(2,1)}, f32[1,1,128,2560]{3,2,1,0:T(8,128)}, bf16[32,256]{1,0:T(8,128)(2,1)}, bf16[4,1,1,32,2560]{4,3,2,1,0:T(8,128)(2,1)}, bf16[4,1,1,32,256]{4,3,2,1,0:T(8,128)(2,1)S(1)}) custom-call(s32[1]{0:T(128)} %bitcast.106.step_ref, ...), custom_call_target="tpu_custom_call", output_to_operand_aliasing={{1}: (13, {}), {3}: (16, {}), {4}: (17, {})} | custom-call | flops 146800640 | bytes 7536640 | tf_op jit(solution)/shard_map/while/body/eval_jaxpr/pallas_call | solution.py:250
  61.0 1.3 %collective-permute-start = (bf16[1,32,2560]{2,1,0:T(8,128)(2,1)}, bf16[1,32,2560]{2,1,0:T(8,128)(2,1)S(1)}, u32[]{:S(2)}, u32[]{:S(2)}) collective-permute-start(bf16[1,32,2560]{2,1,0:T(8,128)(2,1)} %bitcast.125), channel_id=1, source_target_pairs={{8,0},{16,8},{24,16},{9,1},{17,9},{25,17},{10,2},{18,10},{26,18},{... | collective-permute-start | bytes 491528 | tf_op jit(solution)/shard_map/while/body/eval_jaxpr/ppermute | solution.py:20
  62.3 6.1 %collective-permute-done = bf16[1,32,2560]{2,1,0:T(8,128)(2,1)S(1)} collective-permute-done((bf16[1,32,2560]{2,1,0:T(8,128)(2,1)}, bf16[1,32,2560]{2,1,0:T(8,128)(2,1)S(1)}, u32[]{:S(2)}, u32[]{:S(2)}) %collective-permute-start) | collective-permute-done | bytes 163872 | tf_op jit(solution)/shard_map/while/body/eval_jaxpr/ppermute | solution.py:20
  68.4 5.5 %eval_jaxpr.5 = (bf16[32,2560]{1,0:T(8,128)(2,1)}, f32[1,1,128,2560]{3,2,1,0:T(8,128)}, bf16[32,256]{1,0:T(8,128)(2,1)}, bf16[4,1,1,32,2560]{4,3,2,1,0:T(8,128)(2,1)}, bf16[4,1,1,32,256]{4,3,2,1,0:T(8,128)(2,1)S(1)}) custom-call(s32[1]{0:T(128)} %bitcast.106.step_ref, ...), custom_call_target="tpu_custom_call", output_to_operand_aliasing={{1}: (13, {}), {3}: (16, {}), {4}: (17, {})} | custom-call | flops 146800640 | bytes 7536640 | tf_op jit(solution)/shard_map/while/body/eval_jaxpr/pallas_call | solution.py:250
  73.9 1.3 %collective-permute-start = (bf16[1,32,2560]{2,1,0:T(8,128)(2,1)}, bf16[1,32,2560]{2,1,0:T(8,128)(2,1)S(1)}, u32[]{:S(2)}, u32[]{:S(2)}) collective-permute-start(bf16[1,32,2560]{2,1,0:T(8,128)(2,1)} %bitcast.125), channel_id=1, source_target_pairs={{8,0},{16,8},{24,16},{9,1},{17,9},{25,17},{10,2},{18,10},{26,18},{... | collective-permute-start | bytes 491528 | tf_op jit(solution)/shard_map/while/body/eval_jaxpr/ppermute | solution.py:20
  75.2 6.1 %collective-permute-done = bf16[1,32,2560]{2,1,0:T(8,128)(2,1)S(1)} collective-permute-done((bf16[1,32,2560]{2,1,0:T(8,128)(2,1)}, bf16[1,32,2560]{2,1,0:T(8,128)(2,1)S(1)}, u32[]{:S(2)}, u32[]{:S(2)}) %collective-permute-start) | collective-permute-done | bytes 163872 | tf_op jit(solution)/shard_map/while/body/eval_jaxpr/ppermute | solution.py:20
  81.3 5.5 %eval_jaxpr.5 = (bf16[32,2560]{1,0:T(8,128)(2,1)}, f32[1,1,128,2560]{3,2,1,0:T(8,128)}, bf16[32,256]{1,0:T(8,128)(2,1)}, bf16[4,1,1,32,2560]{4,3,2,1,0:T(8,128)(2,1)}, bf16[4,1,1,32,256]{4,3,2,1,0:T(8,128)(2,1)S(1)}) custom-call(s32[1]{0:T(128)} %bitcast.106.step_ref, ...), custom_call_target="tpu_custom_call", output_to_operand_aliasing={{1}: (13, {}), {3}: (16, {}), {4}: (17, {})} | custom-call | flops 146800640 | bytes 7536640 | tf_op jit(solution)/shard_map/while/body/eval_jaxpr/pallas_call | solution.py:250
  86.8 1.3 %collective-permute-start = (bf16[1,32,2560]{2,1,0:T(8,128)(2,1)}, bf16[1,32,2560]{2,1,0:T(8,128)(2,1)S(1)}, u32[]{:S(2)}, u32[]{:S(2)}) collective-permute-start(bf16[1,32,2560]{2,1,0:T(8,128)(2,1)} %bitcast.125), channel_id=1, source_target_pairs={{8,0},{16,8},{24,16},{9,1},{17,9},{25,17},{10,2},{18,10},{26,18},{... | collective-permute-start | bytes 491528 | tf_op jit(solution)/shard_map/while/body/eval_jaxpr/ppermute | solution.py:20
  88.1 6.1 %collective-permute-done = bf16[1,32,2560]{2,1,0:T(8,128)(2,1)S(1)} collective-permute-done((bf16[1,32,2560]{2,1,0:T(8,128)(2,1)}, bf16[1,32,2560]{2,1,0:T(8,128)(2,1)S(1)}, u32[]{:S(2)}, u32[]{:S(2)}) %collective-permute-start) | collective-permute-done | bytes 163872 | tf_op jit(solution)/shard_map/while/body/eval_jaxpr/ppermute | solution.py:20
  94.2 5.5 %eval_jaxpr.5 = (bf16[32,2560]{1,0:T(8,128)(2,1)}, f32[1,1,128,2560]{3,2,1,0:T(8,128)}, bf16[32,256]{1,0:T(8,128)(2,1)}, bf16[4,1,1,32,2560]{4,3,2,1,0:T(8,128)(2,1)}, bf16[4,1,1,32,256]{4,3,2,1,0:T(8,128)(2,1)S(1)}) custom-call(s32[1]{0:T(128)} %bitcast.106.step_ref, ...), custom_call_target="tpu_custom_call", output_to_operand_aliasing={{1}: (13, {}), {3}: (16, {}), {4}: (17, {})} | custom-call | flops 146800640 | bytes 7536640 | tf_op jit(solution)/shard_map/while/body/eval_jaxpr/pallas_call | solution.py:250
  99.7 1.3 %collective-permute-start = (bf16[1,32,2560]{2,1,0:T(8,128)(2,1)}, bf16[1,32,2560]{2,1,0:T(8,128)(2,1)S(1)}, u32[]{:S(2)}, u32[]{:S(2)}) collective-permute-start(bf16[1,32,2560]{2,1,0:T(8,128)(2,1)} %bitcast.125), channel_id=1, source_target_pairs={{8,0},{16,8},{24,16},{9,1},{17,9},{25,17},{10,2},{18,10},{26,18},{... | collective-permute-start | bytes 491528 | tf_op jit(solution)/shard_map/while/body/eval_jaxpr/ppermute | solution.py:20
  101.0 6.1 %collective-permute-done = bf16[1,32,2560]{2,1,0:T(8,128)(2,1)S(1)} collective-permute-done((bf16[1,32,2560]{2,1,0:T(8,128)(2,1)}, bf16[1,32,2560]{2,1,0:T(8,128)(2,1)S(1)}, u32[]{:S(2)}, u32[]{:S(2)}) %collective-permute-start) | collective-permute-done | bytes 163872 | tf_op jit(solution)/shard_map/while/body/eval_jaxpr/ppermute | solution.py:20
  107.1 5.5 %shard_map.59 = (bf16[32,2560]{1,0:T(8,128)(2,1)}, f32[1,1,128,2560]{3,2,1,0:T(8,128)}, bf16[32,256]{1,0:T(8,128)(2,1)}, bf16[4,1,1,32,2560]{4,3,2,1,0:T(8,128)(2,1)}, bf16[4,1,1,32,256]{4,3,2,1,0:T(8,128)(2,1)S(1)}) custom-call(s32[1]{0:T(128)} %constant.44.clone.1.step_ref, ...), custom_call_target="tpu_custom_call", output_to_operand_aliasing={{1}: (13, {}), {3}: (16, {}), {4}: (17, {})} | custom-call | flops 146800640 | bytes 7536640 | tf_op jit(solution)/shard_map/pallas_call | solution.py:250
  112.6 9.8 %all_gather.3 = bf16[8,1,128,256]{3,2,1,0:T(8,128)(2,1)S(1)} all-gather(bf16[1,1,128,256]{3,2,1,0:T(8,128)(2,1)S(1)} %bitcast.119), channel_id=1, replica_groups=mesh['section'=4,'dp'=8] {'dp'}, dimensions={0}, use_global_device_ids=true | all-gather | bytes 589824 | tf_op jit(solution)/shard_map/all_gather | solution.py:397
  122.5 2.1 %fusion.8 = f32[1,320,256]{2,1,0:T(8,128)} fusion(bf16[8,1,128,320]{2,3,1,0:T(8,128)(2,1)} %all-to-all-done, bf16[8,1,128,256]{3,2,1,0:T(8,128)(2,1)S(1)} %all_gather.3), kind=kOutput, calls=%fused_computation.17 | convolution fusion | flops 167854080 | bytes 1507328 | tf_op jit(solution)/shard_map/glrd,glrc->ldc/dot_general | solution.py:398
  (38 shorter events, 4.4 us)
Async XLA Ops:
  0.6 7.6 %copy-start.1 = (bf16[1,1,128,2560]{3,2,1,0:T(8,128)(2,1)S(1)}, bf16[1,1,128,2560]{3,2,1,0:T(8,128)(2,1)}, u32[]{:S(2)}) copy-start(bf16[1,1,128,2560]{3,2,1,0:T(8,128)(2,1)} %param.6) | copy-start | bytes 1966084
  0.6 7.6 %copy-start = (bf16[1,2560,256]{2,1,0:T(8,128)(2,1)S(1)}, bf16[1,2560,256]{2,1,0:T(8,128)(2,1)}, u32[]{:S(2)}) copy-start(bf16[1,2560,256]{2,1,0:T(8,128)(2,1)} %w_ref.1) | copy-start | bytes 3932164
  3.0 119.5 %all-to-all-start = ((bf16[8,1,128,320]{2,3,1,0:T(8,128)(2,1)}), bf16[8,1,128,320]{2,3,1,0:T(8,128)(2,1)}, u32[]{:S(2)}, u32[]{:S(2)}) async-start(bf16[8,1,128,320]{2,3,1,0:T(8,128)(2,1)} %bitcast.30), calls=%async_computation | async-start | bytes 1310720 | tf_op jit(solution)/shard_map/all_to_all | solution.py:395
  8.2 1.8 %copy-start.6 = (f32[1,1,128,40]{2,3,1,0:T(8,128)S(1)}, f32[1,1,128,40]{2,3,1,0:T(8,128)}, u32[]{:S(2)}) copy-start(f32[1,1,128,40]{2,3,1,0:T(8,128)} %param.8) | copy-start | bytes 61444
  12.1 4.4 %copy-start.4 = (f32[4,2560]{1,0:T(4,128)}, f32[4,2560]{1,0:T(4,128)S(1)}, u32[]{:S(2)}) copy-start(f32[4,2560]{1,0:T(4,128)S(1)} %fusion.18) | copy-start | bytes 122884
  14.0 2.6 %copy-start.2 = (bf16[4,32,2560]{2,1,0:T(8,128)(2,1)}, bf16[4,32,2560]{2,1,0:T(8,128)(2,1)S(1)}, u32[]{:S(2)}) copy-start(bf16[4,32,2560]{2,1,0:T(8,128)(2,1)S(1)} %get-tuple-element.338) | copy-start | bytes 1966084
  17.5 1.7 %copy-start.3 = (f32[4,32,32]{2,1,0:T(8,128)S(1)}, f32[4,32,32]{2,1,0:T(8,128)}, u32[]{:S(2)}) copy-start(f32[4,32,32]{2,1,0:T(8,128)} %convolution_multiply_fusion) | copy-start | bytes 49156
  23.4 1.8 %copy-start.5 = (f32[4,2560]{1,0:T(4,128)S(1)}, f32[4,2560]{1,0:T(4,128)}, u32[]{:S(2)}) copy-start(f32[4,2560]{1,0:T(4,128)} %copy-done.4) | copy-start | bytes 122884
  33.1 8.9 %collective-permute-start = (bf16[1,32,2560]{2,1,0:T(8,128)(2,1)}, bf16[1,32,2560]{2,1,0:T(8,128)(2,1)S(1)}, u32[]{:S(2)}, u32[]{:S(2)}) collective-permute-start(bf16[1,32,2560]{2,1,0:T(8,128)(2,1)} %bitcast.125), channel_id=1, source_target_pairs={{8,0},{16,8},{24,16},{9,1},{17,9},{25,17},{10,2},{18,10},{26,18},{... | collective-permute-start | bytes 491528 | tf_op jit(solution)/shard_map/while/body/eval_jaxpr/ppermute | solution.py:20
  47.5 8.0 %collective-permute-start = (bf16[1,32,2560]{2,1,0:T(8,128)(2,1)}, bf16[1,32,2560]{2,1,0:T(8,128)(2,1)S(1)}, u32[]{:S(2)}, u32[]{:S(2)}) collective-permute-start(bf16[1,32,2560]{2,1,0:T(8,128)(2,1)} %bitcast.125), channel_id=1, source_target_pairs={{8,0},{16,8},{24,16},{9,1},{17,9},{25,17},{10,2},{18,10},{26,18},{... | collective-permute-start | bytes 491528 | tf_op jit(solution)/shard_map/while/body/eval_jaxpr/ppermute | solution.py:20
  61.0 7.4 %collective-permute-start = (bf16[1,32,2560]{2,1,0:T(8,128)(2,1)}, bf16[1,32,2560]{2,1,0:T(8,128)(2,1)S(1)}, u32[]{:S(2)}, u32[]{:S(2)}) collective-permute-start(bf16[1,32,2560]{2,1,0:T(8,128)(2,1)} %bitcast.125), channel_id=1, source_target_pairs={{8,0},{16,8},{24,16},{9,1},{17,9},{25,17},{10,2},{18,10},{26,18},{... | collective-permute-start | bytes 491528 | tf_op jit(solution)/shard_map/while/body/eval_jaxpr/ppermute | solution.py:20
  73.9 7.4 %collective-permute-start = (bf16[1,32,2560]{2,1,0:T(8,128)(2,1)}, bf16[1,32,2560]{2,1,0:T(8,128)(2,1)S(1)}, u32[]{:S(2)}, u32[]{:S(2)}) collective-permute-start(bf16[1,32,2560]{2,1,0:T(8,128)(2,1)} %bitcast.125), channel_id=1, source_target_pairs={{8,0},{16,8},{24,16},{9,1},{17,9},{25,17},{10,2},{18,10},{26,18},{... | collective-permute-start | bytes 491528 | tf_op jit(solution)/shard_map/while/body/eval_jaxpr/ppermute | solution.py:20
  86.8 7.4 %collective-permute-start = (bf16[1,32,2560]{2,1,0:T(8,128)(2,1)}, bf16[1,32,2560]{2,1,0:T(8,128)(2,1)S(1)}, u32[]{:S(2)}, u32[]{:S(2)}) collective-permute-start(bf16[1,32,2560]{2,1,0:T(8,128)(2,1)} %bitcast.125), channel_id=1, source_target_pairs={{8,0},{16,8},{24,16},{9,1},{17,9},{25,17},{10,2},{18,10},{26,18},{... | collective-permute-start | bytes 491528 | tf_op jit(solution)/shard_map/while/body/eval_jaxpr/ppermute | solution.py:20
  99.7 7.4 %collective-permute-start = (bf16[1,32,2560]{2,1,0:T(8,128)(2,1)}, bf16[1,32,2560]{2,1,0:T(8,128)(2,1)S(1)}, u32[]{:S(2)}, u32[]{:S(2)}) collective-permute-start(bf16[1,32,2560]{2,1,0:T(8,128)(2,1)} %bitcast.125), channel_id=1, source_target_pairs={{8,0},{16,8},{24,16},{9,1},{17,9},{25,17},{10,2},{18,10},{26,18},{... | collective-permute-start | bytes 491528 | tf_op jit(solution)/shard_map/while/body/eval_jaxpr/ppermute | solution.py:20

commit v18 on v14

--- a/solution.py
+++ b/solution.py
@@ -138,7 +138,8 @@
 def step_kernel(
     step_ref, tab_ref, wt_ref, dec_ref, inc_ref, top_ref, x_ref, b_ref, c_ref, tail_ref, lead_ref, xt_ref,
     sb_ref, r_ref, end_ref, w_ref, gs_ref, ms_ref, out_ref, rnew_ref, dbc_ref, gstore_ref, mstore_ref,
-    v_ref, gx_ref, tail_buf, lead_buf, xt_buf, sb_buf, r_buf, w_buf, sems, *, factor, width,
+    v_ref, gx_ref, tail_buf, lead_buf, xt_buf, sb_buf, r_buf, w_buf, sems, wt_buf, dec_buf,
+    head_sems, *, factor, width,
     level_pos, levels, level_no, seq_no
 ):
     base = (step_ref[0] * levels + level_pos) * 3
@@ -151,6 +152,27 @@
         pltpu.make_async_copy(sb_ref.at[blk, level_no, seq_no], sb_buf, sems.at[4]),
         pltpu.make_async_copy(w_ref.at[level_no], w_buf, sems.at[5]),
     ]
+    pairs = dec_buf.shape[0]
+    chunks = 4 if pairs % 4 == 0 else 1
+    per_chunk = pairs // chunks
+    heads_chunk = per_chunk * (wt_buf.shape[0] // pairs)
+    head_fetches = []
+    for part in range(chunks):
+        head_fetches.append((
+            pltpu.make_async_copy(
+                wt_ref.at[blk, level_no, seq_no, pl.ds(part * heads_chunk, heads_chunk)],
+                wt_buf.at[pl.ds(part * heads_chunk, heads_chunk)],
+                head_sems.at[2 * part],
+            ),
+            pltpu.make_async_copy(
+                dec_ref.at[blk, level_no, seq_no, pl.ds(part * per_chunk, per_chunk)],
+                dec_buf.at[pl.ds(part * per_chunk, per_chunk)],
+                head_sems.at[2 * part + 1],
+            ),
+        ))
+    for pair_fetch in head_fetches:
+        for fetch in pair_fetch:
+            fetch.start()
     for fetch in fetches:
         fetch.start()
     f32 = jnp.float32
@@ -168,21 +190,24 @@
     mix_acc = jnp.zeros((per_pair * length, length), f32)
     for q in range(features // lanes):
         cols = slice(q * lanes, (q + 1) * lanes)
+        if q % per_chunk == 0:
+            for fetch in head_fetches[q // per_chunk]:
+                fetch.wait()
         v_q = v_ref[:, cols]
         x_q = x_ref[:, cols]
         stacked = jnp.concatenate([jnp.where(m, v_q, jnp.zeros_like(v_q)) for m in masks], axis=0)
         gx_q = jnp.dot(
-            wt_ref[per_pair * q], stacked[0:length], preferred_element_type=f32
+            wt_buf[per_pair * q], stacked[0:length], preferred_element_type=f32
         )
         for e in range(1, per_pair):
             gx_q = gx_q + jnp.dot(
-                wt_ref[per_pair * q + e],
+                wt_buf[per_pair * q + e],
                 stacked[e * length:(e + 1) * length],
                 preferred_element_type=f32,
             )
         gx_ref[:, cols] = gx_q
         pair_dots = lax.dot_general(stacked, x_q, nt, preferred_element_type=f32)
-        mix_acc = mix_acc + dec_ref[q] * pair_dots
+        mix_acc = mix_acc + dec_buf[q] * pair_dots
     mixing = mix_acc[0:length]
     for e in range(1, per_pair):
         mixing = mixing + mix_acc[e * length:(e + 1) * length]
@@ -225,7 +250,7 @@
         tail = (0,) * (a.ndim - 3)
         return pl.BlockSpec(shape, lambda i, c, t: (t[(c[0] * levels + level_pos) * 3], level_no, seq_no) + tail)
 
-    in_specs = [lead_block(a) for a in (wt2, dec2)]
+    in_specs = [pl.BlockSpec(memory_space=pl.ANY)] * 2
     in_specs.append(pl.BlockSpec((None, length, features), lambda i, c, t: (seq_no, 0, 0)))
     in_specs.append(pl.BlockSpec((None, None, length, features), lambda i, c, t: (t[(c[0] * levels + level_pos) * 3], seq_no, 0, 0)))
     in_hbm = pl.BlockSpec(memory_space=pl.ANY)
@@ -272,6 +297,9 @@
                 pltpu.VMEM(carried.shape[2:], jnp.float32),
                 pltpu.VMEM(w_bc.shape[1:], w_bc.dtype),
                 pltpu.SemaphoreType.DMA((6,)),
+                pltpu.VMEM(wt2.shape[3:], wt2.dtype),
+                pltpu.VMEM(dec2.shape[3:], dec2.dtype),
+                pltpu.SemaphoreType.DMA((8,)),
             ],
         ),
         input_output_aliases={13: 1, 16: 3, 17: 4},

time: 123 us -> 129 us (1.049)
  Pallas kernels: 38.3 us -> 43.6 us
    pallas_call x7, Pallas kernels: 38.3 us -> 43.6 us  [fused_step(): pl.pallas_call(functools.partial(step_kernel, factor=factor, width=width,...]
  transfers between devices with their start and end apart: 7 -> 7, of which waited for: 6 -> 6; matrix products, arithmetic and copies ran while one was open for 14% -> 13% of each run, Pallas kernels for 31% -> 34%
where the time goes in v18:
time: 129 us; the launch traced here: 128 us
  Pallas kernels  43.6 us (34%)
  waiting for transfers between devices  38.8 us (30%)
  starting transfers between devices  12.9 us (10%)
  blocking collectives  9.79 us (8%)
  matrix products  9 us (7%)
  other arithmetic  6.98 us (5%)
  local copies, waits for them, and re-layouts  5.69 us (4%)
    pallas_call x7, Pallas kernels, fused_step(): pl.pallas_call(functools.partial(step_kernel, factor=factor, width=width,...  43.6 us
    ppermute x6, waiting for transfers between devices, passed_along(): return lax.ppermute(block, axis, route)  38.8 us
    all_gather x1, blocking collectives, shards(): maps_all = lax.all_gather(maps_here, 'dp', axis=0, tiled=True)  9.79 us
    ppermute x6, starting transfers between devices, passed_along(): return lax.ppermute(block, axis, route)  7.75 us
    all_to_all x1, starting transfers between devices, shards(): rows_all = lax.all_to_all(rows_here, 'dp', 0, 0, tiled=True)  5.17 us
    dot_general x3, matrix products, per_lane(): jnp.einsum('...h,hd->...d', a, spread_heads, precision=lax.Precision.HIGH...  3.81 us
  transfers between devices with their start and end apart: 7, of which 6 were waited for; matrix products, arithmetic and copies ran while one was open for 13% of the time, Pallas kernels for 34%

profile of v18, /device:TPU:0, one launch (start us, length us, event | category | flops | bytes accessed | tf_op | source)
XLA Modules:
  0.0 127.7 jit_solution(7794525134745919492)
XLA Ops:
  0.7 2.4 %copy.32 = bf16[1,1,128,2560]{2,3,1,0:T(8,128)(2,1)} copy(bf16[1,1,128,2560]{3,2,1,0:T(8,128)(2,1)} %param.6) | data formatting | bytes 1310720 | tf_op args[0]
  3.0 5.2 %all-to-all-start = ((bf16[8,1,128,320]{2,3,1,0:T(8,128)(2,1)}), bf16[8,1,128,320]{2,3,1,0:T(8,128)(2,1)}, u32[]{:S(2)}, u32[]{:S(2)}) async-start(bf16[8,1,128,320]{2,3,1,0:T(8,128)(2,1)} %bitcast.30), calls=%async_computation | async-start | bytes 1310720 | tf_op jit(solution)/shard_map/all_to_all | solution.py:421
  9.6 1.8 %convolution_bitcast_fusion.lead_ref = f32[4,1,1,32,2560]{4,3,2,1,0:T(8,128)} fusion(s32[2560]{0:T(1024)S(1)} %add_select_fusion, f32[4,1,1,32,40]{4,3,2,1,0:T(8,128)S(1)} %reduce_window_sum.11), kind=kOutput, calls=%fused_computation | convolution fusion | flops 157388800 | bytes 1341440 | tf_op jit(solution)/shard_map/...h,hd->...d/dot_general | solution.py:348
  11.6 1.8 %fusion.4 = (bf16[4,32,2560]{2,1,0:T(8,128)(2,1)S(1)}, f32[4,32,2560]{2,1,0:T(8,128)}) fusion(bf16[4,32,2560]{2,1,0:T(8,128)(2,1)S(1)} %bitcast.110, s32[2560]{0:T(1024)S(1)} %add_select_fusion, f32[4,40]{1,0:T(4,128)S(1)} %bitcast.123, f32[4,1,1,32,40]{4,3,2,1,0:T(8,128)S(1)} %reduce_window_sum.11), kind=kOutput, calls=%fused_computation.12 | convolution fusion | flops 158376960 | bytes 2652800 | tf_op jit(solution)/shard_map/...h,hd->...d/dot_general | solution.py:348
  13.4 2.6 %fusion.16 = f32[3,128,2560]{2,1,0:T(8,128)} fusion(bf16[4,32,2560]{2,1,0:T(8,128)(2,1)S(1)} %get-tuple-element.338, bf16[4,1,1,32,256]{4,3,2,1,0:T(8,128)(2,1)S(1)} %bitcast.120), kind=kOutput, calls=%fused_computation.24 | convolution fusion | flops 62914560 | bytes 4448256 | tf_op jit(solution)/shard_map/mlsnj,mlsjd->mlsnd/dot_general | solution.py:358
  17.0 1.7 %multiply_convert_fusion.wt_ref = bf16[4,1,1,40,32,32]{5,4,3,2,1,0:T(8,128)(2,1)} fusion(f32[4,32,32]{2,1,0:T(8,128)S(1)} %convolution_multiply_fusion, f32[4,40,32]{2,1,0:T(8,128)S(1)} %copy.28, pred[32,32]{1,0:T(8,128)(4,1)S(1)} %iota_compare_fusion.3), kind=kLoop, calls=%fused_computation.3 | loop fusion | flops 819200 | bytes 365568 | tf_op jit(solution)/shard_map/vmap(vmap(vmap()))/convert_element_type | solution.py:128
  18.7 2.5 %fusion.23 = (bf16[1,1,1,128,2560]{4,3,2,1,0:T(8,128)(2,1)S(1)}, bf16[1,1,1,128,2560]{4,3,2,1,0:T(8,128)(2,1)S(1)}, bf16[1,1,1,128,2560]{4,3,2,1,0:T(8,128)(2,1)S(1)}) fusion(f32[3,128,2560]{2,1,0:T(8,128)} %fusion.16, f32[2560]{0:T(1024)S(1)} %get-tuple-element.296, f32[2560]{0:T(1024)S(1)} %get-tuple-element.294, f32[2560]{0:T(1024)S(1)} %get-tuple-element.295), kind=kLoop, calls=%fused_computation.30 | loop fusion | flops 2621440 | bytes 5928960 | tf_op jit(solution)/shard_map/convert_element_type | solution.py:368
  21.2 1.8 %pad_maximum_fusion.sb_ref = bf16[4,1,1,128,2560]{4,3,2,1,0:T(8,128)(2,1)} fusion(bf16[1,1,1,128,2560]{4,3,2,1,0:T(8,128)(2,1)S(1)} %get-tuple-element.334, bf16[1,1,1,128,2560]{4,3,2,1,0:T(8,128)(2,1)S(1)} %get-tuple-element.333, bf16[1,1,1,128,2560]{4,3,2,1,0:T(8,128)(2,1)S(1)} %get-tuple-element.335, bf16[4]{0:T(256)(128)(2,1)S(1)} %pad.clone), kind=kLoop, calls=%fused_computation.1 | loop fusion | flops 3932160 | bytes 4587528 | tf_op jit(solution)/shard_map/concatenate | solution.py:369
  23.4 1.2 broadcast.401
  24.6 0.9 broadcast_in_dim.99
  25.5 84.0 %while.19 = (s32[]{:T(128)}, bf16[1,32,2560]{2,1,0:T(8,128)(2,1)S(1)}, f32[1,1,128,2560]{3,2,1,0:T(8,128)}, bf16[4,1,1,32,2560]{4,3,2,1,0:T(8,128)(2,1)}, bf16[4...) while((s32[]{:T(128)}, ...), condition=%wide.region_2.3_spmd, body=%wide.region_1.2_spmd.sunk | while | flops 146800640 | bytes 8192213 | solution.py:410
  25.5 6.3 %eval_jaxpr.5 = (bf16[32,2560]{1,0:T(8,128)(2,1)}, f32[1,1,128,2560]{3,2,1,0:T(8,128)}, bf16[32,256]{1,0:T(8,128)(2,1)}, bf16[4,1,1,32,2560]{4,3,2,1,0:T(8,128)(2,1)}, bf16[4,1,1,32,256]{4,3,2,1,0:T(8,128)(2,1)S(1)}) custom-call(s32[1]{0:T(128)} %bitcast.106.step_ref, ...), custom_call_target="tpu_custom_call", output_to_operand_aliasing={{1}: (13, {}), {3}: (16, {}), {4}: (17, {})} | custom-call | flops 146800640 | bytes 7536640 | tf_op jit(solution)/shard_map/while/body/eval_jaxpr/pallas_call | solution.py:273
  31.7 1.3 %collective-permute-start = (bf16[1,32,2560]{2,1,0:T(8,128)(2,1)}, bf16[1,32,2560]{2,1,0:T(8,128)(2,1)S(1)}, u32[]{:S(2)}, u32[]{:S(2)}) collective-permute-start(bf16[1,32,2560]{2,1,0:T(8,128)(2,1)} %bitcast.124), channel_id=1, source_target_pairs={{8,0},{16,8},{24,16},{9,1},{17,9},{25,17},{10,2},{18,10},{26,18},{... | collective-permute-start | bytes 491528 | tf_op jit(solution)/shard_map/while/body/eval_jaxpr/ppermute | solution.py:20
  33.0 7.6 %collective-permute-done = bf16[1,32,2560]{2,1,0:T(8,128)(2,1)S(1)} collective-permute-done((bf16[1,32,2560]{2,1,0:T(8,128)(2,1)}, bf16[1,32,2560]{2,1,0:T(8,128)(2,1)S(1)}, u32[]{:S(2)}, u32[]{:S(2)}) %collective-permute-start) | collective-permute-done | bytes 163872 | tf_op jit(solution)/shard_map/while/body/eval_jaxpr/ppermute | solution.py:20
  40.6 6.2 %eval_jaxpr.5 = (bf16[32,2560]{1,0:T(8,128)(2,1)}, f32[1,1,128,2560]{3,2,1,0:T(8,128)}, bf16[32,256]{1,0:T(8,128)(2,1)}, bf16[4,1,1,32,2560]{4,3,2,1,0:T(8,128)(2,1)}, bf16[4,1,1,32,256]{4,3,2,1,0:T(8,128)(2,1)S(1)}) custom-call(s32[1]{0:T(128)} %bitcast.106.step_ref, ...), custom_call_target="tpu_custom_call", output_to_operand_aliasing={{1}: (13, {}), {3}: (16, {}), {4}: (17, {})} | custom-call | flops 146800640 | bytes 7536640 | tf_op jit(solution)/shard_map/while/body/eval_jaxpr/pallas_call | solution.py:273
  46.9 1.3 %collective-permute-start = (bf16[1,32,2560]{2,1,0:T(8,128)(2,1)}, bf16[1,32,2560]{2,1,0:T(8,128)(2,1)S(1)}, u32[]{:S(2)}, u32[]{:S(2)}) collective-permute-start(bf16[1,32,2560]{2,1,0:T(8,128)(2,1)} %bitcast.124), channel_id=1, source_target_pairs={{8,0},{16,8},{24,16},{9,1},{17,9},{25,17},{10,2},{18,10},{26,18},{... | collective-permute-start | bytes 491528 | tf_op jit(solution)/shard_map/while/body/eval_jaxpr/ppermute | solution.py:20
  48.2 6.7 %collective-permute-done = bf16[1,32,2560]{2,1,0:T(8,128)(2,1)S(1)} collective-permute-done((bf16[1,32,2560]{2,1,0:T(8,128)(2,1)}, bf16[1,32,2560]{2,1,0:T(8,128)(2,1)S(1)}, u32[]{:S(2)}, u32[]{:S(2)}) %collective-permute-start) | collective-permute-done | bytes 163872 | tf_op jit(solution)/shard_map/while/body/eval_jaxpr/ppermute | solution.py:20
  54.9 6.2 %eval_jaxpr.5 = (bf16[32,2560]{1,0:T(8,128)(2,1)}, f32[1,1,128,2560]{3,2,1,0:T(8,128)}, bf16[32,256]{1,0:T(8,128)(2,1)}, bf16[4,1,1,32,2560]{4,3,2,1,0:T(8,128)(2,1)}, bf16[4,1,1,32,256]{4,3,2,1,0:T(8,128)(2,1)S(1)}) custom-call(s32[1]{0:T(128)} %bitcast.106.step_ref, ...), custom_call_target="tpu_custom_call", output_to_operand_aliasing={{1}: (13, {}), {3}: (16, {}), {4}: (17, {})} | custom-call | flops 146800640 | bytes 7536640 | tf_op jit(solution)/shard_map/while/body/eval_jaxpr/pallas_call | solution.py:273
  61.1 1.3 %collective-permute-start = (bf16[1,32,2560]{2,1,0:T(8,128)(2,1)}, bf16[1,32,2560]{2,1,0:T(8,128)(2,1)S(1)}, u32[]{:S(2)}, u32[]{:S(2)}) collective-permute-start(bf16[1,32,2560]{2,1,0:T(8,128)(2,1)} %bitcast.124), channel_id=1, source_target_pairs={{8,0},{16,8},{24,16},{9,1},{17,9},{25,17},{10,2},{18,10},{26,18},{... | collective-permute-start | bytes 491528 | tf_op jit(solution)/shard_map/while/body/eval_jaxpr/ppermute | solution.py:20
  62.4 6.1 %collective-permute-done = bf16[1,32,2560]{2,1,0:T(8,128)(2,1)S(1)} collective-permute-done((bf16[1,32,2560]{2,1,0:T(8,128)(2,1)}, bf16[1,32,2560]{2,1,0:T(8,128)(2,1)S(1)}, u32[]{:S(2)}, u32[]{:S(2)}) %collective-permute-start) | collective-permute-done | bytes 163872 | tf_op jit(solution)/shard_map/while/body/eval_jaxpr/ppermute | solution.py:20
  68.5 6.2 %eval_jaxpr.5 = (bf16[32,2560]{1,0:T(8,128)(2,1)}, f32[1,1,128,2560]{3,2,1,0:T(8,128)}, bf16[32,256]{1,0:T(8,128)(2,1)}, bf16[4,1,1,32,2560]{4,3,2,1,0:T(8,128)(2,1)}, bf16[4,1,1,32,256]{4,3,2,1,0:T(8,128)(2,1)S(1)}) custom-call(s32[1]{0:T(128)} %bitcast.106.step_ref, ...), custom_call_target="tpu_custom_call", output_to_operand_aliasing={{1}: (13, {}), {3}: (16, {}), {4}: (17, {})} | custom-call | flops 146800640 | bytes 7536640 | tf_op jit(solution)/shard_map/while/body/eval_jaxpr/pallas_call | solution.py:273
  74.8 1.3 %collective-permute-start = (bf16[1,32,2560]{2,1,0:T(8,128)(2,1)}, bf16[1,32,2560]{2,1,0:T(8,128)(2,1)S(1)}, u32[]{:S(2)}, u32[]{:S(2)}) collective-permute-start(bf16[1,32,2560]{2,1,0:T(8,128)(2,1)} %bitcast.124), channel_id=1, source_target_pairs={{8,0},{16,8},{24,16},{9,1},{17,9},{25,17},{10,2},{18,10},{26,18},{... | collective-permute-start | bytes 491528 | tf_op jit(solution)/shard_map/while/body/eval_jaxpr/ppermute | solution.py:20
  76.1 6.1 %collective-permute-done = bf16[1,32,2560]{2,1,0:T(8,128)(2,1)S(1)} collective-permute-done((bf16[1,32,2560]{2,1,0:T(8,128)(2,1)}, bf16[1,32,2560]{2,1,0:T(8,128)(2,1)S(1)}, u32[]{:S(2)}, u32[]{:S(2)}) %collective-permute-start) | collective-permute-done | bytes 163872 | tf_op jit(solution)/shard_map/while/body/eval_jaxpr/ppermute | solution.py:20
  82.2 6.2 %eval_jaxpr.5 = (bf16[32,2560]{1,0:T(8,128)(2,1)}, f32[1,1,128,2560]{3,2,1,0:T(8,128)}, bf16[32,256]{1,0:T(8,128)(2,1)}, bf16[4,1,1,32,2560]{4,3,2,1,0:T(8,128)(2,1)}, bf16[4,1,1,32,256]{4,3,2,1,0:T(8,128)(2,1)S(1)}) custom-call(s32[1]{0:T(128)} %bitcast.106.step_ref, ...), custom_call_target="tpu_custom_call", output_to_operand_aliasing={{1}: (13, {}), {3}: (16, {}), {4}: (17, {})} | custom-call | flops 146800640 | bytes 7536640 | tf_op jit(solution)/shard_map/while/body/eval_jaxpr/pallas_call | solution.py:273
  88.4 1.3 %collective-permute-start = (bf16[1,32,2560]{2,1,0:T(8,128)(2,1)}, bf16[1,32,2560]{2,1,0:T(8,128)(2,1)S(1)}, u32[]{:S(2)}, u32[]{:S(2)}) collective-permute-start(bf16[1,32,2560]{2,1,0:T(8,128)(2,1)} %bitcast.124), channel_id=1, source_target_pairs={{8,0},{16,8},{24,16},{9,1},{17,9},{25,17},{10,2},{18,10},{26,18},{... | collective-permute-start | bytes 491528 | tf_op jit(solution)/shard_map/while/body/eval_jaxpr/ppermute | solution.py:20
  89.7 6.1 %collective-permute-done = bf16[1,32,2560]{2,1,0:T(8,128)(2,1)S(1)} collective-permute-done((bf16[1,32,2560]{2,1,0:T(8,128)(2,1)}, bf16[1,32,2560]{2,1,0:T(8,128)(2,1)S(1)}, u32[]{:S(2)}, u32[]{:S(2)}) %collective-permute-start) | collective-permute-done | bytes 163872 | tf_op jit(solution)/shard_map/while/body/eval_jaxpr/ppermute | solution.py:20
  95.9 6.2 %eval_jaxpr.5 = (bf16[32,2560]{1,0:T(8,128)(2,1)}, f32[1,1,128,2560]{3,2,1,0:T(8,128)}, bf16[32,256]{1,0:T(8,128)(2,1)}, bf16[4,1,1,32,2560]{4,3,2,1,0:T(8,128)(2,1)}, bf16[4,1,1,32,256]{4,3,2,1,0:T(8,128)(2,1)S(1)}) custom-call(s32[1]{0:T(128)} %bitcast.106.step_ref, ...), custom_call_target="tpu_custom_call", output_to_operand_aliasing={{1}: (13, {}), {3}: (16, {}), {4}: (17, {})} | custom-call | flops 146800640 | bytes 7536640 | tf_op jit(solution)/shard_map/while/body/eval_jaxpr/pallas_call | solution.py:273
  102.1 1.3 %collective-permute-start = (bf16[1,32,2560]{2,1,0:T(8,128)(2,1)}, bf16[1,32,2560]{2,1,0:T(8,128)(2,1)S(1)}, u32[]{:S(2)}, u32[]{:S(2)}) collective-permute-start(bf16[1,32,2560]{2,1,0:T(8,128)(2,1)} %bitcast.124), channel_id=1, source_target_pairs={{8,0},{16,8},{24,16},{9,1},{17,9},{25,17},{10,2},{18,10},{26,18},{... | collective-permute-start | bytes 491528 | tf_op jit(solution)/shard_map/while/body/eval_jaxpr/ppermute | solution.py:20
  103.4 6.1 %collective-permute-done = bf16[1,32,2560]{2,1,0:T(8,128)(2,1)S(1)} collective-permute-done((bf16[1,32,2560]{2,1,0:T(8,128)(2,1)}, bf16[1,32,2560]{2,1,0:T(8,128)(2,1)S(1)}, u32[]{:S(2)}, u32[]{:S(2)}) %collective-permute-start) | collective-permute-done | bytes 163872 | tf_op jit(solution)/shard_map/while/body/eval_jaxpr/ppermute | solution.py:20
  109.5 6.2 %shard_map.59 = (bf16[32,2560]{1,0:T(8,128)(2,1)}, f32[1,1,128,2560]{3,2,1,0:T(8,128)}, bf16[32,256]{1,0:T(8,128)(2,1)}, bf16[4,1,1,32,2560]{4,3,2,1,0:T(8,128)(2,1)}, bf16[4,1,1,32,256]{4,3,2,1,0:T(8,128)(2,1)S(1)}) custom-call(s32[1]{0:T(128)} %constant.45.clone.1.step_ref, ...), custom_call_target="tpu_custom_call", output_to_operand_aliasing={{1}: (13, {}), {3}: (16, {}), {4}: (17, {})} | custom-call | flops 146800640 | bytes 7536640 | tf_op jit(solution)/shard_map/pallas_call | solution.py:273
  115.8 9.8 %all_gather.3 = bf16[8,1,128,256]{3,2,1,0:T(8,128)(2,1)S(1)} all-gather(bf16[1,1,128,256]{3,2,1,0:T(8,128)(2,1)S(1)} %bitcast.115), channel_id=1, replica_groups=mesh['section'=4,'dp'=8] {'dp'}, dimensions={0}, use_global_device_ids=true | all-gather | bytes 589824 | tf_op jit(solution)/shard_map/all_gather | solution.py:423
  125.5 2.1 %fusion.8 = f32[1,320,256]{2,1,0:T(8,128)} fusion(bf16[8,1,128,320]{2,3,1,0:T(8,128)(2,1)} %all-to-all-done, bf16[8,1,128,256]{3,2,1,0:T(8,128)(2,1)S(1)} %all_gather.3), kind=kOutput, calls=%fused_computation.17 | convolution fusion | flops 167854080 | bytes 1507328 | tf_op jit(solution)/shard_map/glrd,glrc->ldc/dot_general | solution.py:424
  (37 shorter events, 3.0 us)
Async XLA Ops:
  0.6 7.6 %copy-start.1 = (bf16[1,1,128,2560]{3,2,1,0:T(8,128)(2,1)S(1)}, bf16[1,1,128,2560]{3,2,1,0:T(8,128)(2,1)}, u32[]{:S(2)}) copy-start(bf16[1,1,128,2560]{3,2,1,0:T(8,128)(2,1)} %param.6) | copy-start | bytes 1966084
  0.6 7.6 %copy-start = (bf16[1,2560,256]{2,1,0:T(8,128)(2,1)S(1)}, bf16[1,2560,256]{2,1,0:T(8,128)(2,1)}, u32[]{:S(2)}) copy-start(bf16[1,2560,256]{2,1,0:T(8,128)(2,1)} %w_ref.1) | copy-start | bytes 3932164
  3.0 122.5 %all-to-all-start = ((bf16[8,1,128,320]{2,3,1,0:T(8,128)(2,1)}), bf16[8,1,128,320]{2,3,1,0:T(8,128)(2,1)}, u32[]{:S(2)}, u32[]{:S(2)}) async-start(bf16[8,1,128,320]{2,3,1,0:T(8,128)(2,1)} %bitcast.30), calls=%async_computation | async-start | bytes 1310720 | tf_op jit(solution)/shard_map/all_to_all | solution.py:421
  8.2 1.2 copy-start.5
  11.6 4.4 %copy-start.3 = (f32[4,2560]{1,0:T(4,128)}, f32[4,2560]{1,0:T(4,128)S(1)}, u32[]{:S(2)}) copy-start(f32[4,2560]{1,0:T(4,128)S(1)} %fusion.18) | copy-start | bytes 122884
  13.4 2.6 %copy-start.2 = (bf16[4,32,2560]{2,1,0:T(8,128)(2,1)}, bf16[4,32,2560]{2,1,0:T(8,128)(2,1)S(1)}, u32[]{:S(2)}) copy-start(bf16[4,32,2560]{2,1,0:T(8,128)(2,1)S(1)} %get-tuple-element.338) | copy-start | bytes 1966084
  21.2 1.8 %copy-start.4 = (f32[4,2560]{1,0:T(4,128)S(1)}, f32[4,2560]{1,0:T(4,128)}, u32[]{:S(2)}) copy-start(f32[4,2560]{1,0:T(4,128)} %copy-done.3) | copy-start | bytes 122884
  31.7 8.9 %collective-permute-start = (bf16[1,32,2560]{2,1,0:T(8,128)(2,1)}, bf16[1,32,2560]{2,1,0:T(8,128)(2,1)S(1)}, u32[]{:S(2)}, u32[]{:S(2)}) collective-permute-start(bf16[1,32,2560]{2,1,0:T(8,128)(2,1)} %bitcast.124), channel_id=1, source_target_pairs={{8,0},{16,8},{24,16},{9,1},{17,9},{25,17},{10,2},{18,10},{26,18},{... | collective-permute-start | bytes 491528 | tf_op jit(solution)/shard_map/while/body/eval_jaxpr/ppermute | solution.py:20
  46.9 8.0 %collective-permute-start = (bf16[1,32,2560]{2,1,0:T(8,128)(2,1)}, bf16[1,32,2560]{2,1,0:T(8,128)(2,1)S(1)}, u32[]{:S(2)}, u32[]{:S(2)}) collective-permute-start(bf16[1,32,2560]{2,1,0:T(8,128)(2,1)} %bitcast.124), channel_id=1, source_target_pairs={{8,0},{16,8},{24,16},{9,1},{17,9},{25,17},{10,2},{18,10},{26,18},{... | collective-permute-start | bytes 491528 | tf_op jit(solution)/shard_map/while/body/eval_jaxpr/ppermute | solution.py:20
  61.1 7.4 %collective-permute-start = (bf16[1,32,2560]{2,1,0:T(8,128)(2,1)}, bf16[1,32,2560]{2,1,0:T(8,128)(2,1)S(1)}, u32[]{:S(2)}, u32[]{:S(2)}) collective-permute-start(bf16[1,32,2560]{2,1,0:T(8,128)(2,1)} %bitcast.124), channel_id=1, source_target_pairs={{8,0},{16,8},{24,16},{9,1},{17,9},{25,17},{10,2},{18,10},{26,18},{... | collective-permute-start | bytes 491528 | tf_op jit(solution)/shard_map/while/body/eval_jaxpr/ppermute | solution.py:20
  74.8 7.4 %collective-permute-start = (bf16[1,32,2560]{2,1,0:T(8,128)(2,1)}, bf16[1,32,2560]{2,1,0:T(8,128)(2,1)S(1)}, u32[]{:S(2)}, u32[]{:S(2)}) collective-permute-start(bf16[1,32,2560]{2,1,0:T(8,128)(2,1)} %bitcast.124), channel_id=1, source_target_pairs={{8,0},{16,8},{24,16},{9,1},{17,9},{25,17},{10,2},{18,10},{26,18},{... | collective-permute-start | bytes 491528 | tf_op jit(solution)/shard_map/while/body/eval_jaxpr/ppermute | solution.py:20
  88.4 7.4 %collective-permute-start = (bf16[1,32,2560]{2,1,0:T(8,128)(2,1)}, bf16[1,32,2560]{2,1,0:T(8,128)(2,1)S(1)}, u32[]{:S(2)}, u32[]{:S(2)}) collective-permute-start(bf16[1,32,2560]{2,1,0:T(8,128)(2,1)} %bitcast.124), channel_id=1, source_target_pairs={{8,0},{16,8},{24,16},{9,1},{17,9},{25,17},{10,2},{18,10},{26,18},{... | collective-permute-start | bytes 491528 | tf_op jit(solution)/shard_map/while/body/eval_jaxpr/ppermute | solution.py:20
  102.1 7.4 %collective-permute-start = (bf16[1,32,2560]{2,1,0:T(8,128)(2,1)}, bf16[1,32,2560]{2,1,0:T(8,128)(2,1)S(1)}, u32[]{:S(2)}, u32[]{:S(2)}) collective-permute-start(bf16[1,32,2560]{2,1,0:T(8,128)(2,1)} %bitcast.124), channel_id=1, source_target_pairs={{8,0},{16,8},{24,16},{9,1},{17,9},{25,17},{10,2},{18,10},{26,18},{... | collective-permute-start | bytes 491528 | tf_op jit(solution)/shard_map/while/body/eval_jaxpr/ppermute | solution.py:20

commit v19 on v9

--- a/solution.py
+++ b/solution.py
@@ -126,13 +126,11 @@
     decays_t = jnp.where(upper, jnp.exp(spread_t), 0.0)
     scores_t = jnp.dot(in_b, out_b.T, preferred_element_type=jnp.float32)
     weighted = (factor * decays_t * scores_t[None]).astype(jnp.bfloat16)
-    tail_inputs = (tail_decay[:, :, None] * inputs_b.astype(jnp.float32)).astype(jnp.bfloat16)
     return dict(
         decays=decays,
         tail=tail_decay,
         lead=leading,
         weighted=weighted,
-        tail_inputs=tail_inputs,
         ending=jnp.exp(ending),
     )
 
@@ -298,18 +296,21 @@
 
     tail_full = per_lane(consts["tail"])
     lead_full = per_lane(consts["lead"])
-    xt_full = consts["tail_inputs"].reshape(lead_dims + (block_len, features))
+    x_flat = x_blk.reshape(lead_dims + (block_len, features))
+    xt_full = (tail_full * x_flat.astype(jnp.float32)).astype(jnp.bfloat16)
     end_row = per_lane(consts["ending"])[..., None, :]
     fresh_t = jnp.einsum(
-        "mlsjn,mlsjd->mlsnd", in_blk, xt_full, preferred_element_type=jnp.float32
+        "mlsnj,mlsjd->mlsnd",
+        jnp.swapaxes(in_blk[: MICRO - 1], -1, -2),
+        xt_full[: MICRO - 1],
+        preferred_element_type=jnp.float32,
     )
     state_now = jnp.zeros(fresh_t.shape[1:], jnp.float32)
-    saved = []
-    for block_no in range(MICRO):
-        saved.append(state_now.astype(jnp.bfloat16))
+    saved = [state_now.astype(jnp.bfloat16)[None]]
+    for block_no in range(MICRO - 1):
         state_now = end_row[block_no] * state_now + fresh_t[block_no]
-    states_t = jnp.stack(saved)
-    x_flat = x_blk.reshape(lead_dims + (block_len, features))
+        saved.append(state_now.astype(jnp.bfloat16)[None])
+    states_t = jnp.concatenate(saved, axis=0)
     per_block = (wt2, dec2, x_flat, in_blk, out_blk, tail_full, lead_full, xt_full, states_t, end_row)
     per_block = lax.optimization_barrier(per_block)
 

time: 127 us -> 121 us (0.953)
  local copies, waits for them, and re-layouts: 9.65 us -> 5.69 us
    mul x3 -> x0, local copies, waits for them, and re-layouts: 4.17 us -> none  [block_consts(): tail_decay[:, :, None] * inputs_b.astype(jnp.float32)]
    another operation x1 -> x0, other arithmetic: 1.79 us -> none  [shards(): states_t = jnp.stack(saved)]
    concatenate x0 -> x1, other arithmetic: none -> 1.79 us  [shards(): states_t = jnp.concatenate(saved, axis=0)]
    convert_element_type x2 -> x1, other arithmetic: 3.5 us -> 2.49 us  [shards(): saved.append(state_now.astype(jnp.bfloat16)[None])]
  transfers between devices with their start and end apart: 7 -> 7, of which waited for: 6 -> 6; matrix products, arithmetic and copies ran while one was open for 18% -> 14% of each run, Pallas kernels for 29% -> 31%
where the time goes in v19:
time: 121 us
  waiting for transfers between devices  38.8 us (32%)
  Pallas kernels  37.1 us (31%)
  starting transfers between devices  12.9 us (11%)
  blocking collectives  9.79 us (8%)
  matrix products  8.99 us (7%)
  other arithmetic  6.98 us (6%)
  local copies, waits for them, and re-layouts  5.69 us (5%)
    ppermute x6, waiting for transfers between devices, passed_along(): return lax.ppermute(block, axis, route)  38.8 us
    pallas_call x7, Pallas kernels, fused_step(): pl.pallas_call(functools.partial(step_kernel, factor=factor, width=width,...  37.1 us
    all_gather x1, blocking collectives, shards(): maps_all = lax.all_gather(maps_here, 'dp', axis=0, tiled=True)  9.79 us
    ppermute x6, starting transfers between devices, passed_along(): return lax.ppermute(block, axis, route)  7.68 us
    all_to_all x1, starting transfers between devices, shards(): rows_all = lax.all_to_all(rows_here, 'dp', 0, 0, tiled=True)  5.17 us
    dot_general x3, matrix products, per_lane(): jnp.einsum('...h,hd->...d', a, spread_heads, precision=lax.Precision.HIGH...  3.81 us
    dot_general x1, matrix products, shards(): jnp.einsum('mlsnj,mlsjd->mlsnd', jnp.swapaxes(in_blk[:MICRO - 1], -1, -2)...  2.57 us
    convert_element_type x1, other arithmetic, shards(): saved.append(state_now.astype(jnp.bfloat16)[None])  2.49 us
  transfers between devices with their start and end apart: 7, of which 6 were waited for; matrix products, arithmetic and copies ran while one was open for 14% of the time, Pallas kernels for 31%

profile of v19, /device:TPU:0, one launch (start us, length us, event | category | flops | bytes accessed | tf_op | source)
XLA Modules:
  0.0 121.0 jit_solution(1423137457960329553)
XLA Ops:
  0.7 2.4 %copy.32 = bf16[1,1,128,2560]{2,3,1,0:T(8,128)(2,1)} copy(bf16[1,1,128,2560]{3,2,1,0:T(8,128)(2,1)} %param.6) | data formatting | bytes 1310720 | tf_op args[0]
  3.0 5.2 %all-to-all-start = ((bf16[8,1,128,320]{2,3,1,0:T(8,128)(2,1)}), bf16[8,1,128,320]{2,3,1,0:T(8,128)(2,1)}, u32[]{:S(2)}, u32[]{:S(2)}) async-start(bf16[8,1,128,320]{2,3,1,0:T(8,128)(2,1)} %bitcast.30), calls=%async_computation | async-start | bytes 1310720 | tf_op jit(solution)/shard_map/all_to_all | solution.py:365
  9.6 1.8 %convolution_bitcast_fusion.lead_ref = f32[4,1,1,32,2560]{4,3,2,1,0:T(8,128)} fusion(s32[2560]{0:T(1024)S(1)} %add_select_fusion, f32[4,1,1,32,40]{4,3,2,1,0:T(8,128)S(1)} %reduce_window_sum.11), kind=kOutput, calls=%fused_computation | convolution fusion | flops 157388800 | bytes 1341440 | tf_op jit(solution)/shard_map/...h,hd->...d/dot_general | solution.py:292
  11.6 1.8 %fusion.4 = (bf16[4,32,2560]{2,1,0:T(8,128)(2,1)S(1)}, f32[4,32,2560]{2,1,0:T(8,128)}) fusion(bf16[4,32,2560]{2,1,0:T(8,128)(2,1)S(1)} %bitcast.110, s32[2560]{0:T(1024)S(1)} %add_select_fusion, f32[4,40]{1,0:T(4,128)S(1)} %bitcast.123, f32[4,1,1,32,40]{4,3,2,1,0:T(8,128)S(1)} %reduce_window_sum.11), kind=kOutput, calls=%fused_computation.12 | convolution fusion | flops 158376960 | bytes 2652800 | tf_op jit(solution)/shard_map/...h,hd->...d/dot_general | solution.py:292
  13.4 2.6 %fusion.16 = f32[3,128,2560]{2,1,0:T(8,128)} fusion(bf16[4,32,2560]{2,1,0:T(8,128)(2,1)S(1)} %get-tuple-element.338, bf16[4,1,1,32,256]{4,3,2,1,0:T(8,128)(2,1)S(1)} %bitcast.120), kind=kOutput, calls=%fused_computation.24 | convolution fusion | flops 62914560 | bytes 4448256 | tf_op jit(solution)/shard_map/mlsnj,mlsjd->mlsnd/dot_general | solution.py:302
  17.0 1.7 %multiply_convert_fusion.wt_ref = bf16[4,1,1,40,32,32]{5,4,3,2,1,0:T(8,128)(2,1)} fusion(f32[4,32,32]{2,1,0:T(8,128)S(1)} %convolution_multiply_fusion, f32[4,40,32]{2,1,0:T(8,128)S(1)} %copy.28, pred[32,32]{1,0:T(8,128)(4,1)S(1)} %iota_compare_fusion.3), kind=kLoop, calls=%fused_computation.3 | loop fusion | flops 819200 | bytes 365568 | tf_op jit(solution)/shard_map/vmap(vmap(vmap()))/convert_element_type | solution.py:128
  18.7 2.5 %fusion.23 = (bf16[1,1,1,128,2560]{4,3,2,1,0:T(8,128)(2,1)S(1)}, bf16[1,1,1,128,2560]{4,3,2,1,0:T(8,128)(2,1)S(1)}, bf16[1,1,1,128,2560]{4,3,2,1,0:T(8,128)(2,1)S(1)}) fusion(f32[3,128,2560]{2,1,0:T(8,128)} %fusion.16, f32[2560]{0:T(1024)S(1)} %get-tuple-element.296, f32[2560]{0:T(1024)S(1)} %get-tuple-element.294, f32[2560]{0:T(1024)S(1)} %get-tuple-element.295), kind=kLoop, calls=%fused_computation.30 | loop fusion | flops 2621440 | bytes 5928960 | tf_op jit(solution)/shard_map/convert_element_type | solution.py:312
  21.2 1.8 %pad_maximum_fusion.sb_ref = bf16[4,1,1,128,2560]{4,3,2,1,0:T(8,128)(2,1)} fusion(bf16[1,1,1,128,2560]{4,3,2,1,0:T(8,128)(2,1)S(1)} %get-tuple-element.334, bf16[1,1,1,128,2560]{4,3,2,1,0:T(8,128)(2,1)S(1)} %get-tuple-element.333, bf16[1,1,1,128,2560]{4,3,2,1,0:T(8,128)(2,1)S(1)} %get-tuple-element.335, bf16[4]{0:T(256)(128)(2,1)S(1)} %pad.clone), kind=kLoop, calls=%fused_computation.1 | loop fusion | flops 3932160 | bytes 4587528 | tf_op jit(solution)/shard_map/concatenate | solution.py:313
  23.4 1.2 broadcast.401
  24.6 0.9 broadcast_in_dim.99
  25.5 78.3 %while.19 = (s32[]{:T(128)}, bf16[1,32,2560]{2,1,0:T(8,128)(2,1)S(1)}, f32[1,1,128,2560]{3,2,1,0:T(8,128)}, bf16[4,1,1,32,2560]{4,3,2,1,0:T(8,128)(2,1)}, bf16[4...) while((s32[]{:T(128)}, ...), condition=%wide.region_2.3_spmd, body=%wide.region_1.2_spmd.sunk | while | flops 146800640 | bytes 8192213 | solution.py:354
  25.5 5.3 %eval_jaxpr.5 = (bf16[32,2560]{1,0:T(8,128)(2,1)}, f32[1,1,128,2560]{3,2,1,0:T(8,128)}, bf16[32,256]{1,0:T(8,128)(2,1)}, bf16[4,1,1,32,2560]{4,3,2,1,0:T(8,128)(2,1)}, bf16[4,1,1,32,256]{4,3,2,1,0:T(8,128)(2,1)S(1)}) custom-call(s32[1]{0:T(128)} %bitcast.106.step_ref, ...), custom_call_target="tpu_custom_call", output_to_operand_aliasing={{1}: (13, {}), {3}: (16, {}), {4}: (17, {})} | custom-call | flops 146800640 | bytes 7536640 | tf_op jit(solution)/shard_map/while/body/eval_jaxpr/pallas_call | solution.py:228
  30.8 1.3 %collective-permute-start = (bf16[1,32,2560]{2,1,0:T(8,128)(2,1)}, bf16[1,32,2560]{2,1,0:T(8,128)(2,1)S(1)}, u32[]{:S(2)}, u32[]{:S(2)}) collective-permute-start(bf16[1,32,2560]{2,1,0:T(8,128)(2,1)} %bitcast.124), channel_id=1, source_target_pairs={{8,0},{16,8},{24,16},{9,1},{17,9},{25,17},{10,2},{18,10},{26,18},{... | collective-permute-start | bytes 491528 | tf_op jit(solution)/shard_map/while/body/eval_jaxpr/ppermute | solution.py:20
  32.1 7.6 %collective-permute-done = bf16[1,32,2560]{2,1,0:T(8,128)(2,1)S(1)} collective-permute-done((bf16[1,32,2560]{2,1,0:T(8,128)(2,1)}, bf16[1,32,2560]{2,1,0:T(8,128)(2,1)S(1)}, u32[]{:S(2)}, u32[]{:S(2)}) %collective-permute-start) | collective-permute-done | bytes 163872 | tf_op jit(solution)/shard_map/while/body/eval_jaxpr/ppermute | solution.py:20
  39.7 5.3 %eval_jaxpr.5 = (bf16[32,2560]{1,0:T(8,128)(2,1)}, f32[1,1,128,2560]{3,2,1,0:T(8,128)}, bf16[32,256]{1,0:T(8,128)(2,1)}, bf16[4,1,1,32,2560]{4,3,2,1,0:T(8,128)(2,1)}, bf16[4,1,1,32,256]{4,3,2,1,0:T(8,128)(2,1)S(1)}) custom-call(s32[1]{0:T(128)} %bitcast.106.step_ref, ...), custom_call_target="tpu_custom_call", output_to_operand_aliasing={{1}: (13, {}), {3}: (16, {}), {4}: (17, {})} | custom-call | flops 146800640 | bytes 7536640 | tf_op jit(solution)/shard_map/while/body/eval_jaxpr/pallas_call | solution.py:228
  45.0 1.3 %collective-permute-start = (bf16[1,32,2560]{2,1,0:T(8,128)(2,1)}, bf16[1,32,2560]{2,1,0:T(8,128)(2,1)S(1)}, u32[]{:S(2)}, u32[]{:S(2)}) collective-permute-start(bf16[1,32,2560]{2,1,0:T(8,128)(2,1)} %bitcast.124), channel_id=1, source_target_pairs={{8,0},{16,8},{24,16},{9,1},{17,9},{25,17},{10,2},{18,10},{26,18},{... | collective-permute-start | bytes 491528 | tf_op jit(solution)/shard_map/while/body/eval_jaxpr/ppermute | solution.py:20
  46.3 6.7 %collective-permute-done = bf16[1,32,2560]{2,1,0:T(8,128)(2,1)S(1)} collective-permute-done((bf16[1,32,2560]{2,1,0:T(8,128)(2,1)}, bf16[1,32,2560]{2,1,0:T(8,128)(2,1)S(1)}, u32[]{:S(2)}, u32[]{:S(2)}) %collective-permute-start) | collective-permute-done | bytes 163872 | tf_op jit(solution)/shard_map/while/body/eval_jaxpr/ppermute | solution.py:20
  53.0 5.3 %eval_jaxpr.5 = (bf16[32,2560]{1,0:T(8,128)(2,1)}, f32[1,1,128,2560]{3,2,1,0:T(8,128)}, bf16[32,256]{1,0:T(8,128)(2,1)}, bf16[4,1,1,32,2560]{4,3,2,1,0:T(8,128)(2,1)}, bf16[4,1,1,32,256]{4,3,2,1,0:T(8,128)(2,1)S(1)}) custom-call(s32[1]{0:T(128)} %bitcast.106.step_ref, ...), custom_call_target="tpu_custom_call", output_to_operand_aliasing={{1}: (13, {}), {3}: (16, {}), {4}: (17, {})} | custom-call | flops 146800640 | bytes 7536640 | tf_op jit(solution)/shard_map/while/body/eval_jaxpr/pallas_call | solution.py:228
  58.3 1.3 %collective-permute-start = (bf16[1,32,2560]{2,1,0:T(8,128)(2,1)}, bf16[1,32,2560]{2,1,0:T(8,128)(2,1)S(1)}, u32[]{:S(2)}, u32[]{:S(2)}) collective-permute-start(bf16[1,32,2560]{2,1,0:T(8,128)(2,1)} %bitcast.124), channel_id=1, source_target_pairs={{8,0},{16,8},{24,16},{9,1},{17,9},{25,17},{10,2},{18,10},{26,18},{... | collective-permute-start | bytes 491528 | tf_op jit(solution)/shard_map/while/body/eval_jaxpr/ppermute | solution.py:20
  59.5 6.1 %collective-permute-done = bf16[1,32,2560]{2,1,0:T(8,128)(2,1)S(1)} collective-permute-done((bf16[1,32,2560]{2,1,0:T(8,128)(2,1)}, bf16[1,32,2560]{2,1,0:T(8,128)(2,1)S(1)}, u32[]{:S(2)}, u32[]{:S(2)}) %collective-permute-start) | collective-permute-done | bytes 163872 | tf_op jit(solution)/shard_map/while/body/eval_jaxpr/ppermute | solution.py:20
  65.7 5.3 %eval_jaxpr.5 = (bf16[32,2560]{1,0:T(8,128)(2,1)}, f32[1,1,128,2560]{3,2,1,0:T(8,128)}, bf16[32,256]{1,0:T(8,128)(2,1)}, bf16[4,1,1,32,2560]{4,3,2,1,0:T(8,128)(2,1)}, bf16[4,1,1,32,256]{4,3,2,1,0:T(8,128)(2,1)S(1)}) custom-call(s32[1]{0:T(128)} %bitcast.106.step_ref, ...), custom_call_target="tpu_custom_call", output_to_operand_aliasing={{1}: (13, {}), {3}: (16, {}), {4}: (17, {})} | custom-call | flops 146800640 | bytes 7536640 | tf_op jit(solution)/shard_map/while/body/eval_jaxpr/pallas_call | solution.py:228
  71.0 1.3 %collective-permute-start = (bf16[1,32,2560]{2,1,0:T(8,128)(2,1)}, bf16[1,32,2560]{2,1,0:T(8,128)(2,1)S(1)}, u32[]{:S(2)}, u32[]{:S(2)}) collective-permute-start(bf16[1,32,2560]{2,1,0:T(8,128)(2,1)} %bitcast.124), channel_id=1, source_target_pairs={{8,0},{16,8},{24,16},{9,1},{17,9},{25,17},{10,2},{18,10},{26,18},{... | collective-permute-start | bytes 491528 | tf_op jit(solution)/shard_map/while/body/eval_jaxpr/ppermute | solution.py:20
  72.3 6.1 %collective-permute-done = bf16[1,32,2560]{2,1,0:T(8,128)(2,1)S(1)} collective-permute-done((bf16[1,32,2560]{2,1,0:T(8,128)(2,1)}, bf16[1,32,2560]{2,1,0:T(8,128)(2,1)S(1)}, u32[]{:S(2)}, u32[]{:S(2)}) %collective-permute-start) | collective-permute-done | bytes 163872 | tf_op jit(solution)/shard_map/while/body/eval_jaxpr/ppermute | solution.py:20
  78.4 5.3 %eval_jaxpr.5 = (bf16[32,2560]{1,0:T(8,128)(2,1)}, f32[1,1,128,2560]{3,2,1,0:T(8,128)}, bf16[32,256]{1,0:T(8,128)(2,1)}, bf16[4,1,1,32,2560]{4,3,2,1,0:T(8,128)(2,1)}, bf16[4,1,1,32,256]{4,3,2,1,0:T(8,128)(2,1)S(1)}) custom-call(s32[1]{0:T(128)} %bitcast.106.step_ref, ...), custom_call_target="tpu_custom_call", output_to_operand_aliasing={{1}: (13, {}), {3}: (16, {}), {4}: (17, {})} | custom-call | flops 146800640 | bytes 7536640 | tf_op jit(solution)/shard_map/while/body/eval_jaxpr/pallas_call | solution.py:228
  83.7 1.3 %collective-permute-start = (bf16[1,32,2560]{2,1,0:T(8,128)(2,1)}, bf16[1,32,2560]{2,1,0:T(8,128)(2,1)S(1)}, u32[]{:S(2)}, u32[]{:S(2)}) collective-permute-start(bf16[1,32,2560]{2,1,0:T(8,128)(2,1)} %bitcast.124), channel_id=1, source_target_pairs={{8,0},{16,8},{24,16},{9,1},{17,9},{25,17},{10,2},{18,10},{26,18},{... | collective-permute-start | bytes 491528 | tf_op jit(solution)/shard_map/while/body/eval_jaxpr/ppermute | solution.py:20
  85.0 6.1 %collective-permute-done = bf16[1,32,2560]{2,1,0:T(8,128)(2,1)S(1)} collective-permute-done((bf16[1,32,2560]{2,1,0:T(8,128)(2,1)}, bf16[1,32,2560]{2,1,0:T(8,128)(2,1)S(1)}, u32[]{:S(2)}, u32[]{:S(2)}) %collective-permute-start) | collective-permute-done | bytes 163872 | tf_op jit(solution)/shard_map/while/body/eval_jaxpr/ppermute | solution.py:20
  91.1 5.3 %eval_jaxpr.5 = (bf16[32,2560]{1,0:T(8,128)(2,1)}, f32[1,1,128,2560]{3,2,1,0:T(8,128)}, bf16[32,256]{1,0:T(8,128)(2,1)}, bf16[4,1,1,32,2560]{4,3,2,1,0:T(8,128)(2,1)}, bf16[4,1,1,32,256]{4,3,2,1,0:T(8,128)(2,1)S(1)}) custom-call(s32[1]{0:T(128)} %bitcast.106.step_ref, ...), custom_call_target="tpu_custom_call", output_to_operand_aliasing={{1}: (13, {}), {3}: (16, {}), {4}: (17, {})} | custom-call | flops 146800640 | bytes 7536640 | tf_op jit(solution)/shard_map/while/body/eval_jaxpr/pallas_call | solution.py:228
  96.4 1.3 %collective-permute-start = (bf16[1,32,2560]{2,1,0:T(8,128)(2,1)}, bf16[1,32,2560]{2,1,0:T(8,128)(2,1)S(1)}, u32[]{:S(2)}, u32[]{:S(2)}) collective-permute-start(bf16[1,32,2560]{2,1,0:T(8,128)(2,1)} %bitcast.124), channel_id=1, source_target_pairs={{8,0},{16,8},{24,16},{9,1},{17,9},{25,17},{10,2},{18,10},{26,18},{... | collective-permute-start | bytes 491528 | tf_op jit(solution)/shard_map/while/body/eval_jaxpr/ppermute | solution.py:20
  97.7 6.1 %collective-permute-done = bf16[1,32,2560]{2,1,0:T(8,128)(2,1)S(1)} collective-permute-done((bf16[1,32,2560]{2,1,0:T(8,128)(2,1)}, bf16[1,32,2560]{2,1,0:T(8,128)(2,1)S(1)}, u32[]{:S(2)}, u32[]{:S(2)}) %collective-permute-start) | collective-permute-done | bytes 163872 | tf_op jit(solution)/shard_map/while/body/eval_jaxpr/ppermute | solution.py:20
  103.8 5.3 %shard_map.59 = (bf16[32,2560]{1,0:T(8,128)(2,1)}, f32[1,1,128,2560]{3,2,1,0:T(8,128)}, bf16[32,256]{1,0:T(8,128)(2,1)}, bf16[4,1,1,32,2560]{4,3,2,1,0:T(8,128)(2,1)}, bf16[4,1,1,32,256]{4,3,2,1,0:T(8,128)(2,1)S(1)}) custom-call(s32[1]{0:T(128)} %constant.45.clone.1.step_ref, ...), custom_call_target="tpu_custom_call", output_to_operand_aliasing={{1}: (13, {}), {3}: (16, {}), {4}: (17, {})} | custom-call | flops 146800640 | bytes 7536640 | tf_op jit(solution)/shard_map/pallas_call | solution.py:228
  109.1 9.8 %all_gather.3 = bf16[8,1,128,256]{3,2,1,0:T(8,128)(2,1)S(1)} all-gather(bf16[1,1,128,256]{3,2,1,0:T(8,128)(2,1)S(1)} %bitcast.115), channel_id=1, replica_groups=mesh['section'=4,'dp'=8] {'dp'}, dimensions={0}, use_global_device_ids=true | all-gather | bytes 589824 | tf_op jit(solution)/shard_map/all_gather | solution.py:367
  118.9 2.1 %fusion.8 = f32[1,320,256]{2,1,0:T(8,128)} fusion(bf16[8,1,128,320]{2,3,1,0:T(8,128)(2,1)} %all-to-all-done, bf16[8,1,128,256]{3,2,1,0:T(8,128)(2,1)S(1)} %all_gather.3), kind=kOutput, calls=%fused_computation.17 | convolution fusion | flops 167854080 | bytes 1507328 | tf_op jit(solution)/shard_map/glrd,glrc->ldc/dot_general | solution.py:368
  (37 shorter events, 3.0 us)
Async XLA Ops:
  0.6 7.6 %copy-start.1 = (bf16[1,1,128,2560]{3,2,1,0:T(8,128)(2,1)S(1)}, bf16[1,1,128,2560]{3,2,1,0:T(8,128)(2,1)}, u32[]{:S(2)}) copy-start(bf16[1,1,128,2560]{3,2,1,0:T(8,128)(2,1)} %param.6) | copy-start | bytes 1966084
  0.6 7.6 %copy-start = (bf16[1,2560,256]{2,1,0:T(8,128)(2,1)S(1)}, bf16[1,2560,256]{2,1,0:T(8,128)(2,1)}, u32[]{:S(2)}) copy-start(bf16[1,2560,256]{2,1,0:T(8,128)(2,1)} %w_ref.1) | copy-start | bytes 3932164
  3.0 115.9 %all-to-all-start = ((bf16[8,1,128,320]{2,3,1,0:T(8,128)(2,1)}), bf16[8,1,128,320]{2,3,1,0:T(8,128)(2,1)}, u32[]{:S(2)}, u32[]{:S(2)}) async-start(bf16[8,1,128,320]{2,3,1,0:T(8,128)(2,1)} %bitcast.30), calls=%async_computation | async-start | bytes 1310720 | tf_op jit(solution)/shard_map/all_to_all | solution.py:365
  8.2 1.2 copy-start.5
  11.6 4.4 %copy-start.3 = (f32[4,2560]{1,0:T(4,128)}, f32[4,2560]{1,0:T(4,128)S(1)}, u32[]{:S(2)}) copy-start(f32[4,2560]{1,0:T(4,128)S(1)} %fusion.18) | copy-start | bytes 122884
  13.4 2.6 %copy-start.2 = (bf16[4,32,2560]{2,1,0:T(8,128)(2,1)}, bf16[4,32,2560]{2,1,0:T(8,128)(2,1)S(1)}, u32[]{:S(2)}) copy-start(bf16[4,32,2560]{2,1,0:T(8,128)(2,1)S(1)} %get-tuple-element.338) | copy-start | bytes 1966084
  21.2 1.8 %copy-start.4 = (f32[4,2560]{1,0:T(4,128)S(1)}, f32[4,2560]{1,0:T(4,128)}, u32[]{:S(2)}) copy-start(f32[4,2560]{1,0:T(4,128)} %copy-done.3) | copy-start | bytes 122884
  30.8 8.9 %collective-permute-start = (bf16[1,32,2560]{2,1,0:T(8,128)(2,1)}, bf16[1,32,2560]{2,1,0:T(8,128)(2,1)S(1)}, u32[]{:S(2)}, u32[]{:S(2)}) collective-permute-start(bf16[1,32,2560]{2,1,0:T(8,128)(2,1)} %bitcast.124), channel_id=1, source_target_pairs={{8,0},{16,8},{24,16},{9,1},{17,9},{25,17},{10,2},{18,10},{26,18},{... | collective-permute-start | bytes 491528 | tf_op jit(solution)/shard_map/while/body/eval_jaxpr/ppermute | solution.py:20
  45.0 8.0 %collective-permute-start = (bf16[1,32,2560]{2,1,0:T(8,128)(2,1)}, bf16[1,32,2560]{2,1,0:T(8,128)(2,1)S(1)}, u32[]{:S(2)}, u32[]{:S(2)}) collective-permute-start(bf16[1,32,2560]{2,1,0:T(8,128)(2,1)} %bitcast.124), channel_id=1, source_target_pairs={{8,0},{16,8},{24,16},{9,1},{17,9},{25,17},{10,2},{18,10},{26,18},{... | collective-permute-start | bytes 491528 | tf_op jit(solution)/shard_map/while/body/eval_jaxpr/ppermute | solution.py:20
  58.3 7.4 %collective-permute-start = (bf16[1,32,2560]{2,1,0:T(8,128)(2,1)}, bf16[1,32,2560]{2,1,0:T(8,128)(2,1)S(1)}, u32[]{:S(2)}, u32[]{:S(2)}) collective-permute-start(bf16[1,32,2560]{2,1,0:T(8,128)(2,1)} %bitcast.124), channel_id=1, source_target_pairs={{8,0},{16,8},{24,16},{9,1},{17,9},{25,17},{10,2},{18,10},{26,18},{... | collective-permute-start | bytes 491528 | tf_op jit(solution)/shard_map/while/body/eval_jaxpr/ppermute | solution.py:20
  71.0 7.4 %collective-permute-start = (bf16[1,32,2560]{2,1,0:T(8,128)(2,1)}, bf16[1,32,2560]{2,1,0:T(8,128)(2,1)S(1)}, u32[]{:S(2)}, u32[]{:S(2)}) collective-permute-start(bf16[1,32,2560]{2,1,0:T(8,128)(2,1)} %bitcast.124), channel_id=1, source_target_pairs={{8,0},{16,8},{24,16},{9,1},{17,9},{25,17},{10,2},{18,10},{26,18},{... | collective-permute-start | bytes 491528 | tf_op jit(solution)/shard_map/while/body/eval_jaxpr/ppermute | solution.py:20
  83.7 7.4 %collective-permute-start = (bf16[1,32,2560]{2,1,0:T(8,128)(2,1)}, bf16[1,32,2560]{2,1,0:T(8,128)(2,1)S(1)}, u32[]{:S(2)}, u32[]{:S(2)}) collective-permute-start(bf16[1,32,2560]{2,1,0:T(8,128)(2,1)} %bitcast.124), channel_id=1, source_target_pairs={{8,0},{16,8},{24,16},{9,1},{17,9},{25,17},{10,2},{18,10},{26,18},{... | collective-permute-start | bytes 491528 | tf_op jit(solution)/shard_map/while/body/eval_jaxpr/ppermute | solution.py:20
  96.4 7.4 %collective-permute-start = (bf16[1,32,2560]{2,1,0:T(8,128)(2,1)}, bf16[1,32,2560]{2,1,0:T(8,128)(2,1)S(1)}, u32[]{:S(2)}, u32[]{:S(2)}) collective-permute-start(bf16[1,32,2560]{2,1,0:T(8,128)(2,1)} %bitcast.124), channel_id=1, source_target_pairs={{8,0},{16,8},{24,16},{9,1},{17,9},{25,17},{10,2},{18,10},{26,18},{... | collective-permute-start | bytes 491528 | tf_op jit(solution)/shard_map/while/body/eval_jaxpr/ppermute | solution.py:20

commit v20 on v19

--- a/solution.py
+++ b/solution.py
@@ -169,14 +169,15 @@
                 stacked[e * length:(e + 1) * length],
                 preferred_element_type=f32,
             )
-        rbb_q = jnp.dot(in_map, rb_t[:, cols], preferred_element_type=f32)
-        gx_ref[:, cols] = gx_q + tail_ref[:, cols] * rbb_q
+        gx_ref[:, cols] = gx_q
         pair_dots = lax.dot_general(stacked, x_q, nt, preferred_element_type=f32)
         mix_acc = mix_acc + dec_ref[q] * pair_dots
     mixing = mix_acc[0:length]
     for e in range(1, per_pair):
         mixing = mixing + mix_acc[e * length:(e + 1) * length]
     mixing = mixing.astype(bf16)
+    rbb = jnp.dot(in_map, rb_t, preferred_element_type=f32)
+    gx_ref[...] = gx_ref[...] + tail_ref[...] * rbb
     v = v_ref[...]
     lead_grads = (lead_ref[...] * v.astype(f32)).astype(bf16)
     grad_inmap = factor * lax.dot_general(mixing, out_map, tn, preferred_element_type=f32)

time: 121 us -> 121 us (level)
  transfers between devices with their start and end apart: 7 -> 7, of which waited for: 6 -> 6; matrix products, arithmetic and copies ran while one was open for 14% -> 14% of each run, Pallas kernels for 31% -> 30%
where the time goes in v20:
time: 121 us; the launch traced here: 120 us
  waiting for transfers between devices  38.8 us (32%)
  Pallas kernels  36.6 us (30%)
  starting transfers between devices  12.9 us (11%)
  blocking collectives  9.78 us (8%)
  matrix products  8.99 us (7%)
  other arithmetic  6.98 us (6%)
  local copies, waits for them, and re-layouts  5.69 us (5%)
    ppermute x6, waiting for transfers between devices, passed_along(): return lax.ppermute(block, axis, route)  38.8 us
    pallas_call x7, Pallas kernels, fused_step(): pl.pallas_call(functools.partial(step_kernel, factor=factor, width=width,...  36.6 us
    all_gather x1, blocking collectives, shards(): maps_all = lax.all_gather(maps_here, 'dp', axis=0, tiled=True)  9.78 us
    ppermute x6, starting transfers between devices, passed_along(): return lax.ppermute(block, axis, route)  7.68 us
    all_to_all x1, starting transfers between devices, shards(): rows_all = lax.all_to_all(rows_here, 'dp', 0, 0, tiled=True)  5.17 us
    dot_general x3, matrix products, per_lane(): jnp.einsum('...h,hd->...d', a, spread_heads, precision=lax.Precision.HIGH...  3.81 us
    dot_general x1, matrix products, shards(): jnp.einsum('mlsnj,mlsjd->mlsnd', jnp.swapaxes(in_blk[:MICRO - 1], -1, -2)...  2.57 us
    convert_element_type x1, other arithmetic, shards(): saved.append(state_now.astype(jnp.bfloat16)[None])  2.49 us
  transfers between devices with their start and end apart: 7, of which 6 were waited for; matrix products, arithmetic and copies ran while one was open for 14% of the time, Pallas kernels for 30%

profile of v20, /device:TPU:0, one launch (start us, length us, event | category | flops | bytes accessed | tf_op | source)
XLA Modules:
  0.0 120.5 jit_solution(17006942757611722218)
XLA Ops:
  0.7 2.4 %copy.32 = bf16[1,1,128,2560]{2,3,1,0:T(8,128)(2,1)} copy(bf16[1,1,128,2560]{3,2,1,0:T(8,128)(2,1)} %param.6) | data formatting | bytes 1310720 | tf_op args[0]
  3.0 5.2 %all-to-all-start = ((bf16[8,1,128,320]{2,3,1,0:T(8,128)(2,1)}), bf16[8,1,128,320]{2,3,1,0:T(8,128)(2,1)}, u32[]{:S(2)}, u32[]{:S(2)}) async-start(bf16[8,1,128,320]{2,3,1,0:T(8,128)(2,1)} %bitcast.30), calls=%async_computation | async-start | bytes 1310720 | tf_op jit(solution)/shard_map/all_to_all | solution.py:366
  9.6 1.8 %convolution_bitcast_fusion.lead_ref = f32[4,1,1,32,2560]{4,3,2,1,0:T(8,128)} fusion(s32[2560]{0:T(1024)S(1)} %add_select_fusion, f32[4,1,1,32,40]{4,3,2,1,0:T(8,128)S(1)} %reduce_window_sum.11), kind=kOutput, calls=%fused_computation | convolution fusion | flops 157388800 | bytes 1341440 | tf_op jit(solution)/shard_map/...h,hd->...d/dot_general | solution.py:293
  11.6 1.8 %fusion.4 = (bf16[4,32,2560]{2,1,0:T(8,128)(2,1)S(1)}, f32[4,32,2560]{2,1,0:T(8,128)}) fusion(bf16[4,32,2560]{2,1,0:T(8,128)(2,1)S(1)} %bitcast.110, s32[2560]{0:T(1024)S(1)} %add_select_fusion, f32[4,40]{1,0:T(4,128)S(1)} %bitcast.123, f32[4,1,1,32,40]{4,3,2,1,0:T(8,128)S(1)} %reduce_window_sum.11), kind=kOutput, calls=%fused_computation.12 | convolution fusion | flops 158376960 | bytes 2652800 | tf_op jit(solution)/shard_map/...h,hd->...d/dot_general | solution.py:293
  13.4 2.6 %fusion.16 = f32[3,128,2560]{2,1,0:T(8,128)} fusion(bf16[4,32,2560]{2,1,0:T(8,128)(2,1)S(1)} %get-tuple-element.338, bf16[4,1,1,32,256]{4,3,2,1,0:T(8,128)(2,1)S(1)} %bitcast.120), kind=kOutput, calls=%fused_computation.24 | convolution fusion | flops 62914560 | bytes 4448256 | tf_op jit(solution)/shard_map/mlsnj,mlsjd->mlsnd/dot_general | solution.py:303
  17.0 1.7 %multiply_convert_fusion.wt_ref = bf16[4,1,1,40,32,32]{5,4,3,2,1,0:T(8,128)(2,1)} fusion(f32[4,32,32]{2,1,0:T(8,128)S(1)} %convolution_multiply_fusion, f32[4,40,32]{2,1,0:T(8,128)S(1)} %copy.28, pred[32,32]{1,0:T(8,128)(4,1)S(1)} %iota_compare_fusion.3), kind=kLoop, calls=%fused_computation.3 | loop fusion | flops 819200 | bytes 365568 | tf_op jit(solution)/shard_map/vmap(vmap(vmap()))/convert_element_type | solution.py:128
  18.7 2.5 %fusion.23 = (bf16[1,1,1,128,2560]{4,3,2,1,0:T(8,128)(2,1)S(1)}, bf16[1,1,1,128,2560]{4,3,2,1,0:T(8,128)(2,1)S(1)}, bf16[1,1,1,128,2560]{4,3,2,1,0:T(8,128)(2,1)S(1)}) fusion(f32[3,128,2560]{2,1,0:T(8,128)} %fusion.16, f32[2560]{0:T(1024)S(1)} %get-tuple-element.296, f32[2560]{0:T(1024)S(1)} %get-tuple-element.294, f32[2560]{0:T(1024)S(1)} %get-tuple-element.295), kind=kLoop, calls=%fused_computation.30 | loop fusion | flops 2621440 | bytes 5928960 | tf_op jit(solution)/shard_map/convert_element_type | solution.py:313
  21.2 1.8 %pad_maximum_fusion.sb_ref = bf16[4,1,1,128,2560]{4,3,2,1,0:T(8,128)(2,1)} fusion(bf16[1,1,1,128,2560]{4,3,2,1,0:T(8,128)(2,1)S(1)} %get-tuple-element.334, bf16[1,1,1,128,2560]{4,3,2,1,0:T(8,128)(2,1)S(1)} %get-tuple-element.333, bf16[1,1,1,128,2560]{4,3,2,1,0:T(8,128)(2,1)S(1)} %get-tuple-element.335, bf16[4]{0:T(256)(128)(2,1)S(1)} %pad.clone), kind=kLoop, calls=%fused_computation.1 | loop fusion | flops 3932160 | bytes 4587528 | tf_op jit(solution)/shard_map/concatenate | solution.py:314
  23.4 1.2 broadcast.401
  24.6 0.9 broadcast_in_dim.99
  25.5 77.9 %while.19 = (s32[]{:T(128)}, bf16[1,32,2560]{2,1,0:T(8,128)(2,1)S(1)}, f32[1,1,128,2560]{3,2,1,0:T(8,128)}, bf16[4,1,1,32,2560]{4,3,2,1,0:T(8,128)(2,1)}, bf16[4...) while((s32[]{:T(128)}, ...), condition=%wide.region_2.3_spmd, body=%wide.region_1.2_spmd.sunk | while | flops 146800640 | bytes 8192213 | solution.py:355
  25.5 5.2 %eval_jaxpr.5 = (bf16[32,2560]{1,0:T(8,128)(2,1)}, f32[1,1,128,2560]{3,2,1,0:T(8,128)}, bf16[32,256]{1,0:T(8,128)(2,1)}, bf16[4,1,1,32,2560]{4,3,2,1,0:T(8,128)(2,1)}, bf16[4,1,1,32,256]{4,3,2,1,0:T(8,128)(2,1)S(1)}) custom-call(s32[1]{0:T(128)} %bitcast.106.step_ref, ...), custom_call_target="tpu_custom_call", output_to_operand_aliasing={{1}: (13, {}), {3}: (16, {}), {4}: (17, {})} | custom-call | flops 146800640 | bytes 7536640 | tf_op jit(solution)/shard_map/while/body/eval_jaxpr/pallas_call | solution.py:229
  30.7 1.3 %collective-permute-start = (bf16[1,32,2560]{2,1,0:T(8,128)(2,1)}, bf16[1,32,2560]{2,1,0:T(8,128)(2,1)S(1)}, u32[]{:S(2)}, u32[]{:S(2)}) collective-permute-start(bf16[1,32,2560]{2,1,0:T(8,128)(2,1)} %bitcast.124), channel_id=1, source_target_pairs={{8,0},{16,8},{24,16},{9,1},{17,9},{25,17},{10,2},{18,10},{26,18},{... | collective-permute-start | bytes 491528 | tf_op jit(solution)/shard_map/while/body/eval_jaxpr/ppermute | solution.py:20
  32.0 7.6 %collective-permute-done = bf16[1,32,2560]{2,1,0:T(8,128)(2,1)S(1)} collective-permute-done((bf16[1,32,2560]{2,1,0:T(8,128)(2,1)}, bf16[1,32,2560]{2,1,0:T(8,128)(2,1)S(1)}, u32[]{:S(2)}, u32[]{:S(2)}) %collective-permute-start) | collective-permute-done | bytes 163872 | tf_op jit(solution)/shard_map/while/body/eval_jaxpr/ppermute | solution.py:20
  39.6 5.2 %eval_jaxpr.5 = (bf16[32,2560]{1,0:T(8,128)(2,1)}, f32[1,1,128,2560]{3,2,1,0:T(8,128)}, bf16[32,256]{1,0:T(8,128)(2,1)}, bf16[4,1,1,32,2560]{4,3,2,1,0:T(8,128)(2,1)}, bf16[4,1,1,32,256]{4,3,2,1,0:T(8,128)(2,1)S(1)}) custom-call(s32[1]{0:T(128)} %bitcast.106.step_ref, ...), custom_call_target="tpu_custom_call", output_to_operand_aliasing={{1}: (13, {}), {3}: (16, {}), {4}: (17, {})} | custom-call | flops 146800640 | bytes 7536640 | tf_op jit(solution)/shard_map/while/body/eval_jaxpr/pallas_call | solution.py:229
  44.8 1.3 %collective-permute-start = (bf16[1,32,2560]{2,1,0:T(8,128)(2,1)}, bf16[1,32,2560]{2,1,0:T(8,128)(2,1)S(1)}, u32[]{:S(2)}, u32[]{:S(2)}) collective-permute-start(bf16[1,32,2560]{2,1,0:T(8,128)(2,1)} %bitcast.124), channel_id=1, source_target_pairs={{8,0},{16,8},{24,16},{9,1},{17,9},{25,17},{10,2},{18,10},{26,18},{... | collective-permute-start | bytes 491528 | tf_op jit(solution)/shard_map/while/body/eval_jaxpr/ppermute | solution.py:20
  46.1 6.7 %collective-permute-done = bf16[1,32,2560]{2,1,0:T(8,128)(2,1)S(1)} collective-permute-done((bf16[1,32,2560]{2,1,0:T(8,128)(2,1)}, bf16[1,32,2560]{2,1,0:T(8,128)(2,1)S(1)}, u32[]{:S(2)}, u32[]{:S(2)}) %collective-permute-start) | collective-permute-done | bytes 163872 | tf_op jit(solution)/shard_map/while/body/eval_jaxpr/ppermute | solution.py:20
  52.8 5.2 %eval_jaxpr.5 = (bf16[32,2560]{1,0:T(8,128)(2,1)}, f32[1,1,128,2560]{3,2,1,0:T(8,128)}, bf16[32,256]{1,0:T(8,128)(2,1)}, bf16[4,1,1,32,2560]{4,3,2,1,0:T(8,128)(2,1)}, bf16[4,1,1,32,256]{4,3,2,1,0:T(8,128)(2,1)S(1)}) custom-call(s32[1]{0:T(128)} %bitcast.106.step_ref, ...), custom_call_target="tpu_custom_call", output_to_operand_aliasing={{1}: (13, {}), {3}: (16, {}), {4}: (17, {})} | custom-call | flops 146800640 | bytes 7536640 | tf_op jit(solution)/shard_map/while/body/eval_jaxpr/pallas_call | solution.py:229
  58.0 1.3 %collective-permute-start = (bf16[1,32,2560]{2,1,0:T(8,128)(2,1)}, bf16[1,32,2560]{2,1,0:T(8,128)(2,1)S(1)}, u32[]{:S(2)}, u32[]{:S(2)}) collective-permute-start(bf16[1,32,2560]{2,1,0:T(8,128)(2,1)} %bitcast.124), channel_id=1, source_target_pairs={{8,0},{16,8},{24,16},{9,1},{17,9},{25,17},{10,2},{18,10},{26,18},{... | collective-permute-start | bytes 491528 | tf_op jit(solution)/shard_map/while/body/eval_jaxpr/ppermute | solution.py:20
  59.3 6.1 %collective-permute-done = bf16[1,32,2560]{2,1,0:T(8,128)(2,1)S(1)} collective-permute-done((bf16[1,32,2560]{2,1,0:T(8,128)(2,1)}, bf16[1,32,2560]{2,1,0:T(8,128)(2,1)S(1)}, u32[]{:S(2)}, u32[]{:S(2)}) %collective-permute-start) | collective-permute-done | bytes 163872 | tf_op jit(solution)/shard_map/while/body/eval_jaxpr/ppermute | solution.py:20
  65.4 5.2 %eval_jaxpr.5 = (bf16[32,2560]{1,0:T(8,128)(2,1)}, f32[1,1,128,2560]{3,2,1,0:T(8,128)}, bf16[32,256]{1,0:T(8,128)(2,1)}, bf16[4,1,1,32,2560]{4,3,2,1,0:T(8,128)(2,1)}, bf16[4,1,1,32,256]{4,3,2,1,0:T(8,128)(2,1)S(1)}) custom-call(s32[1]{0:T(128)} %bitcast.106.step_ref, ...), custom_call_target="tpu_custom_call", output_to_operand_aliasing={{1}: (13, {}), {3}: (16, {}), {4}: (17, {})} | custom-call | flops 146800640 | bytes 7536640 | tf_op jit(solution)/shard_map/while/body/eval_jaxpr/pallas_call | solution.py:229
  70.7 1.3 %collective-permute-start = (bf16[1,32,2560]{2,1,0:T(8,128)(2,1)}, bf16[1,32,2560]{2,1,0:T(8,128)(2,1)S(1)}, u32[]{:S(2)}, u32[]{:S(2)}) collective-permute-start(bf16[1,32,2560]{2,1,0:T(8,128)(2,1)} %bitcast.124), channel_id=1, source_target_pairs={{8,0},{16,8},{24,16},{9,1},{17,9},{25,17},{10,2},{18,10},{26,18},{... | collective-permute-start | bytes 491528 | tf_op jit(solution)/shard_map/while/body/eval_jaxpr/ppermute | solution.py:20
  72.0 6.1 %collective-permute-done = bf16[1,32,2560]{2,1,0:T(8,128)(2,1)S(1)} collective-permute-done((bf16[1,32,2560]{2,1,0:T(8,128)(2,1)}, bf16[1,32,2560]{2,1,0:T(8,128)(2,1)S(1)}, u32[]{:S(2)}, u32[]{:S(2)}) %collective-permute-start) | collective-permute-done | bytes 163872 | tf_op jit(solution)/shard_map/while/body/eval_jaxpr/ppermute | solution.py:20
  78.1 5.2 %eval_jaxpr.5 = (bf16[32,2560]{1,0:T(8,128)(2,1)}, f32[1,1,128,2560]{3,2,1,0:T(8,128)}, bf16[32,256]{1,0:T(8,128)(2,1)}, bf16[4,1,1,32,2560]{4,3,2,1,0:T(8,128)(2,1)}, bf16[4,1,1,32,256]{4,3,2,1,0:T(8,128)(2,1)S(1)}) custom-call(s32[1]{0:T(128)} %bitcast.106.step_ref, ...), custom_call_target="tpu_custom_call", output_to_operand_aliasing={{1}: (13, {}), {3}: (16, {}), {4}: (17, {})} | custom-call | flops 146800640 | bytes 7536640 | tf_op jit(solution)/shard_map/while/body/eval_jaxpr/pallas_call | solution.py:229
  83.3 1.3 %collective-permute-start = (bf16[1,32,2560]{2,1,0:T(8,128)(2,1)}, bf16[1,32,2560]{2,1,0:T(8,128)(2,1)S(1)}, u32[]{:S(2)}, u32[]{:S(2)}) collective-permute-start(bf16[1,32,2560]{2,1,0:T(8,128)(2,1)} %bitcast.124), channel_id=1, source_target_pairs={{8,0},{16,8},{24,16},{9,1},{17,9},{25,17},{10,2},{18,10},{26,18},{... | collective-permute-start | bytes 491528 | tf_op jit(solution)/shard_map/while/body/eval_jaxpr/ppermute | solution.py:20
  84.6 6.1 %collective-permute-done = bf16[1,32,2560]{2,1,0:T(8,128)(2,1)S(1)} collective-permute-done((bf16[1,32,2560]{2,1,0:T(8,128)(2,1)}, bf16[1,32,2560]{2,1,0:T(8,128)(2,1)S(1)}, u32[]{:S(2)}, u32[]{:S(2)}) %collective-permute-start) | collective-permute-done | bytes 163872 | tf_op jit(solution)/shard_map/while/body/eval_jaxpr/ppermute | solution.py:20
  90.7 5.2 %eval_jaxpr.5 = (bf16[32,2560]{1,0:T(8,128)(2,1)}, f32[1,1,128,2560]{3,2,1,0:T(8,128)}, bf16[32,256]{1,0:T(8,128)(2,1)}, bf16[4,1,1,32,2560]{4,3,2,1,0:T(8,128)(2,1)}, bf16[4,1,1,32,256]{4,3,2,1,0:T(8,128)(2,1)S(1)}) custom-call(s32[1]{0:T(128)} %bitcast.106.step_ref, ...), custom_call_target="tpu_custom_call", output_to_operand_aliasing={{1}: (13, {}), {3}: (16, {}), {4}: (17, {})} | custom-call | flops 146800640 | bytes 7536640 | tf_op jit(solution)/shard_map/while/body/eval_jaxpr/pallas_call | solution.py:229
  95.9 1.3 %collective-permute-start = (bf16[1,32,2560]{2,1,0:T(8,128)(2,1)}, bf16[1,32,2560]{2,1,0:T(8,128)(2,1)S(1)}, u32[]{:S(2)}, u32[]{:S(2)}) collective-permute-start(bf16[1,32,2560]{2,1,0:T(8,128)(2,1)} %bitcast.124), channel_id=1, source_target_pairs={{8,0},{16,8},{24,16},{9,1},{17,9},{25,17},{10,2},{18,10},{26,18},{... | collective-permute-start | bytes 491528 | tf_op jit(solution)/shard_map/while/body/eval_jaxpr/ppermute | solution.py:20
  97.2 6.1 %collective-permute-done = bf16[1,32,2560]{2,1,0:T(8,128)(2,1)S(1)} collective-permute-done((bf16[1,32,2560]{2,1,0:T(8,128)(2,1)}, bf16[1,32,2560]{2,1,0:T(8,128)(2,1)S(1)}, u32[]{:S(2)}, u32[]{:S(2)}) %collective-permute-start) | collective-permute-done | bytes 163872 | tf_op jit(solution)/shard_map/while/body/eval_jaxpr/ppermute | solution.py:20
  103.3 5.2 %shard_map.59 = (bf16[32,2560]{1,0:T(8,128)(2,1)}, f32[1,1,128,2560]{3,2,1,0:T(8,128)}, bf16[32,256]{1,0:T(8,128)(2,1)}, bf16[4,1,1,32,2560]{4,3,2,1,0:T(8,128)(2,1)}, bf16[4,1,1,32,256]{4,3,2,1,0:T(8,128)(2,1)S(1)}) custom-call(s32[1]{0:T(128)} %constant.45.clone.1.step_ref, ...), custom_call_target="tpu_custom_call", output_to_operand_aliasing={{1}: (13, {}), {3}: (16, {}), {4}: (17, {})} | custom-call | flops 146800640 | bytes 7536640 | tf_op jit(solution)/shard_map/pallas_call | solution.py:229
  108.6 9.8 %all_gather.3 = bf16[8,1,128,256]{3,2,1,0:T(8,128)(2,1)S(1)} all-gather(bf16[1,1,128,256]{3,2,1,0:T(8,128)(2,1)S(1)} %bitcast.115), channel_id=1, replica_groups=mesh['section'=4,'dp'=8] {'dp'}, dimensions={0}, use_global_device_ids=true | all-gather | bytes 589824 | tf_op jit(solution)/shard_map/all_gather | solution.py:368
  118.3 2.1 %fusion.8 = f32[1,320,256]{2,1,0:T(8,128)} fusion(bf16[8,1,128,320]{2,3,1,0:T(8,128)(2,1)} %all-to-all-done, bf16[8,1,128,256]{3,2,1,0:T(8,128)(2,1)S(1)} %all_gather.3), kind=kOutput, calls=%fused_computation.17 | convolution fusion | flops 167854080 | bytes 1507328 | tf_op jit(solution)/shard_map/glrd,glrc->ldc/dot_general | solution.py:369
  (37 shorter events, 3.0 us)
Async XLA Ops:
  0.6 7.6 %copy-start.1 = (bf16[1,1,128,2560]{3,2,1,0:T(8,128)(2,1)S(1)}, bf16[1,1,128,2560]{3,2,1,0:T(8,128)(2,1)}, u32[]{:S(2)}) copy-start(bf16[1,1,128,2560]{3,2,1,0:T(8,128)(2,1)} %param.6) | copy-start | bytes 1966084
  0.6 7.6 %copy-start = (bf16[1,2560,256]{2,1,0:T(8,128)(2,1)S(1)}, bf16[1,2560,256]{2,1,0:T(8,128)(2,1)}, u32[]{:S(2)}) copy-start(bf16[1,2560,256]{2,1,0:T(8,128)(2,1)} %w_ref.1) | copy-start | bytes 3932164
  3.0 115.3 %all-to-all-start = ((bf16[8,1,128,320]{2,3,1,0:T(8,128)(2,1)}), bf16[8,1,128,320]{2,3,1,0:T(8,128)(2,1)}, u32[]{:S(2)}, u32[]{:S(2)}) async-start(bf16[8,1,128,320]{2,3,1,0:T(8,128)(2,1)} %bitcast.30), calls=%async_computation | async-start | bytes 1310720 | tf_op jit(solution)/shard_map/all_to_all | solution.py:366
  8.2 1.2 copy-start.5
  11.6 4.4 %copy-start.3 = (f32[4,2560]{1,0:T(4,128)}, f32[4,2560]{1,0:T(4,128)S(1)}, u32[]{:S(2)}) copy-start(f32[4,2560]{1,0:T(4,128)S(1)} %fusion.18) | copy-start | bytes 122884
  13.4 2.6 %copy-start.2 = (bf16[4,32,2560]{2,1,0:T(8,128)(2,1)}, bf16[4,32,2560]{2,1,0:T(8,128)(2,1)S(1)}, u32[]{:S(2)}) copy-start(bf16[4,32,2560]{2,1,0:T(8,128)(2,1)S(1)} %get-tuple-element.338) | copy-start | bytes 1966084
  21.2 1.8 %copy-start.4 = (f32[4,2560]{1,0:T(4,128)S(1)}, f32[4,2560]{1,0:T(4,128)}, u32[]{:S(2)}) copy-start(f32[4,2560]{1,0:T(4,128)} %copy-done.3) | copy-start | bytes 122884
  30.7 8.9 %collective-permute-start = (bf16[1,32,2560]{2,1,0:T(8,128)(2,1)}, bf16[1,32,2560]{2,1,0:T(8,128)(2,1)S(1)}, u32[]{:S(2)}, u32[]{:S(2)}) collective-permute-start(bf16[1,32,2560]{2,1,0:T(8,128)(2,1)} %bitcast.124), channel_id=1, source_target_pairs={{8,0},{16,8},{24,16},{9,1},{17,9},{25,17},{10,2},{18,10},{26,18},{... | collective-permute-start | bytes 491528 | tf_op jit(solution)/shard_map/while/body/eval_jaxpr/ppermute | solution.py:20
  44.8 8.0 %collective-permute-start = (bf16[1,32,2560]{2,1,0:T(8,128)(2,1)}, bf16[1,32,2560]{2,1,0:T(8,128)(2,1)S(1)}, u32[]{:S(2)}, u32[]{:S(2)}) collective-permute-start(bf16[1,32,2560]{2,1,0:T(8,128)(2,1)} %bitcast.124), channel_id=1, source_target_pairs={{8,0},{16,8},{24,16},{9,1},{17,9},{25,17},{10,2},{18,10},{26,18},{... | collective-permute-start | bytes 491528 | tf_op jit(solution)/shard_map/while/body/eval_jaxpr/ppermute | solution.py:20
  58.0 7.4 %collective-permute-start = (bf16[1,32,2560]{2,1,0:T(8,128)(2,1)}, bf16[1,32,2560]{2,1,0:T(8,128)(2,1)S(1)}, u32[]{:S(2)}, u32[]{:S(2)}) collective-permute-start(bf16[1,32,2560]{2,1,0:T(8,128)(2,1)} %bitcast.124), channel_id=1, source_target_pairs={{8,0},{16,8},{24,16},{9,1},{17,9},{25,17},{10,2},{18,10},{26,18},{... | collective-permute-start | bytes 491528 | tf_op jit(solution)/shard_map/while/body/eval_jaxpr/ppermute | solution.py:20
  70.7 7.4 %collective-permute-start = (bf16[1,32,2560]{2,1,0:T(8,128)(2,1)}, bf16[1,32,2560]{2,1,0:T(8,128)(2,1)S(1)}, u32[]{:S(2)}, u32[]{:S(2)}) collective-permute-start(bf16[1,32,2560]{2,1,0:T(8,128)(2,1)} %bitcast.124), channel_id=1, source_target_pairs={{8,0},{16,8},{24,16},{9,1},{17,9},{25,17},{10,2},{18,10},{26,18},{... | collective-permute-start | bytes 491528 | tf_op jit(solution)/shard_map/while/body/eval_jaxpr/ppermute | solution.py:20
  83.3 7.4 %collective-permute-start = (bf16[1,32,2560]{2,1,0:T(8,128)(2,1)}, bf16[1,32,2560]{2,1,0:T(8,128)(2,1)S(1)}, u32[]{:S(2)}, u32[]{:S(2)}) collective-permute-start(bf16[1,32,2560]{2,1,0:T(8,128)(2,1)} %bitcast.124), channel_id=1, source_target_pairs={{8,0},{16,8},{24,16},{9,1},{17,9},{25,17},{10,2},{18,10},{26,18},{... | collective-permute-start | bytes 491528 | tf_op jit(solution)/shard_map/while/body/eval_jaxpr/ppermute | solution.py:20
  95.9 7.4 %collective-permute-start = (bf16[1,32,2560]{2,1,0:T(8,128)(2,1)}, bf16[1,32,2560]{2,1,0:T(8,128)(2,1)S(1)}, u32[]{:S(2)}, u32[]{:S(2)}) collective-permute-start(bf16[1,32,2560]{2,1,0:T(8,128)(2,1)} %bitcast.124), channel_id=1, source_target_pairs={{8,0},{16,8},{24,16},{9,1},{17,9},{25,17},{10,2},{18,10},{26,18},{... | collective-permute-start | bytes 491528 | tf_op jit(solution)/shard_map/while/body/eval_jaxpr/ppermute | solution.py:20
